TPU v7x, 256 devices: a whole 4x4x8 slice. The times are simulated.
256 devices in a mesh: grp: 4 (over x_lo, core), gx: 16 (over z, x_hi), gy: 4 (over y).
Axes of the slice: x: 4 (x_hi: 2, x_lo: 2; x = x_hi * 2 + x_lo), y: 4, z: 8, core: 2. Of those that a mesh axis runs over, the one named last changes fastest.
Arguments:
- conc: float32 [4, 32, 1024, 1024], P('grp', None, 'gx', 'gy'), may hold values from 0 to 1
- velocity: bfloat16 [3, 4, 32, 1024, 1024], P(None, 'grp', None, 'gx', 'gy'), may hold values from -0.119628906 to 0.119628906
- porosity: bfloat16 [4, 32, 1024, 1024], P('grp', None, 'gx', 'gy'), may hold values from 0.099609375 to 0.3984375
- saturation: bfloat16 [4, 32, 1024, 1024], P('grp', None, 'gx', 'gy'), may hold values from 0.29882812 to 1
- layer_counts: int32 [8], replicated, may hold values from 1 to 24, 96 in all
- electrodes: int32 [4, 2], replicated, may hold values from 0 to 2097151
- init_potential: float32 [4, 8, 512, 512], P(None, None, 'gx', 'gy'), may hold values from -6 to 6
Outputs:
- conc_next: float32 [4, 32, 1024, 1024], P('grp', None, 'gx', 'gy')
- conductivity: float32 [8, 512, 512], P(None, 'gx', 'gy')
- potential: float32 [4, 8, 512, 512], P('grp', None, 'gx', 'gy')
Inputs may be any that keep to these rules, and one draw needn't show every extreme that they name: layer_counts sums to 96; its largest entry is exactly 24.
All inputs are finite; a program needn't handle non-finite values.
Results may differ from a plain program's by a relative error of at most 0.0014.
Values may be sent and summed in bfloat16 or wider, within the bound.
No kernel may reach another device: no remote copies, remote signals or barrier semaphores. Data moves between devices by JAX's collectives and lax.ppermute only.
A program may use at most 128 MiB of HBM per device.

v0:
```python
import jax
import jax.numpy as jnp
from jax import lax
from jax.sharding import PartitionSpec as P

SWEEPS = 3


KAPPA = 0.06
OMEGA = 0.8
AMPLITUDE = 40.0
ARCHIE = 20.0


def with_halo(shard, sides, width):
    for axis, dim in sides:
        devices, length = (lax.axis_size(axis), shard.shape[dim])
        up = [(i, (i + 1) % devices) for i in range(devices - 1)]
        down = [(j, i) for i, j in up]
        last = lax.slice_in_dim(shard, length - width, length, axis=dim)
        initial = lax.slice_in_dim(shard, 0, width, axis=dim)
        before = lax.ppermute(last, axis, up)
        after = lax.ppermute(initial, axis, down)
        shard = jnp.concatenate([before, shard, after], axis=dim)
    return shard


def neighbours(padded, direction_index):
    leading = [slice(None)] * (padded.ndim - 3)
    middle = [slice(1, -1)] * 3
    below_slices = list(middle)
    below_slices[direction_index] = slice(0, -2)
    above_slices = list(middle)
    above_slices[direction_index] = slice(2, None)
    return (padded[tuple(leading + below_slices)], padded[tuple(leading + above_slices)])


def tendency(padded, speeds):
    center = padded[1:-1, 1:-1, 1:-1]
    running = -6.0 * KAPPA * center
    for direction_index in range(3):
        below_cells, above_cells = neighbours(padded, direction_index)
        speed_comp = speeds[direction_index]
        running = (
            running
            + KAPPA * (below_cells + above_cells)
            - (
                jnp.maximum(speed_comp, 0.0) * (center - below_cells)
                + jnp.minimum(speed_comp, 0.0) * (above_cells - center)
            )
        )
    return running


def section_halo(values):
    return with_halo(values, (("grp", 0), ("gx", 1), ("gy", 2)), 1)


def potential_halo(values):
    return with_halo(values, (("gx", 2), ("gy", 3)), 1)


def face_terms(cond_padded, center):
    faces = []
    diagonal = jnp.zeros_like(center)
    for direction_index in range(3):
        below_cells, above_cells = neighbours(cond_padded, direction_index)
        face_below = 0.5 * (center + below_cells)
        face_above = 0.5 * (center + above_cells)
        faces.append((face_below, face_above))
        diagonal = diagonal + face_below + face_above
    return (faces, diagonal)


def sweep_once(potential, faces, diagonal, source_terms, pot_wide):
    coupled = jnp.zeros_like(potential)
    for direction_index in range(3):
        below_cells, above_cells = neighbours(pot_wide, direction_index)
        coupled = (
            coupled
            + faces[direction_index][0] * below_cells
            + faces[direction_index][1] * above_cells
        )
    applied = diagonal * potential - coupled
    return potential + OMEGA * (source_terms - applied) / diagonal


def on_device(conc, velocity, porosity, saturation, layer_counts, electrodes, init_potential):
    group_index = lax.axis_index("grp")
    row_index = lax.axis_index("gx")
    column_index = lax.axis_index("gy")
    active = group_index < 3
    field = jnp.where(active, conc[0], 0.0)
    speeds = velocity[:, 0].astype(jnp.float32)
    layers, tile_x, tile_y = field.shape
    section_one = jnp.where(active, field + tendency(section_halo(field), speeds), 0.0)
    advanced = 0.5 * (field + section_one + tendency(section_halo(section_one), speeds))
    advanced = jnp.where(active, advanced, 0.0)
    poro = porosity[0].astype(jnp.float32)
    water = saturation[0].astype(jnp.float32)
    sigma = ARCHIE * jnp.exp(advanced) * poro * poro * water * water
    coarse_x = tile_x // 2
    coarse_y = tile_y // 2
    coarse = sigma.reshape(layers, coarse_x, 2, coarse_y, 2).sum(axis=(2, 4))
    ends = jnp.cumsum(layer_counts)
    starts = ends - layer_counts
    layer_ids = group_index * layers + jnp.arange(layers, dtype=jnp.int32)
    member = (
        (layer_ids[None, :] >= starts[:, None]) & (layer_ids[None, :] < ends[:, None]) & active
    ).astype(jnp.float32)
    weights = member / (4.0 * layer_counts.astype(jnp.float32))[:, None]
    resist_layers = layer_counts.shape[0]
    partial_cond = jnp.dot(
        weights, coarse.reshape(layers, coarse_x * coarse_y), precision=lax.Precision.HIGHEST
    ).reshape(resist_layers, coarse_x, coarse_y)
    conductivity = lax.psum(partial_cond, "grp")
    grid_x = coarse_x * lax.axis_size("gx")
    grid_y = coarse_y * lax.axis_size("gy")
    potential = lax.dynamic_slice_in_dim(init_potential, group_index, 1, 0)
    poles = lax.dynamic_slice_in_dim(electrodes, group_index, 1, 0)
    cond_padded = jnp.pad(
        with_halo(conductivity, (("gx", 1), ("gy", 2)), 1), ((1, 1), (0, 0), (0, 0))
    )
    faces, diagonal = face_terms(cond_padded, conductivity)
    flat_ids = (
        jnp.arange(resist_layers, dtype=jnp.int32)[:, None, None] * (grid_x * grid_y)
        + (row_index * coarse_x + jnp.arange(coarse_x, dtype=jnp.int32))[None, :, None] * grid_y
        + (column_index * coarse_y + jnp.arange(coarse_y, dtype=jnp.int32))[None, None, :]
    )
    source_terms = AMPLITUDE * (
        (flat_ids[None] == poles[:, 0, None, None, None]).astype(jnp.float32)
        - (flat_ids[None] == poles[:, 1, None, None, None]).astype(jnp.float32)
    )
    for sweep_index in range(SWEEPS):
        pot_wide = jnp.pad(potential_halo(potential), ((0, 0), (1, 1), (0, 0), (0, 0)))
        potential = sweep_once(potential, faces, diagonal, source_terms, pot_wide)
    return (advanced[None], conductivity, potential)


def solution(mesh):
    in_specs = (
        P("grp", None, "gx", "gy"),
        P(None, "grp", None, "gx", "gy"),
        P("grp", None, "gx", "gy"),
        P("grp", None, "gx", "gy"),
        P(),
        P(),
        P(None, None, "gx", "gy"),
    )
    out_specs = (P("grp", None, "gx", "gy"), P(None, "gx", "gy"), P("grp", None, "gx", "gy"))
    return jax.shard_map(
        on_device, mesh=mesh, in_specs=in_specs, out_specs=out_specs, check_vma=False
    )
```

profile of v0, /device:TPU:102, one launch (start us, length us, event | category | flops | bytes accessed | tf_op | source)
XLA Modules:
  0.0 271.1 jit_solution(4352050345593786454)
XLA Ops:
  11.0 3.6 %collective-permute-start.1 = (f32[1,64,256]{2,1,0:T(8,128)S(1)}, f32[1,64,256]{2,1,0:T(8,128)S(1)}, u32[]{:S(2)}, u32[]{:S(2)}) collective-permute-start(f32[1,64,256]{2,1,0:T(8,128)S(1)} %get-tuple-element.28), channel_id=1, source_target_pairs={{64,0},{128,64},{192,128},{65,1},{129,65},{193,129},{66,2},{130,66... | collective-permute-start | bytes 196616 | tf_op jit(solution)/shard_map/ppermute | solution.py:23
  15.3 5.9 %collective-permute-start.16 = (f32[1,8,1,128]{3,1,2,0:T(8,128)S(1)}, f32[1,8,1,128]{3,1,2,0:T(8,128)S(1)}, u32[]{:S(2)}, u32[]{:S(2)}) collective-permute-start(f32[1,8,1,128]{3,1,2,0:T(8,128)S(1)} %get-tuple-element.44), channel_id=1, source_target_pairs={{0,4},{4,8},{8,12},{12,16},{16,20},{20,24},{24,28},{28,32},{32,36}... | collective-permute-start | bytes 12296 | tf_op jit(solution)/shard_map/ppermute | solution.py:22
  27.2 7.5 %collective-permute-start.2 = (f32[34,1,256]{2,1,0:T(1,128)S(1)}, f32[34,1,256]{2,1,0:T(1,128)S(1)}, u32[]{:S(2)}, u32[]{:S(2)}) collective-permute-start(f32[34,1,256]{2,1,0:T(1,128)S(1)} %get-tuple-element.23), channel_id=1, source_target_pairs={{0,4},{4,8},{8,12},{12,16},{16,20},{20,24},{24,28},{28,32},{32,36}... | collective-permute-start | bytes 104456 | tf_op jit(solution)/shard_map/ppermute | solution.py:22
  36.8 7.4 %collective-permute-done.3 = f32[34,1,256]{2,1,0:T(1,128)S(1)} collective-permute-done((f32[34,1,256]{2,1,0:T(1,128)S(1)}, f32[34,1,256]{2,1,0:T(1,128)S(1)}, u32[]{:S(2)}, u32[]{:S(2)}) %collective-permute-start.3) | collective-permute-done | bytes 34848 | tf_op jit(solution)/shard_map/ppermute | solution.py:23
  48.2 3.5 %collective-permute-start.4 = (f32[34,66,1]{1,2,0:T(1,128)S(1)}, f32[34,66,1]{1,2,0:T(1,128)S(1)}, u32[]{:S(2)}, u32[]{:S(2)}) collective-permute-start(f32[34,66,1]{1,2,0:T(1,128)S(1)} %copy.29), channel_id=1, source_target_pairs={{0,1},{1,2},{2,3},{4,5},{5,6},{6,7},{8,9},{9,10},{10,11},{12,13},{... | collective-permute-start | bytes 26936 | tf_op jit(solution)/shard_map/ppermute | solution.py:22
  54.1 5.5 %convert_element_type.50 = f32[3,1,32,64,256]{4,3,2,1,0:T(8,128)} convert(bf16[3,1,32,64,256]{4,3,2,1,0:T(8,128)(2,1)} %param.8) | non-fusion elementwise | flops 1572864 | bytes 9437184 | tf_op jit(solution)/shard_map/convert_element_type | solution.py:94
  62.8 14.5 %fusion.31 = f32[32,64,256]{2,1,0:T(8,128)S(1)} fusion(f32[32,64,256]{2,1,0:T(8,128)} %copy-done.1, f32[34,1,256]{2,1,0:T(1,128)S(1)} %collective-permute-done.3, f32[1,64,256]{2,1,0:T(8,128)S(1)} %collective-permute-done.1, f32[1,64,256]{2,1,0:T(8,128)S(1)} %collective-permute-done, f32[34,1,256]{2,1,0:T(1,128)S(1)} %collective-permute-done.2, ...), kind=kLoop, calls=%fused_computation.66 | loop fusion | flops 28311552 | bytes 10704417 | tf_op jit(solution)/shard_map/jit(_where)/select_n | solution.py:96
  79.2 3.6 %collective-permute-start.7 = (f32[1,64,256]{2,1,0:T(8,128)S(1)}, f32[1,64,256]{2,1,0:T(8,128)S(1)}, u32[]{:S(2)}, u32[]{:S(2)}) collective-permute-start(f32[1,64,256]{2,1,0:T(8,128)S(1)} %get-tuple-element.26), channel_id=1, source_target_pairs={{64,0},{128,64},{192,128},{65,1},{129,65},{193,129},{66,2},{130,66... | collective-permute-start | bytes 196616 | tf_op jit(solution)/shard_map/ppermute | solution.py:23
  86.7 5.4 %collective-permute-start.9 = (f32[34,1,256]{2,1,0:T(1,128)S(1)}, f32[34,1,256]{2,1,0:T(1,128)S(1)}, u32[]{:S(2)}, u32[]{:S(2)}) collective-permute-start(f32[34,1,256]{2,1,0:T(1,128)S(1)} %get-tuple-element.22), channel_id=1, source_target_pairs={{4,0},{8,4},{12,8},{16,12},{20,16},{24,20},{28,24},{32,28},{36,32}... | collective-permute-start | bytes 104456 | tf_op jit(solution)/shard_map/ppermute | solution.py:23
  92.7 3.4 %collective-permute-done.9 = f32[34,1,256]{2,1,0:T(1,128)S(1)} collective-permute-done((f32[34,1,256]{2,1,0:T(1,128)S(1)}, f32[34,1,256]{2,1,0:T(1,128)S(1)}, u32[]{:S(2)}, u32[]{:S(2)}) %collective-permute-start.9) | collective-permute-done | bytes 34848 | tf_op jit(solution)/shard_map/ppermute | solution.py:23
  100.1 4.6 %collective-permute-start.10 = (f32[34,66,1]{1,2,0:T(1,128)S(1)}, f32[34,66,1]{1,2,0:T(1,128)S(1)}, u32[]{:S(2)}, u32[]{:S(2)}) collective-permute-start(f32[34,66,1]{1,2,0:T(1,128)S(1)} %copy.33), channel_id=1, source_target_pairs={{0,1},{1,2},{2,3},{4,5},{5,6},{6,7},{8,9},{9,10},{10,11},{12,13},{... | collective-permute-start | bytes 26936 | tf_op jit(solution)/shard_map/ppermute | solution.py:22
  109.4 2.6 collective-permute-done.11
  113.6 11.8 %multiply_multiply_fusion = (f32[32,64,256]{2,1,0:T(8,128)}, f32[32,64,256]{2,1,0:T(8,128)}) fusion(bf16[1,32,64,256]{3,2,1,0:T(8,128)(2,1)} %param.10, bf16[1,32,64,256]{3,2,1,0:T(8,128)(2,1)} %param.9, f32[32,64,256]{2,1,0:T(8,128)S(1)} %fusion.31, f32[3,1,32,64,256]{4,3,2,1,0:T(8,128)} %convert_element_type.50, f32[34,66,1]{2,1,0:T(8,128)} %copy.36, ...), kind=kLoop, calls=%fused_computation | loop fusion | flops 33554432 | bytes 16996896 | tf_op jit(solution)/shard_map/mul | solution.py:101
  125.4 6.4 %copy.37 = f32[32,64,256]{0,2,1:T(8,128)} copy(f32[32,64,256]{2,1,0:T(8,128)} %get-tuple-element.15) | data formatting | bytes 4194304 | tf_op jit(solution)/shard_map/mul | solution.py:101
  131.8 9.5 %reduce_sum.9 = f32[32,32,128]{0,2,1:T(8,128)S(1)} reduce(f32[32,32,2,128,2]{0,4,3,2,1:T(2,128)} %bitcast.106, f32[]{:T(128)} %constant.8.clone.1), dimensions={2,4}, to_apply=%region_1.2 | reduce | flops 393216 | bytes 2621444 | tf_op jit(solution)/shard_map/reduce_sum | solution.py:104
  143.8 38.9 %all-reduce.6.cloned.1.call-done = f32[8,32,128]{2,0,1:T(8,128)} async-done(((f32[8,32,128]{2,0,1:T(8,128)}), f32[8,32,128]{2,0,1:T(8,128)}) %all-reduce.6.cloned.1.call-update) | async-done | bytes 131088 | tf_op jit(solution)/shard_map/psum | solution.py:116
  183.4 5.3 %collective-permute-start.12 = (f32[8,1,128]{2,0,1:T(8,128)S(1)}, f32[8,1,128]{2,0,1:T(8,128)S(1)}, u32[]{:S(2)}, u32[]{:S(2)}) collective-permute-start(f32[8,1,128]{2,0,1:T(8,128)S(1)} %get-tuple-element.42), channel_id=1, source_target_pairs={{0,4},{4,8},{8,12},{12,16},{16,20},{20,24},{24,28},{28,32},{32,36}... | collective-permute-start | bytes 12296 | tf_op jit(solution)/shard_map/ppermute | solution.py:22
  188.8 3.4 %collective-permute-start.18 = (f32[1,8,34,1]{3,1,2,0:T(8,128)S(1)}, f32[1,8,34,1]{3,1,2,0:T(8,128)S(1)}, u32[]{:S(2)}, u32[]{:S(2)}) collective-permute-start(f32[1,8,34,1]{3,1,2,0:T(8,128)S(1)} %get-tuple-element.35), channel_id=1, source_target_pairs={{0,1},{1,2},{2,3},{4,5},{5,6},{6,7},{8,9},{9,10},{10,11},{12,13},{... | collective-permute-start | bytes 3272 | tf_op jit(solution)/shard_map/ppermute | solution.py:22
  193.5 2.0 collective-permute-start.13
  196.5 6.1 %collective-permute-done.13 = f32[8,1,128]{2,0,1:T(8,128)S(1)} collective-permute-done((f32[8,1,128]{2,0,1:T(8,128)S(1)}, f32[8,1,128]{2,0,1:T(8,128)S(1)}, u32[]{:S(2)}, u32[]{:S(2)}) %collective-permute-start.13) | collective-permute-done | bytes 4128 | tf_op jit(solution)/shard_map/ppermute | solution.py:23
  202.8 4.6 %collective-permute-start.14 = (f32[8,34,1]{2,0,1:T(8,128)S(1)}, f32[8,34,1]{2,0,1:T(8,128)S(1)}, u32[]{:S(2)}, u32[]{:S(2)}) collective-permute-start(f32[8,34,1]{2,0,1:T(8,128)S(1)} %get-tuple-element.33), channel_id=1, source_target_pairs={{0,1},{1,2},{2,3},{4,5},{5,6},{6,7},{8,9},{9,10},{10,11},{12,13},{... | collective-permute-start | bytes 3272 | tf_op jit(solution)/shard_map/ppermute | solution.py:22
  209.9 4.4 %collective-permute-done.15 = f32[8,34,1]{2,0,1:T(8,128)S(1)} collective-permute-done((f32[8,34,1]{2,0,1:T(8,128)S(1)}, f32[8,34,1]{2,0,1:T(8,128)S(1)}, u32[]{:S(2)}, u32[]{:S(2)}) %collective-permute-start.15) | collective-permute-done | bytes 1120 | tf_op jit(solution)/shard_map/ppermute | solution.py:23
  216.4 2.1 collective-permute-start.20
  218.5 5.2 %collective-permute-start.21 = (f32[1,8,1,128]{3,1,2,0:T(8,128)S(1)}, f32[1,8,1,128]{3,1,2,0:T(8,128)S(1)}, u32[]{:S(2)}, u32[]{:S(2)}) collective-permute-start(f32[1,8,1,128]{3,1,2,0:T(8,128)S(1)} %get-tuple-element.40), channel_id=1, source_target_pairs={{4,0},{8,4},{12,8},{16,12},{20,16},{24,20},{28,24},{32,28},{36,32}... | collective-permute-start | bytes 12296 | tf_op jit(solution)/shard_map/ppermute | solution.py:23
  223.8 3.9 %collective-permute-done.21 = f32[1,8,1,128]{3,1,2,0:T(8,128)S(1)} collective-permute-done((f32[1,8,1,128]{3,1,2,0:T(8,128)S(1)}, f32[1,8,1,128]{3,1,2,0:T(8,128)S(1)}, u32[]{:S(2)}, u32[]{:S(2)}) %collective-permute-start.21) | collective-permute-done | bytes 4128 | tf_op jit(solution)/shard_map/ppermute | solution.py:23
  227.7 3.4 %collective-permute-start.22 = (f32[1,8,34,1]{3,1,2,0:T(8,128)S(1)}, f32[1,8,34,1]{3,1,2,0:T(8,128)S(1)}, u32[]{:S(2)}, u32[]{:S(2)}) collective-permute-start(f32[1,8,34,1]{3,1,2,0:T(8,128)S(1)} %get-tuple-element.31), channel_id=1, source_target_pairs={{0,1},{1,2},{2,3},{4,5},{5,6},{6,7},{8,9},{9,10},{10,11},{12,13},{... | collective-permute-start | bytes 3272 | tf_op jit(solution)/shard_map/ppermute | solution.py:22
  233.7 4.4 %collective-permute-done.23 = f32[1,8,34,1]{3,1,2,0:T(8,128)S(1)} collective-permute-done((f32[1,8,34,1]{3,1,2,0:T(8,128)S(1)}, f32[1,8,34,1]{3,1,2,0:T(8,128)S(1)}, u32[]{:S(2)}, u32[]{:S(2)}) %collective-permute-start.23) | collective-permute-done | bytes 1120 | tf_op jit(solution)/shard_map/ppermute | solution.py:23
  240.2 2.0 collective-permute-start.24
  242.2 5.4 %collective-permute-start.25 = (f32[1,8,1,128]{3,1,2,0:T(8,128)S(1)}, f32[1,8,1,128]{3,1,2,0:T(8,128)S(1)}, u32[]{:S(2)}, u32[]{:S(2)}) collective-permute-start(f32[1,8,1,128]{3,1,2,0:T(8,128)S(1)} %get-tuple-element.38), channel_id=1, source_target_pairs={{4,0},{8,4},{12,8},{16,12},{20,16},{24,20},{28,24},{32,28},{36,32}... | collective-permute-start | bytes 12296 | tf_op jit(solution)/shard_map/ppermute | solution.py:23
  247.6 3.7 %collective-permute-done.25 = f32[1,8,1,128]{3,1,2,0:T(8,128)S(1)} collective-permute-done((f32[1,8,1,128]{3,1,2,0:T(8,128)S(1)}, f32[1,8,1,128]{3,1,2,0:T(8,128)S(1)}, u32[]{:S(2)}, u32[]{:S(2)}) %collective-permute-start.25) | collective-permute-done | bytes 4128 | tf_op jit(solution)/shard_map/ppermute | solution.py:23
  251.4 3.1 %collective-permute-start.26 = (f32[1,8,34,1]{3,1,2,0:T(8,128)S(1)}, f32[1,8,34,1]{3,1,2,0:T(8,128)S(1)}, u32[]{:S(2)}, u32[]{:S(2)}) collective-permute-start(f32[1,8,34,1]{3,1,2,0:T(8,128)S(1)} %get-tuple-element.29), channel_id=1, source_target_pairs={{0,1},{1,2},{2,3},{4,5},{5,6},{6,7},{8,9},{9,10},{10,11},{12,13},{... | collective-permute-start | bytes 3272 | tf_op jit(solution)/shard_map/ppermute | solution.py:22
  257.1 4.4 %collective-permute-done.27 = f32[1,8,34,1]{3,1,2,0:T(8,128)S(1)} collective-permute-done((f32[1,8,34,1]{3,1,2,0:T(8,128)S(1)}, f32[1,8,34,1]{3,1,2,0:T(8,128)S(1)}, u32[]{:S(2)}, u32[]{:S(2)}) %collective-permute-start.27) | collective-permute-done | bytes 1120 | tf_op jit(solution)/shard_map/ppermute | solution.py:23
  (107 shorter events, 58.9 us)
Async XLA Ops:
  7.2 175.5 %all-reduce.6.cloned.1.call-start = ((), (), s32[]{:S(2)}) async-start(), calls=%async_computation | async-start | bytes 262144 | tf_op jit(solution)/shard_map/psum | solution.py:116
  9.0 18.1 %collective-permute-start = (f32[1,64,256]{2,1,0:T(8,128)S(1)}, f32[1,64,256]{2,1,0:T(8,128)S(1)}, u32[]{:S(2)}, u32[]{:S(2)}) collective-permute-start(f32[1,64,256]{2,1,0:T(8,128)S(1)} %get-tuple-element.27), channel_id=1, source_target_pairs={{0,64},{64,128},{128,192},{1,65},{65,129},{129,193},{2,66},{66,130... | collective-permute-start | bytes 196616 | tf_op jit(solution)/shard_map/ppermute | solution.py:22
  11.0 16.2 %collective-permute-start.1 = (f32[1,64,256]{2,1,0:T(8,128)S(1)}, f32[1,64,256]{2,1,0:T(8,128)S(1)}, u32[]{:S(2)}, u32[]{:S(2)}) collective-permute-start(f32[1,64,256]{2,1,0:T(8,128)S(1)} %get-tuple-element.28), channel_id=1, source_target_pairs={{64,0},{128,64},{192,128},{65,1},{129,65},{193,129},{66,2},{130,66... | collective-permute-start | bytes 196616 | tf_op jit(solution)/shard_map/ppermute | solution.py:23
  15.3 92.5 %collective-permute-start.16 = (f32[1,8,1,128]{3,1,2,0:T(8,128)S(1)}, f32[1,8,1,128]{3,1,2,0:T(8,128)S(1)}, u32[]{:S(2)}, u32[]{:S(2)}) collective-permute-start(f32[1,8,1,128]{3,1,2,0:T(8,128)S(1)} %get-tuple-element.44), channel_id=1, source_target_pairs={{0,4},{4,8},{8,12},{12,16},{16,20},{20,24},{24,28},{28,32},{32,36}... | collective-permute-start | bytes 12296 | tf_op jit(solution)/shard_map/ppermute | solution.py:22
  21.2 122.6 %collective-permute-start.17 = (f32[1,8,1,128]{3,1,2,0:T(8,128)}, f32[1,8,1,128]{3,1,2,0:T(8,128)S(1)}, u32[]{:S(2)}, u32[]{:S(2)}) collective-permute-start(f32[1,8,1,128]{3,1,2,0:T(8,128)} %get-tuple-element.43), channel_id=1, source_target_pairs={{4,0},{8,4},{12,8},{16,12},{20,16},{24,20},{28,24},{32,28},{36,32}... | collective-permute-start | bytes 12296 | tf_op jit(solution)/shard_map/ppermute | solution.py:23
  27.2 9.6 %collective-permute-start.2 = (f32[34,1,256]{2,1,0:T(1,128)S(1)}, f32[34,1,256]{2,1,0:T(1,128)S(1)}, u32[]{:S(2)}, u32[]{:S(2)}) collective-permute-start(f32[34,1,256]{2,1,0:T(1,128)S(1)} %get-tuple-element.23), channel_id=1, source_target_pairs={{0,4},{4,8},{8,12},{12,16},{16,20},{20,24},{24,28},{28,32},{32,36}... | collective-permute-start | bytes 104456 | tf_op jit(solution)/shard_map/ppermute | solution.py:22
  34.8 9.4 %collective-permute-start.3 = (f32[34,1,256]{2,1,0:T(1,128)S(1)}, f32[34,1,256]{2,1,0:T(1,128)S(1)}, u32[]{:S(2)}, u32[]{:S(2)}) collective-permute-start(f32[34,1,256]{2,1,0:T(1,128)S(1)} %get-tuple-element.24), channel_id=1, source_target_pairs={{4,0},{8,4},{12,8},{16,12},{20,16},{24,20},{28,24},{32,28},{36,32}... | collective-permute-start | bytes 104456 | tf_op jit(solution)/shard_map/ppermute | solution.py:23
  48.2 11.3 %collective-permute-start.4 = (f32[34,66,1]{1,2,0:T(1,128)S(1)}, f32[34,66,1]{1,2,0:T(1,128)S(1)}, u32[]{:S(2)}, u32[]{:S(2)}) collective-permute-start(f32[34,66,1]{1,2,0:T(1,128)S(1)} %copy.29), channel_id=1, source_target_pairs={{0,1},{1,2},{2,3},{4,5},{5,6},{6,7},{8,9},{9,10},{10,11},{12,13},{... | collective-permute-start | bytes 26936 | tf_op jit(solution)/shard_map/ppermute | solution.py:22
  52.2 8.9 %collective-permute-start.5 = (f32[34,66,1]{1,2,0:T(1,128)S(1)}, f32[34,66,1]{1,2,0:T(1,128)S(1)}, u32[]{:S(2)}, u32[]{:S(2)}) collective-permute-start(f32[34,66,1]{1,2,0:T(1,128)S(1)} %copy.31), channel_id=1, source_target_pairs={{1,0},{2,1},{3,2},{5,4},{6,5},{7,6},{9,8},{10,9},{11,10},{13,12},{... | collective-permute-start | bytes 26936 | tf_op jit(solution)/shard_map/ppermute | solution.py:23
  77.3 6.1 %collective-permute-start.6 = (f32[1,64,256]{2,1,0:T(8,128)S(1)}, f32[1,64,256]{2,1,0:T(8,128)S(1)}, u32[]{:S(2)}, u32[]{:S(2)}) collective-permute-start(f32[1,64,256]{2,1,0:T(8,128)S(1)} %get-tuple-element.25), channel_id=1, source_target_pairs={{0,64},{64,128},{128,192},{1,65},{65,129},{129,193},{2,66},{66,130... | collective-permute-start | bytes 196616 | tf_op jit(solution)/shard_map/ppermute | solution.py:22
  79.2 5.5 %collective-permute-start.7 = (f32[1,64,256]{2,1,0:T(8,128)S(1)}, f32[1,64,256]{2,1,0:T(8,128)S(1)}, u32[]{:S(2)}, u32[]{:S(2)}) collective-permute-start(f32[1,64,256]{2,1,0:T(8,128)S(1)} %get-tuple-element.26), channel_id=1, source_target_pairs={{64,0},{128,64},{192,128},{65,1},{129,65},{193,129},{66,2},{130,66... | collective-permute-start | bytes 196616 | tf_op jit(solution)/shard_map/ppermute | solution.py:23
  84.8 8.0 %collective-permute-start.8 = (f32[34,1,256]{2,1,0:T(1,128)S(1)}, f32[34,1,256]{2,1,0:T(1,128)S(1)}, u32[]{:S(2)}, u32[]{:S(2)}) collective-permute-start(f32[34,1,256]{2,1,0:T(1,128)S(1)} %get-tuple-element.21), channel_id=1, source_target_pairs={{0,4},{4,8},{8,12},{12,16},{16,20},{20,24},{24,28},{28,32},{32,36}... | collective-permute-start | bytes 104456 | tf_op jit(solution)/shard_map/ppermute | solution.py:22
  86.7 9.4 %collective-permute-start.9 = (f32[34,1,256]{2,1,0:T(1,128)S(1)}, f32[34,1,256]{2,1,0:T(1,128)S(1)}, u32[]{:S(2)}, u32[]{:S(2)}) collective-permute-start(f32[34,1,256]{2,1,0:T(1,128)S(1)} %get-tuple-element.22), channel_id=1, source_target_pairs={{4,0},{8,4},{12,8},{16,12},{20,16},{24,20},{28,24},{32,28},{36,32}... | collective-permute-start | bytes 104456 | tf_op jit(solution)/shard_map/ppermute | solution.py:23
  100.1 7.8 %collective-permute-start.10 = (f32[34,66,1]{1,2,0:T(1,128)S(1)}, f32[34,66,1]{1,2,0:T(1,128)S(1)}, u32[]{:S(2)}, u32[]{:S(2)}) collective-permute-start(f32[34,66,1]{1,2,0:T(1,128)S(1)} %copy.33), channel_id=1, source_target_pairs={{0,1},{1,2},{2,3},{4,5},{5,6},{6,7},{8,9},{9,10},{10,11},{12,13},{... | collective-permute-start | bytes 26936 | tf_op jit(solution)/shard_map/ppermute | solution.py:22
  106.4 5.7 %collective-permute-start.11 = (f32[34,66,1]{1,2,0:T(1,128)S(1)}, f32[34,66,1]{1,2,0:T(1,128)S(1)}, u32[]{:S(2)}, u32[]{:S(2)}) collective-permute-start(f32[34,66,1]{1,2,0:T(1,128)S(1)} %copy.35), channel_id=1, source_target_pairs={{1,0},{2,1},{3,2},{5,4},{6,5},{7,6},{9,8},{10,9},{11,10},{13,12},{... | collective-permute-start | bytes 26936 | tf_op jit(solution)/shard_map/ppermute | solution.py:23
  141.9 72.7 %copy-start.4 = (s32[8,32]{0,1:T(8,128)S(1)}, s32[8,32]{0,1:T(8,128)}, u32[]{:S(2)}) copy-start(s32[8,32]{0,1:T(8,128)} %broadcast_add_fusion) | copy-start | bytes 3076
  141.9 72.7 %copy-start.5 = (s32[128]{0:T(128)S(1)}, s32[128]{0:T(128)}, u32[]{:S(2)}) copy-start(s32[128]{0:T(128)} %iota_add_fusion) | copy-start | bytes 1540
  182.7 31.9 %copy-start.3 = (f32[8,32,128]{2,0,1:T(8,128)S(1)}, f32[8,32,128]{2,0,1:T(8,128)}, u32[]{:S(2)}) copy-start(f32[8,32,128]{2,0,1:T(8,128)} %all-reduce.6.cloned.1.call-done) | copy-start | bytes 393220
  183.4 12.2 %collective-permute-start.12 = (f32[8,1,128]{2,0,1:T(8,128)S(1)}, f32[8,1,128]{2,0,1:T(8,128)S(1)}, u32[]{:S(2)}, u32[]{:S(2)}) collective-permute-start(f32[8,1,128]{2,0,1:T(8,128)S(1)} %get-tuple-element.42), channel_id=1, source_target_pairs={{0,4},{4,8},{8,12},{12,16},{16,20},{20,24},{24,28},{28,32},{32,36}... | collective-permute-start | bytes 12296 | tf_op jit(solution)/shard_map/ppermute | solution.py:22
  188.8 19.8 %collective-permute-start.18 = (f32[1,8,34,1]{3,1,2,0:T(8,128)S(1)}, f32[1,8,34,1]{3,1,2,0:T(8,128)S(1)}, u32[]{:S(2)}, u32[]{:S(2)}) collective-permute-start(f32[1,8,34,1]{3,1,2,0:T(8,128)S(1)} %get-tuple-element.35), channel_id=1, source_target_pairs={{0,1},{1,2},{2,3},{4,5},{5,6},{6,7},{8,9},{9,10},{10,11},{12,13},{... | collective-permute-start | bytes 3272 | tf_op jit(solution)/shard_map/ppermute | solution.py:22
  192.2 16.4 %collective-permute-start.19 = (f32[1,8,34,1]{3,1,2,0:T(8,128)S(1)}, f32[1,8,34,1]{3,1,2,0:T(8,128)S(1)}, u32[]{:S(2)}, u32[]{:S(2)}) collective-permute-start(f32[1,8,34,1]{3,1,2,0:T(8,128)S(1)} %get-tuple-element.36), channel_id=1, source_target_pairs={{1,0},{2,1},{3,2},{5,4},{6,5},{7,6},{9,8},{10,9},{11,10},{13,12},{... | collective-permute-start | bytes 3272 | tf_op jit(solution)/shard_map/ppermute | solution.py:23
  193.5 9.1 %collective-permute-start.13 = (f32[8,1,128]{2,0,1:T(8,128)S(1)}, f32[8,1,128]{2,0,1:T(8,128)S(1)}, u32[]{:S(2)}, u32[]{:S(2)}) collective-permute-start(f32[8,1,128]{2,0,1:T(8,128)S(1)} %get-tuple-element.41), channel_id=1, source_target_pairs={{4,0},{8,4},{12,8},{16,12},{20,16},{24,20},{28,24},{32,28},{36,32}... | collective-permute-start | bytes 12296 | tf_op jit(solution)/shard_map/ppermute | solution.py:23
  202.8 7.1 %collective-permute-start.14 = (f32[8,34,1]{2,0,1:T(8,128)S(1)}, f32[8,34,1]{2,0,1:T(8,128)S(1)}, u32[]{:S(2)}, u32[]{:S(2)}) collective-permute-start(f32[8,34,1]{2,0,1:T(8,128)S(1)} %get-tuple-element.33), channel_id=1, source_target_pairs={{0,1},{1,2},{2,3},{4,5},{5,6},{6,7},{8,9},{9,10},{10,11},{12,13},{... | collective-permute-start | bytes 3272 | tf_op jit(solution)/shard_map/ppermute | solution.py:22
  207.3 6.9 %collective-permute-start.15 = (f32[8,34,1]{2,0,1:T(8,128)S(1)}, f32[8,34,1]{2,0,1:T(8,128)S(1)}, u32[]{:S(2)}, u32[]{:S(2)}) collective-permute-start(f32[8,34,1]{2,0,1:T(8,128)S(1)} %get-tuple-element.34), channel_id=1, source_target_pairs={{1,0},{2,1},{3,2},{5,4},{6,5},{7,6},{9,8},{10,9},{11,10},{13,12},{... | collective-permute-start | bytes 3272 | tf_op jit(solution)/shard_map/ppermute | solution.py:23
  216.4 7.4 %collective-permute-start.20 = (f32[1,8,1,128]{3,1,2,0:T(8,128)S(1)}, f32[1,8,1,128]{3,1,2,0:T(8,128)S(1)}, u32[]{:S(2)}, u32[]{:S(2)}) collective-permute-start(f32[1,8,1,128]{3,1,2,0:T(8,128)S(1)} %get-tuple-element.39), channel_id=1, source_target_pairs={{0,4},{4,8},{8,12},{12,16},{16,20},{20,24},{24,28},{28,32},{32,36}... | collective-permute-start | bytes 12296 | tf_op jit(solution)/shard_map/ppermute | solution.py:22
  218.5 9.1 %collective-permute-start.21 = (f32[1,8,1,128]{3,1,2,0:T(8,128)S(1)}, f32[1,8,1,128]{3,1,2,0:T(8,128)S(1)}, u32[]{:S(2)}, u32[]{:S(2)}) collective-permute-start(f32[1,8,1,128]{3,1,2,0:T(8,128)S(1)} %get-tuple-element.40), channel_id=1, source_target_pairs={{4,0},{8,4},{12,8},{16,12},{20,16},{24,20},{28,24},{32,28},{36,32}... | collective-permute-start | bytes 12296 | tf_op jit(solution)/shard_map/ppermute | solution.py:23
  227.7 6.0 %collective-permute-start.22 = (f32[1,8,34,1]{3,1,2,0:T(8,128)S(1)}, f32[1,8,34,1]{3,1,2,0:T(8,128)S(1)}, u32[]{:S(2)}, u32[]{:S(2)}) collective-permute-start(f32[1,8,34,1]{3,1,2,0:T(8,128)S(1)} %get-tuple-element.31), channel_id=1, source_target_pairs={{0,1},{1,2},{2,3},{4,5},{5,6},{6,7},{8,9},{9,10},{10,11},{12,13},{... | collective-permute-start | bytes 3272 | tf_op jit(solution)/shard_map/ppermute | solution.py:22
  231.1 6.9 %collective-permute-start.23 = (f32[1,8,34,1]{3,1,2,0:T(8,128)S(1)}, f32[1,8,34,1]{3,1,2,0:T(8,128)S(1)}, u32[]{:S(2)}, u32[]{:S(2)}) collective-permute-start(f32[1,8,34,1]{3,1,2,0:T(8,128)S(1)} %get-tuple-element.32), channel_id=1, source_target_pairs={{1,0},{2,1},{3,2},{5,4},{6,5},{7,6},{9,8},{10,9},{11,10},{13,12},{... | collective-permute-start | bytes 3272 | tf_op jit(solution)/shard_map/ppermute | solution.py:23
  240.2 7.4 %collective-permute-start.24 = (f32[1,8,1,128]{3,1,2,0:T(8,128)S(1)}, f32[1,8,1,128]{3,1,2,0:T(8,128)S(1)}, u32[]{:S(2)}, u32[]{:S(2)}) collective-permute-start(f32[1,8,1,128]{3,1,2,0:T(8,128)S(1)} %get-tuple-element.37), channel_id=1, source_target_pairs={{0,4},{4,8},{8,12},{12,16},{16,20},{20,24},{24,28},{28,32},{32,36}... | collective-permute-start | bytes 12296 | tf_op jit(solution)/shard_map/ppermute | solution.py:22
  242.2 9.1 %collective-permute-start.25 = (f32[1,8,1,128]{3,1,2,0:T(8,128)S(1)}, f32[1,8,1,128]{3,1,2,0:T(8,128)S(1)}, u32[]{:S(2)}, u32[]{:S(2)}) collective-permute-start(f32[1,8,1,128]{3,1,2,0:T(8,128)S(1)} %get-tuple-element.38), channel_id=1, source_target_pairs={{4,0},{8,4},{12,8},{16,12},{20,16},{24,20},{28,24},{32,28},{36,32}... | collective-permute-start | bytes 12296 | tf_op jit(solution)/shard_map/ppermute | solution.py:23
  251.4 5.7 %collective-permute-start.26 = (f32[1,8,34,1]{3,1,2,0:T(8,128)S(1)}, f32[1,8,34,1]{3,1,2,0:T(8,128)S(1)}, u32[]{:S(2)}, u32[]{:S(2)}) collective-permute-start(f32[1,8,34,1]{3,1,2,0:T(8,128)S(1)} %get-tuple-element.29), channel_id=1, source_target_pairs={{0,1},{1,2},{2,3},{4,5},{5,6},{6,7},{8,9},{9,10},{10,11},{12,13},{... | collective-permute-start | bytes 3272 | tf_op jit(solution)/shard_map/ppermute | solution.py:22
  254.5 6.9 %collective-permute-start.27 = (f32[1,8,34,1]{3,1,2,0:T(8,128)S(1)}, f32[1,8,34,1]{3,1,2,0:T(8,128)S(1)}, u32[]{:S(2)}, u32[]{:S(2)}) collective-permute-start(f32[1,8,34,1]{3,1,2,0:T(8,128)S(1)} %get-tuple-element.30), channel_id=1, source_target_pairs={{1,0},{2,1},{3,2},{5,4},{6,5},{7,6},{9,8},{10,9},{11,10},{13,12},{... | collective-permute-start | bytes 3272 | tf_op jit(solution)/shard_map/ppermute | solution.py:23
  (6 other events, 48.7 us)
Sparse Core Ops, SparseCore 0:
  143.8 38.8 all-reduce.5
where the time goes:
time: 274 us; the launch traced here: 271 us
  starting transfers between devices  88.2 us (32%)
  waiting for transfers between devices  83.4 us (30%)
  other arithmetic  55.4 us (20%)
  local copies, waits for them, and re-layouts  27.6 us (10%)
  between operations  14.6 us (5%)
    ppermute x14, starting transfers between devices, with_halo(): before = lax.ppermute(last, axis, up)  51.1 us
    ppermute x14, waiting for transfers between devices, with_halo(): after = lax.ppermute(initial, axis, down)  41.6 us
    psum x1, waiting for transfers between devices, on_device(): conductivity = lax.psum(partial_cond, 'grp')  38.9 us
    ppermute x14, starting transfers between devices, with_halo(): after = lax.ppermute(initial, axis, down)  37.1 us
    select_n x1, other arithmetic, on_device(): jnp.where(active, field + tendency(section_halo(field), speeds), 0.0)  14.5 us
    mul x1, other arithmetic, on_device(): sigma = ARCHIE * jnp.exp(advanced) * poro * poro * water * water  11.8 us
    reduce_sum x1, other arithmetic, on_device(): coarse = sigma.reshape(layers, coarse_x, 2, coarse_y, 2).sum(axis=(2, 4))  9.53 us
    mul x1, local copies, waits for them, and re-layouts, on_device(): sigma = ARCHIE * jnp.exp(advanced) * poro * poro * water * water  6.37 us
  transfers between devices with their start and end apart: 29, of which 14 were waited for; matrix products, arithmetic and copies ran while one was open for 28% of the time, Pallas kernels for 0%

commit v1 on v0

v1 whole, which is shorter than its diff:
```python
import jax
import jax.numpy as jnp
from jax import lax
from jax.sharding import PartitionSpec as P

SWEEPS = 3


KAPPA = 0.06
OMEGA = 0.8
AMPLITUDE = 40.0
ARCHIE = 20.0


def with_halo(shard, sides, width, top=None):
    for axis, dim in sides:
        devices, length = (lax.axis_size(axis), shard.shape[dim])
        last_member = devices if (axis != "grp" or top is None) else top
        up = [(i, i + 1) for i in range(last_member - 1)]
        down = [(j, i) for i, j in up]
        last = lax.slice_in_dim(shard, length - width, length, axis=dim)
        initial = lax.slice_in_dim(shard, 0, width, axis=dim)
        before = lax.ppermute(last, axis, up)
        after = lax.ppermute(initial, axis, down)
        shard = jnp.concatenate([before, shard, after], axis=dim)
    return shard


def neighbours(padded, direction_index):
    leading = [slice(None)] * (padded.ndim - 3)
    middle = [slice(1, -1)] * 3
    below_slices = list(middle)
    below_slices[direction_index] = slice(0, -2)
    above_slices = list(middle)
    above_slices[direction_index] = slice(2, None)
    return (padded[tuple(leading + below_slices)], padded[tuple(leading + above_slices)])


def tendency(padded, speeds):
    center = padded[1:-1, 1:-1, 1:-1]
    running = -6.0 * KAPPA * center
    for direction_index in range(3):
        below_cells, above_cells = neighbours(padded, direction_index)
        speed_comp = speeds[direction_index]
        running = (
            running
            + KAPPA * (below_cells + above_cells)
            - (
                jnp.maximum(speed_comp, 0.0) * (center - below_cells)
                + jnp.minimum(speed_comp, 0.0) * (above_cells - center)
            )
        )
    return running


def inside(start, count, total):
    ids = start + jnp.arange(count, dtype=jnp.int32)
    return (ids >= 0) & (ids < total)


def grp_sum(partial):
    pair = lax.ppermute(partial, "grp", [(0, 1), (1, 0), (2, 3), (3, 2)])
    partial = partial + pair
    pair = lax.ppermute(partial, "grp", [(0, 2), (2, 0), (1, 3), (3, 1)])
    return partial + pair


def on_device(conc, velocity, porosity, saturation, layer_counts, electrodes, init_potential):
    group_index = lax.axis_index("grp")
    row_index = lax.axis_index("gx")
    column_index = lax.axis_index("gy")
    groups = lax.axis_size("grp")
    rows = lax.axis_size("gx")
    columns = lax.axis_size("gy")
    active = group_index < 3
    field = conc[0]
    layers, tile_x, tile_y = field.shape
    slabs = 3
    speeds = velocity[:, 0]

    field_wide = with_halo(field, (("grp", 0), ("gx", 1), ("gy", 2)), 2, top=slabs)
    speeds_wide = with_halo(speeds, (("grp", 1), ("gx", 2), ("gy", 3)), 1, top=slabs).astype(
        jnp.float32
    )

    section_wide = field_wide[1:-1, 1:-1, 1:-1] + tendency(field_wide, speeds_wide)
    keep = (
        inside(group_index * layers - 1, layers + 2, slabs * layers)[:, None, None]
        & inside(row_index * tile_x - 1, tile_x + 2, rows * tile_x)[None, :, None]
        & inside(column_index * tile_y - 1, tile_y + 2, columns * tile_y)[None, None, :]
    )
    section_wide = jnp.where(keep, section_wide, 0.0)
    advanced = 0.5 * (
        field
        + section_wide[1:-1, 1:-1, 1:-1]
        + tendency(section_wide, speeds_wide[:, 1:-1, 1:-1, 1:-1])
    )
    advanced = jnp.where(active, advanced, 0.0)

    poro = porosity[0].astype(jnp.float32)
    water = saturation[0].astype(jnp.float32)
    sigma = ARCHIE * jnp.exp(advanced) * poro * poro * water * water
    coarse_x = tile_x // 2
    coarse_y = tile_y // 2
    pool_y = (
        jnp.arange(tile_y, dtype=jnp.int32)[:, None] // 2
        == jnp.arange(coarse_y, dtype=jnp.int32)[None, :]
    ).astype(jnp.float32)
    half = jnp.einsum("zxy,yc->zxc", sigma, pool_y, precision=lax.Precision.HIGHEST)
    coarse = half.reshape(layers, coarse_x, 2, coarse_y).sum(axis=2)

    ends = jnp.cumsum(layer_counts)
    starts = ends - layer_counts
    layer_ids = group_index * layers + jnp.arange(layers, dtype=jnp.int32)
    member = (
        (layer_ids[None, :] >= starts[:, None]) & (layer_ids[None, :] < ends[:, None]) & active
    ).astype(jnp.float32)
    weights = member / (4.0 * layer_counts.astype(jnp.float32))[:, None]
    resist_layers = layer_counts.shape[0]
    partial_cond = jnp.dot(
        weights, coarse.reshape(layers, coarse_x * coarse_y), precision=lax.Precision.HIGHEST
    ).reshape(resist_layers, coarse_x, coarse_y)
    conductivity = grp_sum(partial_cond)

    grid_x = coarse_x * rows
    grid_y = coarse_y * columns
    depth = SWEEPS
    potential = lax.dynamic_slice_in_dim(init_potential, group_index, 1, 0)
    potential = with_halo(potential, (("gx", 2), ("gy", 3)), depth)
    poles = lax.dynamic_slice_in_dim(electrodes, group_index, 1, 0)

    cond_wide = with_halo(conductivity, (("gx", 1), ("gy", 2)), depth)
    cond_wide = jnp.pad(cond_wide, ((1, 1), (0, 0), (0, 0)))
    wide_x = coarse_x + 2 * depth
    wide_y = coarse_y + 2 * depth
    gx_ids = row_index * coarse_x - depth + jnp.arange(wide_x, dtype=jnp.int32)
    gy_ids = column_index * coarse_y - depth + jnp.arange(wide_y, dtype=jnp.int32)
    flat_ids = (
        jnp.arange(resist_layers, dtype=jnp.int32)[:, None, None] * (grid_x * grid_y)
        + gx_ids[None, :, None] * grid_y
        + gy_ids[None, None, :]
    )
    source_terms = AMPLITUDE * (
        (flat_ids[None] == poles[:, 0, None, None, None]).astype(jnp.float32)
        - (flat_ids[None] == poles[:, 1, None, None, None]).astype(jnp.float32)
    )
    on_grid = (
        ((gx_ids >= 0) & (gx_ids < grid_x))[:, None] & ((gy_ids >= 0) & (gy_ids < grid_y))[None, :]
    )

    for sweep_index in range(SWEEPS):
        m = sweep_index + 1
        nx, ny = wide_x - 2 * m, wide_y - 2 * m
        center_c = cond_wide[1:-1, m : m + nx, m : m + ny]
        faces = []
        diagonal = jnp.zeros_like(center_c)
        for d in range(3):
            if d == 0:
                lo = cond_wide[0:-2, m : m + nx, m : m + ny]
                hi = cond_wide[2:, m : m + nx, m : m + ny]
            elif d == 1:
                lo = cond_wide[1:-1, m - 1 : m - 1 + nx, m : m + ny]
                hi = cond_wide[1:-1, m + 1 : m + 1 + nx, m : m + ny]
            else:
                lo = cond_wide[1:-1, m : m + nx, m - 1 : m - 1 + ny]
                hi = cond_wide[1:-1, m : m + nx, m + 1 : m + 1 + ny]
            face_below = 0.5 * (center_c + lo)
            face_above = 0.5 * (center_c + hi)
            faces.append((face_below, face_above))
            diagonal = diagonal + face_below + face_above
        pot_z = jnp.pad(potential, ((0, 0), (1, 1), (0, 0), (0, 0)))
        pot_c = potential[:, :, 1:-1, 1:-1]
        coupled = jnp.zeros_like(pot_c)
        for d in range(3):
            if d == 0:
                lo = pot_z[:, 0:-2, 1:-1, 1:-1]
                hi = pot_z[:, 2:, 1:-1, 1:-1]
            elif d == 1:
                lo = potential[:, :, 0:-2, 1:-1]
                hi = potential[:, :, 2:, 1:-1]
            else:
                lo = potential[:, :, 1:-1, 0:-2]
                hi = potential[:, :, 1:-1, 2:]
            coupled = coupled + faces[d][0] * lo + faces[d][1] * hi
        applied = diagonal * pot_c - coupled
        rhs = source_terms[:, :, m : m + nx, m : m + ny]
        updated = pot_c + OMEGA * (rhs - applied) / diagonal
        potential = jnp.where(on_grid[m : m + nx, m : m + ny], updated, 0.0)

    return (advanced[None], conductivity, potential)


def solution(mesh):
    in_specs = (
        P("grp", None, "gx", "gy"),
        P(None, "grp", None, "gx", "gy"),
        P("grp", None, "gx", "gy"),
        P("grp", None, "gx", "gy"),
        P(),
        P(),
        P(None, None, "gx", "gy"),
    )
    out_specs = (P("grp", None, "gx", "gy"), P(None, "gx", "gy"), P("grp", None, "gx", "gy"))
    return jax.shard_map(
        on_device, mesh=mesh, in_specs=in_specs, out_specs=out_specs, check_vma=False
    )
```

time: 274 us -> 179 us (0.65)
  waiting for transfers between devices: 83.4 us -> 11.3 us
  starting transfers between devices: 88.2 us -> 67 us
  between operations: 14.6 us -> 1.35 us
  local copies, waits for them, and re-layouts: 27.6 us -> 35 us
  matrix products: 1.74 us -> 4.68 us
    psum x1 -> x0, waiting for transfers between devices: 38.9 us -> none  [on_device(): conductivity = lax.psum(partial_cond, 'grp')]
    ppermute x14 -> x10, waiting for transfers between devices: 41.6 us -> 5.71 us  [with_halo(): after = lax.ppermute(initial, axis, down)]
    ppermute x14 -> x10, starting transfers between devices: 37.1 us -> 23.6 us  [with_halo(): after = lax.ppermute(initial, axis, down)]
    mul x2, other arithmetic: 11.8 us -> 1.44 us  [the longest x1 1.43 us: on_device(): AMPLITUDE * ((flat_ids[None] == poles[:, 0, None, None, None]).astype(jnp...]
    concatenate x8 -> x7, other arithmetic: 1.79 us -> 10.7 us  [with_halo(): shard = jnp.concatenate([before, shard, after], axis=dim)]
    reduce_sum x1, other arithmetic: 9.53 us -> 1.28 us  [on_device(): coarse = half.reshape(layers, coarse_x, 2, coarse_y).sum(axis=2)]
    ppermute x14 -> x10, starting transfers between devices: 51.1 us -> 43.3 us  [with_halo(): before = lax.ppermute(last, axis, up)]
    select_n x3 -> x6, other arithmetic: 18 us -> 24.9 us  [the longest x1 14.2 us: on_device(): section_wide = jnp.where(keep, section_wide, 0.0)]
  transfers between devices with their start and end apart: 29 -> 22, of which waited for: 14 -> 5; matrix products, arithmetic and copies ran while one was open for 28% -> 52% of each run, Pallas kernels for 0% -> 0%
where the time goes in v1:
time: 179 us; the launch traced here: 177 us
  starting transfers between devices  67 us (37%)
  other arithmetic  57.9 us (32%)
  local copies, waits for them, and re-layouts  35 us (20%)
  waiting for transfers between devices  11.3 us (6%)
  matrix products  4.68 us (3%)
    ppermute x10, starting transfers between devices, with_halo(): before = lax.ppermute(last, axis, up)  43.3 us
    ppermute x10, starting transfers between devices, with_halo(): after = lax.ppermute(initial, axis, down)  23.6 us
    select_n x1, other arithmetic, on_device(): section_wide = jnp.where(keep, section_wide, 0.0)  14.2 us
    slice x9, local copies, waits for them, and re-layouts, with_halo(): last = lax.slice_in_dim(shard, length - width, length, axis=dim)  11.3 us
    convert_element_type x1, other arithmetic, on_device(): with_halo(speeds, (('grp', 1), ('gx', 2), ('gy', 3)), 1, top=slabs)  11.1 us
    concatenate x7, other arithmetic, with_halo(): shard = jnp.concatenate([before, shard, after], axis=dim)  10.7 us
    slice x5, local copies, waits for them, and re-layouts, with_halo(): initial = lax.slice_in_dim(shard, 0, width, axis=dim)  7.5 us
    select_n x1, other arithmetic, on_device(): advanced = jnp.where(active, advanced, 0.0)  7.49 us
  transfers between devices with their start and end apart: 22, of which 5 were waited for; matrix products, arithmetic and copies ran while one was open for 52% of the time, Pallas kernels for 0%

profile of v1, /device:TPU:102, one launch (start us, length us, event | category | flops | bytes accessed | tf_op | source)
XLA Modules:
  0.0 177.3 jit_solution(9843076372977842082)
XLA Ops:
  3.7 4.3 %collective-permute-start.7 = (bf16[3,1,64,256]{3,2,1,0:T(8,128)(2,1)S(1)}, bf16[3,1,64,256]{3,2,1,0:T(8,128)(2,1)S(1)}, u32[]{:S(2)}, u32[]{:S(2)}) collective-permute-start(bf16[3,1,64,256]{3,2,1,0:T(8,128)(2,1)S(1)} %get-tuple-element.20), channel_id=1, source_target_pairs={{64,0},{128,64},{65,1},{129,65},{66,2},{130,66},{67,3},{131,67},{6... | collective-permute-start | bytes 294920 | tf_op jit(solution)/shard_map/ppermute | solution.py:24
  11.0 4.3 %collective-permute-start.1 = (f32[2,64,256]{2,1,0:T(8,128)}, f32[2,64,256]{2,1,0:T(8,128)S(1)}, u32[]{:S(2)}, u32[]{:S(2)}) collective-permute-start(f32[2,64,256]{2,1,0:T(8,128)} %get-tuple-element.26), channel_id=1, source_target_pairs={{64,0},{128,64},{65,1},{129,65},{66,2},{130,66},{67,3},{131,67},{6... | collective-permute-start | bytes 393224 | tf_op jit(solution)/shard_map/ppermute | solution.py:24
  15.9 5.9 %collective-permute-start.14 = (f32[1,8,3,128]{3,1,2,0:T(8,128)}, f32[1,8,3,128]{3,1,2,0:T(8,128)}, u32[]{:S(2)}, u32[]{:S(2)}) collective-permute-start(f32[1,8,3,128]{3,1,2,0:T(8,128)} %copy.60), channel_id=1, source_target_pairs={{0,4},{4,8},{8,12},{12,16},{16,20},{20,24},{24,28},{28,32},{32,36}... | collective-permute-start | bytes 36872 | tf_op jit(solution)/shard_map/ppermute | solution.py:23
  32.9 4.0 %collective-permute-start.8 = (bf16[3,34,1,256]{3,1,2,0:T(8,128)(2,1)S(1)}, bf16[3,34,1,256]{3,1,2,0:T(8,128)(2,1)S(1)}, u32[]{:S(2)}, u32[]{:S(2)}) collective-permute-start(bf16[3,34,1,256]{3,1,2,0:T(8,128)(2,1)S(1)} %copy.37), channel_id=1, source_target_pairs={{0,4},{4,8},{8,12},{12,16},{16,20},{20,24},{24,28},{28,32},{32,36}... | collective-permute-start | bytes 156680 | tf_op jit(solution)/shard_map/ppermute | solution.py:23
  37.0 3.3 %collective-permute-start.9 = (bf16[3,34,1,256]{3,1,2,0:T(8,128)(2,1)S(1)}, bf16[3,34,1,256]{3,1,2,0:T(8,128)(2,1)S(1)}, u32[]{:S(2)}, u32[]{:S(2)}) collective-permute-start(bf16[3,34,1,256]{3,1,2,0:T(8,128)(2,1)S(1)} %copy.38), channel_id=1, source_target_pairs={{4,0},{8,4},{12,8},{16,12},{20,16},{24,20},{28,24},{32,28},{36,32}... | collective-permute-start | bytes 156680 | tf_op jit(solution)/shard_map/ppermute | solution.py:24
  41.0 6.1 %collective-permute-start.2 = (f32[36,2,256]{2,1,0:T(2,128)}, f32[36,2,256]{2,1,0:T(2,128)}, u32[]{:S(2)}, u32[]{:S(2)}) collective-permute-start(f32[36,2,256]{2,1,0:T(2,128)} %get-tuple-element.23), channel_id=1, source_target_pairs={{0,4},{4,8},{8,12},{12,16},{16,20},{20,24},{24,28},{28,32},{32,36}... | collective-permute-start | bytes 221192 | tf_op jit(solution)/shard_map/ppermute | solution.py:23
  47.2 1.9 %collective-permute-start.3 = (f32[36,2,256]{2,1,0:T(2,128)}, f32[36,2,256]{2,1,0:T(2,128)}, u32[]{:S(2)}, u32[]{:S(2)}) collective-permute-start(f32[36,2,256]{2,1,0:T(2,128)} %get-tuple-element.24), channel_id=1, source_target_pairs={{4,0},{8,4},{12,8},{16,12},{20,16},{24,20},{28,24},{32,28},{36,32}... | collective-permute-start | bytes 221192 | tf_op jit(solution)/shard_map/ppermute | solution.py:24
  49.3 3.2 %pad_maximum_fusion.11 = bf16[3,34,66,256]{3,2,1,0:T(8,128)(2,1)S(1)} fusion(bf16[3,34,1,256]{3,2,1,0:T(2,128)(2,1)S(1)} %copy.40, bf16[3,1,64,256]{3,2,1,0:T(8,128)(2,1)} %copy-done.5, bf16[3,32,64,256]{3,2,1,0:T(8,128)(2,1)S(1)} %bitcast.233, bf16[3,1,64,256]{3,2,1,0:T(8,128)(2,1)S(1)} %collective-permute-done.6, bf16[3,34,1,256]{3,2,1,0:T(2,128)(2,1)S(1)} %copy.39), kind=kLoop, calls=%fused_computation.12 | loop fusion | flops 17233920 | bytes 6893568 | tf_op jit(solution)/shard_map/concatenate | solution.py:25
  52.6 2.8 %fusion.117 = (bf16[3,34,66,1]{3,2,1,0:T(8,128)(2,1)}, bf16[3,34,66,1]{3,2,1,0:T(8,128)(2,1)}) fusion(bf16[3,34,66,256]{3,2,1,0:T(8,128)(2,1)S(1)} %pad_maximum_fusion.11), kind=kLoop, calls=%fused_computation.224 | loop fusion | bytes 53856 | tf_op jit(solution)/shard_map/slice | solution.py:21
  55.3 3.1 %copy.41 = bf16[3,34,66,1]{2,1,3,0:T(8,128)(2,1)} copy(bf16[3,34,66,1]{3,2,1,0:T(8,128)(2,1)} %get-tuple-element.15) | data formatting | bytes 26928 | tf_op jit(solution)/shard_map/slice | solution.py:21
  58.4 3.5 %collective-permute-start.10 = (bf16[3,34,66,1]{2,1,3,0:T(8,128)(2,1)}, bf16[3,34,66,1]{2,1,3,0:T(8,128)(2,1)S(1)}, u32[]{:S(2)}, u32[]{:S(2)}) collective-permute-start(bf16[3,34,66,1]{2,1,3,0:T(8,128)(2,1)} %copy.41), channel_id=1, source_target_pairs={{0,1},{1,2},{2,3},{4,5},{5,6},{6,7},{8,9},{9,10},{10,11},{12,13},{... | collective-permute-start | bytes 40400 | tf_op jit(solution)/shard_map/ppermute | solution.py:23
  61.9 3.1 %copy.42 = bf16[3,34,66,1]{2,1,3,0:T(8,128)(2,1)} copy(bf16[3,34,66,1]{3,2,1,0:T(8,128)(2,1)} %get-tuple-element.16) | data formatting | bytes 26928 | tf_op jit(solution)/shard_map/slice | solution.py:22
  67.6 2.5 %collective-permute-start.15 = (f32[1,8,3,128]{3,1,2,0:T(8,128)}, f32[1,8,3,128]{3,1,2,0:T(8,128)}, u32[]{:S(2)}, u32[]{:S(2)}) collective-permute-start(f32[1,8,3,128]{3,1,2,0:T(8,128)} %copy.61), channel_id=1, source_target_pairs={{4,0},{8,4},{12,8},{16,12},{20,16},{24,20},{28,24},{32,28},{36,32}... | collective-permute-start | bytes 36872 | tf_op jit(solution)/shard_map/ppermute | solution.py:24
  70.1 2.1 %copy.43 = bf16[3,34,66,1]{3,2,1,0:T(8,128)(2,1)} copy(bf16[3,34,66,1]{2,1,3,0:T(8,128)(2,1)S(1)} %collective-permute-done.10) | data formatting | bytes 26928 | tf_op jit(solution)/shard_map/ppermute | solution.py:23
  72.2 2.8 %copy.44 = bf16[3,34,66,1]{3,2,1,0:T(8,128)(2,1)} copy(bf16[3,34,66,1]{2,1,3,0:T(8,128)(2,1)} %collective-permute-done.11) | data formatting | bytes 26928 | tf_op jit(solution)/shard_map/ppermute | solution.py:24
  76.2 1.9 %fusion.119 = (f32[36,68,2]{2,1,0:T(8,128)}, f32[36,68,2]{2,1,0:T(8,128)}) fusion(f32[36,68,256]{2,1,0:T(8,128)S(1)} %pad_maximum_fusion.12), kind=kLoop, calls=%fused_computation.226 | loop fusion | bytes 78336 | tf_op jit(solution)/shard_map/slice | solution.py:22
  78.2 1.8 %copy.33 = f32[36,68,2]{1,2,0:T(2,128)S(1)} copy(f32[36,68,2]{2,1,0:T(8,128)} %get-tuple-element.22) | data formatting | bytes 39168 | tf_op jit(solution)/shard_map/slice | solution.py:21
  80.0 5.2 %collective-permute-start.4 = (f32[36,68,2]{1,2,0:T(2,128)S(1)}, f32[36,68,2]{1,2,0:T(2,128)}, u32[]{:S(2)}, u32[]{:S(2)}) collective-permute-start(f32[36,68,2]{1,2,0:T(2,128)S(1)} %copy.33), channel_id=1, source_target_pairs={{0,1},{1,2},{2,3},{4,5},{5,6},{6,7},{8,9},{9,10},{10,11},{12,13},{... | collective-permute-start | bytes 58760 | tf_op jit(solution)/shard_map/ppermute | solution.py:23
  85.1 2.4 %copy.34 = f32[36,68,2]{1,2,0:T(2,128)} copy(f32[36,68,2]{2,1,0:T(8,128)} %get-tuple-element.21) | data formatting | bytes 39168 | tf_op jit(solution)/shard_map/slice | solution.py:22
  89.0 11.1 %maximum_convert_fusion = f32[3,34,66,258]{3,2,1,0:T(8,128)} fusion(bf16[3,34,66,1]{3,2,1,0:T(8,128)(2,1)} %copy.44, bf16[3,34,1,256]{3,2,1,0:T(2,128)(2,1)S(1)} %copy.40, bf16[3,1,64,256]{3,2,1,0:T(8,128)(2,1)} %copy-done.5, bf16[3,32,64,256]{3,2,1,0:T(8,128)(2,1)} %bitcast.232, bf16[3,1,64,256]{3,2,1,0:T(8,128)(2,1)S(1)} %collective-permute-done.6, ...), kind=kLoop, calls=%fused_computation | loop fusion | flops 24315984 | bytes 10421136 | tf_op jit(solution)/shard_map/convert_element_type | solution.py:82
  100.1 2.3 %copy.35 = f32[36,68,2]{2,1,0:T(8,128)} copy(f32[36,68,2]{1,2,0:T(2,128)} %collective-permute-done.4) | data formatting | bytes 39168 | tf_op jit(solution)/shard_map/ppermute | solution.py:23
  102.5 2.4 %copy.36 = f32[36,68,2]{2,1,0:T(8,128)} copy(f32[36,68,2]{1,2,0:T(2,128)} %collective-permute-done.5) | data formatting | bytes 39168 | tf_op jit(solution)/shard_map/ppermute | solution.py:24
  104.9 5.7 %pad_maximum_fusion = f32[36,68,260]{2,1,0:T(8,128)S(1)} fusion(f32[36,68,2]{2,1,0:T(8,128)} %copy.36, f32[36,2,256]{2,1,0:T(2,128)} %collective-permute-done.3, f32[2,64,256]{2,1,0:T(8,128)S(1)} %collective-permute-done.1, f32[32,64,256]{2,1,0:T(8,128)S(1)} %bitcast.228, f32[2,64,256]{2,1,0:T(8,128)S(1)} %collective-permute-done, ...), kind=kLoop, calls=%fused_computation.1 | loop fusion | flops 3818880 | bytes 5091840 | tf_op jit(solution)/shard_map/concatenate | solution.py:25
  110.7 14.2 %fusion.3 = f32[34,66,258]{2,1,0:T(8,128)S(1)} fusion(f32[3,34,66,258]{3,2,1,0:T(8,128)} %maximum_convert_fusion, f32[36,2,256]{2,1,0:T(2,128)} %collective-permute-done.3, f32[2,64,256]{2,1,0:T(8,128)S(1)} %collective-permute-done.1, f32[32,64,256]{2,1,0:T(8,128)S(1)} %bitcast.229, f32[2,64,256]{2,1,0:T(8,128)S(1)} %collective-permute-done, ...), kind=kLoop, calls=%fused_computation.17 | loop fusion | flops 27210744 | bytes 23390694 | tf_op jit(solution)/shard_map/jit(_where)/select_n | solution.py:92
  124.9 7.5 %fusion.17 = f32[32,64,256]{2,1,0:T(8,128)} fusion(f32[3,34,66,258]{3,2,1,0:T(8,128)S(1)} %bitcast.225, f32[34,66,258]{2,1,0:T(8,128)S(1)} %fusion.3, pred[]{:T(512)S(6)} %lt.68, f32[1,32,64,256]{3,2,1,0:T(8,128)S(1)} %copy-done.1), kind=kLoop, calls=%fused_computation.40 | loop fusion | flops 19922944 | bytes 25165824 | tf_op jit(solution)/shard_map/jit(_where)/select_n | solution.py:98
  132.5 4.0 %fusion.10 = f32[32,64,128]{2,1,0:T(8,128)S(1)} fusion(f32[32,64,256]{2,1,0:T(8,128)} %fusion.17, bf16[1,32,64,256]{3,2,1,0:T(8,128)(2,1)} %param.10, bf16[1,32,64,256]{3,2,1,0:T(8,128)(2,1)} %param.9, s32[256]{0:T(256)S(1)} %copy-done.9), kind=kOutput, calls=%fused_computation.32 | convolution fusion | flops 809009152 | bytes 5243904 | tf_op jit(solution)/shard_map/zxy,yc->zxc/dot_general | solution.py:109
  140.9 4.8 %collective-permute-done.13 = f32[8,32,128]{2,0,1:T(8,128)S(1)} collective-permute-done((f32[8,32,128]{2,0,1:T(8,128)S(1)}, f32[8,32,128]{2,0,1:T(8,128)S(1)}, u32[]{:S(2)}, u32[]{:S(2)}) %collective-permute-start.13) | collective-permute-done | bytes 131104 | tf_op jit(solution)/shard_map/ppermute | solution.py:64
  145.7 6.9 %collective-permute-start.18 = (f32[8,3,128]{2,0,1:T(8,128)S(1)}, f32[8,3,128]{2,0,1:T(8,128)S(1)}, u32[]{:S(2)}, u32[]{:S(2)}) collective-permute-start(f32[8,3,128]{2,0,1:T(8,128)S(1)} %get-tuple-element.33), channel_id=1, source_target_pairs={{0,4},{4,8},{8,12},{12,16},{16,20},{20,24},{24,28},{28,32},{32,36}... | collective-permute-start | bytes 36872 | tf_op jit(solution)/shard_map/ppermute | solution.py:23
  152.6 1.9 %collective-permute-start.19 = (f32[8,3,128]{2,0,1:T(8,128)S(1)}, f32[8,3,128]{2,0,1:T(8,128)S(1)}, u32[]{:S(2)}, u32[]{:S(2)}) collective-permute-start(f32[8,3,128]{2,0,1:T(8,128)S(1)} %get-tuple-element.34), channel_id=1, source_target_pairs={{4,0},{8,4},{12,8},{16,12},{20,16},{24,20},{28,24},{32,28},{36,32}... | collective-permute-start | bytes 36872 | tf_op jit(solution)/shard_map/ppermute | solution.py:24
  154.6 4.6 %collective-permute-start.16 = (f32[1,8,38,3]{3,1,2,0:T(8,128)S(1)}, f32[1,8,38,3]{3,1,2,0:T(8,128)S(1)}, u32[]{:S(2)}, u32[]{:S(2)}) collective-permute-start(f32[1,8,38,3]{3,1,2,0:T(8,128)S(1)} %get-tuple-element.31), channel_id=1, source_target_pairs={{0,1},{1,2},{2,3},{4,5},{5,6},{6,7},{8,9},{9,10},{10,11},{12,13},{... | collective-permute-start | bytes 10952 | tf_op jit(solution)/shard_map/ppermute | solution.py:23
  161.9 4.6 %collective-permute-start.20 = (f32[8,38,3]{2,0,1:T(8,128)S(1)}, f32[8,38,3]{2,0,1:T(8,128)S(1)}, u32[]{:S(2)}, u32[]{:S(2)}) collective-permute-start(f32[8,38,3]{2,0,1:T(8,128)S(1)} %get-tuple-element.29), channel_id=1, source_target_pairs={{0,1},{1,2},{2,3},{4,5},{5,6},{6,7},{8,9},{9,10},{10,11},{12,13},{... | collective-permute-start | bytes 10952 | tf_op jit(solution)/shard_map/ppermute | solution.py:23
  169.2 4.4 %collective-permute-done.21 = f32[8,38,3]{2,0,1:T(8,128)S(1)} collective-permute-done((f32[8,38,3]{2,0,1:T(8,128)S(1)}, f32[8,38,3]{2,0,1:T(8,128)S(1)}, u32[]{:S(2)}, u32[]{:S(2)}) %collective-permute-start.21) | collective-permute-done | bytes 3680 | tf_op jit(solution)/shard_map/ppermute | solution.py:24
  (125 shorter events, 37.2 us)
Async XLA Ops:
  0.6 14.6 %copy-start = (f32[4,8,32,128]{3,2,1,0:T(8,128)S(1)}, f32[4,8,32,128]{3,2,1,0:T(8,128)}, u32[]{:S(2)}) copy-start(f32[4,8,32,128]{3,2,1,0:T(8,128)} %param.13) | copy-start | bytes 1572868
  0.6 39.7 %copy-start.1 = (f32[1,32,64,256]{3,2,1,0:T(8,128)S(1)}, f32[1,32,64,256]{3,2,1,0:T(8,128)}, u32[]{:S(2)}) copy-start(f32[1,32,64,256]{3,2,1,0:T(8,128)} %param.7) | copy-start | bytes 6291460
  2.4 29.0 %collective-permute-start.6 = (bf16[3,1,64,256]{3,2,1,0:T(8,128)(2,1)}, bf16[3,1,64,256]{3,2,1,0:T(8,128)(2,1)S(1)}, u32[]{:S(2)}, u32[]{:S(2)}) collective-permute-start(bf16[3,1,64,256]{3,2,1,0:T(8,128)(2,1)} %get-tuple-element.19), channel_id=1, source_target_pairs={{0,64},{64,128},{1,65},{65,129},{2,66},{66,130},{3,67},{67,131},{4... | collective-permute-start | bytes 294920 | tf_op jit(solution)/shard_map/ppermute | solution.py:23
  3.7 27.7 %collective-permute-start.7 = (bf16[3,1,64,256]{3,2,1,0:T(8,128)(2,1)S(1)}, bf16[3,1,64,256]{3,2,1,0:T(8,128)(2,1)S(1)}, u32[]{:S(2)}, u32[]{:S(2)}) collective-permute-start(bf16[3,1,64,256]{3,2,1,0:T(8,128)(2,1)S(1)} %get-tuple-element.20), channel_id=1, source_target_pairs={{64,0},{128,64},{65,1},{129,65},{66,2},{130,66},{67,3},{131,67},{6... | collective-permute-start | bytes 294920 | tf_op jit(solution)/shard_map/ppermute | solution.py:24
  9.7 30.6 %collective-permute-start = (f32[2,64,256]{2,1,0:T(8,128)}, f32[2,64,256]{2,1,0:T(8,128)S(1)}, u32[]{:S(2)}, u32[]{:S(2)}) collective-permute-start(f32[2,64,256]{2,1,0:T(8,128)} %get-tuple-element.25), channel_id=1, source_target_pairs={{0,64},{64,128},{1,65},{65,129},{2,66},{66,130},{3,67},{67,131},{4... | collective-permute-start | bytes 393224 | tf_op jit(solution)/shard_map/ppermute | solution.py:23
  11.0 29.3 %collective-permute-start.1 = (f32[2,64,256]{2,1,0:T(8,128)}, f32[2,64,256]{2,1,0:T(8,128)S(1)}, u32[]{:S(2)}, u32[]{:S(2)}) collective-permute-start(f32[2,64,256]{2,1,0:T(8,128)} %get-tuple-element.26), channel_id=1, source_target_pairs={{64,0},{128,64},{65,1},{129,65},{66,2},{130,66},{67,3},{131,67},{6... | collective-permute-start | bytes 393224 | tf_op jit(solution)/shard_map/ppermute | solution.py:24
  15.3 14.2 %copy-start.6 = (f32[1,8,32,128]{3,2,1,0:T(8,128)}, f32[1,8,32,128]{3,2,1,0:T(8,128)S(1)}, u32[]{:S(2)}) copy-start(f32[1,8,32,128]{3,2,1,0:T(8,128)S(1)} %constant_dynamic-slice_fusion.1) | copy-start | bytes 393220
  15.9 123.0 %collective-permute-start.14 = (f32[1,8,3,128]{3,1,2,0:T(8,128)}, f32[1,8,3,128]{3,1,2,0:T(8,128)}, u32[]{:S(2)}, u32[]{:S(2)}) collective-permute-start(f32[1,8,3,128]{3,1,2,0:T(8,128)} %copy.60), channel_id=1, source_target_pairs={{0,4},{4,8},{8,12},{12,16},{16,20},{20,24},{24,28},{28,32},{32,36}... | collective-permute-start | bytes 36872 | tf_op jit(solution)/shard_map/ppermute | solution.py:23
  31.4 17.9 %copy-start.2 = (bf16[3,1,32,64,256]{4,3,2,1,0:T(8,128)(2,1)S(1)}, bf16[3,1,32,64,256]{4,3,2,1,0:T(8,128)(2,1)}, u32[]{:S(2)}) copy-start(bf16[3,1,32,64,256]{4,3,2,1,0:T(8,128)(2,1)} %param.8) | copy-start | bytes 9437188
  31.4 17.7 %copy-start.5 = (bf16[3,1,64,256]{3,2,1,0:T(8,128)(2,1)}, bf16[3,1,64,256]{3,2,1,0:T(8,128)(2,1)S(1)}, u32[]{:S(2)}) copy-start(bf16[3,1,64,256]{3,2,1,0:T(8,128)(2,1)S(1)} %collective-permute-done.7) | copy-start | bytes 294916
  32.9 16.2 %collective-permute-start.8 = (bf16[3,34,1,256]{3,1,2,0:T(8,128)(2,1)S(1)}, bf16[3,34,1,256]{3,1,2,0:T(8,128)(2,1)S(1)}, u32[]{:S(2)}, u32[]{:S(2)}) collective-permute-start(bf16[3,34,1,256]{3,1,2,0:T(8,128)(2,1)S(1)} %copy.37), channel_id=1, source_target_pairs={{0,4},{4,8},{8,12},{12,16},{16,20},{20,24},{24,28},{28,32},{32,36}... | collective-permute-start | bytes 156680 | tf_op jit(solution)/shard_map/ppermute | solution.py:23
  37.0 12.2 %collective-permute-start.9 = (bf16[3,34,1,256]{3,1,2,0:T(8,128)(2,1)S(1)}, bf16[3,34,1,256]{3,1,2,0:T(8,128)(2,1)S(1)}, u32[]{:S(2)}, u32[]{:S(2)}) collective-permute-start(bf16[3,34,1,256]{3,1,2,0:T(8,128)(2,1)S(1)} %copy.38), channel_id=1, source_target_pairs={{4,0},{8,4},{12,8},{16,12},{20,16},{24,20},{28,24},{32,28},{36,32}... | collective-permute-start | bytes 156680 | tf_op jit(solution)/shard_map/ppermute | solution.py:24
  41.0 34.0 %collective-permute-start.2 = (f32[36,2,256]{2,1,0:T(2,128)}, f32[36,2,256]{2,1,0:T(2,128)}, u32[]{:S(2)}, u32[]{:S(2)}) collective-permute-start(f32[36,2,256]{2,1,0:T(2,128)} %get-tuple-element.23), channel_id=1, source_target_pairs={{0,4},{4,8},{8,12},{12,16},{16,20},{20,24},{24,28},{28,32},{32,36}... | collective-permute-start | bytes 221192 | tf_op jit(solution)/shard_map/ppermute | solution.py:23
  47.2 27.8 %collective-permute-start.3 = (f32[36,2,256]{2,1,0:T(2,128)}, f32[36,2,256]{2,1,0:T(2,128)}, u32[]{:S(2)}, u32[]{:S(2)}) collective-permute-start(f32[36,2,256]{2,1,0:T(2,128)} %get-tuple-element.24), channel_id=1, source_target_pairs={{4,0},{8,4},{12,8},{16,12},{20,16},{24,20},{28,24},{32,28},{36,32}... | collective-permute-start | bytes 221192 | tf_op jit(solution)/shard_map/ppermute | solution.py:24
  58.4 9.1 %collective-permute-start.10 = (bf16[3,34,66,1]{2,1,3,0:T(8,128)(2,1)}, bf16[3,34,66,1]{2,1,3,0:T(8,128)(2,1)S(1)}, u32[]{:S(2)}, u32[]{:S(2)}) collective-permute-start(bf16[3,34,66,1]{2,1,3,0:T(8,128)(2,1)} %copy.41), channel_id=1, source_target_pairs={{0,1},{1,2},{2,3},{4,5},{5,6},{6,7},{8,9},{9,10},{10,11},{12,13},{... | collective-permute-start | bytes 40400 | tf_op jit(solution)/shard_map/ppermute | solution.py:23
  65.1 7.2 %collective-permute-start.11 = (bf16[3,34,66,1]{2,1,3,0:T(8,128)(2,1)}, bf16[3,34,66,1]{2,1,3,0:T(8,128)(2,1)}, u32[]{:S(2)}, u32[]{:S(2)}) collective-permute-start(bf16[3,34,66,1]{2,1,3,0:T(8,128)(2,1)} %copy.42), channel_id=1, source_target_pairs={{1,0},{2,1},{3,2},{5,4},{6,5},{7,6},{9,8},{10,9},{11,10},{13,12},{... | collective-permute-start | bytes 40400 | tf_op jit(solution)/shard_map/ppermute | solution.py:24
  67.6 72.6 %collective-permute-start.15 = (f32[1,8,3,128]{3,1,2,0:T(8,128)}, f32[1,8,3,128]{3,1,2,0:T(8,128)}, u32[]{:S(2)}, u32[]{:S(2)}) collective-permute-start(f32[1,8,3,128]{3,1,2,0:T(8,128)} %copy.61), channel_id=1, source_target_pairs={{4,0},{8,4},{12,8},{16,12},{20,16},{24,20},{28,24},{32,28},{36,32}... | collective-permute-start | bytes 36872 | tf_op jit(solution)/shard_map/ppermute | solution.py:24
  80.0 20.2 %collective-permute-start.4 = (f32[36,68,2]{1,2,0:T(2,128)S(1)}, f32[36,68,2]{1,2,0:T(2,128)}, u32[]{:S(2)}, u32[]{:S(2)}) collective-permute-start(f32[36,68,2]{1,2,0:T(2,128)S(1)} %copy.33), channel_id=1, source_target_pairs={{0,1},{1,2},{2,3},{4,5},{5,6},{6,7},{8,9},{9,10},{10,11},{12,13},{... | collective-permute-start | bytes 58760 | tf_op jit(solution)/shard_map/ppermute | solution.py:23
  87.6 14.9 %collective-permute-start.5 = (f32[36,68,2]{1,2,0:T(2,128)}, f32[36,68,2]{1,2,0:T(2,128)}, u32[]{:S(2)}, u32[]{:S(2)}) collective-permute-start(f32[36,68,2]{1,2,0:T(2,128)} %copy.34), channel_id=1, source_target_pairs={{1,0},{2,1},{3,2},{5,4},{6,5},{7,6},{9,8},{10,9},{11,10},{13,12},{... | collective-permute-start | bytes 58760 | tf_op jit(solution)/shard_map/ppermute | solution.py:24
  104.9 20.0 %slice-start = ((s8[11280384]{0:T(1024)(128)(4,1)}), s8[4194304]{0:T(1024)(128)(4,1)S(1)}, s32[]{:S(2)}) async-start(s8[11280384]{0:T(1024)(128)(4,1)} %bitcast.224), calls=%async_computation | async-start | bytes 8388608
  110.7 14.3 %slice-start.1 = ((s8[11280384]{0:T(1024)(128)(4,1)}), s8[4194304]{0:T(1024)(128)(4,1)S(1)}, s32[]{:S(2)}) async-start(s8[11280384]{0:T(1024)(128)(4,1)} %bitcast.224), calls=%async_computation.1 | async-start | bytes 8388608
  110.7 14.2 %slice-start.2 = ((s8[11280384]{0:T(1024)(128)(4,1)}), s8[2891776]{0:T(1024)(128)(4,1)S(1)}, s32[]{:S(2)}) async-start(s8[11280384]{0:T(1024)(128)(4,1)} %bitcast.224), calls=%async_computation.2 | async-start | bytes 5783552
  124.9 7.5 %copy-start.9 = (s32[256]{0:T(256)S(1)}, s32[256]{0:T(256)}, u32[]{:S(2)}) copy-start(s32[256]{0:T(256)} %and_select_fusion) | copy-start | bytes 3076
  132.5 7.6 %copy-start.7 = (f32[1,8,32,128]{3,2,1,0:T(8,128)S(1)}, f32[1,8,32,128]{3,2,1,0:T(8,128)}, u32[]{:S(2)}) copy-start(f32[1,8,32,128]{3,2,1,0:T(8,128)} %copy-done.6) | copy-start | bytes 393220
  138.5 1.4 collective-permute-start.12
  140.0 5.7 %collective-permute-start.13 = (f32[8,32,128]{2,0,1:T(8,128)S(1)}, f32[8,32,128]{2,0,1:T(8,128)S(1)}, u32[]{:S(2)}, u32[]{:S(2)}) collective-permute-start(f32[8,32,128]{2,0,1:T(8,128)S(1)} %add.380), channel_id=1, source_target_pairs={{0,128},{128,0},{64,192},{192,64},{1,129},{129,1},{65,193},{193,65... | collective-permute-start | bytes 393224 | tf_op jit(solution)/shard_map/ppermute | solution.py:64
  145.7 14.8 %collective-permute-start.18 = (f32[8,3,128]{2,0,1:T(8,128)S(1)}, f32[8,3,128]{2,0,1:T(8,128)S(1)}, u32[]{:S(2)}, u32[]{:S(2)}) collective-permute-start(f32[8,3,128]{2,0,1:T(8,128)S(1)} %get-tuple-element.33), channel_id=1, source_target_pairs={{0,4},{4,8},{8,12},{12,16},{16,20},{20,24},{24,28},{28,32},{32,36}... | collective-permute-start | bytes 36872 | tf_op jit(solution)/shard_map/ppermute | solution.py:23
  152.6 9.2 %collective-permute-start.19 = (f32[8,3,128]{2,0,1:T(8,128)S(1)}, f32[8,3,128]{2,0,1:T(8,128)S(1)}, u32[]{:S(2)}, u32[]{:S(2)}) collective-permute-start(f32[8,3,128]{2,0,1:T(8,128)S(1)} %get-tuple-element.34), channel_id=1, source_target_pairs={{4,0},{8,4},{12,8},{16,12},{20,16},{24,20},{28,24},{32,28},{36,32}... | collective-permute-start | bytes 36872 | tf_op jit(solution)/shard_map/ppermute | solution.py:24
  154.6 13.2 %collective-permute-start.16 = (f32[1,8,38,3]{3,1,2,0:T(8,128)S(1)}, f32[1,8,38,3]{3,1,2,0:T(8,128)S(1)}, u32[]{:S(2)}, u32[]{:S(2)}) collective-permute-start(f32[1,8,38,3]{3,1,2,0:T(8,128)S(1)} %get-tuple-element.31), channel_id=1, source_target_pairs={{0,1},{1,2},{2,3},{4,5},{5,6},{6,7},{8,9},{9,10},{10,11},{12,13},{... | collective-permute-start | bytes 10952 | tf_op jit(solution)/shard_map/ppermute | solution.py:23
  159.2 8.6 %collective-permute-start.17 = (f32[1,8,38,3]{3,1,2,0:T(8,128)S(1)}, f32[1,8,38,3]{3,1,2,0:T(8,128)S(1)}, u32[]{:S(2)}, u32[]{:S(2)}) collective-permute-start(f32[1,8,38,3]{3,1,2,0:T(8,128)S(1)} %get-tuple-element.32), channel_id=1, source_target_pairs={{1,0},{2,1},{3,2},{5,4},{6,5},{7,6},{9,8},{10,9},{11,10},{13,12},{... | collective-permute-start | bytes 10952 | tf_op jit(solution)/shard_map/ppermute | solution.py:24
  161.9 7.3 %collective-permute-start.20 = (f32[8,38,3]{2,0,1:T(8,128)S(1)}, f32[8,38,3]{2,0,1:T(8,128)S(1)}, u32[]{:S(2)}, u32[]{:S(2)}) collective-permute-start(f32[8,38,3]{2,0,1:T(8,128)S(1)} %get-tuple-element.29), channel_id=1, source_target_pairs={{0,1},{1,2},{2,3},{4,5},{5,6},{6,7},{8,9},{9,10},{10,11},{12,13},{... | collective-permute-start | bytes 10952 | tf_op jit(solution)/shard_map/ppermute | solution.py:23
  166.5 7.1 %collective-permute-start.21 = (f32[8,38,3]{2,0,1:T(8,128)S(1)}, f32[8,38,3]{2,0,1:T(8,128)S(1)}, u32[]{:S(2)}, u32[]{:S(2)}) collective-permute-start(f32[8,38,3]{2,0,1:T(8,128)S(1)} %get-tuple-element.30), channel_id=1, source_target_pairs={{1,0},{2,1},{3,2},{5,4},{6,5},{7,6},{9,8},{10,9},{11,10},{13,12},{... | collective-permute-start | bytes 10952 | tf_op jit(solution)/shard_map/ppermute | solution.py:24
  (11 other events, 57.4 us)

commit v2 on v1

--- a/solution.py
+++ b/solution.py
@@ -1,5 +1,9 @@
+import functools
+
 import jax
 import jax.numpy as jnp
+from jax.experimental import pallas as pl
+from jax.experimental.pallas import tpu as pltpu
 from jax import lax
 from jax.sharding import PartitionSpec as P
 
@@ -24,6 +28,193 @@
         after = lax.ppermute(initial, axis, down)
         shard = jnp.concatenate([before, shard, after], axis=dim)
     return shard
+
+
+def transport_halo(c, u, slabs):
+    f32 = jnp.float32
+    u = u.astype(f32)
+    nz, nx, ny = c.shape
+
+    def chain(axis, members):
+        up = [(i, i + 1) for i in range(members - 1)]
+        return up, [(j, i) for i, j in up]
+
+    up, down = chain("grp", slabs)
+    below = lax.ppermute(jnp.concatenate([c[nz - 2 :], u[:, nz - 1]], 0), "grp", up)
+    above = lax.ppermute(jnp.concatenate([c[:2], u[:, 0]], 0), "grp", down)
+    zlo_c, zlo_u = below[:2], below[2:]
+    zhi_c, zhi_u = above[:2], above[2:]
+
+    def zext_c(rows):
+        return jnp.concatenate([zlo_c[:, rows], c[:, rows], zhi_c[:, rows]], 0)
+
+    def zext_u(row):
+        core = jnp.concatenate([zlo_u[:, None, row], u[:, :, row], zhi_u[:, None, row]], 1)
+        return jnp.pad(core, ((0, 0), (1, 1), (0, 0)))
+
+    rows = lax.axis_size("gx")
+    up, down = chain("gx", rows)
+    send_up = jnp.concatenate([zext_c(slice(nx - 2, nx)), jnp.swapaxes(zext_u(nx - 1), 0, 1)], 1)
+    send_dn = jnp.concatenate([zext_c(slice(0, 2)), jnp.swapaxes(zext_u(0), 0, 1)], 1)
+    bx = lax.ppermute(send_up, "gx", up)
+    ax = lax.ppermute(send_dn, "gx", down)
+
+    def xz_c(lanes):
+        core = jnp.concatenate([zlo_c[..., lanes], c[..., lanes], zhi_c[..., lanes]], 0)
+        return jnp.concatenate([bx[:, 0:2, lanes], core, ax[:, 0:2, lanes]], 1)
+
+    def xz_u(lane):
+        core = jnp.pad(
+            jnp.concatenate([zlo_u[:, None, :, lane], u[..., lane], zhi_u[:, None, :, lane]], 1),
+            ((0, 0), (1, 1), (0, 0)),
+        )
+        lo = jnp.swapaxes(bx[:, 2:5, lane], 0, 1)[:, :, None]
+        hi = jnp.swapaxes(ax[:, 2:5, lane], 0, 1)[:, :, None]
+        zero = jnp.zeros_like(lo)
+        return jnp.moveaxis(jnp.concatenate([zero, lo, core, hi, zero], 2), 0, 2)
+
+    columns = lax.axis_size("gy")
+    up, down = chain("gy", columns)
+    by = lax.ppermute(jnp.concatenate([xz_c(slice(ny - 2, ny)), xz_u(ny - 1)], 2), "gy", up)
+    ay = lax.ppermute(jnp.concatenate([xz_c(slice(0, 2)), xz_u(0)], 2), "gy", down)
+
+    xc = jnp.concatenate([ax[:, 0:2], jnp.zeros((nz + 4, 4, ny), f32), bx[:, 0:2]], 1)
+    xu_hi = jnp.swapaxes(ax[1:-1, 2:5], 0, 1)[:, :, None]
+    xu_lo = jnp.swapaxes(bx[1:-1, 2:5], 0, 1)[:, :, None]
+    xu = jnp.concatenate([xu_hi, jnp.zeros((3, nz + 2, 6, ny), f32), xu_lo], 2)
+    yc = jnp.concatenate([ay[..., 0:2], jnp.zeros((nz + 4, nx + 4, 124), f32), by[..., 0:2]], 2)
+    yc = jnp.pad(yc, ((0, 0), (6, 6), (0, 0)))
+    yu_hi = jnp.moveaxis(ay[1:-1, :, 2:5], 2, 0)[..., None]
+    yu_lo = jnp.moveaxis(by[1:-1, :, 2:5], 2, 0)[..., None]
+    yu = jnp.concatenate([yu_hi, jnp.zeros((3, nz + 2, nx + 4, 126), f32), yu_lo], 3)
+    yu = jnp.pad(yu, ((0, 0), (0, 0), (6, 6), (0, 0)))
+    return zlo_c, zhi_c, zlo_u, zhi_u, xc, xu, yc, yu
+
+
+def roll(values, shift, axis):
+    return pltpu.roll(values, shift % values.shape[axis], axis)
+
+
+def stencil(c, below, above, speeds):
+    running = -6.0 * KAPPA * c
+    for d in range(3):
+        b, a, s = below[d], above[d], speeds[d]
+        running = running + KAPPA * (b + a) - (
+            jnp.maximum(s, 0.0) * (c - b) + jnp.minimum(s, 0.0) * (a - c)
+        )
+    return running
+
+
+def transport_kernel(
+    grid, place, weights, c_ref, v_ref, poro_ref, sat_ref, zlo_c, zhi_c, zlo_u, zhi_u,
+    xc, xu, yc, yu, pool_y, pool_x, adv_ref, part_ref, F, U, S,
+):
+    nz, nx, ny = c_ref.shape
+    wx, wy = F.shape[1], F.shape[2]
+    f32 = jnp.float32
+    F[0:2, 8 : 8 + nx, 0:ny] = zlo_c[...]
+    F[nz + 2 : nz + 4, 8 : 8 + nx, 0:ny] = zhi_c[...]
+
+    def put_c(z, carry):
+        F[z + 2, 8 : 8 + nx, 0:ny] = c_ref[z]
+        return carry
+
+    lax.fori_loop(0, nz, put_c, 0)
+    F[:, 0:8, 0:ny] = xc[...]
+    F[:, wx - 8 : wx, 0:ny] = xc[...]
+    F[:, :, ny:wy] = yc[...]
+    for d in range(3):
+        U[d, 0, 8 : 8 + nx, 0:ny] = zlo_u[d]
+        U[d, nz + 1, 8 : 8 + nx, 0:ny] = zhi_u[d]
+
+        def put_u(z, carry, d=d):
+            U[d, z + 1, 8 : 8 + nx, 0:ny] = v_ref[d, 0, z].astype(f32)
+            return carry
+
+        lax.fori_loop(0, nz, put_u, 0)
+        U[d, :, 0:8, 0:ny] = xu[d]
+        U[d, :, wx - 8 : wx, 0:ny] = xu[d]
+        U[d, :, :, ny:wy] = yu[d]
+
+    total_z, total_x, total_y = grid
+    gz0 = place[0] * nz - 1
+    gx = place[1] * nx - 8 + lax.broadcasted_iota(jnp.int32, (wx, wy), 0)
+    lane = lax.broadcasted_iota(jnp.int32, (wx, wy), 1)
+    gy = place[2] * ny + jnp.where(lane < ny + (wy - ny) // 2, lane, lane - wy)
+    plane = (gx >= 0) & (gx < total_x) & (gy >= 0) & (gy < total_y)
+
+    def first(k, carry):
+        c0 = F[k + 1]
+        below = (F[k], roll(c0, 1, 0), roll(c0, 1, 1))
+        above = (F[k + 2], roll(c0, -1, 0), roll(c0, -1, 1))
+        speeds = (U[0, k], U[1, k], U[2, k])
+        section = c0 + stencil(c0, below, above, speeds)
+        z = gz0 + k
+        keep = plane & (z >= 0) & (z < total_z)
+        S[k] = jnp.where(keep, section, 0.0)
+        return carry
+
+    lax.fori_loop(0, nz + 2, first, 0)
+
+    part_ref[...] = jnp.zeros(part_ref.shape, f32)
+    live = place[3] > 0
+
+    def core(values):
+        return values[8 : 8 + nx, 0:ny]
+
+    def second(j, carry):
+        s_mid = S[j + 1]
+        s0 = core(s_mid)
+        below = (core(S[j]), core(roll(s_mid, 1, 0)), core(roll(s_mid, 1, 1)))
+        above = (core(S[j + 2]), core(roll(s_mid, -1, 0)), core(roll(s_mid, -1, 1)))
+        speeds = tuple(v_ref[d, 0, j].astype(f32) for d in range(3))
+        c0 = c_ref[j]
+        adv = 0.5 * (c0 + s0 + stencil(s0, below, above, speeds))
+        adv = jnp.where(live, adv, 0.0)
+        adv_ref[0, j] = adv
+        p = poro_ref[0, j].astype(f32)
+        w = sat_ref[0, j].astype(f32)
+        sigma = ARCHIE * jnp.exp(adv) * p * p * w * w
+        half = jnp.dot(sigma, pool_y[...], precision=lax.Precision.HIGHEST, preferred_element_type=f32)
+        coarse = jnp.dot(pool_x[...], half, precision=lax.Precision.HIGHEST, preferred_element_type=f32)
+        for e in range(part_ref.shape[0]):
+            part_ref[e] = part_ref[e] + weights[e, j] * coarse
+        return carry
+
+    lax.fori_loop(0, nz, second, 0)
+
+
+def transport_call(place, weights, c, velocity, porosity, saturation, *pieces, grid):
+    nz, nx, ny = c.shape
+    wx, wy = nx + 16, ny + 128
+    resist_layers = weights.shape[0]
+    pool_y = (
+        jnp.arange(ny, dtype=jnp.int32)[:, None] // 2 == jnp.arange(ny // 2, dtype=jnp.int32)[None, :]
+    ).astype(jnp.float32)
+    pool_x = (
+        jnp.arange(nx // 2, dtype=jnp.int32)[:, None] == jnp.arange(nx, dtype=jnp.int32)[None, :] // 2
+    ).astype(jnp.float32)
+    vmem = pl.BlockSpec(memory_space=pltpu.VMEM)
+    smem = pl.BlockSpec(memory_space=pltpu.SMEM)
+    cells = nz * nx * ny
+    return pl.pallas_call(
+        functools.partial(transport_kernel, grid),
+        out_shape=(
+            jax.ShapeDtypeStruct((1, nz, nx, ny), jnp.float32),
+            jax.ShapeDtypeStruct((resist_layers, nx // 2, ny // 2), jnp.float32),
+        ),
+        in_specs=[smem, smem] + [vmem] * 14,
+        out_specs=(vmem, vmem),
+        scratch_shapes=[
+            pltpu.VMEM((nz + 4, wx, wy), jnp.float32),
+            pltpu.VMEM((3, nz + 2, wx, wy), jnp.float32),
+            pltpu.VMEM((nz + 2, wx, wy), jnp.float32),
+        ],
+        compiler_params=pltpu.CompilerParams(vmem_limit_bytes=60 * 1024 * 1024),
+        cost_estimate=pl.CostEstimate(
+            flops=200 * cells, transcendentals=cells, bytes_accessed=40 * cells
+        ),
+    )(place, weights, c, velocity, porosity, saturation, *pieces, pool_y, pool_x)
 
 
 def neighbours(padded, direction_index):
@@ -78,37 +269,6 @@
     slabs = 3
     speeds = velocity[:, 0]
 
-    field_wide = with_halo(field, (("grp", 0), ("gx", 1), ("gy", 2)), 2, top=slabs)
-    speeds_wide = with_halo(speeds, (("grp", 1), ("gx", 2), ("gy", 3)), 1, top=slabs).astype(
-        jnp.float32
-    )
-
-    section_wide = field_wide[1:-1, 1:-1, 1:-1] + tendency(field_wide, speeds_wide)
-    keep = (
-        inside(group_index * layers - 1, layers + 2, slabs * layers)[:, None, None]
-        & inside(row_index * tile_x - 1, tile_x + 2, rows * tile_x)[None, :, None]
-        & inside(column_index * tile_y - 1, tile_y + 2, columns * tile_y)[None, None, :]
-    )
-    section_wide = jnp.where(keep, section_wide, 0.0)
-    advanced = 0.5 * (
-        field
-        + section_wide[1:-1, 1:-1, 1:-1]
-        + tendency(section_wide, speeds_wide[:, 1:-1, 1:-1, 1:-1])
-    )
-    advanced = jnp.where(active, advanced, 0.0)
-
-    poro = porosity[0].astype(jnp.float32)
-    water = saturation[0].astype(jnp.float32)
-    sigma = ARCHIE * jnp.exp(advanced) * poro * poro * water * water
-    coarse_x = tile_x // 2
-    coarse_y = tile_y // 2
-    pool_y = (
-        jnp.arange(tile_y, dtype=jnp.int32)[:, None] // 2
-        == jnp.arange(coarse_y, dtype=jnp.int32)[None, :]
-    ).astype(jnp.float32)
-    half = jnp.einsum("zxy,yc->zxc", sigma, pool_y, precision=lax.Precision.HIGHEST)
-    coarse = half.reshape(layers, coarse_x, 2, coarse_y).sum(axis=2)
-
     ends = jnp.cumsum(layer_counts)
     starts = ends - layer_counts
     layer_ids = group_index * layers + jnp.arange(layers, dtype=jnp.int32)
@@ -117,20 +277,26 @@
     ).astype(jnp.float32)
     weights = member / (4.0 * layer_counts.astype(jnp.float32))[:, None]
     resist_layers = layer_counts.shape[0]
-    partial_cond = jnp.dot(
-        weights, coarse.reshape(layers, coarse_x * coarse_y), precision=lax.Precision.HIGHEST
-    ).reshape(resist_layers, coarse_x, coarse_y)
+    coarse_x = tile_x // 2
+    coarse_y = tile_y // 2
+
+    pieces = transport_halo(field, speeds, slabs)
+    place = jnp.stack([group_index, row_index, column_index, active.astype(jnp.int32)])
+    advanced, partial_cond = transport_call(
+        place, weights, field, velocity, porosity, saturation, *pieces,
+        grid=(slabs * layers, rows * tile_x, columns * tile_y),
+    )
     conductivity = grp_sum(partial_cond)
 
     grid_x = coarse_x * rows
     grid_y = coarse_y * columns
     depth = SWEEPS
     potential = lax.dynamic_slice_in_dim(init_potential, group_index, 1, 0)
-    potential = with_halo(potential, (("gx", 2), ("gy", 3)), depth)
     poles = lax.dynamic_slice_in_dim(electrodes, group_index, 1, 0)
 
-    cond_wide = with_halo(conductivity, (("gx", 1), ("gy", 2)), depth)
-    cond_wide = jnp.pad(cond_wide, ((1, 1), (0, 0), (0, 0)))
+    both = with_halo(jnp.concatenate([conductivity, potential[0]], axis=0), (("gx", 1), ("gy", 2)), depth)
+    cond_wide = jnp.pad(both[:resist_layers], ((1, 1), (0, 0), (0, 0)))
+    potential = both[None, resist_layers:]
     wide_x = coarse_x + 2 * depth
     wide_y = coarse_y + 2 * depth
     gx_ids = row_index * coarse_x - depth + jnp.arange(wide_x, dtype=jnp.int32)
@@ -187,7 +353,7 @@
         updated = pot_c + OMEGA * (rhs - applied) / diagonal
         potential = jnp.where(on_grid[m : m + nx, m : m + ny], updated, 0.0)
 
-    return (advanced[None], conductivity, potential)
+    return (advanced, conductivity, potential)
 
 
 def solution(mesh):

time: 179 us -> 147 us (0.82)
  other arithmetic: 57.9 us -> 24.4 us
  Pallas kernels: 0 us -> 32.4 us
  starting transfers between devices: 67 us -> 36.6 us
  waiting for transfers between devices: 11.3 us -> 19.4 us
  matrix products: 4.68 us -> 0 us
  local copies, waits for them, and re-layouts: 35 us -> 32 us
    ppermute x10 -> x2, starting transfers between devices: 43.3 us -> 10 us  [with_halo(): before = lax.ppermute(last, axis, up)]
    pallas_call x0 -> x1, Pallas kernels: none -> 32.4 us  [transport_call(): pl.pallas_call(functools.partial(transport_kernel, grid), out_shape=(jax....]
    select_n x3 -> x2, other arithmetic: 22.3 us -> 0.53 us  [the longest x1 0.52 us: transport_call(): jnp.arange(nx, dtype=jnp.int32)[None, :] // 2]
    ppermute x0 -> x6, starting transfers between devices: none -> 20.9 us  [the longest x1 6.14 us: transport_halo(): bx = lax.ppermute(send_up, 'gx', up)]
    ppermute x10 -> x2, starting transfers between devices: 23.6 us -> 3.21 us  [with_halo(): after = lax.ppermute(initial, axis, down)]
    slice x5 -> x40, local copies, waits for them, and re-layouts: 7.5 us -> 19.9 us  [the longest x3 9.37 us: xz_u(): u[..., lane]]
    slice x9 -> x1, local copies, waits for them, and re-layouts: 11.3 us -> 0.16 us  [with_halo(): last = lax.slice_in_dim(shard, length - width, length, axis=dim)]
    concatenate x7 -> x3, other arithmetic: 10.7 us -> 0.74 us  [with_halo(): shard = jnp.concatenate([before, shard, after], axis=dim)]
  transfers between devices with their start and end apart: 22 -> 12, of which waited for: 5 -> 5; matrix products, arithmetic and copies ran while one was open for 52% -> 23% of each run, Pallas kernels for 0% -> 0%
where the time goes in v2:
time: 147 us; the launch traced here: 146 us
  starting transfers between devices  36.6 us (25%)
  Pallas kernels  32.4 us (22%)
  local copies, waits for them, and re-layouts  32 us (22%)
  other arithmetic  24.4 us (17%)
  waiting for transfers between devices  19.4 us (13%)
    pallas_call x1, Pallas kernels, transport_call(): pl.pallas_call(functools.partial(transport_kernel, grid), out_shape=(jax....  32.4 us
    ppermute x2, waiting for transfers between devices, with_halo(): after = lax.ppermute(initial, axis, down)  11.6 us
    ppermute x2, starting transfers between devices, with_halo(): before = lax.ppermute(last, axis, up)  10 us
    slice x3, local copies, waits for them, and re-layouts, xz_u(): u[..., lane]  9.37 us
    ppermute x1, starting transfers between devices, transport_halo(): bx = lax.ppermute(send_up, 'gx', up)  6.14 us
    ppermute x1, starting transfers between devices, transport_halo(): lax.ppermute(jnp.concatenate([xz_c(slice(ny - 2, ny)), xz_u(ny - 1)], 2),...  4.55 us
    ppermute x1, starting transfers between devices, transport_halo(): above = lax.ppermute(jnp.concatenate([c[:2], u[:, 0]], 0), 'grp', down)  4.27 us
    concatenate x1, other arithmetic, transport_halo(): jnp.concatenate([yu_hi, jnp.zeros((3, nz + 2, nx + 4, 126), f32), yu_lo], 3)  4.25 us
  transfers between devices with their start and end apart: 12, of which 5 were waited for; matrix products, arithmetic and copies ran while one was open for 23% of the time, Pallas kernels for 0%

profile of v2, /device:TPU:102, one launch (start us, length us, event | category | flops | bytes accessed | tf_op | source)
XLA Modules:
  0.0 146.1 jit_solution(123191895760042776)
XLA Ops:
  0.7 3.0 %bitcast_convert_fusion = f32[3,32,64,256]{3,2,0,1:T(8,128)S(1)} fusion(bf16[3,1,32,64,256]{4,3,2,1,0:T(8,128)(2,1)} %v_ref.1), kind=kLoop, calls=%fused_computation.1 | loop fusion | flops 1572864 | bytes 9437184 | tf_op jit(solution)/shard_map/convert_element_type | solution.py:35
  4.4 1.3 collective-permute-start
  6.5 4.3 %collective-permute-start.1 = (f32[5,64,256]{2,1,0:T(8,128)}, f32[5,64,256]{2,1,0:T(8,128)S(1)}, u32[]{:S(2)}, u32[]{:S(2)}) collective-permute-start(f32[5,64,256]{2,1,0:T(8,128)} %pad_maximum_fusion.6), channel_id=1, source_target_pairs={{64,0},{128,64},{65,1},{129,65},{66,2},{130,66},{67,3},{131,67},{6... | collective-permute-start | bytes 983048 | tf_op jit(solution)/shard_map/ppermute | solution.py:44
  10.9 3.7 %fusion.72 = (f32[3,32,64,1]{3,2,0,1:T(8,128)}, f32[3,32,64,1]{3,2,0,1:T(8,128)}) fusion(f32[3,32,64,256]{3,2,0,1:T(8,128)S(1)} %bitcast_convert_fusion), kind=kLoop, calls=%fused_computation.192 | loop fusion | bytes 98304 | tf_op jit(solution)/shard_map/slice | solution.py:68
  15.3 1.7 %fusion.74 = (f32[32,64,2]{2,1,0:T(8,128)}, f32[32,64,2]{2,1,0:T(8,128)}) fusion(f32[32,64,256]{2,1,0:T(8,128)S(1)} %bitcast.156), kind=kLoop, calls=%fused_computation.194 | loop fusion | bytes 65536 | tf_op jit(solution)/shard_map/slice | solution.py:63
  17.5 3.1 %copy.250 = f32[3,32,64,1]{2,1,0,3:T(8,128)} copy(f32[3,32,64,1]{3,2,0,1:T(8,128)} %get-tuple-element.15) | data formatting | bytes 49152 | tf_op jit(solution)/shard_map/slice | solution.py:68
  21.7 2.5 %copy.259 = f32[3,32,64,1]{2,1,0,3:T(8,128)S(1)} copy(f32[3,32,64,1]{3,2,0,1:T(8,128)} %get-tuple-element.16) | data formatting | bytes 49152 | tf_op jit(solution)/shard_map/slice | solution.py:68
  27.8 1.2 fusion.70.pool_x
  31.3 3.3 %collective-permute-start.2 = (f32[36,5,256]{2,0,1:T(8,128)S(1)}, f32[36,5,256]{2,0,1:T(8,128)S(1)}, u32[]{:S(2)}, u32[]{:S(2)}) collective-permute-start(f32[36,5,256]{2,0,1:T(8,128)S(1)} %pad_maximum_fusion.9), channel_id=1, source_target_pairs={{4,0},{8,4},{12,8},{16,12},{20,16},{24,20},{28,24},{32,28},{36,32}... | collective-permute-start | bytes 552968 | tf_op jit(solution)/shard_map/ppermute | solution.py:60
  34.7 6.1 %collective-permute-start.3 = (f32[36,5,256]{2,0,1:T(8,128)S(1)}, f32[36,5,256]{2,0,1:T(8,128)S(1)}, u32[]{:S(2)}, u32[]{:S(2)}) collective-permute-start(f32[36,5,256]{2,0,1:T(8,128)S(1)} %pad_maximum_fusion.10), channel_id=1, source_target_pairs={{0,4},{4,8},{8,12},{12,16},{16,20},{20,24},{24,28},{28,32},{32,36}... | collective-permute-start | bytes 552968 | tf_op jit(solution)/shard_map/ppermute | solution.py:59
  46.4 1.3 collective-permute-start.4
  48.9 4.6 %collective-permute-start.5 = (f32[36,68,5]{1,0,2:T(8,128)S(1)}, f32[36,68,5]{1,0,2:T(8,128)S(1)}, u32[]{:S(2)}, u32[]{:S(2)}) collective-permute-start(f32[36,68,5]{1,0,2:T(8,128)S(1)} %pad_maximum_fusion.16), channel_id=1, source_target_pairs={{0,1},{1,2},{2,3},{4,5},{5,6},{6,7},{8,9},{9,10},{10,11},{12,13},{... | collective-permute-start | bytes 146888 | tf_op jit(solution)/shard_map/ppermute | solution.py:78
  53.8 1.2 pad_maximum_fusion.2.xu
  55.8 2.9 %copy.265 = f32[3,34,68,1]{3,2,1,0:T(8,128)} copy(f32[3,34,68,1]{2,1,0,3:T(8,128)S(1)} %slice_bitcast_fusion.8) | data formatting | bytes 55488 | tf_op jit(solution)/shard_map/broadcast_in_dim | solution.py:87
  58.7 2.9 %copy.266 = f32[3,34,68,1]{3,2,1,0:T(8,128)} copy(f32[3,34,68,1]{2,1,0,3:T(8,128)S(1)} %slice_bitcast_fusion.7) | data formatting | bytes 55488 | tf_op jit(solution)/shard_map/broadcast_in_dim | solution.py:88
  61.6 4.2 %pad_maximum_fusion = f32[3,34,68,128]{3,2,1,0:T(8,128)S(1)} fusion(f32[3,34,68,1]{3,2,1,0:T(8,128)} %copy.266, f32[3,34,68,1]{3,2,1,0:T(8,128)} %copy.265, f32[128]{0:T(128)S(1)} %pad.77.clone), kind=kLoop, calls=%fused_computation | loop fusion | flops 1775616 | bytes 3607232 | tf_op jit(solution)/shard_map/concatenate | solution.py:89
  65.8 2.5 %pad.43.yu = f32[3,34,80,128]{3,2,1,0:T(8,128)} pad(f32[3,34,68,128]{3,2,1,0:T(8,128)S(1)} %pad_maximum_fusion, f32[]{:T(128)} %constant.72.clone.1), padding=0_0x0_0x6_6x0_0 | pad | bytes 7729156 | tf_op jit(solution)/shard_map/jit(_pad)/pad | solution.py:90
  69.9 1.3 pad.42.yc
  71.2 32.4 %shard_map.94 = (f32[1,32,64,256]{3,2,1,0:T(8,128)}, f32[8,32,128]{2,1,0:T(8,128)}) custom-call(s32[4]{0:T(128)} %pad_add_fusion.place, f32[8,32]{1,0:T(8,128)} %convert_divide_fusion.weights, f32[32,64,256]{2,1,0:T(8,128)} %bitcast.154, bf16[3,1,32,64,256]{4,3,2,1,0:T(8,128)(2,1)} %v_ref.1, bf16[1,32,64,256]{3,2,1,0:T(8,128)(2,1)} %poro_ref.1, ...), custom_call_target="tpu_custom_call" | custom-call | flops 104857600 | bytes 20971520 | tf_op jit(solution)/shard_map/pallas_call | solution.py:200
  103.6 1.5 subtract_multiply_fusion
  106.1 2.6 %collective-permute-start.7 = (f32[8,32,128]{2,1,0:T(8,128)S(1)}, f32[8,32,128]{2,1,0:T(8,128)S(1)}, u32[]{:S(2)}, u32[]{:S(2)}) collective-permute-start(f32[8,32,128]{2,1,0:T(8,128)S(1)} %add.275), channel_id=1, source_target_pairs={{0,128},{128,0},{64,192},{192,64},{1,129},{129,1},{65,193},{193,65... | collective-permute-start | bytes 393224 | tf_op jit(solution)/shard_map/ppermute | solution.py:255
  108.7 4.0 %collective-permute-done.7 = f32[8,32,128]{2,1,0:T(8,128)S(1)} collective-permute-done((f32[8,32,128]{2,1,0:T(8,128)S(1)}, f32[8,32,128]{2,1,0:T(8,128)S(1)}, u32[]{:S(2)}, u32[]{:S(2)}) %collective-permute-start.7) | collective-permute-done | bytes 131104 | tf_op jit(solution)/shard_map/ppermute | solution.py:255
  112.8 6.5 %collective-permute-start.8 = (f32[16,3,128]{2,1,0:T(4,128)S(1)}, f32[16,3,128]{2,1,0:T(4,128)S(1)}, u32[]{:S(2)}, u32[]{:S(2)}) collective-permute-start(f32[16,3,128]{2,1,0:T(4,128)S(1)} %get-tuple-element.45), channel_id=1, source_target_pairs={{0,4},{4,8},{8,12},{12,16},{16,20},{20,24},{24,28},{28,32},{32,36}... | collective-permute-start | bytes 73736 | tf_op jit(solution)/shard_map/ppermute | solution.py:27
  119.3 1.9 %collective-permute-start.9 = (f32[16,3,128]{2,1,0:T(4,128)S(1)}, f32[16,3,128]{2,1,0:T(4,128)S(1)}, u32[]{:S(2)}, u32[]{:S(2)}) collective-permute-start(f32[16,3,128]{2,1,0:T(4,128)S(1)} %get-tuple-element.46), channel_id=1, source_target_pairs={{4,0},{8,4},{12,8},{16,12},{20,16},{24,20},{28,24},{32,28},{36,32}... | collective-permute-start | bytes 73736 | tf_op jit(solution)/shard_map/ppermute | solution.py:28
  121.3 7.5 %collective-permute-done.9 = f32[16,3,128]{2,1,0:T(4,128)S(1)} collective-permute-done((f32[16,3,128]{2,1,0:T(4,128)S(1)}, f32[16,3,128]{2,1,0:T(4,128)S(1)}, u32[]{:S(2)}, u32[]{:S(2)}) %collective-permute-start.9) | collective-permute-done | bytes 24608 | tf_op jit(solution)/shard_map/ppermute | solution.py:28
  128.9 3.5 %collective-permute-start.10 = (f32[16,38,3]{2,1,0:T(8,128)S(1)}, f32[16,38,3]{2,1,0:T(8,128)S(1)}, u32[]{:S(2)}, u32[]{:S(2)}) collective-permute-start(f32[16,38,3]{2,1,0:T(8,128)S(1)} %get-tuple-element.31), channel_id=1, source_target_pairs={{0,1},{1,2},{2,3},{4,5},{5,6},{6,7},{8,9},{9,10},{10,11},{12,13},{... | collective-permute-start | bytes 21896 | tf_op jit(solution)/shard_map/ppermute | solution.py:27
  132.4 1.3 collective-permute-start.11
  134.1 3.7 %collective-permute-done.10 = f32[16,38,3]{2,1,0:T(8,128)S(1)} collective-permute-done((f32[16,38,3]{2,1,0:T(8,128)S(1)}, f32[16,38,3]{2,1,0:T(8,128)S(1)}, u32[]{:S(2)}, u32[]{:S(2)}) %collective-permute-start.10) | collective-permute-done | bytes 7328 | tf_op jit(solution)/shard_map/ppermute | solution.py:27
  137.7 4.1 %collective-permute-done.11 = f32[16,38,3]{2,1,0:T(8,128)S(1)} collective-permute-done((f32[16,38,3]{2,1,0:T(8,128)S(1)}, f32[16,38,3]{2,1,0:T(8,128)S(1)}, u32[]{:S(2)}, u32[]{:S(2)}) %collective-permute-start.11) | collective-permute-done | bytes 7328 | tf_op jit(solution)/shard_map/ppermute | solution.py:28
  142.3 1.1 fusion.41
  143.8 1.1 fusion.40
  144.9 1.2 fusion.65
  (140 shorter events, 21.5 us)
Async XLA Ops:
  0.6 108.0 %copy-start = (f32[4,8,32,128]{3,2,1,0:T(8,128)S(1)}, f32[4,8,32,128]{3,2,1,0:T(8,128)}, u32[]{:S(2)}) copy-start(f32[4,8,32,128]{3,2,1,0:T(8,128)} %param.13) | copy-start | bytes 1572868
  0.6 3.0 %copy-start.1 = (f32[1,32,64,256]{3,2,1,0:T(8,128)S(1)}, f32[1,32,64,256]{3,2,1,0:T(8,128)}, u32[]{:S(2)}) copy-start(f32[1,32,64,256]{3,2,1,0:T(8,128)} %param.7) | copy-start | bytes 6291460
  4.4 26.6 %collective-permute-start = (f32[5,64,256]{2,1,0:T(8,128)}, f32[5,64,256]{2,1,0:T(8,128)S(1)}, u32[]{:S(2)}, u32[]{:S(2)}) collective-permute-start(f32[5,64,256]{2,1,0:T(8,128)} %pad_maximum_fusion.5), channel_id=1, source_target_pairs={{0,64},{64,128},{1,65},{65,129},{2,66},{66,130},{3,67},{67,131},{4... | collective-permute-start | bytes 983048 | tf_op jit(solution)/shard_map/ppermute | solution.py:43
  6.5 24.6 %collective-permute-start.1 = (f32[5,64,256]{2,1,0:T(8,128)}, f32[5,64,256]{2,1,0:T(8,128)S(1)}, u32[]{:S(2)}, u32[]{:S(2)}) collective-permute-start(f32[5,64,256]{2,1,0:T(8,128)} %pad_maximum_fusion.6), channel_id=1, source_target_pairs={{64,0},{128,64},{65,1},{129,65},{66,2},{130,66},{67,3},{131,67},{6... | collective-permute-start | bytes 983048 | tf_op jit(solution)/shard_map/ppermute | solution.py:44
  17.0 3.7 %copy-start.4 = (f32[32,64,2]{2,1,0:T(8,128)S(1)}, f32[32,64,2]{2,1,0:T(8,128)}, u32[]{:S(2)}) copy-start(f32[32,64,2]{2,1,0:T(8,128)} %get-tuple-element.21) | copy-start | bytes 49156
  17.5 6.6 %copy-start.3 = (f32[32,64,2]{2,1,0:T(8,128)S(1)}, f32[32,64,2]{2,1,0:T(8,128)}, u32[]{:S(2)}) copy-start(f32[32,64,2]{2,1,0:T(8,128)} %get-tuple-element.22) | copy-start | bytes 49156
  20.7 8.3 %copy-start.8 = (s32[4,2]{0,1:T(2,128)S(1)}, s32[4,2]{0,1:T(2,128)}, u32[]{:S(2)}) copy-start(s32[4,2]{0,1:T(2,128)} %param.12) | copy-start | bytes 100
  21.7 9.4 %copy-start.5 = (f32[32,2,256]{2,1,0:T(2,128)S(1)}, f32[32,2,256]{2,1,0:T(2,128)}, u32[]{:S(2)}) copy-start(f32[32,2,256]{2,1,0:T(2,128)} %get-tuple-element.24) | copy-start | bytes 196612
  24.2 20.3 %copy-start.6 = (f32[3,32,64,1]{2,1,0,3:T(8,128)S(1)}, f32[3,32,64,1]{2,1,0,3:T(8,128)}, u32[]{:S(2)}) copy-start(f32[3,32,64,1]{2,1,0,3:T(8,128)} %copy.250) | copy-start | bytes 73732
  24.6 21.4 %copy-start.7 = (f32[32,64,2]{1,2,0:T(2,128)S(1)}, f32[32,64,2]{1,2,0:T(2,128)}, u32[]{:S(2)}) copy-start(f32[32,64,2]{1,2,0:T(2,128)} %copy.246) | copy-start | bytes 49156
  31.3 13.3 %collective-permute-start.2 = (f32[36,5,256]{2,0,1:T(8,128)S(1)}, f32[36,5,256]{2,0,1:T(8,128)S(1)}, u32[]{:S(2)}, u32[]{:S(2)}) collective-permute-start(f32[36,5,256]{2,0,1:T(8,128)S(1)} %pad_maximum_fusion.9), channel_id=1, source_target_pairs={{4,0},{8,4},{12,8},{16,12},{20,16},{24,20},{28,24},{32,28},{36,32}... | collective-permute-start | bytes 552968 | tf_op jit(solution)/shard_map/ppermute | solution.py:60
  34.7 10.2 %collective-permute-start.3 = (f32[36,5,256]{2,0,1:T(8,128)S(1)}, f32[36,5,256]{2,0,1:T(8,128)S(1)}, u32[]{:S(2)}, u32[]{:S(2)}) collective-permute-start(f32[36,5,256]{2,0,1:T(8,128)S(1)} %pad_maximum_fusion.10), channel_id=1, source_target_pairs={{0,4},{4,8},{8,12},{12,16},{16,20},{20,24},{24,28},{28,32},{32,36}... | collective-permute-start | bytes 552968 | tf_op jit(solution)/shard_map/ppermute | solution.py:59
  46.4 9.4 %collective-permute-start.4 = (f32[36,68,5]{1,0,2:T(8,128)S(1)}, f32[36,68,5]{1,0,2:T(8,128)S(1)}, u32[]{:S(2)}, u32[]{:S(2)}) collective-permute-start(f32[36,68,5]{1,0,2:T(8,128)S(1)} %pad_maximum_fusion.15), channel_id=1, source_target_pairs={{1,0},{2,1},{3,2},{5,4},{6,5},{7,6},{9,8},{10,9},{11,10},{13,12},{... | collective-permute-start | bytes 146888 | tf_op jit(solution)/shard_map/ppermute | solution.py:79
  48.9 9.8 %collective-permute-start.5 = (f32[36,68,5]{1,0,2:T(8,128)S(1)}, f32[36,68,5]{1,0,2:T(8,128)S(1)}, u32[]{:S(2)}, u32[]{:S(2)}) collective-permute-start(f32[36,68,5]{1,0,2:T(8,128)S(1)} %pad_maximum_fusion.16), channel_id=1, source_target_pairs={{0,1},{1,2},{2,3},{4,5},{5,6},{6,7},{8,9},{9,10},{10,11},{12,13},{... | collective-permute-start | bytes 146888 | tf_op jit(solution)/shard_map/ppermute | solution.py:78
  103.6 1.6 %collective-permute-start.6 = (f32[8,32,128]{2,1,0:T(8,128)}, f32[8,32,128]{2,1,0:T(8,128)S(1)}, u32[]{:S(2)}, u32[]{:S(2)}) collective-permute-start(f32[8,32,128]{2,1,0:T(8,128)} %get-tuple-element.6), channel_id=1, source_target_pairs={{0,64},{64,0},{128,192},{192,128},{1,65},{65,1},{129,193},{193,129... | collective-permute-start | bytes 393224 | tf_op jit(solution)/shard_map/ppermute | solution.py:253
  106.1 6.6 %collective-permute-start.7 = (f32[8,32,128]{2,1,0:T(8,128)S(1)}, f32[8,32,128]{2,1,0:T(8,128)S(1)}, u32[]{:S(2)}, u32[]{:S(2)}) collective-permute-start(f32[8,32,128]{2,1,0:T(8,128)S(1)} %add.275), channel_id=1, source_target_pairs={{0,128},{128,0},{64,192},{192,64},{1,129},{129,1},{65,193},{193,65... | collective-permute-start | bytes 393224 | tf_op jit(solution)/shard_map/ppermute | solution.py:255
  112.7 32.2 %copy-start.2 = (f32[8,32,128]{2,1,0:T(8,128)}, f32[8,32,128]{2,1,0:T(8,128)S(1)}, u32[]{:S(2)}) copy-start(f32[8,32,128]{2,1,0:T(8,128)S(1)} %add.276) | copy-start | bytes 393220
  112.8 8.5 %collective-permute-start.8 = (f32[16,3,128]{2,1,0:T(4,128)S(1)}, f32[16,3,128]{2,1,0:T(4,128)S(1)}, u32[]{:S(2)}, u32[]{:S(2)}) collective-permute-start(f32[16,3,128]{2,1,0:T(4,128)S(1)} %get-tuple-element.45), channel_id=1, source_target_pairs={{0,4},{4,8},{8,12},{12,16},{16,20},{20,24},{24,28},{28,32},{32,36}... | collective-permute-start | bytes 73736 | tf_op jit(solution)/shard_map/ppermute | solution.py:27
  119.3 9.4 %collective-permute-start.9 = (f32[16,3,128]{2,1,0:T(4,128)S(1)}, f32[16,3,128]{2,1,0:T(4,128)S(1)}, u32[]{:S(2)}, u32[]{:S(2)}) collective-permute-start(f32[16,3,128]{2,1,0:T(4,128)S(1)} %get-tuple-element.46), channel_id=1, source_target_pairs={{4,0},{8,4},{12,8},{16,12},{20,16},{24,20},{28,24},{32,28},{36,32}... | collective-permute-start | bytes 73736 | tf_op jit(solution)/shard_map/ppermute | solution.py:28
  128.9 8.8 %collective-permute-start.10 = (f32[16,38,3]{2,1,0:T(8,128)S(1)}, f32[16,38,3]{2,1,0:T(8,128)S(1)}, u32[]{:S(2)}, u32[]{:S(2)}) collective-permute-start(f32[16,38,3]{2,1,0:T(8,128)S(1)} %get-tuple-element.31), channel_id=1, source_target_pairs={{0,1},{1,2},{2,3},{4,5},{5,6},{6,7},{8,9},{9,10},{10,11},{12,13},{... | collective-permute-start | bytes 21896 | tf_op jit(solution)/shard_map/ppermute | solution.py:27
  132.4 9.4 %collective-permute-start.11 = (f32[16,38,3]{2,1,0:T(8,128)S(1)}, f32[16,38,3]{2,1,0:T(8,128)S(1)}, u32[]{:S(2)}, u32[]{:S(2)}) collective-permute-start(f32[16,38,3]{2,1,0:T(8,128)S(1)} %get-tuple-element.32), channel_id=1, source_target_pairs={{1,0},{2,1},{3,2},{5,4},{6,5},{7,6},{9,8},{10,9},{11,10},{13,12},{... | collective-permute-start | bytes 21896 | tf_op jit(solution)/shard_map/ppermute | solution.py:28

commit v3 on v2

--- a/solution.py
+++ b/solution.py
@@ -32,7 +32,6 @@
 
 def transport_halo(c, u, slabs):
     f32 = jnp.float32
-    u = u.astype(f32)
     nz, nx, ny = c.shape
 
     def chain(axis, members):
@@ -40,8 +39,8 @@
         return up, [(j, i) for i, j in up]
 
     up, down = chain("grp", slabs)
-    below = lax.ppermute(jnp.concatenate([c[nz - 2 :], u[:, nz - 1]], 0), "grp", up)
-    above = lax.ppermute(jnp.concatenate([c[:2], u[:, 0]], 0), "grp", down)
+    below = lax.ppermute(jnp.concatenate([c[nz - 2 :], u[:, nz - 1].astype(f32)], 0), "grp", up)
+    above = lax.ppermute(jnp.concatenate([c[:2], u[:, 0].astype(f32)], 0), "grp", down)
     zlo_c, zlo_u = below[:2], below[2:]
     zhi_c, zhi_u = above[:2], above[2:]
 
@@ -49,7 +48,9 @@
         return jnp.concatenate([zlo_c[:, rows], c[:, rows], zhi_c[:, rows]], 0)
 
     def zext_u(row):
-        core = jnp.concatenate([zlo_u[:, None, row], u[:, :, row], zhi_u[:, None, row]], 1)
+        core = jnp.concatenate(
+            [zlo_u[:, None, row], u[:, :, row].astype(f32), zhi_u[:, None, row]], 1
+        )
         return jnp.pad(core, ((0, 0), (1, 1), (0, 0)))
 
     rows = lax.axis_size("gx")
@@ -65,7 +66,9 @@
 
     def xz_u(lane):
         core = jnp.pad(
-            jnp.concatenate([zlo_u[:, None, :, lane], u[..., lane], zhi_u[:, None, :, lane]], 1),
+            jnp.concatenate(
+                [zlo_u[:, None, :, lane], u[..., lane].astype(f32), zhi_u[:, None, :, lane]], 1
+            ),
             ((0, 0), (1, 1), (0, 0)),
         )
         lo = jnp.swapaxes(bx[:, 2:5, lane], 0, 1)[:, :, None]
@@ -107,11 +110,19 @@
 
 def transport_kernel(
     grid, place, weights, c_ref, v_ref, poro_ref, sat_ref, zlo_c, zhi_c, zlo_u, zhi_u,
-    xc, xu, yc, yu, pool_y, pool_x, adv_ref, part_ref, F, U, S,
+    xc, xu, yc, yu, adv_ref, part_ref, F, U, S,
 ):
     nz, nx, ny = c_ref.shape
     wx, wy = F.shape[1], F.shape[2]
     f32 = jnp.float32
+    pool_y = (
+        lax.broadcasted_iota(jnp.int32, (ny, ny // 2), 0) // 2
+        == lax.broadcasted_iota(jnp.int32, (ny, ny // 2), 1)
+    ).astype(f32)
+    pool_x = (
+        lax.broadcasted_iota(jnp.int32, (nx // 2, nx), 0)
+        == lax.broadcasted_iota(jnp.int32, (nx // 2, nx), 1) // 2
+    ).astype(f32)
     F[0:2, 8 : 8 + nx, 0:ny] = zlo_c[...]
     F[nz + 2 : nz + 4, 8 : 8 + nx, 0:ny] = zhi_c[...]
 
@@ -175,8 +186,8 @@
         p = poro_ref[0, j].astype(f32)
         w = sat_ref[0, j].astype(f32)
         sigma = ARCHIE * jnp.exp(adv) * p * p * w * w
-        half = jnp.dot(sigma, pool_y[...], precision=lax.Precision.HIGHEST, preferred_element_type=f32)
-        coarse = jnp.dot(pool_x[...], half, precision=lax.Precision.HIGHEST, preferred_element_type=f32)
+        half = jnp.dot(sigma, pool_y, precision=lax.Precision.HIGHEST, preferred_element_type=f32)
+        coarse = jnp.dot(pool_x, half, precision=lax.Precision.HIGHEST, preferred_element_type=f32)
         for e in range(part_ref.shape[0]):
             part_ref[e] = part_ref[e] + weights[e, j] * coarse
         return carry
@@ -188,12 +199,6 @@
     nz, nx, ny = c.shape
     wx, wy = nx + 16, ny + 128
     resist_layers = weights.shape[0]
-    pool_y = (
-        jnp.arange(ny, dtype=jnp.int32)[:, None] // 2 == jnp.arange(ny // 2, dtype=jnp.int32)[None, :]
-    ).astype(jnp.float32)
-    pool_x = (
-        jnp.arange(nx // 2, dtype=jnp.int32)[:, None] == jnp.arange(nx, dtype=jnp.int32)[None, :] // 2
-    ).astype(jnp.float32)
     vmem = pl.BlockSpec(memory_space=pltpu.VMEM)
     smem = pl.BlockSpec(memory_space=pltpu.SMEM)
     cells = nz * nx * ny
@@ -203,7 +208,7 @@
             jax.ShapeDtypeStruct((1, nz, nx, ny), jnp.float32),
             jax.ShapeDtypeStruct((resist_layers, nx // 2, ny // 2), jnp.float32),
         ),
-        in_specs=[smem, smem] + [vmem] * 14,
+        in_specs=[smem, smem] + [vmem] * 12,
         out_specs=(vmem, vmem),
         scratch_shapes=[
             pltpu.VMEM((nz + 4, wx, wy), jnp.float32),
@@ -214,7 +219,7 @@
         cost_estimate=pl.CostEstimate(
             flops=200 * cells, transcendentals=cells, bytes_accessed=40 * cells
         ),
-    )(place, weights, c, velocity, porosity, saturation, *pieces, pool_y, pool_x)
+    )(place, weights, c, velocity, porosity, saturation, *pieces)
 
 
 def neighbours(padded, direction_index):
@@ -249,6 +254,39 @@
     return (ids >= 0) & (ids < total)
 
 
+def plane_halo(values, depth):
+    rows, columns = lax.axis_size("gx"), lax.axis_size("gy")
+    d = depth
+
+    def line(n, step):
+        return [(i, i + step) for i in range(n) if 0 <= i + step < n]
+
+    def flat(i, j):
+        return i * columns + j
+
+    def diagonal(di, dj):
+        return [
+            (flat(i, j), flat(i + di, j + dj))
+            for i in range(rows)
+            for j in range(columns)
+            if 0 <= i + di < rows and 0 <= j + dj < columns
+        ]
+
+    both = ("gx", "gy")
+    lo_x = lax.ppermute(values[:, -d:, :], "gx", line(rows, 1))
+    hi_x = lax.ppermute(values[:, :d, :], "gx", line(rows, -1))
+    lo_y = lax.ppermute(values[:, :, -d:], "gy", line(columns, 1))
+    hi_y = lax.ppermute(values[:, :, :d], "gy", line(columns, -1))
+    lo_lo = lax.ppermute(values[:, -d:, -d:], both, diagonal(1, 1))
+    lo_hi = lax.ppermute(values[:, -d:, :d], both, diagonal(1, -1))
+    hi_lo = lax.ppermute(values[:, :d, -d:], both, diagonal(-1, 1))
+    hi_hi = lax.ppermute(values[:, :d, :d], both, diagonal(-1, -1))
+    top = jnp.concatenate([lo_lo, lo_x, lo_hi], 2)
+    middle = jnp.concatenate([lo_y, values, hi_y], 2)
+    bottom = jnp.concatenate([hi_lo, hi_x, hi_hi], 2)
+    return jnp.concatenate([top, middle, bottom], 1)
+
+
 def grp_sum(partial):
     pair = lax.ppermute(partial, "grp", [(0, 1), (1, 0), (2, 3), (3, 2)])
     partial = partial + pair
@@ -294,7 +332,7 @@
     potential = lax.dynamic_slice_in_dim(init_potential, group_index, 1, 0)
     poles = lax.dynamic_slice_in_dim(electrodes, group_index, 1, 0)
 
-    both = with_halo(jnp.concatenate([conductivity, potential[0]], axis=0), (("gx", 1), ("gy", 2)), depth)
+    both = plane_halo(jnp.concatenate([conductivity, potential[0]], axis=0), depth)
     cond_wide = jnp.pad(both[:resist_layers], ((1, 1), (0, 0), (0, 0)))
     potential = both[None, resist_layers:]
     wide_x = coarse_x + 2 * depth

time: 147 us -> 154 us (1.048); the launches traced: 146 us -> 151 us
  starting transfers between devices: 36.6 us -> 58.7 us
  waiting for transfers between devices: 19.4 us -> 5.37 us
  other arithmetic: 24.4 us -> 21.2 us
    ppermute x6 -> x10, starting transfers between devices: 18.8 us -> 40.6 us  [the longest x1 9.1 us: plane_halo(): lo_lo = lax.ppermute(values[:, -d:, -d:], both, diagonal(1, 1))]
    ppermute x6 -> x10, waiting for transfers between devices: 15.3 us -> 1.23 us  [the longest x1 1.21 us: plane_halo(): lo_x = lax.ppermute(values[:, -d:, :], 'gx', line(rows, 1))]
    slice x6 -> x1, local copies, waits for them, and re-layouts: 9.69 us -> 0.02 us  [transport_halo(): c[:2]]
    convert_element_type x0 -> x2, local copies, waits for them, and re-layouts: none -> 6.1 us  [xz_u(): u[..., lane].astype(f32)]
    unnamed x20 -> x25, local copies, waits for them, and re-layouts: 0.12 us -> 3.98 us
  transfers between devices with their start and end apart: 12 -> 16, of which waited for: 5 -> 3; matrix products, arithmetic and copies ran while one was open for 23% -> 19% of each run, Pallas kernels for 0% -> 0%
where the time goes in v3:
time: 154 us; the launch traced here: 151 us
  starting transfers between devices  58.7 us (38%)
  Pallas kernels  32.6 us (21%)
  local copies, waits for them, and re-layouts  32.2 us (21%)
  other arithmetic  21.2 us (14%)
  waiting for transfers between devices  5.37 us (3%)
    pallas_call x1, Pallas kernels, transport_call(): pl.pallas_call(functools.partial(transport_kernel, grid), out_shape=(jax....  32.6 us
    ppermute x1, starting transfers between devices, plane_halo(): lo_lo = lax.ppermute(values[:, -d:, -d:], both, diagonal(1, 1))  9.1 us
    ppermute x1, starting transfers between devices, plane_halo(): lo_x = lax.ppermute(values[:, -d:, :], 'gx', line(rows, 1))  7.54 us
    ppermute x1, starting transfers between devices, plane_halo(): hi_lo = lax.ppermute(values[:, :d, -d:], both, diagonal(-1, 1))  6.95 us
    ppermute x1, starting transfers between devices, transport_halo(): bx = lax.ppermute(send_up, 'gx', up)  6.14 us
    convert_element_type x2, local copies, waits for them, and re-layouts, xz_u(): u[..., lane].astype(f32)  6.1 us
    ppermute x1, starting transfers between devices, plane_halo(): lo_y = lax.ppermute(values[:, :, -d:], 'gy', line(columns, 1))  5.71 us
    ppermute x1, starting transfers between devices, transport_halo(): lax.ppermute(jnp.concatenate([xz_c(slice(ny - 2, ny)), xz_u(ny - 1)], 2),...  4.73 us
  transfers between devices with their start and end apart: 16, of which 3 were waited for; matrix products, arithmetic and copies ran while one was open for 19% of the time, Pallas kernels for 0%

profile of v3, /device:TPU:102, one launch (start us, length us, event | category | flops | bytes accessed | tf_op | source)
XLA Modules:
  0.0 151.4 jit_solution(17375362338898220679)
XLA Ops:
  0.7 3.8 %copy.301 = bf16[3,1,32,64,256]{4,2,3,0,1:T(8,128)(2,1)S(1)} copy(bf16[3,1,32,64,256]{4,3,2,1,0:T(8,128)(2,1)} %v_ref.1) | data formatting | bytes 6291456 | tf_op args[1]
  5.6 1.3 collective-permute-start
  7.6 4.3 %collective-permute-start.1 = (f32[5,64,256]{2,1,0:T(8,128)}, f32[5,64,256]{2,1,0:T(8,128)S(1)}, u32[]{:S(2)}, u32[]{:S(2)}) collective-permute-start(f32[5,64,256]{2,1,0:T(8,128)} %pad_maximum_fusion.4), channel_id=1, source_target_pairs={{64,0},{128,64},{65,1},{129,65},{66,2},{130,66},{67,3},{131,67},{6... | collective-permute-start | bytes 983048 | tf_op jit(solution)/shard_map/ppermute | solution.py:43
  11.9 3.4 %slice_convert_fusion.1 = (f32[3,32,64,1]{3,1,2,0:T(8,128)}, f32[3,32,64,1]{3,1,2,0:T(8,128)}) fusion(bf16[3,32,64,256]{3,1,2,0:T(8,128)(2,1)S(1)} %bitcast.164), kind=kLoop, calls=%fused_computation.3 | loop fusion | flops 12288 | bytes 73728 | tf_op jit(solution)/shard_map/convert_element_type | solution.py:70
  16.0 1.7 %fusion.79 = (f32[32,64,2]{2,1,0:T(8,128)}, f32[32,64,2]{2,1,0:T(8,128)}) fusion(f32[32,64,256]{2,1,0:T(8,128)S(1)} %bitcast.167), kind=kLoop, calls=%fused_computation.205 | loop fusion | bytes 65536 | tf_op jit(solution)/shard_map/slice | solution.py:64
  17.7 3.4 %copy.277 = f32[3,32,64,1]{2,1,0,3:T(8,128)} copy(f32[3,32,64,1]{3,1,2,0:T(8,128)} %get-tuple-element.15) | data formatting | bytes 49152 | tf_op jit(solution)/shard_map/convert_element_type | solution.py:70
  22.1 2.7 %copy.286 = f32[3,32,64,1]{2,1,0,3:T(8,128)S(1)} copy(f32[3,32,64,1]{3,1,2,0:T(8,128)} %get-tuple-element.16) | data formatting | bytes 49152 | tf_op jit(solution)/shard_map/convert_element_type | solution.py:70
  27.9 3.3 %collective-permute-start.2 = (f32[36,5,256]{2,0,1:T(8,128)S(1)}, f32[36,5,256]{2,0,1:T(8,128)S(1)}, u32[]{:S(2)}, u32[]{:S(2)}) collective-permute-start(f32[36,5,256]{2,0,1:T(8,128)S(1)} %pad_maximum_fusion.6), channel_id=1, source_target_pairs={{4,0},{8,4},{12,8},{16,12},{20,16},{24,20},{28,24},{32,28},{36,32}... | collective-permute-start | bytes 552968 | tf_op jit(solution)/shard_map/ppermute | solution.py:61
  31.3 6.1 %collective-permute-start.3 = (f32[36,5,256]{2,0,1:T(8,128)S(1)}, f32[36,5,256]{2,0,1:T(8,128)S(1)}, u32[]{:S(2)}, u32[]{:S(2)}) collective-permute-start(f32[36,5,256]{2,0,1:T(8,128)S(1)} %pad_maximum_fusion.7), channel_id=1, source_target_pairs={{0,4},{4,8},{8,12},{12,16},{16,20},{20,24},{24,28},{28,32},{32,36}... | collective-permute-start | bytes 552968 | tf_op jit(solution)/shard_map/ppermute | solution.py:60
  43.0 1.3 collective-permute-start.4
  45.5 4.7 %collective-permute-start.5 = (f32[36,68,5]{1,0,2:T(8,128)S(1)}, f32[36,68,5]{1,0,2:T(8,128)S(1)}, u32[]{:S(2)}, u32[]{:S(2)}) collective-permute-start(f32[36,68,5]{1,0,2:T(8,128)S(1)} %pad_maximum_fusion.13), channel_id=1, source_target_pairs={{0,1},{1,2},{2,3},{4,5},{5,6},{6,7},{8,9},{9,10},{10,11},{12,13},{... | collective-permute-start | bytes 146888 | tf_op jit(solution)/shard_map/ppermute | solution.py:81
  50.6 1.2 pad_maximum_fusion.2.xu
  52.6 2.9 %copy.292 = f32[3,34,68,1]{3,2,1,0:T(8,128)} copy(f32[3,34,68,1]{2,1,0,3:T(8,128)S(1)} %slice_bitcast_fusion.6) | data formatting | bytes 55488 | tf_op jit(solution)/shard_map/broadcast_in_dim | solution.py:90
  55.5 2.9 %copy.293 = f32[3,34,68,1]{3,2,1,0:T(8,128)} copy(f32[3,34,68,1]{2,1,0,3:T(8,128)S(1)} %slice_bitcast_fusion.5) | data formatting | bytes 55488 | tf_op jit(solution)/shard_map/broadcast_in_dim | solution.py:91
  58.4 4.2 %pad_maximum_fusion = f32[3,34,68,128]{3,2,1,0:T(8,128)S(1)} fusion(f32[3,34,68,1]{3,2,1,0:T(8,128)} %copy.293, f32[3,34,68,1]{3,2,1,0:T(8,128)} %copy.292, f32[128]{0:T(128)S(1)} %pad.81.clone), kind=kLoop, calls=%fused_computation | loop fusion | flops 1775616 | bytes 3607232 | tf_op jit(solution)/shard_map/concatenate | solution.py:92
  62.6 2.5 %pad.43.yu = f32[3,34,80,128]{3,2,1,0:T(8,128)} pad(f32[3,34,68,128]{3,2,1,0:T(8,128)S(1)} %pad_maximum_fusion, f32[]{:T(128)} %constant.25.clone.1), padding=0_0x0_0x6_6x0_0 | pad | bytes 7729156 | tf_op jit(solution)/shard_map/jit(_pad)/pad | solution.py:93
  66.7 1.3 pad.42.yc
  68.0 32.6 %shard_map.94 = (f32[1,32,64,256]{3,2,1,0:T(8,128)}, f32[8,32,128]{2,1,0:T(8,128)}) custom-call(s32[4]{0:T(128)} %pad_add_fusion.place, f32[8,32]{1,0:T(8,128)} %convert_divide_fusion.weights, f32[32,64,256]{2,1,0:T(8,128)} %bitcast.165, bf16[3,1,32,64,256]{4,3,2,1,0:T(8,128)(2,1)} %v_ref.1, bf16[1,32,64,256]{3,2,1,0:T(8,128)(2,1)} %poro_ref.1, ...), custom_call_target="tpu_custom_call" | custom-call | flops 104857600 | bytes 20971520 | tf_op jit(solution)/shard_map/pallas_call | solution.py:205
  100.5 1.4 subtract_multiply_fusion
  103.0 2.6 %collective-permute-start.7 = (f32[8,32,128]{2,1,0:T(8,128)S(1)}, f32[8,32,128]{2,1,0:T(8,128)S(1)}, u32[]{:S(2)}, u32[]{:S(2)}) collective-permute-start(f32[8,32,128]{2,1,0:T(8,128)S(1)} %add.263), channel_id=1, source_target_pairs={{0,128},{128,0},{64,192},{192,64},{1,129},{129,1},{65,193},{193,65... | collective-permute-start | bytes 393224 | tf_op jit(solution)/shard_map/ppermute | solution.py:293
  105.6 4.0 %collective-permute-done.7 = f32[8,32,128]{2,1,0:T(8,128)S(1)} collective-permute-done((f32[8,32,128]{2,1,0:T(8,128)S(1)}, f32[8,32,128]{2,1,0:T(8,128)S(1)}, u32[]{:S(2)}, u32[]{:S(2)}) %collective-permute-start.7) | collective-permute-done | bytes 131104 | tf_op jit(solution)/shard_map/ppermute | solution.py:293
  109.9 1.3 collective-permute-start.10
  111.2 7.0 %collective-permute-start.13 = (f32[16,3,3]{2,1,0:T(4,128)S(1)}, f32[16,3,3]{2,1,0:T(4,128)S(1)}, u32[]{:S(2)}, u32[]{:S(2)}) collective-permute-start(f32[16,3,3]{2,1,0:T(4,128)S(1)} %get-tuple-element.44), channel_id=1, source_target_pairs={{4,1},{5,2},{6,3},{8,5},{9,6},{10,7},{12,9},{13,10},{14,11},{16,13... | collective-permute-start | bytes 1736 | tf_op jit(solution)/shard_map/ppermute | solution.py:282
  118.1 1.3 collective-permute-start.15
  119.5 5.7 %collective-permute-start.11 = (f32[16,32,3]{2,1,0:T(8,128)S(1)}, f32[16,32,3]{2,1,0:T(8,128)S(1)}, u32[]{:S(2)}, u32[]{:S(2)}) collective-permute-start(f32[16,32,3]{2,1,0:T(8,128)S(1)} %get-tuple-element.49), channel_id=1, source_target_pairs={{0,1},{1,2},{2,3},{4,5},{5,6},{6,7},{8,9},{9,10},{10,11},{12,13},{... | collective-permute-start | bytes 18440 | tf_op jit(solution)/shard_map/ppermute | solution.py:278
  125.2 1.3 collective-permute-start.12
  126.5 9.1 %collective-permute-start.8 = (f32[16,3,3]{2,1,0:T(4,128)S(1)}, f32[16,3,3]{2,1,0:T(4,128)S(1)}, u32[]{:S(2)}, u32[]{:S(2)}) collective-permute-start(f32[16,3,3]{2,1,0:T(4,128)S(1)} %get-tuple-element.43), channel_id=1, source_target_pairs={{0,5},{1,6},{2,7},{4,9},{5,10},{6,11},{8,13},{9,14},{10,15},{12,17... | collective-permute-start | bytes 1736 | tf_op jit(solution)/shard_map/ppermute | solution.py:280
  135.6 1.9 %collective-permute-start.14 = (f32[16,3,128]{2,1,0:T(4,128)S(1)}, f32[16,3,128]{2,1,0:T(4,128)S(1)}, u32[]{:S(2)}, u32[]{:S(2)}) collective-permute-start(f32[16,3,128]{2,1,0:T(4,128)S(1)} %get-tuple-element.48), channel_id=1, source_target_pairs={{4,0},{8,4},{12,8},{16,12},{20,16},{24,20},{28,24},{32,28},{36,32}... | collective-permute-start | bytes 73736 | tf_op jit(solution)/shard_map/ppermute | solution.py:277
  137.6 7.5 %collective-permute-start.9 = (f32[16,3,128]{2,1,0:T(4,128)S(1)}, f32[16,3,128]{2,1,0:T(4,128)S(1)}, u32[]{:S(2)}, u32[]{:S(2)}) collective-permute-start(f32[16,3,128]{2,1,0:T(4,128)S(1)} %get-tuple-element.47), channel_id=1, source_target_pairs={{0,4},{4,8},{8,12},{12,16},{16,20},{20,24},{24,28},{28,32},{32,36}... | collective-permute-start | bytes 73736 | tf_op jit(solution)/shard_map/ppermute | solution.py:276
  145.5 1.2 collective-permute-done.9
  148.9 1.2 fusion.40
  150.2 1.2 fusion.66
  (147 shorter events, 19.9 us)
Async XLA Ops:
  0.6 105.0 %copy-start = (f32[4,8,32,128]{3,2,1,0:T(8,128)S(1)}, f32[4,8,32,128]{3,2,1,0:T(8,128)}, u32[]{:S(2)}) copy-start(f32[4,8,32,128]{3,2,1,0:T(8,128)} %param.13) | copy-start | bytes 1572868
  0.6 4.1 %copy-start.1 = (f32[1,32,64,256]{3,2,1,0:T(8,128)S(1)}, f32[1,32,64,256]{3,2,1,0:T(8,128)}, u32[]{:S(2)}) copy-start(f32[1,32,64,256]{3,2,1,0:T(8,128)} %param.7) | copy-start | bytes 6291460
  5.6 22.1 %collective-permute-start = (f32[5,64,256]{2,1,0:T(8,128)}, f32[5,64,256]{2,1,0:T(8,128)S(1)}, u32[]{:S(2)}, u32[]{:S(2)}) collective-permute-start(f32[5,64,256]{2,1,0:T(8,128)} %pad_maximum_fusion.3), channel_id=1, source_target_pairs={{0,64},{64,128},{1,65},{65,129},{2,66},{66,130},{3,67},{67,131},{4... | collective-permute-start | bytes 983048 | tf_op jit(solution)/shard_map/ppermute | solution.py:42
  7.6 20.0 %collective-permute-start.1 = (f32[5,64,256]{2,1,0:T(8,128)}, f32[5,64,256]{2,1,0:T(8,128)S(1)}, u32[]{:S(2)}, u32[]{:S(2)}) collective-permute-start(f32[5,64,256]{2,1,0:T(8,128)} %pad_maximum_fusion.4), channel_id=1, source_target_pairs={{64,0},{128,64},{65,1},{129,65},{66,2},{130,66},{67,3},{131,67},{6... | collective-permute-start | bytes 983048 | tf_op jit(solution)/shard_map/ppermute | solution.py:43
  17.7 3.4 %copy-start.4 = (f32[32,64,2]{2,1,0:T(8,128)S(1)}, f32[32,64,2]{2,1,0:T(8,128)}, u32[]{:S(2)}) copy-start(f32[32,64,2]{2,1,0:T(8,128)} %get-tuple-element.21) | copy-start | bytes 49156
  17.7 7.1 %copy-start.3 = (f32[32,64,2]{2,1,0:T(8,128)S(1)}, f32[32,64,2]{2,1,0:T(8,128)}, u32[]{:S(2)}) copy-start(f32[32,64,2]{2,1,0:T(8,128)} %get-tuple-element.22) | copy-start | bytes 49156
  21.1 4.4 %copy-start.9 = (s32[8]{0:T(128)S(1)}, s32[8]{0:T(128)}, u32[]{:S(2)}) copy-start(s32[8]{0:T(128)} %param.11) | copy-start | bytes 100
  21.1 4.6 %copy-start.8 = (s32[4,2]{0,1:T(2,128)S(1)}, s32[4,2]{0,1:T(2,128)}, u32[]{:S(2)}) copy-start(s32[4,2]{0,1:T(2,128)} %param.12) | copy-start | bytes 100
  22.1 5.6 %copy-start.5 = (f32[32,2,256]{2,1,0:T(2,128)S(1)}, f32[32,2,256]{2,1,0:T(2,128)}, u32[]{:S(2)}) copy-start(f32[32,2,256]{2,1,0:T(2,128)} %get-tuple-element.24) | copy-start | bytes 196612
  24.8 16.4 %copy-start.6 = (f32[3,32,64,1]{2,1,0,3:T(8,128)S(1)}, f32[3,32,64,1]{2,1,0,3:T(8,128)}, u32[]{:S(2)}) copy-start(f32[3,32,64,1]{2,1,0,3:T(8,128)} %copy.277) | copy-start | bytes 73732
  24.8 17.9 %copy-start.7 = (f32[32,64,2]{1,2,0:T(2,128)S(1)}, f32[32,64,2]{1,2,0:T(2,128)}, u32[]{:S(2)}) copy-start(f32[32,64,2]{1,2,0:T(2,128)} %copy.273) | copy-start | bytes 49156
  27.9 13.3 %collective-permute-start.2 = (f32[36,5,256]{2,0,1:T(8,128)S(1)}, f32[36,5,256]{2,0,1:T(8,128)S(1)}, u32[]{:S(2)}, u32[]{:S(2)}) collective-permute-start(f32[36,5,256]{2,0,1:T(8,128)S(1)} %pad_maximum_fusion.6), channel_id=1, source_target_pairs={{4,0},{8,4},{12,8},{16,12},{20,16},{24,20},{28,24},{32,28},{36,32}... | collective-permute-start | bytes 552968 | tf_op jit(solution)/shard_map/ppermute | solution.py:61
  31.3 10.2 %collective-permute-start.3 = (f32[36,5,256]{2,0,1:T(8,128)S(1)}, f32[36,5,256]{2,0,1:T(8,128)S(1)}, u32[]{:S(2)}, u32[]{:S(2)}) collective-permute-start(f32[36,5,256]{2,0,1:T(8,128)S(1)} %pad_maximum_fusion.7), channel_id=1, source_target_pairs={{0,4},{4,8},{8,12},{12,16},{16,20},{20,24},{24,28},{28,32},{32,36}... | collective-permute-start | bytes 552968 | tf_op jit(solution)/shard_map/ppermute | solution.py:60
  43.0 9.6 %collective-permute-start.4 = (f32[36,68,5]{1,0,2:T(8,128)S(1)}, f32[36,68,5]{1,0,2:T(8,128)S(1)}, u32[]{:S(2)}, u32[]{:S(2)}) collective-permute-start(f32[36,68,5]{1,0,2:T(8,128)S(1)} %pad_maximum_fusion.12), channel_id=1, source_target_pairs={{1,0},{2,1},{3,2},{5,4},{6,5},{7,6},{9,8},{10,9},{11,10},{13,12},{... | collective-permute-start | bytes 146888 | tf_op jit(solution)/shard_map/ppermute | solution.py:82
  45.5 10.0 %collective-permute-start.5 = (f32[36,68,5]{1,0,2:T(8,128)S(1)}, f32[36,68,5]{1,0,2:T(8,128)S(1)}, u32[]{:S(2)}, u32[]{:S(2)}) collective-permute-start(f32[36,68,5]{1,0,2:T(8,128)S(1)} %pad_maximum_fusion.13), channel_id=1, source_target_pairs={{0,1},{1,2},{2,3},{4,5},{5,6},{6,7},{8,9},{9,10},{10,11},{12,13},{... | collective-permute-start | bytes 146888 | tf_op jit(solution)/shard_map/ppermute | solution.py:81
  100.5 1.6 %collective-permute-start.6 = (f32[8,32,128]{2,1,0:T(8,128)}, f32[8,32,128]{2,1,0:T(8,128)S(1)}, u32[]{:S(2)}, u32[]{:S(2)}) collective-permute-start(f32[8,32,128]{2,1,0:T(8,128)} %get-tuple-element.6), channel_id=1, source_target_pairs={{0,64},{64,0},{128,192},{192,128},{1,65},{65,1},{129,193},{193,129... | collective-permute-start | bytes 393224 | tf_op jit(solution)/shard_map/ppermute | solution.py:291
  103.0 6.6 %collective-permute-start.7 = (f32[8,32,128]{2,1,0:T(8,128)S(1)}, f32[8,32,128]{2,1,0:T(8,128)S(1)}, u32[]{:S(2)}, u32[]{:S(2)}) collective-permute-start(f32[8,32,128]{2,1,0:T(8,128)S(1)} %add.263), channel_id=1, source_target_pairs={{0,128},{128,0},{64,192},{192,64},{1,129},{129,1},{65,193},{193,65... | collective-permute-start | bytes 393224 | tf_op jit(solution)/shard_map/ppermute | solution.py:293
  109.6 40.5 %copy-start.2 = (f32[8,32,128]{2,1,0:T(8,128)}, f32[8,32,128]{2,1,0:T(8,128)S(1)}, u32[]{:S(2)}) copy-start(f32[8,32,128]{2,1,0:T(8,128)S(1)} %add.264) | copy-start | bytes 393220
  109.9 16.6 %collective-permute-start.10 = (f32[16,3,3]{2,1,0:T(4,128)S(1)}, f32[16,3,3]{2,1,0:T(4,128)S(1)}, u32[]{:S(2)}, u32[]{:S(2)}) collective-permute-start(f32[16,3,3]{2,1,0:T(4,128)S(1)} %get-tuple-element.45), channel_id=1, source_target_pairs={{1,4},{2,5},{3,6},{5,8},{6,9},{7,10},{9,12},{10,13},{11,14},{13,16... | collective-permute-start | bytes 1736 | tf_op jit(solution)/shard_map/ppermute | solution.py:281
  111.2 24.4 %collective-permute-start.13 = (f32[16,3,3]{2,1,0:T(4,128)S(1)}, f32[16,3,3]{2,1,0:T(4,128)S(1)}, u32[]{:S(2)}, u32[]{:S(2)}) collective-permute-start(f32[16,3,3]{2,1,0:T(4,128)S(1)} %get-tuple-element.44), channel_id=1, source_target_pairs={{4,1},{5,2},{6,3},{8,5},{9,6},{10,7},{12,9},{13,10},{14,11},{16,13... | collective-permute-start | bytes 1736 | tf_op jit(solution)/shard_map/ppermute | solution.py:282
  118.1 19.4 %collective-permute-start.15 = (f32[16,3,3]{2,1,0:T(4,128)S(1)}, f32[16,3,3]{2,1,0:T(4,128)S(1)}, u32[]{:S(2)}, u32[]{:S(2)}) collective-permute-start(f32[16,3,3]{2,1,0:T(4,128)S(1)} %get-tuple-element.46), channel_id=1, source_target_pairs={{5,0},{6,1},{7,2},{9,4},{10,5},{11,6},{13,8},{14,9},{15,10},{17,12... | collective-permute-start | bytes 1736 | tf_op jit(solution)/shard_map/ppermute | solution.py:283
  119.5 26.0 %collective-permute-start.11 = (f32[16,32,3]{2,1,0:T(8,128)S(1)}, f32[16,32,3]{2,1,0:T(8,128)S(1)}, u32[]{:S(2)}, u32[]{:S(2)}) collective-permute-start(f32[16,32,3]{2,1,0:T(8,128)S(1)} %get-tuple-element.49), channel_id=1, source_target_pairs={{0,1},{1,2},{2,3},{4,5},{5,6},{6,7},{8,9},{9,10},{10,11},{12,13},{... | collective-permute-start | bytes 18440 | tf_op jit(solution)/shard_map/ppermute | solution.py:278
  125.2 20.3 %collective-permute-start.12 = (f32[16,32,3]{2,1,0:T(8,128)S(1)}, f32[16,32,3]{2,1,0:T(8,128)S(1)}, u32[]{:S(2)}, u32[]{:S(2)}) collective-permute-start(f32[16,32,3]{2,1,0:T(8,128)S(1)} %get-tuple-element.50), channel_id=1, source_target_pairs={{1,0},{2,1},{3,2},{5,4},{6,5},{7,6},{9,8},{10,9},{11,10},{13,12},{... | collective-permute-start | bytes 18440 | tf_op jit(solution)/shard_map/ppermute | solution.py:279
  126.5 18.9 %collective-permute-start.8 = (f32[16,3,3]{2,1,0:T(4,128)S(1)}, f32[16,3,3]{2,1,0:T(4,128)S(1)}, u32[]{:S(2)}, u32[]{:S(2)}) collective-permute-start(f32[16,3,3]{2,1,0:T(4,128)S(1)} %get-tuple-element.43), channel_id=1, source_target_pairs={{0,5},{1,6},{2,7},{4,9},{5,10},{6,11},{8,13},{9,14},{10,15},{12,17... | collective-permute-start | bytes 1736 | tf_op jit(solution)/shard_map/ppermute | solution.py:280
  135.6 9.8 %collective-permute-start.14 = (f32[16,3,128]{2,1,0:T(4,128)S(1)}, f32[16,3,128]{2,1,0:T(4,128)S(1)}, u32[]{:S(2)}, u32[]{:S(2)}) collective-permute-start(f32[16,3,128]{2,1,0:T(4,128)S(1)} %get-tuple-element.48), channel_id=1, source_target_pairs={{4,0},{8,4},{12,8},{16,12},{20,16},{24,20},{28,24},{32,28},{36,32}... | collective-permute-start | bytes 73736 | tf_op jit(solution)/shard_map/ppermute | solution.py:277
  137.6 9.1 %collective-permute-start.9 = (f32[16,3,128]{2,1,0:T(4,128)S(1)}, f32[16,3,128]{2,1,0:T(4,128)S(1)}, u32[]{:S(2)}, u32[]{:S(2)}) collective-permute-start(f32[16,3,128]{2,1,0:T(4,128)S(1)} %get-tuple-element.47), channel_id=1, source_target_pairs={{0,4},{4,8},{8,12},{12,16},{16,20},{20,24},{24,28},{28,32},{32,36}... | collective-permute-start | bytes 73736 | tf_op jit(solution)/shard_map/ppermute | solution.py:276

commit v4 on v3

--- a/solution.py
+++ b/solution.py
@@ -332,7 +332,7 @@
     potential = lax.dynamic_slice_in_dim(init_potential, group_index, 1, 0)
     poles = lax.dynamic_slice_in_dim(electrodes, group_index, 1, 0)
 
-    both = plane_halo(jnp.concatenate([conductivity, potential[0]], axis=0), depth)
+    both = with_halo(jnp.concatenate([conductivity, potential[0]], axis=0), (("gx", 1), ("gy", 2)), depth)
     cond_wide = jnp.pad(both[:resist_layers], ((1, 1), (0, 0), (0, 0)))
     potential = both[None, resist_layers:]
     wide_x = coarse_x + 2 * depth

time: 154 us -> 143 us (0.929); the launches traced: 151 us -> 143 us
  starting transfers between devices: 58.7 us -> 36.8 us
  waiting for transfers between devices: 5.37 us -> 19.3 us
    ppermute x8 -> x4, starting transfers between devices: 35.1 us -> 13.2 us  [the longest x2 9.99 us: with_halo(): before = lax.ppermute(last, axis, up)]
    ppermute x8 -> x4, waiting for transfers between devices: 1.23 us -> 15.2 us  [the longest x2 11.6 us: with_halo(): after = lax.ppermute(initial, axis, down)]
  transfers between devices with their start and end apart: 16 -> 12, of which waited for: 3 -> 5; matrix products, arithmetic and copies ran while one was open for 19% -> 20% of each run, Pallas kernels for 0% -> 0%
where the time goes in v4:
time: 143 us
  starting transfers between devices  36.8 us (26%)
  Pallas kernels  32.5 us (23%)
  local copies, waits for them, and re-layouts  32.4 us (23%)
  other arithmetic  20.6 us (14%)
  waiting for transfers between devices  19.3 us (13%)
    pallas_call x1, Pallas kernels, transport_call(): pl.pallas_call(functools.partial(transport_kernel, grid), out_shape=(jax....  32.5 us
    ppermute x2, waiting for transfers between devices, with_halo(): after = lax.ppermute(initial, axis, down)  11.6 us
    ppermute x2, starting transfers between devices, with_halo(): before = lax.ppermute(last, axis, up)  9.99 us
    ppermute x1, starting transfers between devices, transport_halo(): bx = lax.ppermute(send_up, 'gx', up)  6.14 us
    convert_element_type x2, local copies, waits for them, and re-layouts, xz_u(): u[..., lane].astype(f32)  6.09 us
    ppermute x1, starting transfers between devices, transport_halo(): lax.ppermute(jnp.concatenate([xz_c(slice(ny - 2, ny)), xz_u(ny - 1)], 2),...  4.73 us
    ppermute x1, starting transfers between devices, transport_halo(): lax.ppermute(jnp.concatenate([c[:2], u[:, 0].astype(f32)], 0), 'grp', down)  4.27 us
    concatenate x1, other arithmetic, transport_halo(): jnp.concatenate([yu_hi, jnp.zeros((3, nz + 2, nx + 4, 126), f32), yu_lo], 3)  4.25 us
  transfers between devices with their start and end apart: 12, of which 5 were waited for; matrix products, arithmetic and copies ran while one was open for 20% of the time, Pallas kernels for 0%

profile of v4, /device:TPU:102, one launch (start us, length us, event | category | flops | bytes accessed | tf_op | source)
XLA Modules:
  0.0 142.9 jit_solution(4606604057615975836)
XLA Ops:
  0.7 3.8 %copy.301 = bf16[3,1,32,64,256]{4,2,3,0,1:T(8,128)(2,1)S(1)} copy(bf16[3,1,32,64,256]{4,3,2,1,0:T(8,128)(2,1)} %v_ref.1) | data formatting | bytes 6291456 | tf_op args[1]
  5.6 1.3 collective-permute-start
  7.7 4.3 %collective-permute-start.1 = (f32[5,64,256]{2,1,0:T(8,128)}, f32[5,64,256]{2,1,0:T(8,128)S(1)}, u32[]{:S(2)}, u32[]{:S(2)}) collective-permute-start(f32[5,64,256]{2,1,0:T(8,128)} %pad_maximum_fusion.6), channel_id=1, source_target_pairs={{64,0},{128,64},{65,1},{129,65},{66,2},{130,66},{67,3},{131,67},{6... | collective-permute-start | bytes 983048 | tf_op jit(solution)/shard_map/ppermute | solution.py:43
  12.0 3.4 %slice_convert_fusion.1 = (f32[3,32,64,1]{3,1,2,0:T(8,128)}, f32[3,32,64,1]{3,1,2,0:T(8,128)}) fusion(bf16[3,32,64,256]{3,1,2,0:T(8,128)(2,1)S(1)} %bitcast.164), kind=kLoop, calls=%fused_computation.3 | loop fusion | flops 12288 | bytes 73728 | tf_op jit(solution)/shard_map/convert_element_type | solution.py:70
  16.0 1.7 %fusion.72 = (f32[32,64,2]{2,1,0:T(8,128)}, f32[32,64,2]{2,1,0:T(8,128)}) fusion(f32[32,64,256]{2,1,0:T(8,128)S(1)} %bitcast.167), kind=kLoop, calls=%fused_computation.186 | loop fusion | bytes 65536 | tf_op jit(solution)/shard_map/slice | solution.py:64
  17.7 3.4 %copy.277 = f32[3,32,64,1]{2,1,0,3:T(8,128)} copy(f32[3,32,64,1]{3,1,2,0:T(8,128)} %get-tuple-element.15) | data formatting | bytes 49152 | tf_op jit(solution)/shard_map/convert_element_type | solution.py:70
  21.1 1.0 copy.273
  22.1 2.7 %copy.286 = f32[3,32,64,1]{2,1,0,3:T(8,128)S(1)} copy(f32[3,32,64,1]{3,1,2,0:T(8,128)} %get-tuple-element.16) | data formatting | bytes 49152 | tf_op jit(solution)/shard_map/convert_element_type | solution.py:70
  28.0 3.3 %collective-permute-start.2 = (f32[36,5,256]{2,0,1:T(8,128)S(1)}, f32[36,5,256]{2,0,1:T(8,128)S(1)}, u32[]{:S(2)}, u32[]{:S(2)}) collective-permute-start(f32[36,5,256]{2,0,1:T(8,128)S(1)} %pad_maximum_fusion.9), channel_id=1, source_target_pairs={{4,0},{8,4},{12,8},{16,12},{20,16},{24,20},{28,24},{32,28},{36,32}... | collective-permute-start | bytes 552968 | tf_op jit(solution)/shard_map/ppermute | solution.py:61
  31.4 6.1 %collective-permute-start.3 = (f32[36,5,256]{2,0,1:T(8,128)S(1)}, f32[36,5,256]{2,0,1:T(8,128)S(1)}, u32[]{:S(2)}, u32[]{:S(2)}) collective-permute-start(f32[36,5,256]{2,0,1:T(8,128)S(1)} %pad_maximum_fusion.10), channel_id=1, source_target_pairs={{0,4},{4,8},{8,12},{12,16},{16,20},{20,24},{24,28},{28,32},{32,36}... | collective-permute-start | bytes 552968 | tf_op jit(solution)/shard_map/ppermute | solution.py:60
  43.0 1.3 collective-permute-start.4
  45.6 4.7 %collective-permute-start.5 = (f32[36,68,5]{1,0,2:T(8,128)S(1)}, f32[36,68,5]{1,0,2:T(8,128)S(1)}, u32[]{:S(2)}, u32[]{:S(2)}) collective-permute-start(f32[36,68,5]{1,0,2:T(8,128)S(1)} %pad_maximum_fusion.16), channel_id=1, source_target_pairs={{0,1},{1,2},{2,3},{4,5},{5,6},{6,7},{8,9},{9,10},{10,11},{12,13},{... | collective-permute-start | bytes 146888 | tf_op jit(solution)/shard_map/ppermute | solution.py:81
  50.7 1.2 pad_maximum_fusion.2.xu
  52.7 2.9 %copy.292 = f32[3,34,68,1]{3,2,1,0:T(8,128)} copy(f32[3,34,68,1]{2,1,0,3:T(8,128)S(1)} %slice_bitcast_fusion.6) | data formatting | bytes 55488 | tf_op jit(solution)/shard_map/broadcast_in_dim | solution.py:90
  55.6 2.9 %copy.293 = f32[3,34,68,1]{3,2,1,0:T(8,128)} copy(f32[3,34,68,1]{2,1,0,3:T(8,128)S(1)} %slice_bitcast_fusion.5) | data formatting | bytes 55488 | tf_op jit(solution)/shard_map/broadcast_in_dim | solution.py:91
  58.5 4.2 %pad_maximum_fusion = f32[3,34,68,128]{3,2,1,0:T(8,128)S(1)} fusion(f32[3,34,68,1]{3,2,1,0:T(8,128)} %copy.293, f32[3,34,68,1]{3,2,1,0:T(8,128)} %copy.292, f32[128]{0:T(128)S(1)} %pad.77.clone), kind=kLoop, calls=%fused_computation | loop fusion | flops 1775616 | bytes 3607232 | tf_op jit(solution)/shard_map/concatenate | solution.py:92
  62.7 2.5 %pad.43.yu = f32[3,34,80,128]{3,2,1,0:T(8,128)} pad(f32[3,34,68,128]{3,2,1,0:T(8,128)S(1)} %pad_maximum_fusion, f32[]{:T(128)} %constant.25.clone.1), padding=0_0x0_0x6_6x0_0 | pad | bytes 7729156 | tf_op jit(solution)/shard_map/jit(_pad)/pad | solution.py:93
  66.8 1.3 pad.42.yc
  68.0 32.5 %shard_map.94 = (f32[1,32,64,256]{3,2,1,0:T(8,128)}, f32[8,32,128]{2,1,0:T(8,128)}) custom-call(s32[4]{0:T(128)} %pad_add_fusion.place, f32[8,32]{1,0:T(8,128)} %convert_divide_fusion.weights, f32[32,64,256]{2,1,0:T(8,128)} %bitcast.165, bf16[3,1,32,64,256]{4,3,2,1,0:T(8,128)(2,1)} %v_ref.1, bf16[1,32,64,256]{3,2,1,0:T(8,128)(2,1)} %poro_ref.1, ...), custom_call_target="tpu_custom_call" | custom-call | flops 104857600 | bytes 20971520 | tf_op jit(solution)/shard_map/pallas_call | solution.py:205
  100.6 1.4 subtract_multiply_fusion
  103.1 2.6 %collective-permute-start.7 = (f32[8,32,128]{2,1,0:T(8,128)S(1)}, f32[8,32,128]{2,1,0:T(8,128)S(1)}, u32[]{:S(2)}, u32[]{:S(2)}) collective-permute-start(f32[8,32,128]{2,1,0:T(8,128)S(1)} %add.263), channel_id=1, source_target_pairs={{0,128},{128,0},{64,192},{192,64},{1,129},{129,1},{65,193},{193,65... | collective-permute-start | bytes 393224 | tf_op jit(solution)/shard_map/ppermute | solution.py:293
  105.7 4.0 %collective-permute-done.7 = f32[8,32,128]{2,1,0:T(8,128)S(1)} collective-permute-done((f32[8,32,128]{2,1,0:T(8,128)S(1)}, f32[8,32,128]{2,1,0:T(8,128)S(1)}, u32[]{:S(2)}, u32[]{:S(2)}) %collective-permute-start.7) | collective-permute-done | bytes 131104 | tf_op jit(solution)/shard_map/ppermute | solution.py:293
  109.7 6.5 %collective-permute-start.8 = (f32[16,3,128]{2,1,0:T(4,128)S(1)}, f32[16,3,128]{2,1,0:T(4,128)S(1)}, u32[]{:S(2)}, u32[]{:S(2)}) collective-permute-start(f32[16,3,128]{2,1,0:T(4,128)S(1)} %get-tuple-element.45), channel_id=1, source_target_pairs={{0,4},{4,8},{8,12},{12,16},{16,20},{20,24},{24,28},{28,32},{32,36}... | collective-permute-start | bytes 73736 | tf_op jit(solution)/shard_map/ppermute | solution.py:27
  116.2 1.9 %collective-permute-start.9 = (f32[16,3,128]{2,1,0:T(4,128)S(1)}, f32[16,3,128]{2,1,0:T(4,128)S(1)}, u32[]{:S(2)}, u32[]{:S(2)}) collective-permute-start(f32[16,3,128]{2,1,0:T(4,128)S(1)} %get-tuple-element.46), channel_id=1, source_target_pairs={{4,0},{8,4},{12,8},{16,12},{20,16},{24,20},{28,24},{32,28},{36,32}... | collective-permute-start | bytes 73736 | tf_op jit(solution)/shard_map/ppermute | solution.py:28
  118.2 7.5 %collective-permute-done.9 = f32[16,3,128]{2,1,0:T(4,128)S(1)} collective-permute-done((f32[16,3,128]{2,1,0:T(4,128)S(1)}, f32[16,3,128]{2,1,0:T(4,128)S(1)}, u32[]{:S(2)}, u32[]{:S(2)}) %collective-permute-start.9) | collective-permute-done | bytes 24608 | tf_op jit(solution)/shard_map/ppermute | solution.py:28
  125.8 3.5 %collective-permute-start.10 = (f32[16,38,3]{2,1,0:T(8,128)S(1)}, f32[16,38,3]{2,1,0:T(8,128)S(1)}, u32[]{:S(2)}, u32[]{:S(2)}) collective-permute-start(f32[16,38,3]{2,1,0:T(8,128)S(1)} %get-tuple-element.31), channel_id=1, source_target_pairs={{0,1},{1,2},{2,3},{4,5},{5,6},{6,7},{8,9},{9,10},{10,11},{12,13},{... | collective-permute-start | bytes 21896 | tf_op jit(solution)/shard_map/ppermute | solution.py:27
  129.3 1.3 collective-permute-start.11
  131.0 3.6 %collective-permute-done.10 = f32[16,38,3]{2,1,0:T(8,128)S(1)} collective-permute-done((f32[16,38,3]{2,1,0:T(8,128)S(1)}, f32[16,38,3]{2,1,0:T(8,128)S(1)}, u32[]{:S(2)}, u32[]{:S(2)}) %collective-permute-start.10) | collective-permute-done | bytes 7328 | tf_op jit(solution)/shard_map/ppermute | solution.py:27
  134.6 4.1 %collective-permute-done.11 = f32[16,38,3]{2,1,0:T(8,128)S(1)} collective-permute-done((f32[16,38,3]{2,1,0:T(8,128)S(1)}, f32[16,38,3]{2,1,0:T(8,128)S(1)}, u32[]{:S(2)}, u32[]{:S(2)}) %collective-permute-start.11) | collective-permute-done | bytes 7328 | tf_op jit(solution)/shard_map/ppermute | solution.py:28
  139.1 1.1 fusion.41
  140.6 1.1 fusion.40
  141.8 1.2 fusion.64
  (139 shorter events, 17.5 us)
Async XLA Ops:
  0.6 105.0 %copy-start = (f32[4,8,32,128]{3,2,1,0:T(8,128)S(1)}, f32[4,8,32,128]{3,2,1,0:T(8,128)}, u32[]{:S(2)}) copy-start(f32[4,8,32,128]{3,2,1,0:T(8,128)} %param.13) | copy-start | bytes 1572868
  0.6 4.1 %copy-start.1 = (f32[1,32,64,256]{3,2,1,0:T(8,128)S(1)}, f32[1,32,64,256]{3,2,1,0:T(8,128)}, u32[]{:S(2)}) copy-start(f32[1,32,64,256]{3,2,1,0:T(8,128)} %param.7) | copy-start | bytes 6291460
  5.6 22.2 %collective-permute-start = (f32[5,64,256]{2,1,0:T(8,128)}, f32[5,64,256]{2,1,0:T(8,128)S(1)}, u32[]{:S(2)}, u32[]{:S(2)}) collective-permute-start(f32[5,64,256]{2,1,0:T(8,128)} %pad_maximum_fusion.5), channel_id=1, source_target_pairs={{0,64},{64,128},{1,65},{65,129},{2,66},{66,130},{3,67},{67,131},{4... | collective-permute-start | bytes 983048 | tf_op jit(solution)/shard_map/ppermute | solution.py:42
  7.7 20.1 %collective-permute-start.1 = (f32[5,64,256]{2,1,0:T(8,128)}, f32[5,64,256]{2,1,0:T(8,128)S(1)}, u32[]{:S(2)}, u32[]{:S(2)}) collective-permute-start(f32[5,64,256]{2,1,0:T(8,128)} %pad_maximum_fusion.6), channel_id=1, source_target_pairs={{64,0},{128,64},{65,1},{129,65},{66,2},{130,66},{67,3},{131,67},{6... | collective-permute-start | bytes 983048 | tf_op jit(solution)/shard_map/ppermute | solution.py:43
  17.7 3.4 %copy-start.4 = (f32[32,64,2]{2,1,0:T(8,128)S(1)}, f32[32,64,2]{2,1,0:T(8,128)}, u32[]{:S(2)}) copy-start(f32[32,64,2]{2,1,0:T(8,128)} %get-tuple-element.21) | copy-start | bytes 49156
  17.7 7.1 %copy-start.3 = (f32[32,64,2]{2,1,0:T(8,128)S(1)}, f32[32,64,2]{2,1,0:T(8,128)}, u32[]{:S(2)}) copy-start(f32[32,64,2]{2,1,0:T(8,128)} %get-tuple-element.22) | copy-start | bytes 49156
  21.1 4.4 %copy-start.9 = (s32[8]{0:T(128)S(1)}, s32[8]{0:T(128)}, u32[]{:S(2)}) copy-start(s32[8]{0:T(128)} %param.11) | copy-start | bytes 100
  21.1 4.6 %copy-start.8 = (s32[4,2]{0,1:T(2,128)S(1)}, s32[4,2]{0,1:T(2,128)}, u32[]{:S(2)}) copy-start(s32[4,2]{0,1:T(2,128)} %param.12) | copy-start | bytes 100
  22.1 5.7 %copy-start.5 = (f32[32,2,256]{2,1,0:T(2,128)S(1)}, f32[32,2,256]{2,1,0:T(2,128)}, u32[]{:S(2)}) copy-start(f32[32,2,256]{2,1,0:T(2,128)} %get-tuple-element.24) | copy-start | bytes 196612
  24.8 16.4 %copy-start.6 = (f32[3,32,64,1]{2,1,0,3:T(8,128)S(1)}, f32[3,32,64,1]{2,1,0,3:T(8,128)}, u32[]{:S(2)}) copy-start(f32[3,32,64,1]{2,1,0,3:T(8,128)} %copy.277) | copy-start | bytes 73732
  24.8 17.9 %copy-start.7 = (f32[32,64,2]{1,2,0:T(2,128)S(1)}, f32[32,64,2]{1,2,0:T(2,128)}, u32[]{:S(2)}) copy-start(f32[32,64,2]{1,2,0:T(2,128)} %copy.273) | copy-start | bytes 49156
  28.0 13.3 %collective-permute-start.2 = (f32[36,5,256]{2,0,1:T(8,128)S(1)}, f32[36,5,256]{2,0,1:T(8,128)S(1)}, u32[]{:S(2)}, u32[]{:S(2)}) collective-permute-start(f32[36,5,256]{2,0,1:T(8,128)S(1)} %pad_maximum_fusion.9), channel_id=1, source_target_pairs={{4,0},{8,4},{12,8},{16,12},{20,16},{24,20},{28,24},{32,28},{36,32}... | collective-permute-start | bytes 552968 | tf_op jit(solution)/shard_map/ppermute | solution.py:61
  31.4 10.2 %collective-permute-start.3 = (f32[36,5,256]{2,0,1:T(8,128)S(1)}, f32[36,5,256]{2,0,1:T(8,128)S(1)}, u32[]{:S(2)}, u32[]{:S(2)}) collective-permute-start(f32[36,5,256]{2,0,1:T(8,128)S(1)} %pad_maximum_fusion.10), channel_id=1, source_target_pairs={{0,4},{4,8},{8,12},{12,16},{16,20},{20,24},{24,28},{28,32},{32,36}... | collective-permute-start | bytes 552968 | tf_op jit(solution)/shard_map/ppermute | solution.py:60
  43.0 9.6 %collective-permute-start.4 = (f32[36,68,5]{1,0,2:T(8,128)S(1)}, f32[36,68,5]{1,0,2:T(8,128)S(1)}, u32[]{:S(2)}, u32[]{:S(2)}) collective-permute-start(f32[36,68,5]{1,0,2:T(8,128)S(1)} %pad_maximum_fusion.15), channel_id=1, source_target_pairs={{1,0},{2,1},{3,2},{5,4},{6,5},{7,6},{9,8},{10,9},{11,10},{13,12},{... | collective-permute-start | bytes 146888 | tf_op jit(solution)/shard_map/ppermute | solution.py:82
  45.6 10.0 %collective-permute-start.5 = (f32[36,68,5]{1,0,2:T(8,128)S(1)}, f32[36,68,5]{1,0,2:T(8,128)S(1)}, u32[]{:S(2)}, u32[]{:S(2)}) collective-permute-start(f32[36,68,5]{1,0,2:T(8,128)S(1)} %pad_maximum_fusion.16), channel_id=1, source_target_pairs={{0,1},{1,2},{2,3},{4,5},{5,6},{6,7},{8,9},{9,10},{10,11},{12,13},{... | collective-permute-start | bytes 146888 | tf_op jit(solution)/shard_map/ppermute | solution.py:81
  100.6 1.6 %collective-permute-start.6 = (f32[8,32,128]{2,1,0:T(8,128)}, f32[8,32,128]{2,1,0:T(8,128)S(1)}, u32[]{:S(2)}, u32[]{:S(2)}) collective-permute-start(f32[8,32,128]{2,1,0:T(8,128)} %get-tuple-element.6), channel_id=1, source_target_pairs={{0,64},{64,0},{128,192},{192,128},{1,65},{65,1},{129,193},{193,129... | collective-permute-start | bytes 393224 | tf_op jit(solution)/shard_map/ppermute | solution.py:291
  103.1 6.6 %collective-permute-start.7 = (f32[8,32,128]{2,1,0:T(8,128)S(1)}, f32[8,32,128]{2,1,0:T(8,128)S(1)}, u32[]{:S(2)}, u32[]{:S(2)}) collective-permute-start(f32[8,32,128]{2,1,0:T(8,128)S(1)} %add.263), channel_id=1, source_target_pairs={{0,128},{128,0},{64,192},{192,64},{1,129},{129,1},{65,193},{193,65... | collective-permute-start | bytes 393224 | tf_op jit(solution)/shard_map/ppermute | solution.py:293
  109.7 32.1 %copy-start.2 = (f32[8,32,128]{2,1,0:T(8,128)}, f32[8,32,128]{2,1,0:T(8,128)S(1)}, u32[]{:S(2)}) copy-start(f32[8,32,128]{2,1,0:T(8,128)S(1)} %add.264) | copy-start | bytes 393220
  109.7 8.5 %collective-permute-start.8 = (f32[16,3,128]{2,1,0:T(4,128)S(1)}, f32[16,3,128]{2,1,0:T(4,128)S(1)}, u32[]{:S(2)}, u32[]{:S(2)}) collective-permute-start(f32[16,3,128]{2,1,0:T(4,128)S(1)} %get-tuple-element.45), channel_id=1, source_target_pairs={{0,4},{4,8},{8,12},{12,16},{16,20},{20,24},{24,28},{28,32},{32,36}... | collective-permute-start | bytes 73736 | tf_op jit(solution)/shard_map/ppermute | solution.py:27
  116.2 9.4 %collective-permute-start.9 = (f32[16,3,128]{2,1,0:T(4,128)S(1)}, f32[16,3,128]{2,1,0:T(4,128)S(1)}, u32[]{:S(2)}, u32[]{:S(2)}) collective-permute-start(f32[16,3,128]{2,1,0:T(4,128)S(1)} %get-tuple-element.46), channel_id=1, source_target_pairs={{4,0},{8,4},{12,8},{16,12},{20,16},{24,20},{28,24},{32,28},{36,32}... | collective-permute-start | bytes 73736 | tf_op jit(solution)/shard_map/ppermute | solution.py:28
  125.8 8.7 %collective-permute-start.10 = (f32[16,38,3]{2,1,0:T(8,128)S(1)}, f32[16,38,3]{2,1,0:T(8,128)S(1)}, u32[]{:S(2)}, u32[]{:S(2)}) collective-permute-start(f32[16,38,3]{2,1,0:T(8,128)S(1)} %get-tuple-element.31), channel_id=1, source_target_pairs={{0,1},{1,2},{2,3},{4,5},{5,6},{6,7},{8,9},{9,10},{10,11},{12,13},{... | collective-permute-start | bytes 21896 | tf_op jit(solution)/shard_map/ppermute | solution.py:27
  129.3 9.3 %collective-permute-start.11 = (f32[16,38,3]{2,1,0:T(8,128)S(1)}, f32[16,38,3]{2,1,0:T(8,128)S(1)}, u32[]{:S(2)}, u32[]{:S(2)}) collective-permute-start(f32[16,38,3]{2,1,0:T(8,128)S(1)} %get-tuple-element.32), channel_id=1, source_target_pairs={{1,0},{2,1},{3,2},{5,4},{6,5},{7,6},{9,8},{10,9},{11,10},{13,12},{... | collective-permute-start | bytes 21896 | tf_op jit(solution)/shard_map/ppermute | solution.py:28

commit v5 on v4

--- a/solution.py
+++ b/solution.py
@@ -110,7 +110,7 @@
 
 def transport_kernel(
     grid, place, weights, c_ref, v_ref, poro_ref, sat_ref, zlo_c, zhi_c, zlo_u, zhi_u,
-    xc, xu, yc, yu, adv_ref, part_ref, F, U, S,
+    xc, xu, yc, yu, adv_ref, part_ref, F, U, S, SG, H,
 ):
     nz, nx, ny = c_ref.shape
     wx, wy = F.shape[1], F.shape[2]
@@ -118,10 +118,6 @@
     pool_y = (
         lax.broadcasted_iota(jnp.int32, (ny, ny // 2), 0) // 2
         == lax.broadcasted_iota(jnp.int32, (ny, ny // 2), 1)
-    ).astype(f32)
-    pool_x = (
-        lax.broadcasted_iota(jnp.int32, (nx // 2, nx), 0)
-        == lax.broadcasted_iota(jnp.int32, (nx // 2, nx), 1) // 2
     ).astype(f32)
     F[0:2, 8 : 8 + nx, 0:ny] = zlo_c[...]
     F[nz + 2 : nz + 4, 8 : 8 + nx, 0:ny] = zhi_c[...]
@@ -167,7 +163,6 @@
 
     lax.fori_loop(0, nz + 2, first, 0)
 
-    part_ref[...] = jnp.zeros(part_ref.shape, f32)
     live = place[3] > 0
 
     def core(values):
@@ -185,14 +180,20 @@
         adv_ref[0, j] = adv
         p = poro_ref[0, j].astype(f32)
         w = sat_ref[0, j].astype(f32)
-        sigma = ARCHIE * jnp.exp(adv) * p * p * w * w
-        half = jnp.dot(sigma, pool_y, precision=lax.Precision.HIGHEST, preferred_element_type=f32)
-        coarse = jnp.dot(pool_x, half, precision=lax.Precision.HIGHEST, preferred_element_type=f32)
-        for e in range(part_ref.shape[0]):
-            part_ref[e] = part_ref[e] + weights[e, j] * coarse
+        SG[pl.ds(pl.multiple_of(j * nx, nx), nx)] = ARCHIE * jnp.exp(adv) * p * p * w * w
         return carry
 
     lax.fori_loop(0, nz, second, 0)
+    H[...] = jnp.dot(SG[...], pool_y, precision=lax.Precision.HIGHEST, preferred_element_type=f32)
+    half_rows = nz * nx // 2
+    coarse = H[pl.ds(0, half_rows, stride=2)] + H[pl.ds(1, half_rows, stride=2)]
+    cx = nx // 2
+    resist_layers = part_ref.shape[0]
+    for e in range(resist_layers):
+        total = jnp.zeros((cx, ny // 2), f32)
+        for z in range(nz):
+            total = total + weights[e, z] * coarse[z * cx : (z + 1) * cx]
+        part_ref[e] = total
 
 
 def transport_call(place, weights, c, velocity, porosity, saturation, *pieces, grid):
@@ -214,6 +215,8 @@
             pltpu.VMEM((nz + 4, wx, wy), jnp.float32),
             pltpu.VMEM((3, nz + 2, wx, wy), jnp.float32),
             pltpu.VMEM((nz + 2, wx, wy), jnp.float32),
+            pltpu.VMEM((nz * nx, ny), jnp.float32),
+            pltpu.VMEM((nz * nx, ny // 2), jnp.float32),
         ],
         compiler_params=pltpu.CompilerParams(vmem_limit_bytes=60 * 1024 * 1024),
         cost_estimate=pl.CostEstimate(

time: 143 us -> 134 us (0.937)
  Pallas kernels: 32.5 us -> 23.6 us
    pallas_call x1, Pallas kernels: 32.5 us -> 23.6 us  [transport_call(): pl.pallas_call(functools.partial(transport_kernel, grid), out_shape=(jax....]
  transfers between devices with their start and end apart: 12 -> 12, of which waited for: 5 -> 5; matrix products, arithmetic and copies ran while one was open for 20% -> 21% of each run, Pallas kernels for 0% -> 0%
where the time goes in v5:
time: 134 us
  starting transfers between devices  37 us (28%)
  local copies, waits for them, and re-layouts  32.4 us (24%)
  Pallas kernels  23.6 us (18%)
  other arithmetic  20.6 us (15%)
  waiting for transfers between devices  19.1 us (14%)
    pallas_call x1, Pallas kernels, transport_call(): pl.pallas_call(functools.partial(transport_kernel, grid), out_shape=(jax....  23.6 us
    ppermute x2, waiting for transfers between devices, with_halo(): after = lax.ppermute(initial, axis, down)  11.6 us
    ppermute x2, starting transfers between devices, with_halo(): before = lax.ppermute(last, axis, up)  10 us
    ppermute x1, starting transfers between devices, transport_halo(): bx = lax.ppermute(send_up, 'gx', up)  6.14 us
    convert_element_type x2, local copies, waits for them, and re-layouts, xz_u(): u[..., lane].astype(f32)  6.09 us
    ppermute x1, starting transfers between devices, transport_halo(): lax.ppermute(jnp.concatenate([xz_c(slice(ny - 2, ny)), xz_u(ny - 1)], 2),...  4.73 us
    ppermute x1, starting transfers between devices, transport_halo(): lax.ppermute(jnp.concatenate([c[:2], u[:, 0].astype(f32)], 0), 'grp', down)  4.27 us
    concatenate x1, other arithmetic, transport_halo(): jnp.concatenate([yu_hi, jnp.zeros((3, nz + 2, nx + 4, 126), f32), yu_lo], 3)  4.25 us
  transfers between devices with their start and end apart: 12, of which 5 were waited for; matrix products, arithmetic and copies ran while one was open for 21% of the time, Pallas kernels for 0%

profile of v5, /device:TPU:102, one launch (start us, length us, event | category | flops | bytes accessed | tf_op | source)
XLA Modules:
  0.0 134.0 jit_solution(7807261333692607157)
XLA Ops:
  0.7 3.8 %copy.301 = bf16[3,1,32,64,256]{4,2,3,0,1:T(8,128)(2,1)S(1)} copy(bf16[3,1,32,64,256]{4,3,2,1,0:T(8,128)(2,1)} %v_ref.1) | data formatting | bytes 6291456 | tf_op args[1]
  5.6 1.3 collective-permute-start
  7.7 4.3 %collective-permute-start.1 = (f32[5,64,256]{2,1,0:T(8,128)}, f32[5,64,256]{2,1,0:T(8,128)S(1)}, u32[]{:S(2)}, u32[]{:S(2)}) collective-permute-start(f32[5,64,256]{2,1,0:T(8,128)} %pad_maximum_fusion.6), channel_id=1, source_target_pairs={{64,0},{128,64},{65,1},{129,65},{66,2},{130,66},{67,3},{131,67},{6... | collective-permute-start | bytes 983048 | tf_op jit(solution)/shard_map/ppermute | solution.py:43
  12.0 3.4 %slice_convert_fusion.1 = (f32[3,32,64,1]{3,1,2,0:T(8,128)}, f32[3,32,64,1]{3,1,2,0:T(8,128)}) fusion(bf16[3,32,64,256]{3,1,2,0:T(8,128)(2,1)S(1)} %bitcast.164), kind=kLoop, calls=%fused_computation.3 | loop fusion | flops 12288 | bytes 73728 | tf_op jit(solution)/shard_map/convert_element_type | solution.py:70
  16.0 1.7 %fusion.72 = (f32[32,64,2]{2,1,0:T(8,128)}, f32[32,64,2]{2,1,0:T(8,128)}) fusion(f32[32,64,256]{2,1,0:T(8,128)S(1)} %bitcast.167), kind=kLoop, calls=%fused_computation.186 | loop fusion | bytes 65536 | tf_op jit(solution)/shard_map/slice | solution.py:64
  17.7 3.4 %copy.277 = f32[3,32,64,1]{2,1,0,3:T(8,128)} copy(f32[3,32,64,1]{3,1,2,0:T(8,128)} %get-tuple-element.15) | data formatting | bytes 49152 | tf_op jit(solution)/shard_map/convert_element_type | solution.py:70
  21.1 1.0 copy.273
  22.1 2.7 %copy.286 = f32[3,32,64,1]{2,1,0,3:T(8,128)S(1)} copy(f32[3,32,64,1]{3,1,2,0:T(8,128)} %get-tuple-element.16) | data formatting | bytes 49152 | tf_op jit(solution)/shard_map/convert_element_type | solution.py:70
  28.0 3.3 %collective-permute-start.2 = (f32[36,5,256]{2,0,1:T(8,128)S(1)}, f32[36,5,256]{2,0,1:T(8,128)S(1)}, u32[]{:S(2)}, u32[]{:S(2)}) collective-permute-start(f32[36,5,256]{2,0,1:T(8,128)S(1)} %pad_maximum_fusion.9), channel_id=1, source_target_pairs={{4,0},{8,4},{12,8},{16,12},{20,16},{24,20},{28,24},{32,28},{36,32}... | collective-permute-start | bytes 552968 | tf_op jit(solution)/shard_map/ppermute | solution.py:61
  31.4 6.1 %collective-permute-start.3 = (f32[36,5,256]{2,0,1:T(8,128)S(1)}, f32[36,5,256]{2,0,1:T(8,128)S(1)}, u32[]{:S(2)}, u32[]{:S(2)}) collective-permute-start(f32[36,5,256]{2,0,1:T(8,128)S(1)} %pad_maximum_fusion.10), channel_id=1, source_target_pairs={{0,4},{4,8},{8,12},{12,16},{16,20},{20,24},{24,28},{28,32},{32,36}... | collective-permute-start | bytes 552968 | tf_op jit(solution)/shard_map/ppermute | solution.py:60
  43.0 1.3 collective-permute-start.4
  45.6 4.7 %collective-permute-start.5 = (f32[36,68,5]{1,0,2:T(8,128)S(1)}, f32[36,68,5]{1,0,2:T(8,128)S(1)}, u32[]{:S(2)}, u32[]{:S(2)}) collective-permute-start(f32[36,68,5]{1,0,2:T(8,128)S(1)} %pad_maximum_fusion.16), channel_id=1, source_target_pairs={{0,1},{1,2},{2,3},{4,5},{5,6},{6,7},{8,9},{9,10},{10,11},{12,13},{... | collective-permute-start | bytes 146888 | tf_op jit(solution)/shard_map/ppermute | solution.py:81
  50.7 1.2 pad_maximum_fusion.2.xu
  52.7 2.9 %copy.292 = f32[3,34,68,1]{3,2,1,0:T(8,128)} copy(f32[3,34,68,1]{2,1,0,3:T(8,128)S(1)} %slice_bitcast_fusion.6) | data formatting | bytes 55488 | tf_op jit(solution)/shard_map/broadcast_in_dim | solution.py:90
  55.6 2.9 %copy.293 = f32[3,34,68,1]{3,2,1,0:T(8,128)} copy(f32[3,34,68,1]{2,1,0,3:T(8,128)S(1)} %slice_bitcast_fusion.5) | data formatting | bytes 55488 | tf_op jit(solution)/shard_map/broadcast_in_dim | solution.py:91
  58.5 4.2 %pad_maximum_fusion = f32[3,34,68,128]{3,2,1,0:T(8,128)S(1)} fusion(f32[3,34,68,1]{3,2,1,0:T(8,128)} %copy.293, f32[3,34,68,1]{3,2,1,0:T(8,128)} %copy.292, f32[128]{0:T(128)S(1)} %pad.77.clone), kind=kLoop, calls=%fused_computation | loop fusion | flops 1775616 | bytes 3607232 | tf_op jit(solution)/shard_map/concatenate | solution.py:92
  62.7 2.5 %pad.43.yu = f32[3,34,80,128]{3,2,1,0:T(8,128)} pad(f32[3,34,68,128]{3,2,1,0:T(8,128)S(1)} %pad_maximum_fusion, f32[]{:T(128)} %constant.25.clone.1), padding=0_0x0_0x6_6x0_0 | pad | bytes 7729156 | tf_op jit(solution)/shard_map/jit(_pad)/pad | solution.py:93
  66.8 1.3 pad.42.yc
  68.0 23.6 %shard_map.94 = (f32[1,32,64,256]{3,2,1,0:T(8,128)}, f32[8,32,128]{2,1,0:T(8,128)}) custom-call(s32[4]{0:T(128)} %pad_add_fusion.place, f32[8,32]{1,0:T(8,128)} %convert_divide_fusion.weights, f32[32,64,256]{2,1,0:T(8,128)} %bitcast.165, bf16[3,1,32,64,256]{4,3,2,1,0:T(8,128)(2,1)} %v_ref.1, bf16[1,32,64,256]{3,2,1,0:T(8,128)(2,1)} %poro_ref.1, ...), custom_call_target="tpu_custom_call" | custom-call | flops 104857600 | bytes 20971520 | tf_op jit(solution)/shard_map/pallas_call | solution.py:206
  91.6 1.4 %subtract_multiply_fusion = f32[1,8,38,134]{3,2,1,0:T(8,128)S(1)} fusion(s32[]{:T(128)} %bitcast.35, s32[]{:T(128)} %bitcast.34, s32[134]{0:T(256)S(1)} %iota_add_fusion, s32[8,38]{1,0:T(8,128)S(1)} %broadcast_add_fusion), kind=kLoop, calls=%fused_computation.85 | loop fusion | flops 285152 | bytes 164704 | tf_op jit(solution)/shard_map/mul | solution.py:350
  94.1 2.6 %collective-permute-start.7 = (f32[8,32,128]{2,1,0:T(8,128)S(1)}, f32[8,32,128]{2,1,0:T(8,128)S(1)}, u32[]{:S(2)}, u32[]{:S(2)}) collective-permute-start(f32[8,32,128]{2,1,0:T(8,128)S(1)} %add.263), channel_id=1, source_target_pairs={{0,128},{128,0},{64,192},{192,64},{1,129},{129,1},{65,193},{193,65... | collective-permute-start | bytes 393224 | tf_op jit(solution)/shard_map/ppermute | solution.py:296
  96.7 4.0 %collective-permute-done.7 = f32[8,32,128]{2,1,0:T(8,128)S(1)} collective-permute-done((f32[8,32,128]{2,1,0:T(8,128)S(1)}, f32[8,32,128]{2,1,0:T(8,128)S(1)}, u32[]{:S(2)}, u32[]{:S(2)}) %collective-permute-start.7) | collective-permute-done | bytes 131104 | tf_op jit(solution)/shard_map/ppermute | solution.py:296
  100.8 6.5 %collective-permute-start.8 = (f32[16,3,128]{2,1,0:T(4,128)S(1)}, f32[16,3,128]{2,1,0:T(4,128)S(1)}, u32[]{:S(2)}, u32[]{:S(2)}) collective-permute-start(f32[16,3,128]{2,1,0:T(4,128)S(1)} %get-tuple-element.45), channel_id=1, source_target_pairs={{0,4},{4,8},{8,12},{12,16},{16,20},{20,24},{24,28},{28,32},{32,36}... | collective-permute-start | bytes 73736 | tf_op jit(solution)/shard_map/ppermute | solution.py:27
  107.3 1.9 %collective-permute-start.9 = (f32[16,3,128]{2,1,0:T(4,128)S(1)}, f32[16,3,128]{2,1,0:T(4,128)S(1)}, u32[]{:S(2)}, u32[]{:S(2)}) collective-permute-start(f32[16,3,128]{2,1,0:T(4,128)S(1)} %get-tuple-element.46), channel_id=1, source_target_pairs={{4,0},{8,4},{12,8},{16,12},{20,16},{24,20},{28,24},{32,28},{36,32}... | collective-permute-start | bytes 73736 | tf_op jit(solution)/shard_map/ppermute | solution.py:28
  109.2 7.5 %collective-permute-done.9 = f32[16,3,128]{2,1,0:T(4,128)S(1)} collective-permute-done((f32[16,3,128]{2,1,0:T(4,128)S(1)}, f32[16,3,128]{2,1,0:T(4,128)S(1)}, u32[]{:S(2)}, u32[]{:S(2)}) %collective-permute-start.9) | collective-permute-done | bytes 24608 | tf_op jit(solution)/shard_map/ppermute | solution.py:28
  116.9 3.5 %collective-permute-start.10 = (f32[16,38,3]{2,1,0:T(8,128)S(1)}, f32[16,38,3]{2,1,0:T(8,128)S(1)}, u32[]{:S(2)}, u32[]{:S(2)}) collective-permute-start(f32[16,38,3]{2,1,0:T(8,128)S(1)} %get-tuple-element.31), channel_id=1, source_target_pairs={{0,1},{1,2},{2,3},{4,5},{5,6},{6,7},{8,9},{9,10},{10,11},{12,13},{... | collective-permute-start | bytes 21896 | tf_op jit(solution)/shard_map/ppermute | solution.py:27
  120.4 1.5 %collective-permute-start.11 = (f32[16,38,3]{2,1,0:T(8,128)S(1)}, f32[16,38,3]{2,1,0:T(8,128)S(1)}, u32[]{:S(2)}, u32[]{:S(2)}) collective-permute-start(f32[16,38,3]{2,1,0:T(8,128)S(1)} %get-tuple-element.32), channel_id=1, source_target_pairs={{1,0},{2,1},{3,2},{5,4},{6,5},{7,6},{9,8},{10,9},{11,10},{13,12},{... | collective-permute-start | bytes 21896 | tf_op jit(solution)/shard_map/ppermute | solution.py:28
  122.2 3.4 %collective-permute-done.10 = f32[16,38,3]{2,1,0:T(8,128)S(1)} collective-permute-done((f32[16,38,3]{2,1,0:T(8,128)S(1)}, f32[16,38,3]{2,1,0:T(8,128)S(1)}, u32[]{:S(2)}, u32[]{:S(2)}) %collective-permute-start.10) | collective-permute-done | bytes 7328 | tf_op jit(solution)/shard_map/ppermute | solution.py:27
  125.6 4.1 %collective-permute-done.11 = f32[16,38,3]{2,1,0:T(8,128)S(1)} collective-permute-done((f32[16,38,3]{2,1,0:T(8,128)S(1)}, f32[16,38,3]{2,1,0:T(8,128)S(1)}, u32[]{:S(2)}, u32[]{:S(2)}) %collective-permute-start.11) | collective-permute-done | bytes 7328 | tf_op jit(solution)/shard_map/ppermute | solution.py:28
  130.2 1.1 fusion.41
  131.6 1.1 fusion.40
  132.8 1.2 fusion.64
  (139 shorter events, 17.5 us)
Async XLA Ops:
  0.6 96.1 %copy-start = (f32[4,8,32,128]{3,2,1,0:T(8,128)S(1)}, f32[4,8,32,128]{3,2,1,0:T(8,128)}, u32[]{:S(2)}) copy-start(f32[4,8,32,128]{3,2,1,0:T(8,128)} %param.13) | copy-start | bytes 1572868
  0.6 4.1 %copy-start.1 = (f32[1,32,64,256]{3,2,1,0:T(8,128)S(1)}, f32[1,32,64,256]{3,2,1,0:T(8,128)}, u32[]{:S(2)}) copy-start(f32[1,32,64,256]{3,2,1,0:T(8,128)} %param.7) | copy-start | bytes 6291460
  5.6 22.2 %collective-permute-start = (f32[5,64,256]{2,1,0:T(8,128)}, f32[5,64,256]{2,1,0:T(8,128)S(1)}, u32[]{:S(2)}, u32[]{:S(2)}) collective-permute-start(f32[5,64,256]{2,1,0:T(8,128)} %pad_maximum_fusion.5), channel_id=1, source_target_pairs={{0,64},{64,128},{1,65},{65,129},{2,66},{66,130},{3,67},{67,131},{4... | collective-permute-start | bytes 983048 | tf_op jit(solution)/shard_map/ppermute | solution.py:42
  7.7 20.1 %collective-permute-start.1 = (f32[5,64,256]{2,1,0:T(8,128)}, f32[5,64,256]{2,1,0:T(8,128)S(1)}, u32[]{:S(2)}, u32[]{:S(2)}) collective-permute-start(f32[5,64,256]{2,1,0:T(8,128)} %pad_maximum_fusion.6), channel_id=1, source_target_pairs={{64,0},{128,64},{65,1},{129,65},{66,2},{130,66},{67,3},{131,67},{6... | collective-permute-start | bytes 983048 | tf_op jit(solution)/shard_map/ppermute | solution.py:43
  17.7 3.4 %copy-start.4 = (f32[32,64,2]{2,1,0:T(8,128)S(1)}, f32[32,64,2]{2,1,0:T(8,128)}, u32[]{:S(2)}) copy-start(f32[32,64,2]{2,1,0:T(8,128)} %get-tuple-element.21) | copy-start | bytes 49156
  17.7 7.1 %copy-start.3 = (f32[32,64,2]{2,1,0:T(8,128)S(1)}, f32[32,64,2]{2,1,0:T(8,128)}, u32[]{:S(2)}) copy-start(f32[32,64,2]{2,1,0:T(8,128)} %get-tuple-element.22) | copy-start | bytes 49156
  21.1 4.4 %copy-start.9 = (s32[8]{0:T(128)S(1)}, s32[8]{0:T(128)}, u32[]{:S(2)}) copy-start(s32[8]{0:T(128)} %param.11) | copy-start | bytes 100
  21.1 4.6 %copy-start.8 = (s32[4,2]{0,1:T(2,128)S(1)}, s32[4,2]{0,1:T(2,128)}, u32[]{:S(2)}) copy-start(s32[4,2]{0,1:T(2,128)} %param.12) | copy-start | bytes 100
  22.1 5.7 %copy-start.5 = (f32[32,2,256]{2,1,0:T(2,128)S(1)}, f32[32,2,256]{2,1,0:T(2,128)}, u32[]{:S(2)}) copy-start(f32[32,2,256]{2,1,0:T(2,128)} %get-tuple-element.24) | copy-start | bytes 196612
  24.8 16.4 %copy-start.6 = (f32[3,32,64,1]{2,1,0,3:T(8,128)S(1)}, f32[3,32,64,1]{2,1,0,3:T(8,128)}, u32[]{:S(2)}) copy-start(f32[3,32,64,1]{2,1,0,3:T(8,128)} %copy.277) | copy-start | bytes 73732
  24.8 17.9 %copy-start.7 = (f32[32,64,2]{1,2,0:T(2,128)S(1)}, f32[32,64,2]{1,2,0:T(2,128)}, u32[]{:S(2)}) copy-start(f32[32,64,2]{1,2,0:T(2,128)} %copy.273) | copy-start | bytes 49156
  28.0 13.3 %collective-permute-start.2 = (f32[36,5,256]{2,0,1:T(8,128)S(1)}, f32[36,5,256]{2,0,1:T(8,128)S(1)}, u32[]{:S(2)}, u32[]{:S(2)}) collective-permute-start(f32[36,5,256]{2,0,1:T(8,128)S(1)} %pad_maximum_fusion.9), channel_id=1, source_target_pairs={{4,0},{8,4},{12,8},{16,12},{20,16},{24,20},{28,24},{32,28},{36,32}... | collective-permute-start | bytes 552968 | tf_op jit(solution)/shard_map/ppermute | solution.py:61
  31.4 10.2 %collective-permute-start.3 = (f32[36,5,256]{2,0,1:T(8,128)S(1)}, f32[36,5,256]{2,0,1:T(8,128)S(1)}, u32[]{:S(2)}, u32[]{:S(2)}) collective-permute-start(f32[36,5,256]{2,0,1:T(8,128)S(1)} %pad_maximum_fusion.10), channel_id=1, source_target_pairs={{0,4},{4,8},{8,12},{12,16},{16,20},{20,24},{24,28},{28,32},{32,36}... | collective-permute-start | bytes 552968 | tf_op jit(solution)/shard_map/ppermute | solution.py:60
  43.0 9.6 %collective-permute-start.4 = (f32[36,68,5]{1,0,2:T(8,128)S(1)}, f32[36,68,5]{1,0,2:T(8,128)S(1)}, u32[]{:S(2)}, u32[]{:S(2)}) collective-permute-start(f32[36,68,5]{1,0,2:T(8,128)S(1)} %pad_maximum_fusion.15), channel_id=1, source_target_pairs={{1,0},{2,1},{3,2},{5,4},{6,5},{7,6},{9,8},{10,9},{11,10},{13,12},{... | collective-permute-start | bytes 146888 | tf_op jit(solution)/shard_map/ppermute | solution.py:82
  45.6 10.0 %collective-permute-start.5 = (f32[36,68,5]{1,0,2:T(8,128)S(1)}, f32[36,68,5]{1,0,2:T(8,128)S(1)}, u32[]{:S(2)}, u32[]{:S(2)}) collective-permute-start(f32[36,68,5]{1,0,2:T(8,128)S(1)} %pad_maximum_fusion.16), channel_id=1, source_target_pairs={{0,1},{1,2},{2,3},{4,5},{5,6},{6,7},{8,9},{9,10},{10,11},{12,13},{... | collective-permute-start | bytes 146888 | tf_op jit(solution)/shard_map/ppermute | solution.py:81
  91.6 1.6 %collective-permute-start.6 = (f32[8,32,128]{2,1,0:T(8,128)}, f32[8,32,128]{2,1,0:T(8,128)S(1)}, u32[]{:S(2)}, u32[]{:S(2)}) collective-permute-start(f32[8,32,128]{2,1,0:T(8,128)} %get-tuple-element.6), channel_id=1, source_target_pairs={{0,64},{64,0},{128,192},{192,128},{1,65},{65,1},{129,193},{193,129... | collective-permute-start | bytes 393224 | tf_op jit(solution)/shard_map/ppermute | solution.py:294
  94.1 6.6 %collective-permute-start.7 = (f32[8,32,128]{2,1,0:T(8,128)S(1)}, f32[8,32,128]{2,1,0:T(8,128)S(1)}, u32[]{:S(2)}, u32[]{:S(2)}) collective-permute-start(f32[8,32,128]{2,1,0:T(8,128)S(1)} %add.263), channel_id=1, source_target_pairs={{0,128},{128,0},{64,192},{192,64},{1,129},{129,1},{65,193},{193,65... | collective-permute-start | bytes 393224 | tf_op jit(solution)/shard_map/ppermute | solution.py:296
  100.7 32.1 %copy-start.2 = (f32[8,32,128]{2,1,0:T(8,128)}, f32[8,32,128]{2,1,0:T(8,128)S(1)}, u32[]{:S(2)}) copy-start(f32[8,32,128]{2,1,0:T(8,128)S(1)} %add.264) | copy-start | bytes 393220
  100.8 8.5 %collective-permute-start.8 = (f32[16,3,128]{2,1,0:T(4,128)S(1)}, f32[16,3,128]{2,1,0:T(4,128)S(1)}, u32[]{:S(2)}, u32[]{:S(2)}) collective-permute-start(f32[16,3,128]{2,1,0:T(4,128)S(1)} %get-tuple-element.45), channel_id=1, source_target_pairs={{0,4},{4,8},{8,12},{12,16},{16,20},{20,24},{24,28},{28,32},{32,36}... | collective-permute-start | bytes 73736 | tf_op jit(solution)/shard_map/ppermute | solution.py:27
  107.3 9.4 %collective-permute-start.9 = (f32[16,3,128]{2,1,0:T(4,128)S(1)}, f32[16,3,128]{2,1,0:T(4,128)S(1)}, u32[]{:S(2)}, u32[]{:S(2)}) collective-permute-start(f32[16,3,128]{2,1,0:T(4,128)S(1)} %get-tuple-element.46), channel_id=1, source_target_pairs={{4,0},{8,4},{12,8},{16,12},{20,16},{24,20},{28,24},{32,28},{36,32}... | collective-permute-start | bytes 73736 | tf_op jit(solution)/shard_map/ppermute | solution.py:28
  116.9 8.7 %collective-permute-start.10 = (f32[16,38,3]{2,1,0:T(8,128)S(1)}, f32[16,38,3]{2,1,0:T(8,128)S(1)}, u32[]{:S(2)}, u32[]{:S(2)}) collective-permute-start(f32[16,38,3]{2,1,0:T(8,128)S(1)} %get-tuple-element.31), channel_id=1, source_target_pairs={{0,1},{1,2},{2,3},{4,5},{5,6},{6,7},{8,9},{9,10},{10,11},{12,13},{... | collective-permute-start | bytes 21896 | tf_op jit(solution)/shard_map/ppermute | solution.py:27
  120.4 9.3 %collective-permute-start.11 = (f32[16,38,3]{2,1,0:T(8,128)S(1)}, f32[16,38,3]{2,1,0:T(8,128)S(1)}, u32[]{:S(2)}, u32[]{:S(2)}) collective-permute-start(f32[16,38,3]{2,1,0:T(8,128)S(1)} %get-tuple-element.32), channel_id=1, source_target_pairs={{1,0},{2,1},{3,2},{5,4},{6,5},{7,6},{9,8},{10,9},{11,10},{13,12},{... | collective-permute-start | bytes 21896 | tf_op jit(solution)/shard_map/ppermute | solution.py:28

commit v6 on v5

--- a/solution.py
+++ b/solution.py
@@ -30,45 +30,111 @@
     return shard
 
 
+def faces_kernel(c_ref, v_ref, zs_up, zs_dn, xr, yc_ref, yu_ref):
+    nzx, ny = c_ref.shape
+    nz = xr.shape[1]
+    nx = nzx // nz
+    f32 = jnp.float32
+    zs_up[0:2] = c_ref[nzx - 2 * nx : nzx].reshape(2, nx, ny)
+    zs_dn[0:2] = c_ref[0 : 2 * nx].reshape(2, nx, ny)
+    for d in range(3):
+        zs_up[2 + d] = v_ref[d, nzx - nx : nzx].astype(f32)
+        zs_dn[2 + d] = v_ref[d, 0:nx].astype(f32)
+    for z in range(nz):
+        base = z * nx
+        xr[0, z : z + 1] = c_ref[base + nx - 2 : base + nx - 1]
+        xr[1, z : z + 1] = c_ref[base + nx - 1 : base + nx]
+        xr[5, z : z + 1] = c_ref[base : base + 1]
+        xr[6, z : z + 1] = c_ref[base + 1 : base + 2]
+        for d in range(3):
+            top = v_ref[d, base + nx - 16 : base + nx].astype(f32)
+            bottom = v_ref[d, base : base + 16].astype(f32)
+            xr[2 + d, z : z + 1] = top[15:16]
+            xr[7 + d, z : z + 1] = bottom[0:1]
+    lane = lax.broadcasted_iota(jnp.int32, (8, ny), 1)
+    row = lax.broadcasted_iota(jnp.int32, (8, ny), 0)
+    pick_c = (
+        ((row == 0) & (lane == ny - 2))
+        | ((row == 1) & (lane == ny - 1))
+        | ((row == 2) & (lane == 0))
+        | ((row == 3) & (lane == 1))
+    )
+    pick_u = ((row == 0) & (lane == ny - 1)) | ((row == 1) & (lane == 0))
+    nt = (((1,), (1,)), ((), ()))
+    yc_ref[...] = lax.dot_general(
+        pick_c.astype(f32), c_ref[...], nt, precision=lax.Precision.HIGHEST,
+        preferred_element_type=f32,
+    )
+    for d in range(3):
+        yu_ref[d] = lax.dot_general(
+            pick_u.astype(jnp.bfloat16), v_ref[d], nt, preferred_element_type=f32
+        )
+
+
+def faces_call(c, velocity):
+    nz, nx, ny = c.shape
+    f32 = jnp.float32
+    vmem = pl.BlockSpec(memory_space=pltpu.VMEM)
+    return pl.pallas_call(
+        faces_kernel,
+        out_shape=(
+            jax.ShapeDtypeStruct((5, nx, ny), f32),
+            jax.ShapeDtypeStruct((5, nx, ny), f32),
+            jax.ShapeDtypeStruct((10, nz, ny), f32),
+            jax.ShapeDtypeStruct((8, nz * nx), f32),
+            jax.ShapeDtypeStruct((3, 8, nz * nx), f32),
+        ),
+        in_specs=[vmem, vmem],
+        out_specs=(vmem,) * 5,
+        compiler_params=pltpu.CompilerParams(vmem_limit_bytes=32 * 1024 * 1024),
+        cost_estimate=pl.CostEstimate(
+            flops=2 * 32 * nz * nx * ny, transcendentals=0, bytes_accessed=10 * nz * nx * ny
+        ),
+    )(c.reshape(nz * nx, ny), velocity.reshape(3, nz * nx, ny))
+
+
 def transport_halo(c, u, slabs):
     f32 = jnp.float32
     nz, nx, ny = c.shape
+    zs_up, zs_dn, xr, ycols, ucols = faces_call(c, u)
+    ycols = ycols.reshape(8, nz, nx)
+    ucols = ucols.reshape(3, 8, nz, nx)
 
     def chain(axis, members):
         up = [(i, i + 1) for i in range(members - 1)]
         return up, [(j, i) for i, j in up]
 
     up, down = chain("grp", slabs)
-    below = lax.ppermute(jnp.concatenate([c[nz - 2 :], u[:, nz - 1].astype(f32)], 0), "grp", up)
-    above = lax.ppermute(jnp.concatenate([c[:2], u[:, 0].astype(f32)], 0), "grp", down)
+    below = lax.ppermute(zs_up, "grp", up)
+    above = lax.ppermute(zs_dn, "grp", down)
     zlo_c, zlo_u = below[:2], below[2:]
     zhi_c, zhi_u = above[:2], above[2:]
 
-    def zext_c(rows):
-        return jnp.concatenate([zlo_c[:, rows], c[:, rows], zhi_c[:, rows]], 0)
-
-    def zext_u(row):
-        core = jnp.concatenate(
-            [zlo_u[:, None, row], u[:, :, row].astype(f32), zhi_u[:, None, row]], 1
-        )
+    def zext_c(rows, picked):
+        return jnp.concatenate([zlo_c[:, rows], jnp.swapaxes(picked, 0, 1), zhi_c[:, rows]], 0)
+
+    def zext_u(row, picked):
+        core = jnp.concatenate([zlo_u[:, None, row], picked, zhi_u[:, None, row]], 1)
         return jnp.pad(core, ((0, 0), (1, 1), (0, 0)))
 
     rows = lax.axis_size("gx")
     up, down = chain("gx", rows)
-    send_up = jnp.concatenate([zext_c(slice(nx - 2, nx)), jnp.swapaxes(zext_u(nx - 1), 0, 1)], 1)
-    send_dn = jnp.concatenate([zext_c(slice(0, 2)), jnp.swapaxes(zext_u(0), 0, 1)], 1)
+    send_up = jnp.concatenate(
+        [zext_c(slice(nx - 2, nx), xr[0:2]), jnp.swapaxes(zext_u(nx - 1, xr[2:5]), 0, 1)], 1
+    )
+    send_dn = jnp.concatenate(
+        [zext_c(slice(0, 2), xr[5:7]), jnp.swapaxes(zext_u(0, xr[7:10]), 0, 1)], 1
+    )
     bx = lax.ppermute(send_up, "gx", up)
     ax = lax.ppermute(send_dn, "gx", down)
 
-    def xz_c(lanes):
-        core = jnp.concatenate([zlo_c[..., lanes], c[..., lanes], zhi_c[..., lanes]], 0)
+    def xz_c(lanes, picked):
+        core = jnp.concatenate([zlo_c[..., lanes], jnp.moveaxis(picked, 0, 2), zhi_c[..., lanes]], 0)
         return jnp.concatenate([bx[:, 0:2, lanes], core, ax[:, 0:2, lanes]], 1)
 
-    def xz_u(lane):
+    def xz_u(lane, picked):
         core = jnp.pad(
-            jnp.concatenate(
-                [zlo_u[:, None, :, lane], u[..., lane].astype(f32), zhi_u[:, None, :, lane]], 1
-            ),
+            jnp.concatenate([zlo_u[:, None, :, lane], picked, zhi_u[:, None, :, lane]], 1),
             ((0, 0), (1, 1), (0, 0)),
         )
         lo = jnp.swapaxes(bx[:, 2:5, lane], 0, 1)[:, :, None]
@@ -78,8 +144,12 @@
 
     columns = lax.axis_size("gy")
     up, down = chain("gy", columns)
-    by = lax.ppermute(jnp.concatenate([xz_c(slice(ny - 2, ny)), xz_u(ny - 1)], 2), "gy", up)
-    ay = lax.ppermute(jnp.concatenate([xz_c(slice(0, 2)), xz_u(0)], 2), "gy", down)
+    by = lax.ppermute(
+        jnp.concatenate([xz_c(slice(ny - 2, ny), ycols[0:2]), xz_u(ny - 1, ucols[:, 0])], 2), "gy", up
+    )
+    ay = lax.ppermute(
+        jnp.concatenate([xz_c(slice(0, 2), ycols[2:4]), xz_u(0, ucols[:, 1])], 2), "gy", down
+    )
 
     xc = jnp.concatenate([ax[:, 0:2], jnp.zeros((nz + 4, 4, ny), f32), bx[:, 0:2]], 1)
     xu_hi = jnp.swapaxes(ax[1:-1, 2:5], 0, 1)[:, :, None]
@@ -321,7 +391,7 @@
     coarse_x = tile_x // 2
     coarse_y = tile_y // 2
 
-    pieces = transport_halo(field, speeds, slabs)
+    pieces = transport_halo(field, velocity, slabs)
     place = jnp.stack([group_index, row_index, column_index, active.astype(jnp.int32)])
     advanced, partial_cond = transport_call(
         place, weights, field, velocity, porosity, saturation, *pieces,

time: 134 us -> 127 us (0.948)
  local copies, waits for them, and re-layouts: 32.4 us -> 22.7 us
  other arithmetic: 20.6 us -> 15.3 us
  waiting for transfers between devices: 19.1 us -> 22.6 us
  Pallas kernels: 23.6 us -> 26.4 us
  starting transfers between devices: 37 us -> 38.5 us
    convert_element_type x2 -> x0, local copies, waits for them, and re-layouts: 6.09 us -> none  [xz_u(): u[..., lane].astype(f32)]
    convert_element_type x3 -> x0, other arithmetic: 3.66 us -> none  [the longest x1 3.37 us: xz_u(): u[..., lane].astype(f32)]
    ppermute x4, waiting for transfers between devices: 0.01 us -> 3.67 us  [the longest x1 3.66 us: transport_halo(): above = lax.ppermute(zs_dn, 'grp', down)]
    slice x7 -> x8, local copies, waits for them, and re-layouts: 3.75 us -> 0.28 us  [the longest x3 0.13 us: transport_halo(): ycols[2:4]]
    pallas_call x0 -> x1, Pallas kernels: none -> 2.76 us  [faces_call(): pl.pallas_call(faces_kernel, out_shape=(jax.ShapeDtypeStruct((5, nx, ny),...]
    concatenate x9 -> x5, other arithmetic: 1.7 us -> 0.1 us  [the longest x1 0.03 us: xz_u(): jnp.concatenate([zlo_u[:, None, :, lane], picked, zhi_u[:, None, :, lane]...]
    ppermute x1, starting transfers between devices: 6.14 us -> 7.54 us  [transport_halo(): bx = lax.ppermute(send_up, 'gx', up)]
    ppermute x1, starting transfers between devices: 3.31 us -> 1.92 us  [transport_halo(): ax = lax.ppermute(send_dn, 'gx', down)]
  transfers between devices with their start and end apart: 12 -> 12, of which waited for: 5 -> 6; matrix products, arithmetic and copies ran while one was open for 21% -> 12% of each run, Pallas kernels for 0% -> 0%
where the time goes in v6:
time: 127 us
  starting transfers between devices  38.5 us (30%)
  Pallas kernels  26.4 us (21%)
  local copies, waits for them, and re-layouts  22.7 us (18%)
  waiting for transfers between devices  22.6 us (18%)
  other arithmetic  15.3 us (12%)
    pallas_call x1, Pallas kernels, transport_call(): pl.pallas_call(functools.partial(transport_kernel, grid), out_shape=(jax....  23.6 us
    ppermute x2, waiting for transfers between devices, with_halo(): after = lax.ppermute(initial, axis, down)  11.6 us
    ppermute x2, starting transfers between devices, with_halo(): before = lax.ppermute(last, axis, up)  10.5 us
    ppermute x1, starting transfers between devices, transport_halo(): bx = lax.ppermute(send_up, 'gx', up)  7.54 us
    ppermute x1, starting transfers between devices, transport_halo(): lax.ppermute(jnp.concatenate([xz_c(slice(ny - 2, ny), ycols[0:2]), xz_u(n...  4.73 us
    ppermute x1, starting transfers between devices, transport_halo(): above = lax.ppermute(zs_dn, 'grp', down)  4.29 us
    concatenate x1, other arithmetic, transport_halo(): jnp.concatenate([yu_hi, jnp.zeros((3, nz + 2, nx + 4, 126), f32), yu_lo], 3)  4.25 us
    ppermute x1, waiting for transfers between devices, grp_sum(): pair = lax.ppermute(partial, 'grp', [(0, 2), (2, 0), (1, 3), (3, 1)])  3.77 us
  transfers between devices with their start and end apart: 12, of which 6 were waited for; matrix products, arithmetic and copies ran while one was open for 12% of the time, Pallas kernels for 0%

profile of v6, /device:TPU:102, one launch (start us, length us, event | category | flops | bytes accessed | tf_op | source)
XLA Modules:
  0.0 126.7 jit_solution(12205725052364220108)
XLA Ops:
  0.7 1.9 %copy-done.1 = bf16[3,1,32,64,256]{4,3,2,1,0:T(8,128)(2,1)S(1)} copy-done((bf16[3,1,32,64,256]{4,3,2,1,0:T(8,128)(2,1)S(1)}, bf16[3,1,32,64,256]{4,3,2,1,0:T(8,128)(2,1)}, u32[]{:S(2)}) %copy-start.1) | copy-done | bytes 3145752
  2.6 1.6 %copy-done.2 = f32[1,32,64,256]{3,2,1,0:T(8,128)S(1)} copy-done((f32[1,32,64,256]{3,2,1,0:T(8,128)S(1)}, f32[1,32,64,256]{3,2,1,0:T(8,128)}, u32[]{:S(2)}) %copy-start.2) | copy-done | bytes 2097176
  4.2 2.8 %shard_map.94 = (f32[5,64,256]{2,1,0:T(8,128)S(1)}, f32[5,64,256]{2,1,0:T(8,128)S(1)}, f32[10,32,256]{2,1,0:T(8,128)S(1)}, f32[8,2048]{1,0:T(8,128)S(1)}, f32[3,8,2048]{2,1,0:T(8,128)S(1)}) custom-call(f32[2048,256]{1,0:T(8,128)S(1)} %bitcast.155, bf16[3,2048,256]{2,1,0:T(8,128)(2,1)S(1)} %bitcast.153), custom_call_target="tpu_custom_call" | custom-call | flops 33554432 | bytes 5242880 | tf_op jit(solution)/shard_map/pallas_call | solution.py:78
  6.9 1.3 %collective-permute-start = (f32[5,64,256]{2,1,0:T(8,128)S(1)}, f32[5,64,256]{2,1,0:T(8,128)S(1)}, u32[]{:S(2)}, u32[]{:S(2)}) collective-permute-start(f32[5,64,256]{2,1,0:T(8,128)S(1)} %get-tuple-element.10), channel_id=1, source_target_pairs={{0,64},{64,128},{1,65},{65,129},{2,66},{66,130},{3,67},{67,131},{4... | collective-permute-start | bytes 983048 | tf_op jit(solution)/shard_map/ppermute | solution.py:108
  8.3 4.3 %collective-permute-start.1 = (f32[5,64,256]{2,1,0:T(8,128)S(1)}, f32[5,64,256]{2,1,0:T(8,128)S(1)}, u32[]{:S(2)}, u32[]{:S(2)}) collective-permute-start(f32[5,64,256]{2,1,0:T(8,128)S(1)} %get-tuple-element.11), channel_id=1, source_target_pairs={{64,0},{128,64},{65,1},{129,65},{66,2},{130,66},{67,3},{131,67},{6... | collective-permute-start | bytes 983048 | tf_op jit(solution)/shard_map/ppermute | solution.py:109
  15.7 3.7 %collective-permute-done.1 = f32[5,64,256]{2,1,0:T(8,128)S(1)} collective-permute-done((f32[5,64,256]{2,1,0:T(8,128)S(1)}, f32[5,64,256]{2,1,0:T(8,128)S(1)}, u32[]{:S(2)}, u32[]{:S(2)}) %collective-permute-start.1) | collective-permute-done | bytes 327712 | tf_op jit(solution)/shard_map/ppermute | solution.py:109
  19.5 1.9 %collective-permute-start.2 = (f32[36,5,256]{2,0,1:T(8,128)S(1)}, f32[36,5,256]{2,0,1:T(8,128)S(1)}, u32[]{:S(2)}, u32[]{:S(2)}) collective-permute-start(f32[36,5,256]{2,0,1:T(8,128)S(1)} %pad_maximum_fusion.7), channel_id=1, source_target_pairs={{4,0},{8,4},{12,8},{16,12},{20,16},{24,20},{28,24},{32,28},{36,32}... | collective-permute-start | bytes 552968 | tf_op jit(solution)/shard_map/ppermute | solution.py:129
  21.5 7.5 %collective-permute-start.3 = (f32[36,5,256]{2,0,1:T(8,128)S(1)}, f32[36,5,256]{2,0,1:T(8,128)S(1)}, u32[]{:S(2)}, u32[]{:S(2)}) collective-permute-start(f32[36,5,256]{2,0,1:T(8,128)S(1)} %pad_maximum_fusion.8), channel_id=1, source_target_pairs={{0,4},{4,8},{8,12},{12,16},{16,20},{20,24},{24,28},{28,32},{32,36}... | collective-permute-start | bytes 552968 | tf_op jit(solution)/shard_map/ppermute | solution.py:128
  34.5 1.3 %collective-permute-start.4 = (f32[36,68,5]{1,0,2:T(8,128)S(1)}, f32[36,68,5]{1,0,2:T(8,128)S(1)}, u32[]{:S(2)}, u32[]{:S(2)}) collective-permute-start(f32[36,68,5]{1,0,2:T(8,128)S(1)} %pad_maximum_fusion.13), channel_id=1, source_target_pairs={{1,0},{2,1},{3,2},{5,4},{6,5},{7,6},{9,8},{10,9},{11,10},{13,12},{... | collective-permute-start | bytes 146888 | tf_op jit(solution)/shard_map/ppermute | solution.py:150
  37.1 4.7 %collective-permute-start.5 = (f32[36,68,5]{1,0,2:T(8,128)S(1)}, f32[36,68,5]{1,0,2:T(8,128)S(1)}, u32[]{:S(2)}, u32[]{:S(2)}) collective-permute-start(f32[36,68,5]{1,0,2:T(8,128)S(1)} %pad_maximum_fusion.14), channel_id=1, source_target_pairs={{0,1},{1,2},{2,3},{4,5},{5,6},{6,7},{8,9},{9,10},{10,11},{12,13},{... | collective-permute-start | bytes 146888 | tf_op jit(solution)/shard_map/ppermute | solution.py:147
  42.1 1.1 pad_maximum_fusion.2.xu
  43.3 0.8 pad_maximum_fusion.6.xc
  44.1 2.9 %copy.214 = f32[3,34,68,1]{3,2,1,0:T(8,128)} copy(f32[3,34,68,1]{2,1,0,3:T(8,128)S(1)} %slice_bitcast_fusion.6) | data formatting | bytes 55488 | tf_op jit(solution)/shard_map/broadcast_in_dim | solution.py:160
  47.0 2.9 %copy.215 = f32[3,34,68,1]{3,2,1,0:T(8,128)} copy(f32[3,34,68,1]{2,1,0,3:T(8,128)S(1)} %slice_bitcast_fusion.5) | data formatting | bytes 55488 | tf_op jit(solution)/shard_map/broadcast_in_dim | solution.py:161
  49.9 4.2 %pad_maximum_fusion = f32[3,34,68,128]{3,2,1,0:T(8,128)S(1)} fusion(f32[3,34,68,1]{3,2,1,0:T(8,128)} %copy.215, f32[3,34,68,1]{3,2,1,0:T(8,128)} %copy.214, f32[128]{0:T(128)S(1)} %pad.77.clone), kind=kLoop, calls=%fused_computation | loop fusion | flops 1775616 | bytes 3607232 | tf_op jit(solution)/shard_map/concatenate | solution.py:162
  54.1 2.5 %pad.43.yu = f32[3,34,80,128]{3,2,1,0:T(8,128)} pad(f32[3,34,68,128]{3,2,1,0:T(8,128)S(1)} %pad_maximum_fusion, f32[]{:T(128)} %constant.25.clone.1), padding=0_0x0_0x6_6x0_0 | pad | bytes 7729156 | tf_op jit(solution)/shard_map/jit(_pad)/pad | solution.py:163
  58.2 1.3 pad.42.yc
  59.5 23.6 %shard_map.95 = (f32[1,32,64,256]{3,2,1,0:T(8,128)}, f32[8,32,128]{2,1,0:T(8,128)}) custom-call(s32[4]{0:T(128)} %pad_add_fusion.place, f32[8,32]{1,0:T(8,128)} %convert_divide_fusion.weights, f32[32,64,256]{2,1,0:T(8,128)} %bitcast.154, bf16[3,1,32,64,256]{4,3,2,1,0:T(8,128)(2,1)} %v_ref.1, bf16[1,32,64,256]{3,2,1,0:T(8,128)(2,1)} %poro_ref.1, ...), custom_call_target="tpu_custom_call" | custom-call | flops 104857600 | bytes 20971520 | tf_op jit(solution)/shard_map/pallas_call | solution.py:276
  83.1 1.4 %subtract_multiply_fusion = f32[1,8,38,134]{3,2,1,0:T(8,128)S(1)} fusion(s32[]{:T(128)} %bitcast.36, s32[]{:T(128)} %bitcast.35, s32[134]{0:T(256)S(1)} %iota_add_fusion, s32[8,38]{1,0:T(8,128)S(1)} %broadcast_add_fusion), kind=kLoop, calls=%fused_computation.80 | loop fusion | flops 285152 | bytes 164704 | tf_op jit(solution)/shard_map/mul | solution.py:420
  84.6 0.9 add.263
  85.5 3.6 %collective-permute-start.7 = (f32[8,32,128]{2,1,0:T(8,128)S(1)}, f32[8,32,128]{2,1,0:T(8,128)S(1)}, u32[]{:S(2)}, u32[]{:S(2)}) collective-permute-start(f32[8,32,128]{2,1,0:T(8,128)S(1)} %add.263), channel_id=1, source_target_pairs={{0,128},{128,0},{64,192},{192,64},{1,129},{129,1},{65,193},{193,65... | collective-permute-start | bytes 393224 | tf_op jit(solution)/shard_map/ppermute | solution.py:366
  89.2 3.8 %collective-permute-done.7 = f32[8,32,128]{2,1,0:T(8,128)S(1)} collective-permute-done((f32[8,32,128]{2,1,0:T(8,128)S(1)}, f32[8,32,128]{2,1,0:T(8,128)S(1)}, u32[]{:S(2)}, u32[]{:S(2)}) %collective-permute-start.7) | collective-permute-done | bytes 131104 | tf_op jit(solution)/shard_map/ppermute | solution.py:366
  93.0 7.0 %collective-permute-start.8 = (f32[16,3,128]{2,1,0:T(4,128)S(1)}, f32[16,3,128]{2,1,0:T(4,128)S(1)}, u32[]{:S(2)}, u32[]{:S(2)}) collective-permute-start(f32[16,3,128]{2,1,0:T(4,128)S(1)} %get-tuple-element.49), channel_id=1, source_target_pairs={{0,4},{4,8},{8,12},{12,16},{16,20},{20,24},{24,28},{28,32},{32,36}... | collective-permute-start | bytes 73736 | tf_op jit(solution)/shard_map/ppermute | solution.py:27
  99.9 1.9 %collective-permute-start.9 = (f32[16,3,128]{2,1,0:T(4,128)S(1)}, f32[16,3,128]{2,1,0:T(4,128)S(1)}, u32[]{:S(2)}, u32[]{:S(2)}) collective-permute-start(f32[16,3,128]{2,1,0:T(4,128)S(1)} %get-tuple-element.50), channel_id=1, source_target_pairs={{4,0},{8,4},{12,8},{16,12},{20,16},{24,20},{28,24},{32,28},{36,32}... | collective-permute-start | bytes 73736 | tf_op jit(solution)/shard_map/ppermute | solution.py:28
  101.9 7.5 %collective-permute-done.9 = f32[16,3,128]{2,1,0:T(4,128)S(1)} collective-permute-done((f32[16,3,128]{2,1,0:T(4,128)S(1)}, f32[16,3,128]{2,1,0:T(4,128)S(1)}, u32[]{:S(2)}, u32[]{:S(2)}) %collective-permute-start.9) | collective-permute-done | bytes 24608 | tf_op jit(solution)/shard_map/ppermute | solution.py:28
  109.6 3.5 %collective-permute-start.10 = (f32[16,38,3]{2,1,0:T(8,128)S(1)}, f32[16,38,3]{2,1,0:T(8,128)S(1)}, u32[]{:S(2)}, u32[]{:S(2)}) collective-permute-start(f32[16,38,3]{2,1,0:T(8,128)S(1)} %get-tuple-element.31), channel_id=1, source_target_pairs={{0,1},{1,2},{2,3},{4,5},{5,6},{6,7},{8,9},{9,10},{10,11},{12,13},{... | collective-permute-start | bytes 21896 | tf_op jit(solution)/shard_map/ppermute | solution.py:27
  113.1 1.5 %collective-permute-start.11 = (f32[16,38,3]{2,1,0:T(8,128)S(1)}, f32[16,38,3]{2,1,0:T(8,128)S(1)}, u32[]{:S(2)}, u32[]{:S(2)}) collective-permute-start(f32[16,38,3]{2,1,0:T(8,128)S(1)} %get-tuple-element.32), channel_id=1, source_target_pairs={{1,0},{2,1},{3,2},{5,4},{6,5},{7,6},{9,8},{10,9},{11,10},{13,12},{... | collective-permute-start | bytes 21896 | tf_op jit(solution)/shard_map/ppermute | solution.py:28
  114.9 3.4 %collective-permute-done.10 = f32[16,38,3]{2,1,0:T(8,128)S(1)} collective-permute-done((f32[16,38,3]{2,1,0:T(8,128)S(1)}, f32[16,38,3]{2,1,0:T(8,128)S(1)}, u32[]{:S(2)}, u32[]{:S(2)}) %collective-permute-start.10) | collective-permute-done | bytes 7328 | tf_op jit(solution)/shard_map/ppermute | solution.py:27
  118.4 4.1 %collective-permute-done.11 = f32[16,38,3]{2,1,0:T(8,128)S(1)} collective-permute-done((f32[16,38,3]{2,1,0:T(8,128)S(1)}, f32[16,38,3]{2,1,0:T(8,128)S(1)}, u32[]{:S(2)}, u32[]{:S(2)}) %collective-permute-start.11) | collective-permute-done | bytes 7328 | tf_op jit(solution)/shard_map/ppermute | solution.py:28
  122.9 1.1 fusion.41
  124.4 1.1 fusion.40
  125.6 1.2 fusion.64
  (126 shorter events, 13.2 us)
Async XLA Ops:
  0.6 88.5 %copy-start = (f32[4,8,32,128]{3,2,1,0:T(8,128)S(1)}, f32[4,8,32,128]{3,2,1,0:T(8,128)}, u32[]{:S(2)}) copy-start(f32[4,8,32,128]{3,2,1,0:T(8,128)} %param.13) | copy-start | bytes 1572868
  0.6 1.9 %copy-start.1 = (bf16[3,1,32,64,256]{4,3,2,1,0:T(8,128)(2,1)S(1)}, bf16[3,1,32,64,256]{4,3,2,1,0:T(8,128)(2,1)}, u32[]{:S(2)}) copy-start(bf16[3,1,32,64,256]{4,3,2,1,0:T(8,128)(2,1)} %v_ref.1) | copy-start | bytes 9437188
  2.6 1.6 %copy-start.2 = (f32[1,32,64,256]{3,2,1,0:T(8,128)S(1)}, f32[1,32,64,256]{3,2,1,0:T(8,128)}, u32[]{:S(2)}) copy-start(f32[1,32,64,256]{3,2,1,0:T(8,128)} %param.7) | copy-start | bytes 6291460
  4.2 9.2 %copy-start.5 = (s32[8]{0:T(128)S(1)}, s32[8]{0:T(128)}, u32[]{:S(2)}) copy-start(s32[8]{0:T(128)} %param.11) | copy-start | bytes 100
  4.2 9.4 %copy-start.4 = (s32[4,2]{0,1:T(2,128)S(1)}, s32[4,2]{0,1:T(2,128)}, u32[]{:S(2)}) copy-start(s32[4,2]{0,1:T(2,128)} %param.12) | copy-start | bytes 100
  6.9 8.7 %collective-permute-start = (f32[5,64,256]{2,1,0:T(8,128)S(1)}, f32[5,64,256]{2,1,0:T(8,128)S(1)}, u32[]{:S(2)}, u32[]{:S(2)}) collective-permute-start(f32[5,64,256]{2,1,0:T(8,128)S(1)} %get-tuple-element.10), channel_id=1, source_target_pairs={{0,64},{64,128},{1,65},{65,129},{2,66},{66,130},{3,67},{67,131},{4... | collective-permute-start | bytes 983048 | tf_op jit(solution)/shard_map/ppermute | solution.py:108
  8.3 11.1 %collective-permute-start.1 = (f32[5,64,256]{2,1,0:T(8,128)S(1)}, f32[5,64,256]{2,1,0:T(8,128)S(1)}, u32[]{:S(2)}, u32[]{:S(2)}) collective-permute-start(f32[5,64,256]{2,1,0:T(8,128)S(1)} %get-tuple-element.11), channel_id=1, source_target_pairs={{64,0},{128,64},{65,1},{129,65},{66,2},{130,66},{67,3},{131,67},{6... | collective-permute-start | bytes 983048 | tf_op jit(solution)/shard_map/ppermute | solution.py:109
  19.5 13.3 %collective-permute-start.2 = (f32[36,5,256]{2,0,1:T(8,128)S(1)}, f32[36,5,256]{2,0,1:T(8,128)S(1)}, u32[]{:S(2)}, u32[]{:S(2)}) collective-permute-start(f32[36,5,256]{2,0,1:T(8,128)S(1)} %pad_maximum_fusion.7), channel_id=1, source_target_pairs={{4,0},{8,4},{12,8},{16,12},{20,16},{24,20},{28,24},{32,28},{36,32}... | collective-permute-start | bytes 552968 | tf_op jit(solution)/shard_map/ppermute | solution.py:129
  21.5 11.6 %collective-permute-start.3 = (f32[36,5,256]{2,0,1:T(8,128)S(1)}, f32[36,5,256]{2,0,1:T(8,128)S(1)}, u32[]{:S(2)}, u32[]{:S(2)}) collective-permute-start(f32[36,5,256]{2,0,1:T(8,128)S(1)} %pad_maximum_fusion.8), channel_id=1, source_target_pairs={{0,4},{4,8},{8,12},{12,16},{16,20},{20,24},{24,28},{28,32},{32,36}... | collective-permute-start | bytes 552968 | tf_op jit(solution)/shard_map/ppermute | solution.py:128
  34.5 9.6 %collective-permute-start.4 = (f32[36,68,5]{1,0,2:T(8,128)S(1)}, f32[36,68,5]{1,0,2:T(8,128)S(1)}, u32[]{:S(2)}, u32[]{:S(2)}) collective-permute-start(f32[36,68,5]{1,0,2:T(8,128)S(1)} %pad_maximum_fusion.13), channel_id=1, source_target_pairs={{1,0},{2,1},{3,2},{5,4},{6,5},{7,6},{9,8},{10,9},{11,10},{13,12},{... | collective-permute-start | bytes 146888 | tf_op jit(solution)/shard_map/ppermute | solution.py:150
  37.1 9.9 %collective-permute-start.5 = (f32[36,68,5]{1,0,2:T(8,128)S(1)}, f32[36,68,5]{1,0,2:T(8,128)S(1)}, u32[]{:S(2)}, u32[]{:S(2)}) collective-permute-start(f32[36,68,5]{1,0,2:T(8,128)S(1)} %pad_maximum_fusion.14), channel_id=1, source_target_pairs={{0,1},{1,2},{2,3},{4,5},{5,6},{6,7},{8,9},{9,10},{10,11},{12,13},{... | collective-permute-start | bytes 146888 | tf_op jit(solution)/shard_map/ppermute | solution.py:147
  83.1 1.6 %collective-permute-start.6 = (f32[8,32,128]{2,1,0:T(8,128)}, f32[8,32,128]{2,1,0:T(8,128)S(1)}, u32[]{:S(2)}, u32[]{:S(2)}) collective-permute-start(f32[8,32,128]{2,1,0:T(8,128)} %get-tuple-element.16), channel_id=1, source_target_pairs={{0,64},{64,0},{128,192},{192,128},{1,65},{65,1},{129,193},{193,129... | collective-permute-start | bytes 393224 | tf_op jit(solution)/shard_map/ppermute | solution.py:364
  85.5 7.4 %collective-permute-start.7 = (f32[8,32,128]{2,1,0:T(8,128)S(1)}, f32[8,32,128]{2,1,0:T(8,128)S(1)}, u32[]{:S(2)}, u32[]{:S(2)}) collective-permute-start(f32[8,32,128]{2,1,0:T(8,128)S(1)} %add.263), channel_id=1, source_target_pairs={{0,128},{128,0},{64,192},{192,64},{1,129},{129,1},{65,193},{193,65... | collective-permute-start | bytes 393224 | tf_op jit(solution)/shard_map/ppermute | solution.py:366
  92.9 32.6 %copy-start.3 = (f32[8,32,128]{2,1,0:T(8,128)}, f32[8,32,128]{2,1,0:T(8,128)S(1)}, u32[]{:S(2)}) copy-start(f32[8,32,128]{2,1,0:T(8,128)S(1)} %add.264) | copy-start | bytes 393220
  93.0 8.9 %collective-permute-start.8 = (f32[16,3,128]{2,1,0:T(4,128)S(1)}, f32[16,3,128]{2,1,0:T(4,128)S(1)}, u32[]{:S(2)}, u32[]{:S(2)}) collective-permute-start(f32[16,3,128]{2,1,0:T(4,128)S(1)} %get-tuple-element.49), channel_id=1, source_target_pairs={{0,4},{4,8},{8,12},{12,16},{16,20},{20,24},{24,28},{28,32},{32,36}... | collective-permute-start | bytes 73736 | tf_op jit(solution)/shard_map/ppermute | solution.py:27
  99.9 9.4 %collective-permute-start.9 = (f32[16,3,128]{2,1,0:T(4,128)S(1)}, f32[16,3,128]{2,1,0:T(4,128)S(1)}, u32[]{:S(2)}, u32[]{:S(2)}) collective-permute-start(f32[16,3,128]{2,1,0:T(4,128)S(1)} %get-tuple-element.50), channel_id=1, source_target_pairs={{4,0},{8,4},{12,8},{16,12},{20,16},{24,20},{28,24},{32,28},{36,32}... | collective-permute-start | bytes 73736 | tf_op jit(solution)/shard_map/ppermute | solution.py:28
  109.6 8.8 %collective-permute-start.10 = (f32[16,38,3]{2,1,0:T(8,128)S(1)}, f32[16,38,3]{2,1,0:T(8,128)S(1)}, u32[]{:S(2)}, u32[]{:S(2)}) collective-permute-start(f32[16,38,3]{2,1,0:T(8,128)S(1)} %get-tuple-element.31), channel_id=1, source_target_pairs={{0,1},{1,2},{2,3},{4,5},{5,6},{6,7},{8,9},{9,10},{10,11},{12,13},{... | collective-permute-start | bytes 21896 | tf_op jit(solution)/shard_map/ppermute | solution.py:27
  113.1 9.4 %collective-permute-start.11 = (f32[16,38,3]{2,1,0:T(8,128)S(1)}, f32[16,38,3]{2,1,0:T(8,128)S(1)}, u32[]{:S(2)}, u32[]{:S(2)}) collective-permute-start(f32[16,38,3]{2,1,0:T(8,128)S(1)} %get-tuple-element.32), channel_id=1, source_target_pairs={{1,0},{2,1},{3,2},{5,4},{6,5},{7,6},{9,8},{10,9},{11,10},{13,12},{... | collective-permute-start | bytes 21896 | tf_op jit(solution)/shard_map/ppermute | solution.py:28

commit v7 on v6

--- a/solution.py
+++ b/solution.py
@@ -155,13 +155,10 @@
     xu_hi = jnp.swapaxes(ax[1:-1, 2:5], 0, 1)[:, :, None]
     xu_lo = jnp.swapaxes(bx[1:-1, 2:5], 0, 1)[:, :, None]
     xu = jnp.concatenate([xu_hi, jnp.zeros((3, nz + 2, 6, ny), f32), xu_lo], 2)
-    yc = jnp.concatenate([ay[..., 0:2], jnp.zeros((nz + 4, nx + 4, 124), f32), by[..., 0:2]], 2)
-    yc = jnp.pad(yc, ((0, 0), (6, 6), (0, 0)))
-    yu_hi = jnp.moveaxis(ay[1:-1, :, 2:5], 2, 0)[..., None]
-    yu_lo = jnp.moveaxis(by[1:-1, :, 2:5], 2, 0)[..., None]
-    yu = jnp.concatenate([yu_hi, jnp.zeros((3, nz + 2, nx + 4, 126), f32), yu_lo], 3)
-    yu = jnp.pad(yu, ((0, 0), (0, 0), (6, 6), (0, 0)))
-    return zlo_c, zhi_c, zlo_u, zhi_u, xc, xu, yc, yu
+    fill = jnp.zeros((nz + 4, nx + 4, 118), f32)
+    yt = jnp.concatenate([ay[..., 0:2], ay[..., 2:5], fill, by[..., 2:5], by[..., 0:2]], 2)
+    yt = jnp.pad(yt, ((0, 0), (6, 6), (0, 0)))
+    return zlo_c, zhi_c, zlo_u, zhi_u, xc, xu, yt
 
 
 def roll(values, shift, axis):
@@ -180,7 +177,7 @@
 
 def transport_kernel(
     grid, place, weights, c_ref, v_ref, poro_ref, sat_ref, zlo_c, zhi_c, zlo_u, zhi_u,
-    xc, xu, yc, yu, adv_ref, part_ref, F, U, S, SG, H,
+    xc, xu, yt, adv_ref, part_ref, F, U, S, SG, H,
 ):
     nz, nx, ny = c_ref.shape
     wx, wy = F.shape[1], F.shape[2]
@@ -199,7 +196,8 @@
     lax.fori_loop(0, nz, put_c, 0)
     F[:, 0:8, 0:ny] = xc[...]
     F[:, wx - 8 : wx, 0:ny] = xc[...]
-    F[:, :, ny:wy] = yc[...]
+    F[:, :, ny:wy] = yt[...]
+    tile_lane = lax.broadcasted_iota(jnp.int32, (wx, wy - ny), 1)
     for d in range(3):
         U[d, 0, 8 : 8 + nx, 0:ny] = zlo_u[d]
         U[d, nz + 1, 8 : 8 + nx, 0:ny] = zhi_u[d]
@@ -211,7 +209,15 @@
         lax.fori_loop(0, nz, put_u, 0)
         U[d, :, 0:8, 0:ny] = xu[d]
         U[d, :, wx - 8 : wx, 0:ny] = xu[d]
-        U[d, :, :, ny:wy] = yu[d]
+
+        def put_y(k, carry, d=d):
+            tile = yt[k + 1]
+            low = roll(tile, -(2 + d), 1)
+            high = roll(tile, 4 - d, 1)
+            U[d, k, :, ny:wy] = jnp.where(tile_lane < (wy - ny) // 2, low, high)
+            return carry
+
+        lax.fori_loop(0, nz + 2, put_y, 0)
 
     total_z, total_x, total_y = grid
     gz0 = place[0] * nz - 1
@@ -279,7 +285,7 @@
             jax.ShapeDtypeStruct((1, nz, nx, ny), jnp.float32),
             jax.ShapeDtypeStruct((resist_layers, nx // 2, ny // 2), jnp.float32),
         ),
-        in_specs=[smem, smem] + [vmem] * 12,
+        in_specs=[smem, smem] + [vmem] * 11,
         out_specs=(vmem, vmem),
         scratch_shapes=[
             pltpu.VMEM((nz + 4, wx, wy), jnp.float32),

time: 127 us -> 125 us (0.984)
  Pallas kernels: 26.4 us -> 33.8 us
  local copies, waits for them, and re-layouts: 22.7 us -> 15.9 us
  other arithmetic: 15.3 us -> 12.7 us
    pallas_call x1, Pallas kernels: 23.6 us -> 31.1 us  [transport_call(): pl.pallas_call(functools.partial(transport_kernel, grid), out_shape=(jax....]
    broadcast_in_dim x6 -> x1, local copies, waits for them, and re-layouts: 5.78 us -> 0.01 us  [transport_halo(): fill = jnp.zeros((nz + 4, nx + 4, 118), f32)]
    concatenate x2 -> x1, other arithmetic: 4.67 us -> 2.07 us  [transport_halo(): jnp.concatenate([ay[..., 0:2], ay[..., 2:5], fill, by[..., 2:5], by[...,...]
    pad x2 -> x1, local copies, waits for them, and re-layouts: 3.71 us -> 1.23 us  [transport_halo(): yt = jnp.pad(yt, ((0, 0), (6, 6), (0, 0)))]
    ppermute x0 -> x1, local copies, waits for them, and re-layouts: none -> 1.6 us  [transport_halo(): lax.ppermute(jnp.concatenate([xz_c(slice(0, 2), ycols[2:4]), xz_u(0, ucol...]
    unnamed x16 -> x14, local copies, waits for them, and re-layouts: 3.57 us -> 3.56 us
  transfers between devices with their start and end apart: 12 -> 12, of which waited for: 6 -> 6; matrix products, arithmetic and copies ran while one was open for 12% -> 11% of each run, Pallas kernels for 0% -> 0%
where the time goes in v7:
time: 125 us
  starting transfers between devices  38.5 us (31%)
  Pallas kernels  33.8 us (27%)
  waiting for transfers between devices  22.7 us (18%)
  local copies, waits for them, and re-layouts  15.9 us (13%)
  other arithmetic  12.7 us (10%)
    pallas_call x1, Pallas kernels, transport_call(): pl.pallas_call(functools.partial(transport_kernel, grid), out_shape=(jax....  31.1 us
    ppermute x2, waiting for transfers between devices, with_halo(): after = lax.ppermute(initial, axis, down)  11.6 us
    ppermute x2, starting transfers between devices, with_halo(): before = lax.ppermute(last, axis, up)  10.5 us
    ppermute x1, starting transfers between devices, transport_halo(): bx = lax.ppermute(send_up, 'gx', up)  7.54 us
    ppermute x1, starting transfers between devices, transport_halo(): lax.ppermute(jnp.concatenate([xz_c(slice(ny - 2, ny), ycols[0:2]), xz_u(n...  4.55 us
    ppermute x1, starting transfers between devices, transport_halo(): above = lax.ppermute(zs_dn, 'grp', down)  4.29 us
    ppermute x1, waiting for transfers between devices, grp_sum(): pair = lax.ppermute(partial, 'grp', [(0, 2), (2, 0), (1, 3), (3, 1)])  3.78 us
    ppermute x1, waiting for transfers between devices, transport_halo(): above = lax.ppermute(zs_dn, 'grp', down)  3.66 us
  transfers between devices with their start and end apart: 12, of which 6 were waited for; matrix products, arithmetic and copies ran while one was open for 11% of the time, Pallas kernels for 0%

profile of v7, /device:TPU:102, one launch (start us, length us, event | category | flops | bytes accessed | tf_op | source)
XLA Modules:
  0.0 124.8 jit_solution(6770248367625920768)
XLA Ops:
  0.7 1.9 %copy-done.1 = bf16[3,1,32,64,256]{4,3,2,1,0:T(8,128)(2,1)S(1)} copy-done((bf16[3,1,32,64,256]{4,3,2,1,0:T(8,128)(2,1)S(1)}, bf16[3,1,32,64,256]{4,3,2,1,0:T(8,128)(2,1)}, u32[]{:S(2)}) %copy-start.1) | copy-done | bytes 3145752
  2.6 1.6 %copy-done.2 = f32[1,32,64,256]{3,2,1,0:T(8,128)S(1)} copy-done((f32[1,32,64,256]{3,2,1,0:T(8,128)S(1)}, f32[1,32,64,256]{3,2,1,0:T(8,128)}, u32[]{:S(2)}) %copy-start.2) | copy-done | bytes 2097176
  4.2 2.8 %shard_map.94 = (f32[5,64,256]{2,1,0:T(8,128)S(1)}, f32[5,64,256]{2,1,0:T(8,128)S(1)}, f32[10,32,256]{2,1,0:T(8,128)S(1)}, f32[8,2048]{1,0:T(8,128)S(1)}, f32[3,8,2048]{2,1,0:T(8,128)S(1)}) custom-call(f32[2048,256]{1,0:T(8,128)S(1)} %bitcast.151, bf16[3,2048,256]{2,1,0:T(8,128)(2,1)S(1)} %bitcast.149), custom_call_target="tpu_custom_call" | custom-call | flops 33554432 | bytes 5242880 | tf_op jit(solution)/shard_map/pallas_call | solution.py:78
  6.9 1.4 %collective-permute-start = (f32[5,64,256]{2,1,0:T(8,128)S(1)}, f32[5,64,256]{2,1,0:T(8,128)S(1)}, u32[]{:S(2)}, u32[]{:S(2)}) collective-permute-start(f32[5,64,256]{2,1,0:T(8,128)S(1)} %get-tuple-element.10), channel_id=1, source_target_pairs={{0,64},{64,128},{1,65},{65,129},{2,66},{66,130},{3,67},{67,131},{4... | collective-permute-start | bytes 983048 | tf_op jit(solution)/shard_map/ppermute | solution.py:108
  8.4 4.3 %collective-permute-start.1 = (f32[5,64,256]{2,1,0:T(8,128)S(1)}, f32[5,64,256]{2,1,0:T(8,128)S(1)}, u32[]{:S(2)}, u32[]{:S(2)}) collective-permute-start(f32[5,64,256]{2,1,0:T(8,128)S(1)} %get-tuple-element.11), channel_id=1, source_target_pairs={{64,0},{128,64},{65,1},{129,65},{66,2},{130,66},{67,3},{131,67},{6... | collective-permute-start | bytes 983048 | tf_op jit(solution)/shard_map/ppermute | solution.py:109
  15.8 3.7 %collective-permute-done.1 = f32[5,64,256]{2,1,0:T(8,128)S(1)} collective-permute-done((f32[5,64,256]{2,1,0:T(8,128)S(1)}, f32[5,64,256]{2,1,0:T(8,128)S(1)}, u32[]{:S(2)}, u32[]{:S(2)}) %collective-permute-start.1) | collective-permute-done | bytes 327712 | tf_op jit(solution)/shard_map/ppermute | solution.py:109
  19.5 1.9 %collective-permute-start.2 = (f32[36,5,256]{2,0,1:T(8,128)S(1)}, f32[36,5,256]{2,0,1:T(8,128)S(1)}, u32[]{:S(2)}, u32[]{:S(2)}) collective-permute-start(f32[36,5,256]{2,0,1:T(8,128)S(1)} %pad_maximum_fusion.6), channel_id=1, source_target_pairs={{4,0},{8,4},{12,8},{16,12},{20,16},{24,20},{28,24},{32,28},{36,32}... | collective-permute-start | bytes 552968 | tf_op jit(solution)/shard_map/ppermute | solution.py:129
  21.5 7.5 %collective-permute-start.3 = (f32[36,5,256]{2,0,1:T(8,128)S(1)}, f32[36,5,256]{2,0,1:T(8,128)S(1)}, u32[]{:S(2)}, u32[]{:S(2)}) collective-permute-start(f32[36,5,256]{2,0,1:T(8,128)S(1)} %pad_maximum_fusion.7), channel_id=1, source_target_pairs={{0,4},{4,8},{8,12},{12,16},{16,20},{20,24},{24,28},{28,32},{32,36}... | collective-permute-start | bytes 552968 | tf_op jit(solution)/shard_map/ppermute | solution.py:128
  30.0 0.7 slice.458.zlo_u
  30.7 0.7 slice.459.zhi_u
  34.6 1.3 %collective-permute-start.4 = (f32[36,68,5]{1,0,2:T(8,128)S(1)}, f32[36,68,5]{1,0,2:T(8,128)S(1)}, u32[]{:S(2)}, u32[]{:S(2)}) collective-permute-start(f32[36,68,5]{1,0,2:T(8,128)S(1)} %pad_maximum_fusion.12), channel_id=1, source_target_pairs={{1,0},{2,1},{3,2},{5,4},{6,5},{7,6},{9,8},{10,9},{11,10},{13,12},{... | collective-permute-start | bytes 146888 | tf_op jit(solution)/shard_map/ppermute | solution.py:150
  37.1 4.6 %collective-permute-start.5 = (f32[36,68,5]{1,0,2:T(8,128)S(1)}, f32[36,68,5]{1,0,2:T(8,128)S(1)}, u32[]{:S(2)}, u32[]{:S(2)}) collective-permute-start(f32[36,68,5]{1,0,2:T(8,128)S(1)} %pad_maximum_fusion.13), channel_id=1, source_target_pairs={{0,1},{1,2},{2,3},{4,5},{5,6},{6,7},{8,9},{9,10},{10,11},{12,13},{... | collective-permute-start | bytes 146888 | tf_op jit(solution)/shard_map/ppermute | solution.py:147
  42.0 1.1 pad_maximum_fusion.1.xu
  43.1 0.8 pad_maximum_fusion.5.xc
  45.1 1.6 %copy.160 = f32[36,68,5]{2,1,0:T(8,128)} copy(f32[36,68,5]{1,0,2:T(8,128)S(1)} %collective-permute-done.4) | data formatting | bytes 97920 | tf_op jit(solution)/shard_map/ppermute | solution.py:150
  46.7 2.1 %pad_maximum_fusion = f32[36,68,128]{2,1,0:T(8,128)S(1)} fusion(f32[36,68,2]{2,1,0:T(8,128)S(1)} %copy.162, f32[36,68,3]{2,1,0:T(8,128)S(1)} %copy.161, f32[36,68,5]{2,1,0:T(8,128)} %copy.160, f32[128]{0:T(128)S(1)} %pad.72.clone), kind=kLoop, calls=%fused_computation | loop fusion | flops 940032 | bytes 1351808 | tf_op jit(solution)/shard_map/concatenate | solution.py:159
  48.8 1.2 pad.38.yt
  50.0 31.1 %shard_map.95 = (f32[1,32,64,256]{3,2,1,0:T(8,128)}, f32[8,32,128]{2,1,0:T(8,128)}) custom-call(s32[4]{0:T(128)} %pad_add_fusion.place, f32[8,32]{1,0:T(8,128)} %convert_divide_fusion.weights, f32[32,64,256]{2,1,0:T(8,128)} %bitcast.150, bf16[3,1,32,64,256]{4,3,2,1,0:T(8,128)(2,1)} %v_ref.1, bf16[1,32,64,256]{3,2,1,0:T(8,128)(2,1)} %poro_ref.1, ...), custom_call_target="tpu_custom_call" | custom-call | flops 104857600 | bytes 20971520 | tf_op jit(solution)/shard_map/pallas_call | solution.py:282
  81.1 1.4 %subtract_multiply_fusion = f32[1,8,38,134]{3,2,1,0:T(8,128)S(1)} fusion(s32[]{:T(128)} %bitcast.32, s32[]{:T(128)} %bitcast.31, s32[134]{0:T(256)S(1)} %iota_add_fusion, s32[8,38]{1,0:T(8,128)S(1)} %broadcast_add_fusion), kind=kLoop, calls=%fused_computation.79 | loop fusion | flops 285152 | bytes 164704 | tf_op jit(solution)/shard_map/mul | solution.py:426
  82.6 0.9 add.261
  83.5 3.6 %collective-permute-start.7 = (f32[8,32,128]{2,1,0:T(8,128)S(1)}, f32[8,32,128]{2,1,0:T(8,128)S(1)}, u32[]{:S(2)}, u32[]{:S(2)}) collective-permute-start(f32[8,32,128]{2,1,0:T(8,128)S(1)} %add.261), channel_id=1, source_target_pairs={{0,128},{128,0},{64,192},{192,64},{1,129},{129,1},{65,193},{193,65... | collective-permute-start | bytes 393224 | tf_op jit(solution)/shard_map/ppermute | solution.py:372
  87.2 3.8 %collective-permute-done.7 = f32[8,32,128]{2,1,0:T(8,128)S(1)} collective-permute-done((f32[8,32,128]{2,1,0:T(8,128)S(1)}, f32[8,32,128]{2,1,0:T(8,128)S(1)}, u32[]{:S(2)}, u32[]{:S(2)}) %collective-permute-start.7) | collective-permute-done | bytes 131104 | tf_op jit(solution)/shard_map/ppermute | solution.py:372
  91.0 7.0 %collective-permute-start.8 = (f32[16,3,128]{2,1,0:T(4,128)S(1)}, f32[16,3,128]{2,1,0:T(4,128)S(1)}, u32[]{:S(2)}, u32[]{:S(2)}) collective-permute-start(f32[16,3,128]{2,1,0:T(4,128)S(1)} %get-tuple-element.49), channel_id=1, source_target_pairs={{0,4},{4,8},{8,12},{12,16},{16,20},{20,24},{24,28},{28,32},{32,36}... | collective-permute-start | bytes 73736 | tf_op jit(solution)/shard_map/ppermute | solution.py:27
  98.0 1.9 %collective-permute-start.9 = (f32[16,3,128]{2,1,0:T(4,128)S(1)}, f32[16,3,128]{2,1,0:T(4,128)S(1)}, u32[]{:S(2)}, u32[]{:S(2)}) collective-permute-start(f32[16,3,128]{2,1,0:T(4,128)S(1)} %get-tuple-element.50), channel_id=1, source_target_pairs={{4,0},{8,4},{12,8},{16,12},{20,16},{24,20},{28,24},{32,28},{36,32}... | collective-permute-start | bytes 73736 | tf_op jit(solution)/shard_map/ppermute | solution.py:28
  100.0 7.5 %collective-permute-done.9 = f32[16,3,128]{2,1,0:T(4,128)S(1)} collective-permute-done((f32[16,3,128]{2,1,0:T(4,128)S(1)}, f32[16,3,128]{2,1,0:T(4,128)S(1)}, u32[]{:S(2)}, u32[]{:S(2)}) %collective-permute-start.9) | collective-permute-done | bytes 24608 | tf_op jit(solution)/shard_map/ppermute | solution.py:28
  107.6 3.5 %collective-permute-start.10 = (f32[16,38,3]{2,1,0:T(8,128)S(1)}, f32[16,38,3]{2,1,0:T(8,128)S(1)}, u32[]{:S(2)}, u32[]{:S(2)}) collective-permute-start(f32[16,38,3]{2,1,0:T(8,128)S(1)} %get-tuple-element.31), channel_id=1, source_target_pairs={{0,1},{1,2},{2,3},{4,5},{5,6},{6,7},{8,9},{9,10},{10,11},{12,13},{... | collective-permute-start | bytes 21896 | tf_op jit(solution)/shard_map/ppermute | solution.py:27
  111.2 1.5 %collective-permute-start.11 = (f32[16,38,3]{2,1,0:T(8,128)S(1)}, f32[16,38,3]{2,1,0:T(8,128)S(1)}, u32[]{:S(2)}, u32[]{:S(2)}) collective-permute-start(f32[16,38,3]{2,1,0:T(8,128)S(1)} %get-tuple-element.32), channel_id=1, source_target_pairs={{1,0},{2,1},{3,2},{5,4},{6,5},{7,6},{9,8},{10,9},{11,10},{13,12},{... | collective-permute-start | bytes 21896 | tf_op jit(solution)/shard_map/ppermute | solution.py:28
  113.0 3.5 %collective-permute-done.10 = f32[16,38,3]{2,1,0:T(8,128)S(1)} collective-permute-done((f32[16,38,3]{2,1,0:T(8,128)S(1)}, f32[16,38,3]{2,1,0:T(8,128)S(1)}, u32[]{:S(2)}, u32[]{:S(2)}) %collective-permute-start.10) | collective-permute-done | bytes 7328 | tf_op jit(solution)/shard_map/ppermute | solution.py:27
  116.5 4.1 %collective-permute-done.11 = f32[16,38,3]{2,1,0:T(8,128)S(1)} collective-permute-done((f32[16,38,3]{2,1,0:T(8,128)S(1)}, f32[16,38,3]{2,1,0:T(8,128)S(1)}, u32[]{:S(2)}, u32[]{:S(2)}) %collective-permute-start.11) | collective-permute-done | bytes 7328 | tf_op jit(solution)/shard_map/ppermute | solution.py:28
  121.0 1.1 fusion.41
  122.5 1.1 fusion.40
  123.7 1.2 fusion.64
  (119 shorter events, 11.3 us)
Async XLA Ops:
  0.6 86.5 %copy-start = (f32[4,8,32,128]{3,2,1,0:T(8,128)S(1)}, f32[4,8,32,128]{3,2,1,0:T(8,128)}, u32[]{:S(2)}) copy-start(f32[4,8,32,128]{3,2,1,0:T(8,128)} %param.13) | copy-start | bytes 1572868
  0.6 1.9 %copy-start.1 = (bf16[3,1,32,64,256]{4,3,2,1,0:T(8,128)(2,1)S(1)}, bf16[3,1,32,64,256]{4,3,2,1,0:T(8,128)(2,1)}, u32[]{:S(2)}) copy-start(bf16[3,1,32,64,256]{4,3,2,1,0:T(8,128)(2,1)} %v_ref.1) | copy-start | bytes 9437188
  2.6 1.6 %copy-start.2 = (f32[1,32,64,256]{3,2,1,0:T(8,128)S(1)}, f32[1,32,64,256]{3,2,1,0:T(8,128)}, u32[]{:S(2)}) copy-start(f32[1,32,64,256]{3,2,1,0:T(8,128)} %param.7) | copy-start | bytes 6291460
  6.9 6.5 %copy-start.5 = (s32[8]{0:T(128)S(1)}, s32[8]{0:T(128)}, u32[]{:S(2)}) copy-start(s32[8]{0:T(128)} %param.11) | copy-start | bytes 100
  6.9 6.7 %copy-start.4 = (s32[4,2]{0,1:T(2,128)S(1)}, s32[4,2]{0,1:T(2,128)}, u32[]{:S(2)}) copy-start(s32[4,2]{0,1:T(2,128)} %param.12) | copy-start | bytes 100
  6.9 8.8 %collective-permute-start = (f32[5,64,256]{2,1,0:T(8,128)S(1)}, f32[5,64,256]{2,1,0:T(8,128)S(1)}, u32[]{:S(2)}, u32[]{:S(2)}) collective-permute-start(f32[5,64,256]{2,1,0:T(8,128)S(1)} %get-tuple-element.10), channel_id=1, source_target_pairs={{0,64},{64,128},{1,65},{65,129},{2,66},{66,130},{3,67},{67,131},{4... | collective-permute-start | bytes 983048 | tf_op jit(solution)/shard_map/ppermute | solution.py:108
  8.4 11.0 %collective-permute-start.1 = (f32[5,64,256]{2,1,0:T(8,128)S(1)}, f32[5,64,256]{2,1,0:T(8,128)S(1)}, u32[]{:S(2)}, u32[]{:S(2)}) collective-permute-start(f32[5,64,256]{2,1,0:T(8,128)S(1)} %get-tuple-element.11), channel_id=1, source_target_pairs={{64,0},{128,64},{65,1},{129,65},{66,2},{130,66},{67,3},{131,67},{6... | collective-permute-start | bytes 983048 | tf_op jit(solution)/shard_map/ppermute | solution.py:109
  19.5 13.3 %collective-permute-start.2 = (f32[36,5,256]{2,0,1:T(8,128)S(1)}, f32[36,5,256]{2,0,1:T(8,128)S(1)}, u32[]{:S(2)}, u32[]{:S(2)}) collective-permute-start(f32[36,5,256]{2,0,1:T(8,128)S(1)} %pad_maximum_fusion.6), channel_id=1, source_target_pairs={{4,0},{8,4},{12,8},{16,12},{20,16},{24,20},{28,24},{32,28},{36,32}... | collective-permute-start | bytes 552968 | tf_op jit(solution)/shard_map/ppermute | solution.py:129
  21.5 11.6 %collective-permute-start.3 = (f32[36,5,256]{2,0,1:T(8,128)S(1)}, f32[36,5,256]{2,0,1:T(8,128)S(1)}, u32[]{:S(2)}, u32[]{:S(2)}) collective-permute-start(f32[36,5,256]{2,0,1:T(8,128)S(1)} %pad_maximum_fusion.7), channel_id=1, source_target_pairs={{0,4},{4,8},{8,12},{12,16},{16,20},{20,24},{24,28},{28,32},{32,36}... | collective-permute-start | bytes 552968 | tf_op jit(solution)/shard_map/ppermute | solution.py:128
  34.6 10.5 %collective-permute-start.4 = (f32[36,68,5]{1,0,2:T(8,128)S(1)}, f32[36,68,5]{1,0,2:T(8,128)S(1)}, u32[]{:S(2)}, u32[]{:S(2)}) collective-permute-start(f32[36,68,5]{1,0,2:T(8,128)S(1)} %pad_maximum_fusion.12), channel_id=1, source_target_pairs={{1,0},{2,1},{3,2},{5,4},{6,5},{7,6},{9,8},{10,9},{11,10},{13,12},{... | collective-permute-start | bytes 146888 | tf_op jit(solution)/shard_map/ppermute | solution.py:150
  37.1 6.8 %collective-permute-start.5 = (f32[36,68,5]{1,0,2:T(8,128)S(1)}, f32[36,68,5]{1,0,2:T(8,128)S(1)}, u32[]{:S(2)}, u32[]{:S(2)}) collective-permute-start(f32[36,68,5]{1,0,2:T(8,128)S(1)} %pad_maximum_fusion.13), channel_id=1, source_target_pairs={{0,1},{1,2},{2,3},{4,5},{5,6},{6,7},{8,9},{9,10},{10,11},{12,13},{... | collective-permute-start | bytes 146888 | tf_op jit(solution)/shard_map/ppermute | solution.py:147
  81.1 1.6 %collective-permute-start.6 = (f32[8,32,128]{2,1,0:T(8,128)}, f32[8,32,128]{2,1,0:T(8,128)S(1)}, u32[]{:S(2)}, u32[]{:S(2)}) collective-permute-start(f32[8,32,128]{2,1,0:T(8,128)} %get-tuple-element.16), channel_id=1, source_target_pairs={{0,64},{64,0},{128,192},{192,128},{1,65},{65,1},{129,193},{193,129... | collective-permute-start | bytes 393224 | tf_op jit(solution)/shard_map/ppermute | solution.py:370
  83.5 7.4 %collective-permute-start.7 = (f32[8,32,128]{2,1,0:T(8,128)S(1)}, f32[8,32,128]{2,1,0:T(8,128)S(1)}, u32[]{:S(2)}, u32[]{:S(2)}) collective-permute-start(f32[8,32,128]{2,1,0:T(8,128)S(1)} %add.261), channel_id=1, source_target_pairs={{0,128},{128,0},{64,192},{192,64},{1,129},{129,1},{65,193},{193,65... | collective-permute-start | bytes 393224 | tf_op jit(solution)/shard_map/ppermute | solution.py:372
  91.0 32.7 %copy-start.3 = (f32[8,32,128]{2,1,0:T(8,128)}, f32[8,32,128]{2,1,0:T(8,128)S(1)}, u32[]{:S(2)}) copy-start(f32[8,32,128]{2,1,0:T(8,128)S(1)} %add.262) | copy-start | bytes 393220
  91.0 8.9 %collective-permute-start.8 = (f32[16,3,128]{2,1,0:T(4,128)S(1)}, f32[16,3,128]{2,1,0:T(4,128)S(1)}, u32[]{:S(2)}, u32[]{:S(2)}) collective-permute-start(f32[16,3,128]{2,1,0:T(4,128)S(1)} %get-tuple-element.49), channel_id=1, source_target_pairs={{0,4},{4,8},{8,12},{12,16},{16,20},{20,24},{24,28},{28,32},{32,36}... | collective-permute-start | bytes 73736 | tf_op jit(solution)/shard_map/ppermute | solution.py:27
  98.0 9.4 %collective-permute-start.9 = (f32[16,3,128]{2,1,0:T(4,128)S(1)}, f32[16,3,128]{2,1,0:T(4,128)S(1)}, u32[]{:S(2)}, u32[]{:S(2)}) collective-permute-start(f32[16,3,128]{2,1,0:T(4,128)S(1)} %get-tuple-element.50), channel_id=1, source_target_pairs={{4,0},{8,4},{12,8},{16,12},{20,16},{24,20},{28,24},{32,28},{36,32}... | collective-permute-start | bytes 73736 | tf_op jit(solution)/shard_map/ppermute | solution.py:28
  107.6 8.8 %collective-permute-start.10 = (f32[16,38,3]{2,1,0:T(8,128)S(1)}, f32[16,38,3]{2,1,0:T(8,128)S(1)}, u32[]{:S(2)}, u32[]{:S(2)}) collective-permute-start(f32[16,38,3]{2,1,0:T(8,128)S(1)} %get-tuple-element.31), channel_id=1, source_target_pairs={{0,1},{1,2},{2,3},{4,5},{5,6},{6,7},{8,9},{9,10},{10,11},{12,13},{... | collective-permute-start | bytes 21896 | tf_op jit(solution)/shard_map/ppermute | solution.py:27
  111.2 9.4 %collective-permute-start.11 = (f32[16,38,3]{2,1,0:T(8,128)S(1)}, f32[16,38,3]{2,1,0:T(8,128)S(1)}, u32[]{:S(2)}, u32[]{:S(2)}) collective-permute-start(f32[16,38,3]{2,1,0:T(8,128)S(1)} %get-tuple-element.32), channel_id=1, source_target_pairs={{1,0},{2,1},{3,2},{5,4},{6,5},{7,6},{9,8},{10,9},{11,10},{13,12},{... | collective-permute-start | bytes 21896 | tf_op jit(solution)/shard_map/ppermute | solution.py:28

commit v8 on v7

--- a/solution.py
+++ b/solution.py
@@ -155,8 +155,9 @@
     xu_hi = jnp.swapaxes(ax[1:-1, 2:5], 0, 1)[:, :, None]
     xu_lo = jnp.swapaxes(bx[1:-1, 2:5], 0, 1)[:, :, None]
     xu = jnp.concatenate([xu_hi, jnp.zeros((3, nz + 2, 6, ny), f32), xu_lo], 2)
+    speeds_y = jnp.stack([by[..., 2:5], ay[..., 2:5]], 3).reshape(nz + 4, nx + 4, 6)
     fill = jnp.zeros((nz + 4, nx + 4, 118), f32)
-    yt = jnp.concatenate([ay[..., 0:2], ay[..., 2:5], fill, by[..., 2:5], by[..., 0:2]], 2)
+    yt = jnp.concatenate([ay[..., 0:2], speeds_y, fill, by[..., 0:2]], 2)
     yt = jnp.pad(yt, ((0, 0), (6, 6), (0, 0)))
     return zlo_c, zhi_c, zlo_u, zhi_u, xc, xu, yt
 
@@ -197,7 +198,6 @@
     F[:, 0:8, 0:ny] = xc[...]
     F[:, wx - 8 : wx, 0:ny] = xc[...]
     F[:, :, ny:wy] = yt[...]
-    tile_lane = lax.broadcasted_iota(jnp.int32, (wx, wy - ny), 1)
     for d in range(3):
         U[d, 0, 8 : 8 + nx, 0:ny] = zlo_u[d]
         U[d, nz + 1, 8 : 8 + nx, 0:ny] = zhi_u[d]
@@ -209,15 +209,7 @@
         lax.fori_loop(0, nz, put_u, 0)
         U[d, :, 0:8, 0:ny] = xu[d]
         U[d, :, wx - 8 : wx, 0:ny] = xu[d]
-
-        def put_y(k, carry, d=d):
-            tile = yt[k + 1]
-            low = roll(tile, -(2 + d), 1)
-            high = roll(tile, 4 - d, 1)
-            U[d, k, :, ny:wy] = jnp.where(tile_lane < (wy - ny) // 2, low, high)
-            return carry
-
-        lax.fori_loop(0, nz + 2, put_y, 0)
+        U[d, :, :, ny:wy] = roll(yt[1 : nz + 3], -(3 + 2 * d), 2)
 
     total_z, total_x, total_y = grid
     gz0 = place[0] * nz - 1

time: 125 us -> 118 us (0.944)
  Pallas kernels: 33.8 us -> 26 us
    pallas_call x1, Pallas kernels: 31.1 us -> 23.2 us  [transport_call(): pl.pallas_call(functools.partial(transport_kernel, grid), out_shape=(jax....]
    ppermute x1 -> x0, local copies, waits for them, and re-layouts: 1.6 us -> none  [transport_halo(): lax.ppermute(jnp.concatenate([xz_c(slice(0, 2), ycols[2:4]), xz_u(0, ucol...]
  transfers between devices with their start and end apart: 12 -> 12, of which waited for: 6 -> 6; matrix products, arithmetic and copies ran while one was open for 11% -> 10% of each run, Pallas kernels for 0% -> 0%
where the time goes in v8:
time: 118 us; the launch traced here: 117 us
  starting transfers between devices  38.5 us (33%)
  Pallas kernels  26 us (22%)
  waiting for transfers between devices  22.7 us (19%)
  local copies, waits for them, and re-layouts  15.9 us (13%)
  other arithmetic  12.7 us (11%)
  between operations  1.23 us (1%)
    pallas_call x1, Pallas kernels, transport_call(): pl.pallas_call(functools.partial(transport_kernel, grid), out_shape=(jax....  23.2 us
    ppermute x2, waiting for transfers between devices, with_halo(): after = lax.ppermute(initial, axis, down)  11.4 us
    ppermute x2, starting transfers between devices, with_halo(): before = lax.ppermute(last, axis, up)  10.5 us
    ppermute x1, starting transfers between devices, transport_halo(): bx = lax.ppermute(send_up, 'gx', up)  7.54 us
    ppermute x1, starting transfers between devices, transport_halo(): lax.ppermute(jnp.concatenate([xz_c(slice(ny - 2, ny), ycols[0:2]), xz_u(n...  4.55 us
    ppermute x1, starting transfers between devices, transport_halo(): above = lax.ppermute(zs_dn, 'grp', down)  4.29 us
    ppermute x1, waiting for transfers between devices, grp_sum(): pair = lax.ppermute(partial, 'grp', [(0, 2), (2, 0), (1, 3), (3, 1)])  3.78 us
    ppermute x2, waiting for transfers between devices, with_halo(): before = lax.ppermute(last, axis, up)  3.68 us
  transfers between devices with their start and end apart: 12, of which 6 were waited for; matrix products, arithmetic and copies ran while one was open for 10% of the time, Pallas kernels for 0%

profile of v8, /device:TPU:102, one launch (start us, length us, event | category | flops | bytes accessed | tf_op | source)
XLA Modules:
  0.0 117.1 jit_solution(9556930872558749920)
XLA Ops:
  0.7 1.9 %copy-done.1 = bf16[3,1,32,64,256]{4,3,2,1,0:T(8,128)(2,1)S(1)} copy-done((bf16[3,1,32,64,256]{4,3,2,1,0:T(8,128)(2,1)S(1)}, bf16[3,1,32,64,256]{4,3,2,1,0:T(8,128)(2,1)}, u32[]{:S(2)}) %copy-start.1) | copy-done | bytes 3145752
  2.6 1.6 %copy-done.2 = f32[1,32,64,256]{3,2,1,0:T(8,128)S(1)} copy-done((f32[1,32,64,256]{3,2,1,0:T(8,128)S(1)}, f32[1,32,64,256]{3,2,1,0:T(8,128)}, u32[]{:S(2)}) %copy-start.2) | copy-done | bytes 2097176
  4.2 2.8 %shard_map.94 = (f32[5,64,256]{2,1,0:T(8,128)S(1)}, f32[5,64,256]{2,1,0:T(8,128)S(1)}, f32[10,32,256]{2,1,0:T(8,128)S(1)}, f32[8,2048]{1,0:T(8,128)S(1)}, f32[3,8,2048]{2,1,0:T(8,128)S(1)}) custom-call(f32[2048,256]{1,0:T(8,128)S(1)} %bitcast.156, bf16[3,2048,256]{2,1,0:T(8,128)(2,1)S(1)} %bitcast.154), custom_call_target="tpu_custom_call" | custom-call | flops 33554432 | bytes 5242880 | tf_op jit(solution)/shard_map/pallas_call | solution.py:78
  6.9 1.4 %collective-permute-start = (f32[5,64,256]{2,1,0:T(8,128)S(1)}, f32[5,64,256]{2,1,0:T(8,128)S(1)}, u32[]{:S(2)}, u32[]{:S(2)}) collective-permute-start(f32[5,64,256]{2,1,0:T(8,128)S(1)} %get-tuple-element.10), channel_id=1, source_target_pairs={{0,64},{64,128},{1,65},{65,129},{2,66},{66,130},{3,67},{67,131},{4... | collective-permute-start | bytes 983048 | tf_op jit(solution)/shard_map/ppermute | solution.py:108
  8.4 4.3 %collective-permute-start.1 = (f32[5,64,256]{2,1,0:T(8,128)S(1)}, f32[5,64,256]{2,1,0:T(8,128)S(1)}, u32[]{:S(2)}, u32[]{:S(2)}) collective-permute-start(f32[5,64,256]{2,1,0:T(8,128)S(1)} %get-tuple-element.11), channel_id=1, source_target_pairs={{64,0},{128,64},{65,1},{129,65},{66,2},{130,66},{67,3},{131,67},{6... | collective-permute-start | bytes 983048 | tf_op jit(solution)/shard_map/ppermute | solution.py:109
  15.8 3.7 %collective-permute-done.1 = f32[5,64,256]{2,1,0:T(8,128)S(1)} collective-permute-done((f32[5,64,256]{2,1,0:T(8,128)S(1)}, f32[5,64,256]{2,1,0:T(8,128)S(1)}, u32[]{:S(2)}, u32[]{:S(2)}) %collective-permute-start.1) | collective-permute-done | bytes 327712 | tf_op jit(solution)/shard_map/ppermute | solution.py:109
  19.5 1.9 %collective-permute-start.2 = (f32[36,5,256]{2,0,1:T(8,128)S(1)}, f32[36,5,256]{2,0,1:T(8,128)S(1)}, u32[]{:S(2)}, u32[]{:S(2)}) collective-permute-start(f32[36,5,256]{2,0,1:T(8,128)S(1)} %pad_maximum_fusion.6), channel_id=1, source_target_pairs={{4,0},{8,4},{12,8},{16,12},{20,16},{24,20},{28,24},{32,28},{36,32}... | collective-permute-start | bytes 552968 | tf_op jit(solution)/shard_map/ppermute | solution.py:129
  21.5 7.5 %collective-permute-start.3 = (f32[36,5,256]{2,0,1:T(8,128)S(1)}, f32[36,5,256]{2,0,1:T(8,128)S(1)}, u32[]{:S(2)}, u32[]{:S(2)}) collective-permute-start(f32[36,5,256]{2,0,1:T(8,128)S(1)} %pad_maximum_fusion.7), channel_id=1, source_target_pairs={{0,4},{4,8},{8,12},{12,16},{16,20},{20,24},{24,28},{28,32},{32,36}... | collective-permute-start | bytes 552968 | tf_op jit(solution)/shard_map/ppermute | solution.py:128
  30.0 0.7 slice.463.zlo_u
  30.7 0.7 slice.464.zhi_u
  34.6 1.3 %collective-permute-start.4 = (f32[36,68,5]{1,0,2:T(8,128)S(1)}, f32[36,68,5]{1,0,2:T(8,128)S(1)}, u32[]{:S(2)}, u32[]{:S(2)}) collective-permute-start(f32[36,68,5]{1,0,2:T(8,128)S(1)} %pad_maximum_fusion.13), channel_id=1, source_target_pairs={{1,0},{2,1},{3,2},{5,4},{6,5},{7,6},{9,8},{10,9},{11,10},{13,12},{... | collective-permute-start | bytes 146888 | tf_op jit(solution)/shard_map/ppermute | solution.py:150
  37.1 4.6 %collective-permute-start.5 = (f32[36,68,5]{1,0,2:T(8,128)S(1)}, f32[36,68,5]{1,0,2:T(8,128)S(1)}, u32[]{:S(2)}, u32[]{:S(2)}) collective-permute-start(f32[36,68,5]{1,0,2:T(8,128)S(1)} %pad_maximum_fusion.14), channel_id=1, source_target_pairs={{0,1},{1,2},{2,3},{4,5},{5,6},{6,7},{8,9},{9,10},{10,11},{12,13},{... | collective-permute-start | bytes 146888 | tf_op jit(solution)/shard_map/ppermute | solution.py:147
  42.0 1.1 pad_maximum_fusion.1.xu
  43.1 0.8 pad_maximum_fusion.5.xc
  45.1 1.6 %copy.170 = f32[36,68,2]{2,1,0:T(8,128)} copy(f32[36,68,2]{1,0,2:T(8,128)S(1)} %slice.498) | data formatting | bytes 39168 | tf_op jit(solution)/shard_map/slice | solution.py:160
  46.7 2.1 %pad_maximum_fusion = f32[36,68,128]{2,1,0:T(8,128)S(1)} fusion(f32[36,68,2]{2,1,0:T(8,128)} %copy.170, f32[36,68,6]{2,1,0:T(8,128)S(1)} %copy.169, f32[36,68,2]{2,1,0:T(8,128)S(1)} %copy.168, f32[128]{0:T(128)S(1)} %pad.73.clone), kind=kLoop, calls=%fused_computation | loop fusion | flops 940032 | bytes 1351808 | tf_op jit(solution)/shard_map/concatenate | solution.py:160
  48.8 1.2 %pad.38.yt = f32[36,80,128]{2,1,0:T(8,128)} pad(f32[36,68,128]{2,1,0:T(8,128)S(1)} %pad_maximum_fusion, f32[]{:T(128)} %constant.25.clone.1), padding=0_0x6_6x0_0 | pad | bytes 2727940 | tf_op jit(solution)/shard_map/jit(_pad)/pad | solution.py:161
  50.0 23.2 %shard_map.95 = (f32[1,32,64,256]{3,2,1,0:T(8,128)}, f32[8,32,128]{2,1,0:T(8,128)}) custom-call(s32[4]{0:T(128)} %pad_add_fusion.place, f32[8,32]{1,0:T(8,128)} %convert_divide_fusion.weights, f32[32,64,256]{2,1,0:T(8,128)} %bitcast.155, bf16[3,1,32,64,256]{4,3,2,1,0:T(8,128)(2,1)} %v_ref.1, bf16[1,32,64,256]{3,2,1,0:T(8,128)(2,1)} %poro_ref.1, ...), custom_call_target="tpu_custom_call" | custom-call | flops 104857600 | bytes 20971520 | tf_op jit(solution)/shard_map/pallas_call | solution.py:274
  73.3 1.4 %subtract_multiply_fusion = f32[1,8,38,134]{3,2,1,0:T(8,128)S(1)} fusion(s32[]{:T(128)} %bitcast.35, s32[]{:T(128)} %bitcast.34, s32[134]{0:T(256)S(1)} %iota_add_fusion, s32[8,38]{1,0:T(8,128)S(1)} %broadcast_add_fusion), kind=kLoop, calls=%fused_computation.79 | loop fusion | flops 285152 | bytes 164704 | tf_op jit(solution)/shard_map/mul | solution.py:418
  74.8 0.9 add.261
  75.8 3.6 %collective-permute-start.7 = (f32[8,32,128]{2,1,0:T(8,128)S(1)}, f32[8,32,128]{2,1,0:T(8,128)S(1)}, u32[]{:S(2)}, u32[]{:S(2)}) collective-permute-start(f32[8,32,128]{2,1,0:T(8,128)S(1)} %add.261), channel_id=1, source_target_pairs={{0,128},{128,0},{64,192},{192,64},{1,129},{129,1},{65,193},{193,65... | collective-permute-start | bytes 393224 | tf_op jit(solution)/shard_map/ppermute | solution.py:364
  79.4 3.8 %collective-permute-done.7 = f32[8,32,128]{2,1,0:T(8,128)S(1)} collective-permute-done((f32[8,32,128]{2,1,0:T(8,128)S(1)}, f32[8,32,128]{2,1,0:T(8,128)S(1)}, u32[]{:S(2)}, u32[]{:S(2)}) %collective-permute-start.7) | collective-permute-done | bytes 131104 | tf_op jit(solution)/shard_map/ppermute | solution.py:364
  83.3 7.0 %collective-permute-start.8 = (f32[16,3,128]{2,1,0:T(4,128)S(1)}, f32[16,3,128]{2,1,0:T(4,128)S(1)}, u32[]{:S(2)}, u32[]{:S(2)}) collective-permute-start(f32[16,3,128]{2,1,0:T(4,128)S(1)} %get-tuple-element.49), channel_id=1, source_target_pairs={{0,4},{4,8},{8,12},{12,16},{16,20},{20,24},{24,28},{28,32},{32,36}... | collective-permute-start | bytes 73736 | tf_op jit(solution)/shard_map/ppermute | solution.py:27
  90.3 2.1 %collective-permute-start.9 = (f32[16,3,128]{2,1,0:T(4,128)S(1)}, f32[16,3,128]{2,1,0:T(4,128)S(1)}, u32[]{:S(2)}, u32[]{:S(2)}) collective-permute-start(f32[16,3,128]{2,1,0:T(4,128)S(1)} %get-tuple-element.50), channel_id=1, source_target_pairs={{4,0},{8,4},{12,8},{16,12},{20,16},{24,20},{28,24},{32,28},{36,32}... | collective-permute-start | bytes 73736 | tf_op jit(solution)/shard_map/ppermute | solution.py:28
  92.4 7.3 %collective-permute-done.9 = f32[16,3,128]{2,1,0:T(4,128)S(1)} collective-permute-done((f32[16,3,128]{2,1,0:T(4,128)S(1)}, f32[16,3,128]{2,1,0:T(4,128)S(1)}, u32[]{:S(2)}, u32[]{:S(2)}) %collective-permute-start.9) | collective-permute-done | bytes 24608 | tf_op jit(solution)/shard_map/ppermute | solution.py:28
  99.9 3.5 %collective-permute-start.10 = (f32[16,38,3]{2,1,0:T(8,128)S(1)}, f32[16,38,3]{2,1,0:T(8,128)S(1)}, u32[]{:S(2)}, u32[]{:S(2)}) collective-permute-start(f32[16,38,3]{2,1,0:T(8,128)S(1)} %get-tuple-element.31), channel_id=1, source_target_pairs={{0,1},{1,2},{2,3},{4,5},{5,6},{6,7},{8,9},{9,10},{10,11},{12,13},{... | collective-permute-start | bytes 21896 | tf_op jit(solution)/shard_map/ppermute | solution.py:27
  103.4 1.3 %collective-permute-start.11 = (f32[16,38,3]{2,1,0:T(8,128)S(1)}, f32[16,38,3]{2,1,0:T(8,128)S(1)}, u32[]{:S(2)}, u32[]{:S(2)}) collective-permute-start(f32[16,38,3]{2,1,0:T(8,128)S(1)} %get-tuple-element.32), channel_id=1, source_target_pairs={{1,0},{2,1},{3,2},{5,4},{6,5},{7,6},{9,8},{10,9},{11,10},{13,12},{... | collective-permute-start | bytes 21896 | tf_op jit(solution)/shard_map/ppermute | solution.py:28
  105.0 3.7 %collective-permute-done.10 = f32[16,38,3]{2,1,0:T(8,128)S(1)} collective-permute-done((f32[16,38,3]{2,1,0:T(8,128)S(1)}, f32[16,38,3]{2,1,0:T(8,128)S(1)}, u32[]{:S(2)}, u32[]{:S(2)}) %collective-permute-start.10) | collective-permute-done | bytes 7328 | tf_op jit(solution)/shard_map/ppermute | solution.py:27
  108.7 4.1 %collective-permute-done.11 = f32[16,38,3]{2,1,0:T(8,128)S(1)} collective-permute-done((f32[16,38,3]{2,1,0:T(8,128)S(1)}, f32[16,38,3]{2,1,0:T(8,128)S(1)}, u32[]{:S(2)}, u32[]{:S(2)}) %collective-permute-start.11) | collective-permute-done | bytes 7328 | tf_op jit(solution)/shard_map/ppermute | solution.py:28
  113.3 1.1 fusion.41
  114.7 1.1 fusion.40
  115.9 1.2 %fusion.64 = f32[1,8,32,128]{3,2,1,0:T(8,128)} fusion(f32[1,8,34,130]{3,2,1,0:T(8,128)S(1)} %fusion.40, f32[8,32,128]{2,1,0:T(8,128)S(1)} %add.262, f32[16,38,3]{2,1,0:T(8,128)S(1)} %collective-permute-done.11, f32[16,3,128]{2,1,0:T(4,128)S(1)} %collective-permute-done.9, f32[8,32,128]{2,1,0:T(8,128)S(1)} %dynamic-slice_bitcast_fusion, ...), kind=kLoop, calls=%fused_computation.121 | loop fusion | flops 1540096 | bytes 2560000 | tf_op jit(solution)/shard_map/jit(_where)/select_n | solution.py:463
  (122 shorter events, 11.3 us)
Async XLA Ops:
  0.6 78.8 %copy-start = (f32[4,8,32,128]{3,2,1,0:T(8,128)S(1)}, f32[4,8,32,128]{3,2,1,0:T(8,128)}, u32[]{:S(2)}) copy-start(f32[4,8,32,128]{3,2,1,0:T(8,128)} %param.13) | copy-start | bytes 1572868
  0.6 1.9 %copy-start.1 = (bf16[3,1,32,64,256]{4,3,2,1,0:T(8,128)(2,1)S(1)}, bf16[3,1,32,64,256]{4,3,2,1,0:T(8,128)(2,1)}, u32[]{:S(2)}) copy-start(bf16[3,1,32,64,256]{4,3,2,1,0:T(8,128)(2,1)} %v_ref.1) | copy-start | bytes 9437188
  2.6 1.6 %copy-start.2 = (f32[1,32,64,256]{3,2,1,0:T(8,128)S(1)}, f32[1,32,64,256]{3,2,1,0:T(8,128)}, u32[]{:S(2)}) copy-start(f32[1,32,64,256]{3,2,1,0:T(8,128)} %param.7) | copy-start | bytes 6291460
  6.9 6.5 %copy-start.5 = (s32[8]{0:T(128)S(1)}, s32[8]{0:T(128)}, u32[]{:S(2)}) copy-start(s32[8]{0:T(128)} %param.11) | copy-start | bytes 100
  6.9 6.7 %copy-start.4 = (s32[4,2]{0,1:T(2,128)S(1)}, s32[4,2]{0,1:T(2,128)}, u32[]{:S(2)}) copy-start(s32[4,2]{0,1:T(2,128)} %param.12) | copy-start | bytes 100
  6.9 8.8 %collective-permute-start = (f32[5,64,256]{2,1,0:T(8,128)S(1)}, f32[5,64,256]{2,1,0:T(8,128)S(1)}, u32[]{:S(2)}, u32[]{:S(2)}) collective-permute-start(f32[5,64,256]{2,1,0:T(8,128)S(1)} %get-tuple-element.10), channel_id=1, source_target_pairs={{0,64},{64,128},{1,65},{65,129},{2,66},{66,130},{3,67},{67,131},{4... | collective-permute-start | bytes 983048 | tf_op jit(solution)/shard_map/ppermute | solution.py:108
  8.4 11.0 %collective-permute-start.1 = (f32[5,64,256]{2,1,0:T(8,128)S(1)}, f32[5,64,256]{2,1,0:T(8,128)S(1)}, u32[]{:S(2)}, u32[]{:S(2)}) collective-permute-start(f32[5,64,256]{2,1,0:T(8,128)S(1)} %get-tuple-element.11), channel_id=1, source_target_pairs={{64,0},{128,64},{65,1},{129,65},{66,2},{130,66},{67,3},{131,67},{6... | collective-permute-start | bytes 983048 | tf_op jit(solution)/shard_map/ppermute | solution.py:109
  19.5 13.3 %collective-permute-start.2 = (f32[36,5,256]{2,0,1:T(8,128)S(1)}, f32[36,5,256]{2,0,1:T(8,128)S(1)}, u32[]{:S(2)}, u32[]{:S(2)}) collective-permute-start(f32[36,5,256]{2,0,1:T(8,128)S(1)} %pad_maximum_fusion.6), channel_id=1, source_target_pairs={{4,0},{8,4},{12,8},{16,12},{20,16},{24,20},{28,24},{32,28},{36,32}... | collective-permute-start | bytes 552968 | tf_op jit(solution)/shard_map/ppermute | solution.py:129
  21.5 11.6 %collective-permute-start.3 = (f32[36,5,256]{2,0,1:T(8,128)S(1)}, f32[36,5,256]{2,0,1:T(8,128)S(1)}, u32[]{:S(2)}, u32[]{:S(2)}) collective-permute-start(f32[36,5,256]{2,0,1:T(8,128)S(1)} %pad_maximum_fusion.7), channel_id=1, source_target_pairs={{0,4},{4,8},{8,12},{12,16},{16,20},{20,24},{24,28},{28,32},{32,36}... | collective-permute-start | bytes 552968 | tf_op jit(solution)/shard_map/ppermute | solution.py:128
  34.6 9.3 %collective-permute-start.4 = (f32[36,68,5]{1,0,2:T(8,128)S(1)}, f32[36,68,5]{1,0,2:T(8,128)S(1)}, u32[]{:S(2)}, u32[]{:S(2)}) collective-permute-start(f32[36,68,5]{1,0,2:T(8,128)S(1)} %pad_maximum_fusion.13), channel_id=1, source_target_pairs={{1,0},{2,1},{3,2},{5,4},{6,5},{7,6},{9,8},{10,9},{11,10},{13,12},{... | collective-permute-start | bytes 146888 | tf_op jit(solution)/shard_map/ppermute | solution.py:150
  37.1 6.8 %collective-permute-start.5 = (f32[36,68,5]{1,0,2:T(8,128)S(1)}, f32[36,68,5]{1,0,2:T(8,128)S(1)}, u32[]{:S(2)}, u32[]{:S(2)}) collective-permute-start(f32[36,68,5]{1,0,2:T(8,128)S(1)} %pad_maximum_fusion.14), channel_id=1, source_target_pairs={{0,1},{1,2},{2,3},{4,5},{5,6},{6,7},{8,9},{9,10},{10,11},{12,13},{... | collective-permute-start | bytes 146888 | tf_op jit(solution)/shard_map/ppermute | solution.py:147
  73.3 1.6 %collective-permute-start.6 = (f32[8,32,128]{2,1,0:T(8,128)}, f32[8,32,128]{2,1,0:T(8,128)S(1)}, u32[]{:S(2)}, u32[]{:S(2)}) collective-permute-start(f32[8,32,128]{2,1,0:T(8,128)} %get-tuple-element.16), channel_id=1, source_target_pairs={{0,64},{64,0},{128,192},{192,128},{1,65},{65,1},{129,193},{193,129... | collective-permute-start | bytes 393224 | tf_op jit(solution)/shard_map/ppermute | solution.py:362
  75.8 7.4 %collective-permute-start.7 = (f32[8,32,128]{2,1,0:T(8,128)S(1)}, f32[8,32,128]{2,1,0:T(8,128)S(1)}, u32[]{:S(2)}, u32[]{:S(2)}) collective-permute-start(f32[8,32,128]{2,1,0:T(8,128)S(1)} %add.261), channel_id=1, source_target_pairs={{0,128},{128,0},{64,192},{192,64},{1,129},{129,1},{65,193},{193,65... | collective-permute-start | bytes 393224 | tf_op jit(solution)/shard_map/ppermute | solution.py:364
  83.2 32.7 %copy-start.3 = (f32[8,32,128]{2,1,0:T(8,128)}, f32[8,32,128]{2,1,0:T(8,128)S(1)}, u32[]{:S(2)}) copy-start(f32[8,32,128]{2,1,0:T(8,128)S(1)} %add.262) | copy-start | bytes 393220
  83.3 9.1 %collective-permute-start.8 = (f32[16,3,128]{2,1,0:T(4,128)S(1)}, f32[16,3,128]{2,1,0:T(4,128)S(1)}, u32[]{:S(2)}, u32[]{:S(2)}) collective-permute-start(f32[16,3,128]{2,1,0:T(4,128)S(1)} %get-tuple-element.49), channel_id=1, source_target_pairs={{0,4},{4,8},{8,12},{12,16},{16,20},{20,24},{24,28},{28,32},{32,36}... | collective-permute-start | bytes 73736 | tf_op jit(solution)/shard_map/ppermute | solution.py:27
  90.3 9.4 %collective-permute-start.9 = (f32[16,3,128]{2,1,0:T(4,128)S(1)}, f32[16,3,128]{2,1,0:T(4,128)S(1)}, u32[]{:S(2)}, u32[]{:S(2)}) collective-permute-start(f32[16,3,128]{2,1,0:T(4,128)S(1)} %get-tuple-element.50), channel_id=1, source_target_pairs={{4,0},{8,4},{12,8},{16,12},{20,16},{24,20},{28,24},{32,28},{36,32}... | collective-permute-start | bytes 73736 | tf_op jit(solution)/shard_map/ppermute | solution.py:28
  99.9 8.8 %collective-permute-start.10 = (f32[16,38,3]{2,1,0:T(8,128)S(1)}, f32[16,38,3]{2,1,0:T(8,128)S(1)}, u32[]{:S(2)}, u32[]{:S(2)}) collective-permute-start(f32[16,38,3]{2,1,0:T(8,128)S(1)} %get-tuple-element.31), channel_id=1, source_target_pairs={{0,1},{1,2},{2,3},{4,5},{5,6},{6,7},{8,9},{9,10},{10,11},{12,13},{... | collective-permute-start | bytes 21896 | tf_op jit(solution)/shard_map/ppermute | solution.py:27
  103.4 9.4 %collective-permute-start.11 = (f32[16,38,3]{2,1,0:T(8,128)S(1)}, f32[16,38,3]{2,1,0:T(8,128)S(1)}, u32[]{:S(2)}, u32[]{:S(2)}) collective-permute-start(f32[16,38,3]{2,1,0:T(8,128)S(1)} %get-tuple-element.32), channel_id=1, source_target_pairs={{1,0},{2,1},{3,2},{5,4},{6,5},{7,6},{9,8},{10,9},{11,10},{13,12},{... | collective-permute-start | bytes 21896 | tf_op jit(solution)/shard_map/ppermute | solution.py:28

commit v9 on v8

--- a/solution.py
+++ b/solution.py
@@ -24,8 +24,12 @@
         down = [(j, i) for i, j in up]
         last = lax.slice_in_dim(shard, length - width, length, axis=dim)
         initial = lax.slice_in_dim(shard, 0, width, axis=dim)
-        before = lax.ppermute(last, axis, up)
-        after = lax.ppermute(initial, axis, down)
+        if dim == shard.ndim - 1:
+            before = jnp.swapaxes(lax.ppermute(jnp.swapaxes(last, -1, -2), axis, up), -1, -2)
+            after = jnp.swapaxes(lax.ppermute(jnp.swapaxes(initial, -1, -2), axis, down), -1, -2)
+        else:
+            before = lax.ppermute(last, axis, up)
+            after = lax.ppermute(initial, axis, down)
         shard = jnp.concatenate([before, shard, after], axis=dim)
     return shard
 
@@ -159,7 +163,7 @@
     fill = jnp.zeros((nz + 4, nx + 4, 118), f32)
     yt = jnp.concatenate([ay[..., 0:2], speeds_y, fill, by[..., 0:2]], 2)
     yt = jnp.pad(yt, ((0, 0), (6, 6), (0, 0)))
-    return zlo_c, zhi_c, zlo_u, zhi_u, xc, xu, yt
+    return below, above, xc, xu, yt
 
 
 def roll(values, shift, axis):
@@ -177,7 +181,7 @@
 
 
 def transport_kernel(
-    grid, place, weights, c_ref, v_ref, poro_ref, sat_ref, zlo_c, zhi_c, zlo_u, zhi_u,
+    grid, place, weights, c_ref, v_ref, poro_ref, sat_ref, z_below, z_above,
     xc, xu, yt, adv_ref, part_ref, F, U, S, SG, H,
 ):
     nz, nx, ny = c_ref.shape
@@ -187,8 +191,8 @@
         lax.broadcasted_iota(jnp.int32, (ny, ny // 2), 0) // 2
         == lax.broadcasted_iota(jnp.int32, (ny, ny // 2), 1)
     ).astype(f32)
-    F[0:2, 8 : 8 + nx, 0:ny] = zlo_c[...]
-    F[nz + 2 : nz + 4, 8 : 8 + nx, 0:ny] = zhi_c[...]
+    F[0:2, 8 : 8 + nx, 0:ny] = z_below[0:2]
+    F[nz + 2 : nz + 4, 8 : 8 + nx, 0:ny] = z_above[0:2]
 
     def put_c(z, carry):
         F[z + 2, 8 : 8 + nx, 0:ny] = c_ref[z]
@@ -199,8 +203,8 @@
     F[:, wx - 8 : wx, 0:ny] = xc[...]
     F[:, :, ny:wy] = yt[...]
     for d in range(3):
-        U[d, 0, 8 : 8 + nx, 0:ny] = zlo_u[d]
-        U[d, nz + 1, 8 : 8 + nx, 0:ny] = zhi_u[d]
+        U[d, 0, 8 : 8 + nx, 0:ny] = z_below[2 + d]
+        U[d, nz + 1, 8 : 8 + nx, 0:ny] = z_above[2 + d]
 
         def put_u(z, carry, d=d):
             U[d, z + 1, 8 : 8 + nx, 0:ny] = v_ref[d, 0, z].astype(f32)
@@ -277,7 +281,7 @@
             jax.ShapeDtypeStruct((1, nz, nx, ny), jnp.float32),
             jax.ShapeDtypeStruct((resist_layers, nx // 2, ny // 2), jnp.float32),
         ),
-        in_specs=[smem, smem] + [vmem] * 11,
+        in_specs=[smem, smem] + [vmem] * 9,
         out_specs=(vmem, vmem),
         scratch_shapes=[
             pltpu.VMEM((nz + 4, wx, wy), jnp.float32),

time: 118 us -> 119 us (level)
  waiting for transfers between devices: 22.7 us -> 28.8 us
  local copies, waits for them, and re-layouts: 15.9 us -> 13.1 us
  starting transfers between devices: 38.5 us -> 36.8 us
    ppermute x0 -> x2, waiting for transfers between devices: none -> 7.56 us  [the longest x1 4.13 us: with_halo(): lax.ppermute(jnp.swapaxes(initial, -1, -2), axis, down)]
    ppermute x0 -> x2, starting transfers between devices: none -> 5.56 us  [the longest x1 4.27 us: with_halo(): lax.ppermute(jnp.swapaxes(last, -1, -2), axis, up)]
    ppermute x2 -> x1, waiting for transfers between devices: 11.4 us -> 7.29 us  [with_halo(): after = lax.ppermute(initial, axis, down)]
    ppermute x2 -> x1, waiting for transfers between devices: 3.68 us -> 0.01 us  [with_halo(): before = lax.ppermute(last, axis, up)]
    ppermute x2 -> x1, starting transfers between devices: 10.5 us -> 7.45 us  [with_halo(): before = lax.ppermute(last, axis, up)]
    ppermute x1, starting transfers between devices: 3.63 us -> 0.65 us  [grp_sum(): pair = lax.ppermute(partial, 'grp', [(0, 2), (2, 0), (1, 3), (3, 1)])]
    slice x5 -> x0, local copies, waits for them, and re-layouts: 2.89 us -> none  [the longest x2 1.37 us: transport_halo(): zlo_c, zlo_u = (below[:2], below[2:])]
    ppermute x1, waiting for transfers between devices: 3.66 us -> 6.08 us  [transport_halo(): above = lax.ppermute(zs_dn, 'grp', down)]
  transfers between devices with their start and end apart: 12 -> 12, of which waited for: 6 -> 8; matrix products, arithmetic and copies ran while one was open for 10% -> 8% of each run, Pallas kernels for 0% -> 0%
where the time goes in v9:
time: 119 us; the launch traced here: 118 us
  starting transfers between devices  36.8 us (31%)
  waiting for transfers between devices  28.8 us (24%)
  Pallas kernels  26 us (22%)
  local copies, waits for them, and re-layouts  13.1 us (11%)
  other arithmetic  12.5 us (11%)
  between operations  1.25 us (1%)
    pallas_call x1, Pallas kernels, transport_call(): pl.pallas_call(functools.partial(transport_kernel, grid), out_shape=(jax....  23.3 us
    ppermute x1, starting transfers between devices, transport_halo(): bx = lax.ppermute(send_up, 'gx', up)  7.54 us
    ppermute x1, starting transfers between devices, with_halo(): before = lax.ppermute(last, axis, up)  7.45 us
    ppermute x1, waiting for transfers between devices, with_halo(): after = lax.ppermute(initial, axis, down)  7.29 us
    ppermute x1, waiting for transfers between devices, transport_halo(): above = lax.ppermute(zs_dn, 'grp', down)  6.08 us
    ppermute x1, waiting for transfers between devices, grp_sum(): pair = lax.ppermute(partial, 'grp', [(0, 2), (2, 0), (1, 3), (3, 1)])  5.02 us
    ppermute x1, starting transfers between devices, transport_halo(): lax.ppermute(jnp.concatenate([xz_c(slice(ny - 2, ny), ycols[0:2]), xz_u(n...  4.55 us
    ppermute x1, starting transfers between devices, transport_halo(): above = lax.ppermute(zs_dn, 'grp', down)  4.29 us
  transfers between devices with their start and end apart: 12, of which 8 were waited for; matrix products, arithmetic and copies ran while one was open for 8% of the time, Pallas kernels for 0%

profile of v9, /device:TPU:102, one launch (start us, length us, event | category | flops | bytes accessed | tf_op | source)
XLA Modules:
  0.0 118.4 jit_solution(2941149391969018565)
XLA Ops:
  0.7 1.9 %copy-done.1 = bf16[3,1,32,64,256]{4,3,2,1,0:T(8,128)(2,1)S(1)} copy-done((bf16[3,1,32,64,256]{4,3,2,1,0:T(8,128)(2,1)S(1)}, bf16[3,1,32,64,256]{4,3,2,1,0:T(8,128)(2,1)}, u32[]{:S(2)}) %copy-start.1) | copy-done | bytes 3145752
  2.6 1.6 %copy-done.2 = f32[1,32,64,256]{3,2,1,0:T(8,128)S(1)} copy-done((f32[1,32,64,256]{3,2,1,0:T(8,128)S(1)}, f32[1,32,64,256]{3,2,1,0:T(8,128)}, u32[]{:S(2)}) %copy-start.2) | copy-done | bytes 2097176
  4.2 2.8 %shard_map.94 = (f32[5,64,256]{2,1,0:T(8,128)S(1)}, f32[5,64,256]{2,1,0:T(8,128)S(1)}, f32[10,32,256]{2,1,0:T(8,128)S(1)}, f32[8,2048]{1,0:T(8,128)S(1)}, f32[3,8,2048]{2,1,0:T(8,128)S(1)}) custom-call(f32[2048,256]{1,0:T(8,128)S(1)} %bitcast.162, bf16[3,2048,256]{2,1,0:T(8,128)(2,1)S(1)} %bitcast.160), custom_call_target="tpu_custom_call" | custom-call | flops 33554432 | bytes 5242880 | tf_op jit(solution)/shard_map/pallas_call | solution.py:82
  6.9 1.4 %collective-permute-start = (f32[5,64,256]{2,1,0:T(8,128)S(1)}, f32[5,64,256]{2,1,0:T(8,128)S(1)}, u32[]{:S(2)}, u32[]{:S(2)}) collective-permute-start(f32[5,64,256]{2,1,0:T(8,128)S(1)} %get-tuple-element.10), channel_id=1, source_target_pairs={{0,64},{64,128},{1,65},{65,129},{2,66},{66,130},{3,67},{67,131},{4... | collective-permute-start | bytes 983048 | tf_op jit(solution)/shard_map/ppermute | solution.py:112
  8.4 4.3 %collective-permute-start.1 = (f32[5,64,256]{2,1,0:T(8,128)S(1)}, f32[5,64,256]{2,1,0:T(8,128)S(1)}, u32[]{:S(2)}, u32[]{:S(2)}) collective-permute-start(f32[5,64,256]{2,1,0:T(8,128)S(1)} %get-tuple-element.11), channel_id=1, source_target_pairs={{64,0},{128,64},{65,1},{129,65},{66,2},{130,66},{67,3},{131,67},{6... | collective-permute-start | bytes 983048 | tf_op jit(solution)/shard_map/ppermute | solution.py:113
  14.2 0.7 convert_divide_fusion.weights
  15.6 6.1 %collective-permute-done.1.z_above = f32[5,64,256]{2,1,0:T(8,128)S(1)} collective-permute-done((f32[5,64,256]{2,1,0:T(8,128)S(1)}, f32[5,64,256]{2,1,0:T(8,128)S(1)}, u32[]{:S(2)}, u32[]{:S(2)}) %collective-permute-start.1) | collective-permute-done | bytes 327712 | tf_op jit(solution)/shard_map/ppermute | solution.py:113
  21.8 1.9 %collective-permute-start.2 = (f32[36,5,256]{2,0,1:T(8,128)S(1)}, f32[36,5,256]{2,0,1:T(8,128)S(1)}, u32[]{:S(2)}, u32[]{:S(2)}) collective-permute-start(f32[36,5,256]{2,0,1:T(8,128)S(1)} %pad_maximum_fusion.6), channel_id=1, source_target_pairs={{4,0},{8,4},{12,8},{16,12},{20,16},{24,20},{28,24},{32,28},{36,32}... | collective-permute-start | bytes 552968 | tf_op jit(solution)/shard_map/ppermute | solution.py:133
  23.8 7.5 %collective-permute-start.3 = (f32[36,5,256]{2,0,1:T(8,128)S(1)}, f32[36,5,256]{2,0,1:T(8,128)S(1)}, u32[]{:S(2)}, u32[]{:S(2)}) collective-permute-start(f32[36,5,256]{2,0,1:T(8,128)S(1)} %pad_maximum_fusion.7), channel_id=1, source_target_pairs={{0,4},{4,8},{8,12},{12,16},{16,20},{20,24},{24,28},{28,32},{32,36}... | collective-permute-start | bytes 552968 | tf_op jit(solution)/shard_map/ppermute | solution.py:132
  32.3 0.8 collective-permute-done.2
  33.4 1.7 %collective-permute-done.3 = f32[36,5,256]{2,0,1:T(8,128)S(1)} collective-permute-done((f32[36,5,256]{2,0,1:T(8,128)S(1)}, f32[36,5,256]{2,0,1:T(8,128)S(1)}, u32[]{:S(2)}, u32[]{:S(2)}) %collective-permute-start.3) | collective-permute-done | bytes 184352 | tf_op jit(solution)/shard_map/ppermute | solution.py:132
  36.6 1.3 %collective-permute-start.4 = (f32[36,68,5]{1,0,2:T(8,128)S(1)}, f32[36,68,5]{1,0,2:T(8,128)S(1)}, u32[]{:S(2)}, u32[]{:S(2)}) collective-permute-start(f32[36,68,5]{1,0,2:T(8,128)S(1)} %pad_maximum_fusion.13), channel_id=1, source_target_pairs={{1,0},{2,1},{3,2},{5,4},{6,5},{7,6},{9,8},{10,9},{11,10},{13,12},{... | collective-permute-start | bytes 146888 | tf_op jit(solution)/shard_map/ppermute | solution.py:154
  39.1 4.6 %collective-permute-start.5 = (f32[36,68,5]{1,0,2:T(8,128)S(1)}, f32[36,68,5]{1,0,2:T(8,128)S(1)}, u32[]{:S(2)}, u32[]{:S(2)}) collective-permute-start(f32[36,68,5]{1,0,2:T(8,128)S(1)} %pad_maximum_fusion.14), channel_id=1, source_target_pairs={{0,1},{1,2},{2,3},{4,5},{5,6},{6,7},{8,9},{9,10},{10,11},{12,13},{... | collective-permute-start | bytes 146888 | tf_op jit(solution)/shard_map/ppermute | solution.py:151
  44.0 1.1 pad_maximum_fusion.1.xu
  45.1 0.8 pad_maximum_fusion.5.xc
  47.2 1.6 %copy.166 = f32[36,68,2]{2,1,0:T(8,128)} copy(f32[36,68,2]{1,0,2:T(8,128)S(1)} %slice.482) | data formatting | bytes 39168 | tf_op jit(solution)/shard_map/slice | solution.py:164
  48.8 2.1 %pad_maximum_fusion = f32[36,68,128]{2,1,0:T(8,128)S(1)} fusion(f32[36,68,2]{2,1,0:T(8,128)} %copy.166, f32[36,68,6]{2,1,0:T(8,128)S(1)} %copy.165, f32[36,68,2]{2,1,0:T(8,128)S(1)} %copy.164, f32[128]{0:T(128)S(1)} %pad.73.clone), kind=kLoop, calls=%fused_computation | loop fusion | flops 940032 | bytes 1351808 | tf_op jit(solution)/shard_map/concatenate | solution.py:164
  50.9 1.2 %pad.38.yt = f32[36,80,128]{2,1,0:T(8,128)} pad(f32[36,68,128]{2,1,0:T(8,128)S(1)} %pad_maximum_fusion, f32[]{:T(128)} %constant.25.clone.1), padding=0_0x6_6x0_0 | pad | bytes 2727940 | tf_op jit(solution)/shard_map/jit(_pad)/pad | solution.py:165
  52.1 23.3 %shard_map.95 = (f32[1,32,64,256]{3,2,1,0:T(8,128)}, f32[8,32,128]{2,1,0:T(8,128)}) custom-call(s32[4]{0:T(128)} %pad_add_fusion.place, f32[8,32]{1,0:T(8,128)} %convert_divide_fusion.weights, f32[32,64,256]{2,1,0:T(8,128)} %bitcast.161, bf16[3,1,32,64,256]{4,3,2,1,0:T(8,128)(2,1)} %v_ref.1, bf16[1,32,64,256]{3,2,1,0:T(8,128)(2,1)} %poro_ref.1, ...), custom_call_target="tpu_custom_call" | custom-call | flops 104857600 | bytes 20971520 | tf_op jit(solution)/shard_map/pallas_call | solution.py:278
  75.4 1.2 %subtract_multiply_fusion = f32[1,8,38,134]{3,2,1,0:T(8,128)S(1)} fusion(s32[]{:T(128)} %bitcast.39, s32[]{:T(128)} %bitcast.38, s32[134]{0:T(256)S(1)} %iota_add_fusion, s32[8,38]{1,0:T(8,128)S(1)} %broadcast_add_fusion), kind=kLoop, calls=%fused_computation.81 | loop fusion | flops 285152 | bytes 164704 | tf_op jit(solution)/shard_map/mul | solution.py:422
  76.9 0.9 add.261
  78.5 5.0 %collective-permute-done.7 = f32[8,32,128]{2,1,0:T(8,128)S(1)} collective-permute-done((f32[8,32,128]{2,1,0:T(8,128)S(1)}, f32[8,32,128]{2,1,0:T(8,128)S(1)}, u32[]{:S(2)}, u32[]{:S(2)}) %collective-permute-start.7) | collective-permute-done | bytes 131104 | tf_op jit(solution)/shard_map/ppermute | solution.py:368
  83.6 7.5 %collective-permute-start.8 = (f32[16,3,128]{2,1,0:T(4,128)S(1)}, f32[16,3,128]{2,1,0:T(4,128)S(1)}, u32[]{:S(2)}, u32[]{:S(2)}) collective-permute-start(f32[16,3,128]{2,1,0:T(4,128)S(1)} %get-tuple-element.49), channel_id=1, source_target_pairs={{0,4},{4,8},{8,12},{12,16},{16,20},{20,24},{24,28},{28,32},{32,36}... | collective-permute-start | bytes 73736 | tf_op jit(solution)/shard_map/ppermute | solution.py:31
  91.1 2.1 %collective-permute-start.9 = (f32[16,3,128]{2,1,0:T(4,128)S(1)}, f32[16,3,128]{2,1,0:T(4,128)S(1)}, u32[]{:S(2)}, u32[]{:S(2)}) collective-permute-start(f32[16,3,128]{2,1,0:T(4,128)S(1)} %get-tuple-element.50), channel_id=1, source_target_pairs={{4,0},{8,4},{12,8},{16,12},{20,16},{24,20},{28,24},{32,28},{36,32}... | collective-permute-start | bytes 73736 | tf_op jit(solution)/shard_map/ppermute | solution.py:32
  93.2 7.3 %collective-permute-done.9 = f32[16,3,128]{2,1,0:T(4,128)S(1)} collective-permute-done((f32[16,3,128]{2,1,0:T(4,128)S(1)}, f32[16,3,128]{2,1,0:T(4,128)S(1)}, u32[]{:S(2)}, u32[]{:S(2)}) %collective-permute-start.9) | collective-permute-done | bytes 24608 | tf_op jit(solution)/shard_map/ppermute | solution.py:32
  100.7 4.3 %collective-permute-start.10 = (f32[16,3,38]{1,2,0:T(8,128)S(1)}, f32[16,3,38]{1,2,0:T(8,128)S(1)}, u32[]{:S(2)}, u32[]{:S(2)}) collective-permute-start(f32[16,3,38]{1,2,0:T(8,128)S(1)} %get-tuple-element.31), channel_id=1, source_target_pairs={{0,1},{1,2},{2,3},{4,5},{5,6},{6,7},{8,9},{9,10},{10,11},{12,13},{... | collective-permute-start | bytes 21896 | tf_op jit(solution)/shard_map/ppermute | solution.py:28
  105.0 1.3 %collective-permute-start.11 = (f32[16,3,38]{1,2,0:T(8,128)S(1)}, f32[16,3,38]{1,2,0:T(8,128)S(1)}, u32[]{:S(2)}, u32[]{:S(2)}) collective-permute-start(f32[16,3,38]{1,2,0:T(8,128)S(1)} %get-tuple-element.32), channel_id=1, source_target_pairs={{1,0},{2,1},{3,2},{5,4},{6,5},{7,6},{9,8},{10,9},{11,10},{13,12},{... | collective-permute-start | bytes 21896 | tf_op jit(solution)/shard_map/ppermute | solution.py:29
  106.6 3.4 %collective-permute-done.10 = f32[16,3,38]{1,2,0:T(8,128)S(1)} collective-permute-done((f32[16,3,38]{1,2,0:T(8,128)S(1)}, f32[16,3,38]{1,2,0:T(8,128)S(1)}, u32[]{:S(2)}, u32[]{:S(2)}) %collective-permute-start.10) | collective-permute-done | bytes 7328 | tf_op jit(solution)/shard_map/ppermute | solution.py:28
  110.1 4.1 %collective-permute-done.11 = f32[16,3,38]{1,2,0:T(8,128)S(1)} collective-permute-done((f32[16,3,38]{1,2,0:T(8,128)S(1)}, f32[16,3,38]{1,2,0:T(8,128)S(1)}, u32[]{:S(2)}, u32[]{:S(2)}) %collective-permute-start.11) | collective-permute-done | bytes 7328 | tf_op jit(solution)/shard_map/ppermute | solution.py:29
  114.6 1.1 fusion.41
  116.1 1.1 fusion.40
  117.3 1.2 fusion.64
  (122 shorter events, 9.9 us)
Async XLA Ops:
  0.6 77.9 %copy-start = (f32[4,8,32,128]{3,2,1,0:T(8,128)S(1)}, f32[4,8,32,128]{3,2,1,0:T(8,128)}, u32[]{:S(2)}) copy-start(f32[4,8,32,128]{3,2,1,0:T(8,128)} %param.13) | copy-start | bytes 1572868
  0.6 1.9 %copy-start.1 = (bf16[3,1,32,64,256]{4,3,2,1,0:T(8,128)(2,1)S(1)}, bf16[3,1,32,64,256]{4,3,2,1,0:T(8,128)(2,1)}, u32[]{:S(2)}) copy-start(bf16[3,1,32,64,256]{4,3,2,1,0:T(8,128)(2,1)} %v_ref.1) | copy-start | bytes 9437188
  2.6 1.6 %copy-start.2 = (f32[1,32,64,256]{3,2,1,0:T(8,128)S(1)}, f32[1,32,64,256]{3,2,1,0:T(8,128)}, u32[]{:S(2)}) copy-start(f32[1,32,64,256]{3,2,1,0:T(8,128)} %param.7) | copy-start | bytes 6291460
  6.9 6.5 %copy-start.7 = (s32[8]{0:T(128)S(1)}, s32[8]{0:T(128)}, u32[]{:S(2)}) copy-start(s32[8]{0:T(128)} %param.11) | copy-start | bytes 100
  6.9 6.7 %copy-start.6 = (s32[4,2]{0,1:T(2,128)S(1)}, s32[4,2]{0,1:T(2,128)}, u32[]{:S(2)}) copy-start(s32[4,2]{0,1:T(2,128)} %param.12) | copy-start | bytes 100
  6.9 8.6 %collective-permute-start = (f32[5,64,256]{2,1,0:T(8,128)S(1)}, f32[5,64,256]{2,1,0:T(8,128)S(1)}, u32[]{:S(2)}, u32[]{:S(2)}) collective-permute-start(f32[5,64,256]{2,1,0:T(8,128)S(1)} %get-tuple-element.10), channel_id=1, source_target_pairs={{0,64},{64,128},{1,65},{65,129},{2,66},{66,130},{3,67},{67,131},{4... | collective-permute-start | bytes 983048 | tf_op jit(solution)/shard_map/ppermute | solution.py:112
  8.4 13.3 %collective-permute-start.1 = (f32[5,64,256]{2,1,0:T(8,128)S(1)}, f32[5,64,256]{2,1,0:T(8,128)S(1)}, u32[]{:S(2)}, u32[]{:S(2)}) collective-permute-start(f32[5,64,256]{2,1,0:T(8,128)S(1)} %get-tuple-element.11), channel_id=1, source_target_pairs={{64,0},{128,64},{65,1},{129,65},{66,2},{130,66},{67,3},{131,67},{6... | collective-permute-start | bytes 983048 | tf_op jit(solution)/shard_map/ppermute | solution.py:113
  15.6 16.7 %copy-start.4 = (f32[5,64,256]{2,1,0:T(8,128)}, f32[5,64,256]{2,1,0:T(8,128)S(1)}, u32[]{:S(2)}) copy-start(f32[5,64,256]{2,1,0:T(8,128)S(1)} %collective-permute-done.z_below) | copy-start | bytes 983044
  21.7 10.7 %copy-start.5 = (f32[5,64,256]{2,1,0:T(8,128)}, f32[5,64,256]{2,1,0:T(8,128)S(1)}, u32[]{:S(2)}) copy-start(f32[5,64,256]{2,1,0:T(8,128)S(1)} %collective-permute-done.1.z_above) | copy-start | bytes 983044
  21.8 11.4 %collective-permute-start.2 = (f32[36,5,256]{2,0,1:T(8,128)S(1)}, f32[36,5,256]{2,0,1:T(8,128)S(1)}, u32[]{:S(2)}, u32[]{:S(2)}) collective-permute-start(f32[36,5,256]{2,0,1:T(8,128)S(1)} %pad_maximum_fusion.6), channel_id=1, source_target_pairs={{4,0},{8,4},{12,8},{16,12},{20,16},{24,20},{28,24},{32,28},{36,32}... | collective-permute-start | bytes 552968 | tf_op jit(solution)/shard_map/ppermute | solution.py:133
  23.8 11.3 %collective-permute-start.3 = (f32[36,5,256]{2,0,1:T(8,128)S(1)}, f32[36,5,256]{2,0,1:T(8,128)S(1)}, u32[]{:S(2)}, u32[]{:S(2)}) collective-permute-start(f32[36,5,256]{2,0,1:T(8,128)S(1)} %pad_maximum_fusion.7), channel_id=1, source_target_pairs={{0,4},{4,8},{8,12},{12,16},{16,20},{20,24},{24,28},{28,32},{32,36}... | collective-permute-start | bytes 552968 | tf_op jit(solution)/shard_map/ppermute | solution.py:132
  36.6 9.4 %collective-permute-start.4 = (f32[36,68,5]{1,0,2:T(8,128)S(1)}, f32[36,68,5]{1,0,2:T(8,128)S(1)}, u32[]{:S(2)}, u32[]{:S(2)}) collective-permute-start(f32[36,68,5]{1,0,2:T(8,128)S(1)} %pad_maximum_fusion.13), channel_id=1, source_target_pairs={{1,0},{2,1},{3,2},{5,4},{6,5},{7,6},{9,8},{10,9},{11,10},{13,12},{... | collective-permute-start | bytes 146888 | tf_op jit(solution)/shard_map/ppermute | solution.py:154
  39.1 6.8 %collective-permute-start.5 = (f32[36,68,5]{1,0,2:T(8,128)S(1)}, f32[36,68,5]{1,0,2:T(8,128)S(1)}, u32[]{:S(2)}, u32[]{:S(2)}) collective-permute-start(f32[36,68,5]{1,0,2:T(8,128)S(1)} %pad_maximum_fusion.14), channel_id=1, source_target_pairs={{0,1},{1,2},{2,3},{4,5},{5,6},{6,7},{8,9},{9,10},{10,11},{12,13},{... | collective-permute-start | bytes 146888 | tf_op jit(solution)/shard_map/ppermute | solution.py:151
  75.4 1.6 %collective-permute-start.6 = (f32[8,32,128]{2,1,0:T(8,128)}, f32[8,32,128]{2,1,0:T(8,128)S(1)}, u32[]{:S(2)}, u32[]{:S(2)}) collective-permute-start(f32[8,32,128]{2,1,0:T(8,128)} %get-tuple-element.16), channel_id=1, source_target_pairs={{0,64},{64,0},{128,192},{192,128},{1,65},{65,1},{129,193},{193,129... | collective-permute-start | bytes 393224 | tf_op jit(solution)/shard_map/ppermute | solution.py:366
  77.9 5.7 %collective-permute-start.7 = (f32[8,32,128]{2,1,0:T(8,128)S(1)}, f32[8,32,128]{2,1,0:T(8,128)S(1)}, u32[]{:S(2)}, u32[]{:S(2)}) collective-permute-start(f32[8,32,128]{2,1,0:T(8,128)S(1)} %add.261), channel_id=1, source_target_pairs={{0,128},{128,0},{64,192},{192,64},{1,129},{129,1},{65,193},{193,65... | collective-permute-start | bytes 393224 | tf_op jit(solution)/shard_map/ppermute | solution.py:368
  83.6 33.7 %copy-start.3 = (f32[8,32,128]{2,1,0:T(8,128)}, f32[8,32,128]{2,1,0:T(8,128)S(1)}, u32[]{:S(2)}) copy-start(f32[8,32,128]{2,1,0:T(8,128)S(1)} %add.262) | copy-start | bytes 393220
  83.6 9.6 %collective-permute-start.8 = (f32[16,3,128]{2,1,0:T(4,128)S(1)}, f32[16,3,128]{2,1,0:T(4,128)S(1)}, u32[]{:S(2)}, u32[]{:S(2)}) collective-permute-start(f32[16,3,128]{2,1,0:T(4,128)S(1)} %get-tuple-element.49), channel_id=1, source_target_pairs={{0,4},{4,8},{8,12},{12,16},{16,20},{20,24},{24,28},{28,32},{32,36}... | collective-permute-start | bytes 73736 | tf_op jit(solution)/shard_map/ppermute | solution.py:31
  91.1 9.4 %collective-permute-start.9 = (f32[16,3,128]{2,1,0:T(4,128)S(1)}, f32[16,3,128]{2,1,0:T(4,128)S(1)}, u32[]{:S(2)}, u32[]{:S(2)}) collective-permute-start(f32[16,3,128]{2,1,0:T(4,128)S(1)} %get-tuple-element.50), channel_id=1, source_target_pairs={{4,0},{8,4},{12,8},{16,12},{20,16},{24,20},{28,24},{32,28},{36,32}... | collective-permute-start | bytes 73736 | tf_op jit(solution)/shard_map/ppermute | solution.py:32
  100.7 9.3 %collective-permute-start.10 = (f32[16,3,38]{1,2,0:T(8,128)S(1)}, f32[16,3,38]{1,2,0:T(8,128)S(1)}, u32[]{:S(2)}, u32[]{:S(2)}) collective-permute-start(f32[16,3,38]{1,2,0:T(8,128)S(1)} %get-tuple-element.31), channel_id=1, source_target_pairs={{0,1},{1,2},{2,3},{4,5},{5,6},{6,7},{8,9},{9,10},{10,11},{12,13},{... | collective-permute-start | bytes 21896 | tf_op jit(solution)/shard_map/ppermute | solution.py:28
  105.0 9.2 %collective-permute-start.11 = (f32[16,3,38]{1,2,0:T(8,128)S(1)}, f32[16,3,38]{1,2,0:T(8,128)S(1)}, u32[]{:S(2)}, u32[]{:S(2)}) collective-permute-start(f32[16,3,38]{1,2,0:T(8,128)S(1)} %get-tuple-element.32), channel_id=1, source_target_pairs={{1,0},{2,1},{3,2},{5,4},{6,5},{7,6},{9,8},{10,9},{11,10},{13,12},{... | collective-permute-start | bytes 21896 | tf_op jit(solution)/shard_map/ppermute | solution.py:29

commit v10 on v9

--- a/solution.py
+++ b/solution.py
@@ -24,12 +24,8 @@
         down = [(j, i) for i, j in up]
         last = lax.slice_in_dim(shard, length - width, length, axis=dim)
         initial = lax.slice_in_dim(shard, 0, width, axis=dim)
-        if dim == shard.ndim - 1:
-            before = jnp.swapaxes(lax.ppermute(jnp.swapaxes(last, -1, -2), axis, up), -1, -2)
-            after = jnp.swapaxes(lax.ppermute(jnp.swapaxes(initial, -1, -2), axis, down), -1, -2)
-        else:
-            before = lax.ppermute(last, axis, up)
-            after = lax.ppermute(initial, axis, down)
+        before = lax.ppermute(last, axis, up)
+        after = lax.ppermute(initial, axis, down)
         shard = jnp.concatenate([before, shard, after], axis=dim)
     return shard
 

time: 119 us -> 119 us (level)
    ppermute x2 -> x0, waiting for transfers between devices: 7.56 us -> none  [the longest x1 4.13 us: with_halo(): lax.ppermute(jnp.swapaxes(initial, -1, -2), axis, down)]
    ppermute x2 -> x0, starting transfers between devices: 5.56 us -> none  [the longest x1 4.27 us: with_halo(): lax.ppermute(jnp.swapaxes(last, -1, -2), axis, up)]
    ppermute x1 -> x2, starting transfers between devices: 7.45 us -> 11.7 us  [with_halo(): before = lax.ppermute(last, axis, up)]
    ppermute x1 -> x2, waiting for transfers between devices: 7.29 us -> 11.4 us  [with_halo(): after = lax.ppermute(initial, axis, down)]
    ppermute x1 -> x2, waiting for transfers between devices: 0.01 us -> 3.43 us  [with_halo(): before = lax.ppermute(last, axis, up)]
    ppermute x1 -> x2, starting transfers between devices: 2.1 us -> 3.39 us  [with_halo(): after = lax.ppermute(initial, axis, down)]
where the time goes in v10:
time: 119 us; the launch traced here: 118 us
  starting transfers between devices  36.8 us (31%)
  waiting for transfers between devices  28.8 us (24%)
  Pallas kernels  26 us (22%)
  local copies, waits for them, and re-layouts  13.1 us (11%)
  other arithmetic  12.5 us (11%)
  between operations  1.25 us (1%)
    pallas_call x1, Pallas kernels, transport_call(): pl.pallas_call(functools.partial(transport_kernel, grid), out_shape=(jax....  23.3 us
    ppermute x2, starting transfers between devices, with_halo(): before = lax.ppermute(last, axis, up)  11.7 us
    ppermute x2, waiting for transfers between devices, with_halo(): after = lax.ppermute(initial, axis, down)  11.4 us
    ppermute x1, starting transfers between devices, transport_halo(): bx = lax.ppermute(send_up, 'gx', up)  7.54 us
    ppermute x1, waiting for transfers between devices, transport_halo(): above = lax.ppermute(zs_dn, 'grp', down)  6.08 us
    ppermute x1, waiting for transfers between devices, grp_sum(): pair = lax.ppermute(partial, 'grp', [(0, 2), (2, 0), (1, 3), (3, 1)])  5.02 us
    ppermute x1, starting transfers between devices, transport_halo(): lax.ppermute(jnp.concatenate([xz_c(slice(ny - 2, ny), ycols[0:2]), xz_u(n...  4.55 us
    ppermute x1, starting transfers between devices, transport_halo(): above = lax.ppermute(zs_dn, 'grp', down)  4.29 us
  transfers between devices with their start and end apart: 12, of which 8 were waited for; matrix products, arithmetic and copies ran while one was open for 8% of the time, Pallas kernels for 0%

profile of v10, /device:TPU:102, one launch (start us, length us, event | category | flops | bytes accessed | tf_op | source)
XLA Modules:
  0.0 118.4 jit_solution(8180506016994298139)
XLA Ops:
  0.7 1.9 %copy-done.1 = bf16[3,1,32,64,256]{4,3,2,1,0:T(8,128)(2,1)S(1)} copy-done((bf16[3,1,32,64,256]{4,3,2,1,0:T(8,128)(2,1)S(1)}, bf16[3,1,32,64,256]{4,3,2,1,0:T(8,128)(2,1)}, u32[]{:S(2)}) %copy-start.1) | copy-done | bytes 3145752
  2.6 1.6 %copy-done.2 = f32[1,32,64,256]{3,2,1,0:T(8,128)S(1)} copy-done((f32[1,32,64,256]{3,2,1,0:T(8,128)S(1)}, f32[1,32,64,256]{3,2,1,0:T(8,128)}, u32[]{:S(2)}) %copy-start.2) | copy-done | bytes 2097176
  4.2 2.8 %shard_map.94 = (f32[5,64,256]{2,1,0:T(8,128)S(1)}, f32[5,64,256]{2,1,0:T(8,128)S(1)}, f32[10,32,256]{2,1,0:T(8,128)S(1)}, f32[8,2048]{1,0:T(8,128)S(1)}, f32[3,8,2048]{2,1,0:T(8,128)S(1)}) custom-call(f32[2048,256]{1,0:T(8,128)S(1)} %bitcast.156, bf16[3,2048,256]{2,1,0:T(8,128)(2,1)S(1)} %bitcast.154), custom_call_target="tpu_custom_call" | custom-call | flops 33554432 | bytes 5242880 | tf_op jit(solution)/shard_map/pallas_call | solution.py:78
  6.9 1.4 %collective-permute-start = (f32[5,64,256]{2,1,0:T(8,128)S(1)}, f32[5,64,256]{2,1,0:T(8,128)S(1)}, u32[]{:S(2)}, u32[]{:S(2)}) collective-permute-start(f32[5,64,256]{2,1,0:T(8,128)S(1)} %get-tuple-element.10), channel_id=1, source_target_pairs={{0,64},{64,128},{1,65},{65,129},{2,66},{66,130},{3,67},{67,131},{4... | collective-permute-start | bytes 983048 | tf_op jit(solution)/shard_map/ppermute | solution.py:108
  8.4 4.3 %collective-permute-start.1 = (f32[5,64,256]{2,1,0:T(8,128)S(1)}, f32[5,64,256]{2,1,0:T(8,128)S(1)}, u32[]{:S(2)}, u32[]{:S(2)}) collective-permute-start(f32[5,64,256]{2,1,0:T(8,128)S(1)} %get-tuple-element.11), channel_id=1, source_target_pairs={{64,0},{128,64},{65,1},{129,65},{66,2},{130,66},{67,3},{131,67},{6... | collective-permute-start | bytes 983048 | tf_op jit(solution)/shard_map/ppermute | solution.py:109
  14.2 0.7 convert_divide_fusion.weights
  15.6 6.1 %collective-permute-done.1.z_above = f32[5,64,256]{2,1,0:T(8,128)S(1)} collective-permute-done((f32[5,64,256]{2,1,0:T(8,128)S(1)}, f32[5,64,256]{2,1,0:T(8,128)S(1)}, u32[]{:S(2)}, u32[]{:S(2)}) %collective-permute-start.1) | collective-permute-done | bytes 327712 | tf_op jit(solution)/shard_map/ppermute | solution.py:109
  21.8 1.9 %collective-permute-start.2 = (f32[36,5,256]{2,0,1:T(8,128)S(1)}, f32[36,5,256]{2,0,1:T(8,128)S(1)}, u32[]{:S(2)}, u32[]{:S(2)}) collective-permute-start(f32[36,5,256]{2,0,1:T(8,128)S(1)} %pad_maximum_fusion.6), channel_id=1, source_target_pairs={{4,0},{8,4},{12,8},{16,12},{20,16},{24,20},{28,24},{32,28},{36,32}... | collective-permute-start | bytes 552968 | tf_op jit(solution)/shard_map/ppermute | solution.py:129
  23.8 7.5 %collective-permute-start.3 = (f32[36,5,256]{2,0,1:T(8,128)S(1)}, f32[36,5,256]{2,0,1:T(8,128)S(1)}, u32[]{:S(2)}, u32[]{:S(2)}) collective-permute-start(f32[36,5,256]{2,0,1:T(8,128)S(1)} %pad_maximum_fusion.7), channel_id=1, source_target_pairs={{0,4},{4,8},{8,12},{12,16},{16,20},{20,24},{24,28},{28,32},{32,36}... | collective-permute-start | bytes 552968 | tf_op jit(solution)/shard_map/ppermute | solution.py:128
  32.3 0.8 collective-permute-done.2
  33.4 1.7 %collective-permute-done.3 = f32[36,5,256]{2,0,1:T(8,128)S(1)} collective-permute-done((f32[36,5,256]{2,0,1:T(8,128)S(1)}, f32[36,5,256]{2,0,1:T(8,128)S(1)}, u32[]{:S(2)}, u32[]{:S(2)}) %collective-permute-start.3) | collective-permute-done | bytes 184352 | tf_op jit(solution)/shard_map/ppermute | solution.py:128
  36.6 1.3 %collective-permute-start.4 = (f32[36,68,5]{1,0,2:T(8,128)S(1)}, f32[36,68,5]{1,0,2:T(8,128)S(1)}, u32[]{:S(2)}, u32[]{:S(2)}) collective-permute-start(f32[36,68,5]{1,0,2:T(8,128)S(1)} %pad_maximum_fusion.13), channel_id=1, source_target_pairs={{1,0},{2,1},{3,2},{5,4},{6,5},{7,6},{9,8},{10,9},{11,10},{13,12},{... | collective-permute-start | bytes 146888 | tf_op jit(solution)/shard_map/ppermute | solution.py:150
  39.1 4.6 %collective-permute-start.5 = (f32[36,68,5]{1,0,2:T(8,128)S(1)}, f32[36,68,5]{1,0,2:T(8,128)S(1)}, u32[]{:S(2)}, u32[]{:S(2)}) collective-permute-start(f32[36,68,5]{1,0,2:T(8,128)S(1)} %pad_maximum_fusion.14), channel_id=1, source_target_pairs={{0,1},{1,2},{2,3},{4,5},{5,6},{6,7},{8,9},{9,10},{10,11},{12,13},{... | collective-permute-start | bytes 146888 | tf_op jit(solution)/shard_map/ppermute | solution.py:147
  44.0 1.1 pad_maximum_fusion.1.xu
  45.1 0.8 pad_maximum_fusion.5.xc
  47.2 1.6 %copy.166 = f32[36,68,2]{2,1,0:T(8,128)} copy(f32[36,68,2]{1,0,2:T(8,128)S(1)} %slice.482) | data formatting | bytes 39168 | tf_op jit(solution)/shard_map/slice | solution.py:160
  48.8 2.1 %pad_maximum_fusion = f32[36,68,128]{2,1,0:T(8,128)S(1)} fusion(f32[36,68,2]{2,1,0:T(8,128)} %copy.166, f32[36,68,6]{2,1,0:T(8,128)S(1)} %copy.165, f32[36,68,2]{2,1,0:T(8,128)S(1)} %copy.164, f32[128]{0:T(128)S(1)} %pad.73.clone), kind=kLoop, calls=%fused_computation | loop fusion | flops 940032 | bytes 1351808 | tf_op jit(solution)/shard_map/concatenate | solution.py:160
  50.9 1.2 %pad.38.yt = f32[36,80,128]{2,1,0:T(8,128)} pad(f32[36,68,128]{2,1,0:T(8,128)S(1)} %pad_maximum_fusion, f32[]{:T(128)} %constant.25.clone.1), padding=0_0x6_6x0_0 | pad | bytes 2727940 | tf_op jit(solution)/shard_map/jit(_pad)/pad | solution.py:161
  52.1 23.3 %shard_map.95 = (f32[1,32,64,256]{3,2,1,0:T(8,128)}, f32[8,32,128]{2,1,0:T(8,128)}) custom-call(s32[4]{0:T(128)} %pad_add_fusion.place, f32[8,32]{1,0:T(8,128)} %convert_divide_fusion.weights, f32[32,64,256]{2,1,0:T(8,128)} %bitcast.155, bf16[3,1,32,64,256]{4,3,2,1,0:T(8,128)(2,1)} %v_ref.1, bf16[1,32,64,256]{3,2,1,0:T(8,128)(2,1)} %poro_ref.1, ...), custom_call_target="tpu_custom_call" | custom-call | flops 104857600 | bytes 20971520 | tf_op jit(solution)/shard_map/pallas_call | solution.py:274
  75.4 1.2 %subtract_multiply_fusion = f32[1,8,38,134]{3,2,1,0:T(8,128)S(1)} fusion(s32[]{:T(128)} %bitcast.35, s32[]{:T(128)} %bitcast.34, s32[134]{0:T(256)S(1)} %iota_add_fusion, s32[8,38]{1,0:T(8,128)S(1)} %broadcast_add_fusion), kind=kLoop, calls=%fused_computation.79 | loop fusion | flops 285152 | bytes 164704 | tf_op jit(solution)/shard_map/mul | solution.py:418
  76.9 0.9 add.261
  78.5 5.0 %collective-permute-done.7 = f32[8,32,128]{2,1,0:T(8,128)S(1)} collective-permute-done((f32[8,32,128]{2,1,0:T(8,128)S(1)}, f32[8,32,128]{2,1,0:T(8,128)S(1)}, u32[]{:S(2)}, u32[]{:S(2)}) %collective-permute-start.7) | collective-permute-done | bytes 131104 | tf_op jit(solution)/shard_map/ppermute | solution.py:364
  83.6 7.5 %collective-permute-start.8 = (f32[16,3,128]{2,1,0:T(4,128)S(1)}, f32[16,3,128]{2,1,0:T(4,128)S(1)}, u32[]{:S(2)}, u32[]{:S(2)}) collective-permute-start(f32[16,3,128]{2,1,0:T(4,128)S(1)} %get-tuple-element.49), channel_id=1, source_target_pairs={{0,4},{4,8},{8,12},{12,16},{16,20},{20,24},{24,28},{28,32},{32,36}... | collective-permute-start | bytes 73736 | tf_op jit(solution)/shard_map/ppermute | solution.py:27
  91.1 2.1 %collective-permute-start.9 = (f32[16,3,128]{2,1,0:T(4,128)S(1)}, f32[16,3,128]{2,1,0:T(4,128)S(1)}, u32[]{:S(2)}, u32[]{:S(2)}) collective-permute-start(f32[16,3,128]{2,1,0:T(4,128)S(1)} %get-tuple-element.50), channel_id=1, source_target_pairs={{4,0},{8,4},{12,8},{16,12},{20,16},{24,20},{28,24},{32,28},{36,32}... | collective-permute-start | bytes 73736 | tf_op jit(solution)/shard_map/ppermute | solution.py:28
  93.2 7.3 %collective-permute-done.9 = f32[16,3,128]{2,1,0:T(4,128)S(1)} collective-permute-done((f32[16,3,128]{2,1,0:T(4,128)S(1)}, f32[16,3,128]{2,1,0:T(4,128)S(1)}, u32[]{:S(2)}, u32[]{:S(2)}) %collective-permute-start.9) | collective-permute-done | bytes 24608 | tf_op jit(solution)/shard_map/ppermute | solution.py:28
  100.7 4.3 %collective-permute-start.10 = (f32[16,38,3]{2,1,0:T(8,128)S(1)}, f32[16,38,3]{2,1,0:T(8,128)S(1)}, u32[]{:S(2)}, u32[]{:S(2)}) collective-permute-start(f32[16,38,3]{2,1,0:T(8,128)S(1)} %get-tuple-element.31), channel_id=1, source_target_pairs={{0,1},{1,2},{2,3},{4,5},{5,6},{6,7},{8,9},{9,10},{10,11},{12,13},{... | collective-permute-start | bytes 21896 | tf_op jit(solution)/shard_map/ppermute | solution.py:27
  105.0 1.3 %collective-permute-start.11 = (f32[16,38,3]{2,1,0:T(8,128)S(1)}, f32[16,38,3]{2,1,0:T(8,128)S(1)}, u32[]{:S(2)}, u32[]{:S(2)}) collective-permute-start(f32[16,38,3]{2,1,0:T(8,128)S(1)} %get-tuple-element.32), channel_id=1, source_target_pairs={{1,0},{2,1},{3,2},{5,4},{6,5},{7,6},{9,8},{10,9},{11,10},{13,12},{... | collective-permute-start | bytes 21896 | tf_op jit(solution)/shard_map/ppermute | solution.py:28
  106.6 3.4 %collective-permute-done.10 = f32[16,38,3]{2,1,0:T(8,128)S(1)} collective-permute-done((f32[16,38,3]{2,1,0:T(8,128)S(1)}, f32[16,38,3]{2,1,0:T(8,128)S(1)}, u32[]{:S(2)}, u32[]{:S(2)}) %collective-permute-start.10) | collective-permute-done | bytes 7328 | tf_op jit(solution)/shard_map/ppermute | solution.py:27
  110.1 4.1 %collective-permute-done.11 = f32[16,38,3]{2,1,0:T(8,128)S(1)} collective-permute-done((f32[16,38,3]{2,1,0:T(8,128)S(1)}, f32[16,38,3]{2,1,0:T(8,128)S(1)}, u32[]{:S(2)}, u32[]{:S(2)}) %collective-permute-start.11) | collective-permute-done | bytes 7328 | tf_op jit(solution)/shard_map/ppermute | solution.py:28
  114.6 1.1 fusion.41
  116.1 1.1 fusion.40
  117.3 1.2 fusion.64
  (122 shorter events, 9.9 us)
Async XLA Ops:
  0.6 77.9 %copy-start = (f32[4,8,32,128]{3,2,1,0:T(8,128)S(1)}, f32[4,8,32,128]{3,2,1,0:T(8,128)}, u32[]{:S(2)}) copy-start(f32[4,8,32,128]{3,2,1,0:T(8,128)} %param.13) | copy-start | bytes 1572868
  0.6 1.9 %copy-start.1 = (bf16[3,1,32,64,256]{4,3,2,1,0:T(8,128)(2,1)S(1)}, bf16[3,1,32,64,256]{4,3,2,1,0:T(8,128)(2,1)}, u32[]{:S(2)}) copy-start(bf16[3,1,32,64,256]{4,3,2,1,0:T(8,128)(2,1)} %v_ref.1) | copy-start | bytes 9437188
  2.6 1.6 %copy-start.2 = (f32[1,32,64,256]{3,2,1,0:T(8,128)S(1)}, f32[1,32,64,256]{3,2,1,0:T(8,128)}, u32[]{:S(2)}) copy-start(f32[1,32,64,256]{3,2,1,0:T(8,128)} %param.7) | copy-start | bytes 6291460
  6.9 6.5 %copy-start.7 = (s32[8]{0:T(128)S(1)}, s32[8]{0:T(128)}, u32[]{:S(2)}) copy-start(s32[8]{0:T(128)} %param.11) | copy-start | bytes 100
  6.9 6.7 %copy-start.6 = (s32[4,2]{0,1:T(2,128)S(1)}, s32[4,2]{0,1:T(2,128)}, u32[]{:S(2)}) copy-start(s32[4,2]{0,1:T(2,128)} %param.12) | copy-start | bytes 100
  6.9 8.6 %collective-permute-start = (f32[5,64,256]{2,1,0:T(8,128)S(1)}, f32[5,64,256]{2,1,0:T(8,128)S(1)}, u32[]{:S(2)}, u32[]{:S(2)}) collective-permute-start(f32[5,64,256]{2,1,0:T(8,128)S(1)} %get-tuple-element.10), channel_id=1, source_target_pairs={{0,64},{64,128},{1,65},{65,129},{2,66},{66,130},{3,67},{67,131},{4... | collective-permute-start | bytes 983048 | tf_op jit(solution)/shard_map/ppermute | solution.py:108
  8.4 13.3 %collective-permute-start.1 = (f32[5,64,256]{2,1,0:T(8,128)S(1)}, f32[5,64,256]{2,1,0:T(8,128)S(1)}, u32[]{:S(2)}, u32[]{:S(2)}) collective-permute-start(f32[5,64,256]{2,1,0:T(8,128)S(1)} %get-tuple-element.11), channel_id=1, source_target_pairs={{64,0},{128,64},{65,1},{129,65},{66,2},{130,66},{67,3},{131,67},{6... | collective-permute-start | bytes 983048 | tf_op jit(solution)/shard_map/ppermute | solution.py:109
  15.6 16.7 %copy-start.4 = (f32[5,64,256]{2,1,0:T(8,128)}, f32[5,64,256]{2,1,0:T(8,128)S(1)}, u32[]{:S(2)}) copy-start(f32[5,64,256]{2,1,0:T(8,128)S(1)} %collective-permute-done.z_below) | copy-start | bytes 983044
  21.7 10.7 %copy-start.5 = (f32[5,64,256]{2,1,0:T(8,128)}, f32[5,64,256]{2,1,0:T(8,128)S(1)}, u32[]{:S(2)}) copy-start(f32[5,64,256]{2,1,0:T(8,128)S(1)} %collective-permute-done.1.z_above) | copy-start | bytes 983044
  21.8 11.4 %collective-permute-start.2 = (f32[36,5,256]{2,0,1:T(8,128)S(1)}, f32[36,5,256]{2,0,1:T(8,128)S(1)}, u32[]{:S(2)}, u32[]{:S(2)}) collective-permute-start(f32[36,5,256]{2,0,1:T(8,128)S(1)} %pad_maximum_fusion.6), channel_id=1, source_target_pairs={{4,0},{8,4},{12,8},{16,12},{20,16},{24,20},{28,24},{32,28},{36,32}... | collective-permute-start | bytes 552968 | tf_op jit(solution)/shard_map/ppermute | solution.py:129
  23.8 11.3 %collective-permute-start.3 = (f32[36,5,256]{2,0,1:T(8,128)S(1)}, f32[36,5,256]{2,0,1:T(8,128)S(1)}, u32[]{:S(2)}, u32[]{:S(2)}) collective-permute-start(f32[36,5,256]{2,0,1:T(8,128)S(1)} %pad_maximum_fusion.7), channel_id=1, source_target_pairs={{0,4},{4,8},{8,12},{12,16},{16,20},{20,24},{24,28},{28,32},{32,36}... | collective-permute-start | bytes 552968 | tf_op jit(solution)/shard_map/ppermute | solution.py:128
  36.6 9.4 %collective-permute-start.4 = (f32[36,68,5]{1,0,2:T(8,128)S(1)}, f32[36,68,5]{1,0,2:T(8,128)S(1)}, u32[]{:S(2)}, u32[]{:S(2)}) collective-permute-start(f32[36,68,5]{1,0,2:T(8,128)S(1)} %pad_maximum_fusion.13), channel_id=1, source_target_pairs={{1,0},{2,1},{3,2},{5,4},{6,5},{7,6},{9,8},{10,9},{11,10},{13,12},{... | collective-permute-start | bytes 146888 | tf_op jit(solution)/shard_map/ppermute | solution.py:150
  39.1 6.8 %collective-permute-start.5 = (f32[36,68,5]{1,0,2:T(8,128)S(1)}, f32[36,68,5]{1,0,2:T(8,128)S(1)}, u32[]{:S(2)}, u32[]{:S(2)}) collective-permute-start(f32[36,68,5]{1,0,2:T(8,128)S(1)} %pad_maximum_fusion.14), channel_id=1, source_target_pairs={{0,1},{1,2},{2,3},{4,5},{5,6},{6,7},{8,9},{9,10},{10,11},{12,13},{... | collective-permute-start | bytes 146888 | tf_op jit(solution)/shard_map/ppermute | solution.py:147
  75.4 1.6 %collective-permute-start.6 = (f32[8,32,128]{2,1,0:T(8,128)}, f32[8,32,128]{2,1,0:T(8,128)S(1)}, u32[]{:S(2)}, u32[]{:S(2)}) collective-permute-start(f32[8,32,128]{2,1,0:T(8,128)} %get-tuple-element.16), channel_id=1, source_target_pairs={{0,64},{64,0},{128,192},{192,128},{1,65},{65,1},{129,193},{193,129... | collective-permute-start | bytes 393224 | tf_op jit(solution)/shard_map/ppermute | solution.py:362
  77.9 5.7 %collective-permute-start.7 = (f32[8,32,128]{2,1,0:T(8,128)S(1)}, f32[8,32,128]{2,1,0:T(8,128)S(1)}, u32[]{:S(2)}, u32[]{:S(2)}) collective-permute-start(f32[8,32,128]{2,1,0:T(8,128)S(1)} %add.261), channel_id=1, source_target_pairs={{0,128},{128,0},{64,192},{192,64},{1,129},{129,1},{65,193},{193,65... | collective-permute-start | bytes 393224 | tf_op jit(solution)/shard_map/ppermute | solution.py:364
  83.6 33.7 %copy-start.3 = (f32[8,32,128]{2,1,0:T(8,128)}, f32[8,32,128]{2,1,0:T(8,128)S(1)}, u32[]{:S(2)}) copy-start(f32[8,32,128]{2,1,0:T(8,128)S(1)} %add.262) | copy-start | bytes 393220
  83.6 9.6 %collective-permute-start.8 = (f32[16,3,128]{2,1,0:T(4,128)S(1)}, f32[16,3,128]{2,1,0:T(4,128)S(1)}, u32[]{:S(2)}, u32[]{:S(2)}) collective-permute-start(f32[16,3,128]{2,1,0:T(4,128)S(1)} %get-tuple-element.49), channel_id=1, source_target_pairs={{0,4},{4,8},{8,12},{12,16},{16,20},{20,24},{24,28},{28,32},{32,36}... | collective-permute-start | bytes 73736 | tf_op jit(solution)/shard_map/ppermute | solution.py:27
  91.1 9.4 %collective-permute-start.9 = (f32[16,3,128]{2,1,0:T(4,128)S(1)}, f32[16,3,128]{2,1,0:T(4,128)S(1)}, u32[]{:S(2)}, u32[]{:S(2)}) collective-permute-start(f32[16,3,128]{2,1,0:T(4,128)S(1)} %get-tuple-element.50), channel_id=1, source_target_pairs={{4,0},{8,4},{12,8},{16,12},{20,16},{24,20},{28,24},{32,28},{36,32}... | collective-permute-start | bytes 73736 | tf_op jit(solution)/shard_map/ppermute | solution.py:28
  100.7 9.3 %collective-permute-start.10 = (f32[16,38,3]{2,1,0:T(8,128)S(1)}, f32[16,38,3]{2,1,0:T(8,128)S(1)}, u32[]{:S(2)}, u32[]{:S(2)}) collective-permute-start(f32[16,38,3]{2,1,0:T(8,128)S(1)} %get-tuple-element.31), channel_id=1, source_target_pairs={{0,1},{1,2},{2,3},{4,5},{5,6},{6,7},{8,9},{9,10},{10,11},{12,13},{... | collective-permute-start | bytes 21896 | tf_op jit(solution)/shard_map/ppermute | solution.py:27
  105.0 9.2 %collective-permute-start.11 = (f32[16,38,3]{2,1,0:T(8,128)S(1)}, f32[16,38,3]{2,1,0:T(8,128)S(1)}, u32[]{:S(2)}, u32[]{:S(2)}) collective-permute-start(f32[16,38,3]{2,1,0:T(8,128)S(1)} %get-tuple-element.32), channel_id=1, source_target_pairs={{1,0},{2,1},{3,2},{5,4},{6,5},{7,6},{9,8},{10,9},{11,10},{13,12},{... | collective-permute-start | bytes 21896 | tf_op jit(solution)/shard_map/ppermute | solution.py:28

commit v11 on v8

--- a/solution.py
+++ b/solution.py
@@ -358,11 +358,20 @@
     return jnp.concatenate([top, middle, bottom], 1)
 
 
-def grp_sum(partial):
-    pair = lax.ppermute(partial, "grp", [(0, 1), (1, 0), (2, 3), (3, 2)])
-    partial = partial + pair
-    pair = lax.ppermute(partial, "grp", [(0, 2), (2, 0), (1, 3), (3, 1)])
-    return partial + pair
+def grp_sum(partial, slabs):
+    groups = lax.axis_size("grp")
+    me = lax.axis_index("grp")
+    received = {}
+    for shift in range(1, groups):
+        pairs = [(g, (g + shift) % groups) for g in range(slabs)]
+        received[shift] = lax.ppermute(partial, "grp", pairs)
+    total = None
+    for owner in range(slabs):
+        share = partial
+        for shift in range(1, groups):
+            share = jnp.where((me - shift) % groups == owner, received[shift], share)
+        total = share if total is None else total + share
+    return total
 
 
 def on_device(conc, velocity, porosity, saturation, layer_counts, electrodes, init_potential):
@@ -395,7 +404,7 @@
         place, weights, field, velocity, porosity, saturation, *pieces,
         grid=(slabs * layers, rows * tile_x, columns * tile_y),
     )
-    conductivity = grp_sum(partial_cond)
+    conductivity = grp_sum(partial_cond, slabs)
 
     grid_x = coarse_x * rows
     grid_y = coarse_y * columns

time: 118 us -> 117 us (level)
  the two profiles are of different devices: /device:TPU:102 before, /device:TPU:128 now
where the time goes in v11:
time: 117 us; the launch traced here: 116 us
  starting transfers between devices  38.7 us (33%)
  Pallas kernels  26 us (22%)
  waiting for transfers between devices  20.9 us (18%)
  local copies, waits for them, and re-layouts  16.7 us (14%)
  other arithmetic  12.7 us (11%)
  between operations  1.36 us (1%)
    pallas_call x1, Pallas kernels, transport_call(): pl.pallas_call(functools.partial(transport_kernel, grid), out_shape=(jax....  23.2 us
    ppermute x2, waiting for transfers between devices, with_halo(): before = lax.ppermute(last, axis, up)  10.6 us
    ppermute x3, starting transfers between devices, grp_sum(): received[shift] = lax.ppermute(partial, 'grp', pairs)  9.75 us
    ppermute x2, starting transfers between devices, with_halo(): before = lax.ppermute(last, axis, up)  8.05 us
    ppermute x1, starting transfers between devices, transport_halo(): lax.ppermute(jnp.concatenate([xz_c(slice(ny - 2, ny), ycols[0:2]), xz_u(n...  4.55 us
    ppermute x2, starting transfers between devices, with_halo(): after = lax.ppermute(initial, axis, down)  4.55 us
    ppermute x1, starting transfers between devices, transport_halo(): ax = lax.ppermute(send_dn, 'gx', down)  4.48 us
    ppermute x1, waiting for transfers between devices, transport_halo(): bx = lax.ppermute(send_up, 'gx', up)  4.39 us
  transfers between devices with their start and end apart: 13, of which 6 were waited for; matrix products, arithmetic and copies ran while one was open for 10% of the time, Pallas kernels for 0%

profile of v11, /device:TPU:128, one launch (start us, length us, event | category | flops | bytes accessed | tf_op | source)
XLA Modules:
  0.0 116.4 jit_solution(13332660137598337922)
XLA Ops:
  0.7 1.9 %copy-done.1 = bf16[3,1,32,64,256]{4,3,2,1,0:T(8,128)(2,1)S(1)} copy-done((bf16[3,1,32,64,256]{4,3,2,1,0:T(8,128)(2,1)S(1)}, bf16[3,1,32,64,256]{4,3,2,1,0:T(8,128)(2,1)}, u32[]{:S(2)}) %copy-start.1) | copy-done | bytes 3145752
  2.6 1.6 %copy-done.2 = f32[1,32,64,256]{3,2,1,0:T(8,128)S(1)} copy-done((f32[1,32,64,256]{3,2,1,0:T(8,128)S(1)}, f32[1,32,64,256]{3,2,1,0:T(8,128)}, u32[]{:S(2)}) %copy-start.2) | copy-done | bytes 2097176
  4.2 2.8 %shard_map.94 = (f32[5,64,256]{2,1,0:T(8,128)S(1)}, f32[5,64,256]{2,1,0:T(8,128)S(1)}, f32[10,32,256]{2,1,0:T(8,128)S(1)}, f32[8,2048]{1,0:T(8,128)S(1)}, f32[3,8,2048]{2,1,0:T(8,128)S(1)}) custom-call(f32[2048,256]{1,0:T(8,128)S(1)} %bitcast.156, bf16[3,2048,256]{2,1,0:T(8,128)(2,1)S(1)} %bitcast.154), custom_call_target="tpu_custom_call" | custom-call | flops 33554432 | bytes 5242880 | tf_op jit(solution)/shard_map/pallas_call | solution.py:78
  6.9 1.9 %collective-permute-start = (f32[5,64,256]{2,1,0:T(8,128)S(1)}, f32[5,64,256]{2,1,0:T(8,128)S(1)}, u32[]{:S(2)}, u32[]{:S(2)}) collective-permute-start(f32[5,64,256]{2,1,0:T(8,128)S(1)} %get-tuple-element.10), channel_id=1, source_target_pairs={{0,64},{64,128},{1,65},{65,129},{2,66},{66,130},{3,67},{67,131},{4... | collective-permute-start | bytes 983048 | tf_op jit(solution)/shard_map/ppermute | solution.py:108
  8.9 1.3 %collective-permute-start.1 = (f32[5,64,256]{2,1,0:T(8,128)S(1)}, f32[5,64,256]{2,1,0:T(8,128)S(1)}, u32[]{:S(2)}, u32[]{:S(2)}) collective-permute-start(f32[5,64,256]{2,1,0:T(8,128)S(1)} %get-tuple-element.11), channel_id=1, source_target_pairs={{64,0},{128,64},{65,1},{129,65},{66,2},{130,66},{67,3},{131,67},{6... | collective-permute-start | bytes 983048 | tf_op jit(solution)/shard_map/ppermute | solution.py:109
  11.9 1.4 %subtract_multiply_fusion = f32[1,8,38,134]{3,2,1,0:T(8,128)S(1)} fusion(s32[]{:T(128)} %bitcast.35, s32[]{:T(128)} %bitcast.34, s32[134]{0:T(256)S(1)} %iota_add_fusion, s32[8,38]{1,0:T(8,128)S(1)} %broadcast_add_fusion), kind=kLoop, calls=%fused_computation.79 | loop fusion | flops 285152 | bytes 164704 | tf_op jit(solution)/shard_map/mul | solution.py:427
  14.7 4.5 %collective-permute-start.2 = (f32[36,5,256]{2,0,1:T(8,128)S(1)}, f32[36,5,256]{2,0,1:T(8,128)S(1)}, u32[]{:S(2)}, u32[]{:S(2)}) collective-permute-start(f32[36,5,256]{2,0,1:T(8,128)S(1)} %pad_maximum_fusion.6), channel_id=1, source_target_pairs={{4,0},{8,4},{12,8},{16,12},{20,16},{24,20},{28,24},{32,28},{36,32}... | collective-permute-start | bytes 552968 | tf_op jit(solution)/shard_map/ppermute | solution.py:129
  19.3 2.9 %collective-permute-start.3 = (f32[36,5,256]{2,0,1:T(8,128)S(1)}, f32[36,5,256]{2,0,1:T(8,128)S(1)}, u32[]{:S(2)}, u32[]{:S(2)}) collective-permute-start(f32[36,5,256]{2,0,1:T(8,128)S(1)} %pad_maximum_fusion.7), channel_id=1, source_target_pairs={{0,4},{4,8},{8,12},{12,16},{16,20},{20,24},{24,28},{28,32},{32,36}... | collective-permute-start | bytes 552968 | tf_op jit(solution)/shard_map/ppermute | solution.py:128
  26.2 4.4 %collective-permute-done.3 = f32[36,5,256]{2,0,1:T(8,128)S(1)} collective-permute-done((f32[36,5,256]{2,0,1:T(8,128)S(1)}, f32[36,5,256]{2,0,1:T(8,128)S(1)}, u32[]{:S(2)}, u32[]{:S(2)}) %collective-permute-start.3) | collective-permute-done | bytes 184352 | tf_op jit(solution)/shard_map/ppermute | solution.py:128
  32.0 1.3 %collective-permute-start.4 = (f32[36,68,5]{1,0,2:T(8,128)S(1)}, f32[36,68,5]{1,0,2:T(8,128)S(1)}, u32[]{:S(2)}, u32[]{:S(2)}) collective-permute-start(f32[36,68,5]{1,0,2:T(8,128)S(1)} %pad_maximum_fusion.13), channel_id=1, source_target_pairs={{1,0},{2,1},{3,2},{5,4},{6,5},{7,6},{9,8},{10,9},{11,10},{13,12},{... | collective-permute-start | bytes 146888 | tf_op jit(solution)/shard_map/ppermute | solution.py:150
  34.6 4.6 %collective-permute-start.5 = (f32[36,68,5]{1,0,2:T(8,128)S(1)}, f32[36,68,5]{1,0,2:T(8,128)S(1)}, u32[]{:S(2)}, u32[]{:S(2)}) collective-permute-start(f32[36,68,5]{1,0,2:T(8,128)S(1)} %pad_maximum_fusion.14), channel_id=1, source_target_pairs={{0,1},{1,2},{2,3},{4,5},{5,6},{6,7},{8,9},{9,10},{10,11},{12,13},{... | collective-permute-start | bytes 146888 | tf_op jit(solution)/shard_map/ppermute | solution.py:147
  39.5 1.1 pad_maximum_fusion.1.xu
  40.6 0.8 pad_maximum_fusion.5.xc
  43.4 1.6 %copy.170 = f32[36,68,2]{2,1,0:T(8,128)} copy(f32[36,68,2]{1,0,2:T(8,128)S(1)} %slice.498) | data formatting | bytes 39168 | tf_op jit(solution)/shard_map/slice | solution.py:160
  45.0 2.1 %pad_maximum_fusion = f32[36,68,128]{2,1,0:T(8,128)S(1)} fusion(f32[36,68,2]{2,1,0:T(8,128)} %copy.170, f32[36,68,6]{2,1,0:T(8,128)S(1)} %copy.169, f32[36,68,2]{2,1,0:T(8,128)S(1)} %copy.168, f32[128]{0:T(128)S(1)} %pad.73.clone), kind=kLoop, calls=%fused_computation | loop fusion | flops 940032 | bytes 1351808 | tf_op jit(solution)/shard_map/concatenate | solution.py:160
  47.1 1.2 %pad.38.yt = f32[36,80,128]{2,1,0:T(8,128)} pad(f32[36,68,128]{2,1,0:T(8,128)S(1)} %pad_maximum_fusion, f32[]{:T(128)} %constant.81.clone.1), padding=0_0x6_6x0_0 | pad | bytes 2727940 | tf_op jit(solution)/shard_map/jit(_pad)/pad | solution.py:161
  48.3 23.2 %shard_map.95 = (f32[1,32,64,256]{3,2,1,0:T(8,128)}, f32[8,32,128]{2,1,0:T(8,128)}) custom-call(s32[4]{0:T(128)} %pad_add_fusion.place, f32[8,32]{1,0:T(8,128)} %convert_divide_fusion.weights, f32[32,64,256]{2,1,0:T(8,128)} %bitcast.155, bf16[3,1,32,64,256]{4,3,2,1,0:T(8,128)(2,1)} %v_ref.1, bf16[1,32,64,256]{3,2,1,0:T(8,128)(2,1)} %poro_ref.1, ...), custom_call_target="tpu_custom_call" | custom-call | flops 104857600 | bytes 20971520 | tf_op jit(solution)/shard_map/pallas_call | solution.py:274
  71.6 1.9 %collective-permute-start.6 = (f32[8,32,128]{2,1,0:T(8,128)}, f32[8,32,128]{2,1,0:T(8,128)S(1)}, u32[]{:S(2)}, u32[]{:S(2)}) collective-permute-start(f32[8,32,128]{2,1,0:T(8,128)} %get-tuple-element.16), channel_id=1, source_target_pairs={{0,192},{64,0},{128,64},{1,193},{65,1},{129,65},{2,194},{66,2},{13... | collective-permute-start | bytes 393224 | tf_op jit(solution)/shard_map/ppermute | solution.py:367
  73.5 6.5 %collective-permute-start.7 = (f32[8,32,128]{2,1,0:T(8,128)}, f32[8,32,128]{2,1,0:T(8,128)S(1)}, u32[]{:S(2)}, u32[]{:S(2)}) collective-permute-start(f32[8,32,128]{2,1,0:T(8,128)} %get-tuple-element.16), channel_id=1, source_target_pairs={{0,128},{64,192},{128,0},{1,129},{65,193},{129,1},{2,130},{66,194}... | collective-permute-start | bytes 393224 | tf_op jit(solution)/shard_map/ppermute | solution.py:367
  80.0 1.3 %collective-permute-start.8 = (f32[8,32,128]{2,1,0:T(8,128)}, f32[8,32,128]{2,1,0:T(8,128)S(1)}, u32[]{:S(2)}, u32[]{:S(2)}) collective-permute-start(f32[8,32,128]{2,1,0:T(8,128)} %get-tuple-element.16), channel_id=1, source_target_pairs={{0,64},{64,128},{128,192},{1,65},{65,129},{129,193},{2,66},{66,130... | collective-permute-start | bytes 393224 | tf_op jit(solution)/shard_map/ppermute | solution.py:367
  81.5 1.7 %collective-permute-done.7 = f32[8,32,128]{2,1,0:T(8,128)S(1)} collective-permute-done((f32[8,32,128]{2,1,0:T(8,128)}, f32[8,32,128]{2,1,0:T(8,128)S(1)}, u32[]{:S(2)}, u32[]{:S(2)}) %collective-permute-start.7) | collective-permute-done | bytes 131104 | tf_op jit(solution)/shard_map/ppermute | solution.py:367
  83.2 1.0 select_add_fusion
  84.2 3.1 %collective-permute-start.10 = (f32[16,3,128]{2,1,0:T(4,128)S(1)}, f32[16,3,128]{2,1,0:T(4,128)S(1)}, u32[]{:S(2)}, u32[]{:S(2)}) collective-permute-start(f32[16,3,128]{2,1,0:T(4,128)S(1)} %get-tuple-element.50), channel_id=1, source_target_pairs={{4,0},{8,4},{12,8},{16,12},{20,16},{24,20},{28,24},{32,28},{36,32}... | collective-permute-start | bytes 73736 | tf_op jit(solution)/shard_map/ppermute | solution.py:28
  87.3 4.3 %collective-permute-start.9 = (f32[16,3,128]{2,1,0:T(4,128)S(1)}, f32[16,3,128]{2,1,0:T(4,128)S(1)}, u32[]{:S(2)}, u32[]{:S(2)}) collective-permute-start(f32[16,3,128]{2,1,0:T(4,128)S(1)} %get-tuple-element.49), channel_id=1, source_target_pairs={{0,4},{4,8},{8,12},{12,16},{16,20},{20,24},{24,28},{28,32},{32,36}... | collective-permute-start | bytes 73736 | tf_op jit(solution)/shard_map/ppermute | solution.py:27
  91.6 5.3 %collective-permute-done.9 = f32[16,3,128]{2,1,0:T(4,128)S(1)} collective-permute-done((f32[16,3,128]{2,1,0:T(4,128)S(1)}, f32[16,3,128]{2,1,0:T(4,128)S(1)}, u32[]{:S(2)}, u32[]{:S(2)}) %collective-permute-start.9) | collective-permute-done | bytes 24608 | tf_op jit(solution)/shard_map/ppermute | solution.py:27
  97.1 3.8 %collective-permute-start.11 = (f32[16,38,3]{2,1,0:T(8,128)S(1)}, f32[16,38,3]{2,1,0:T(8,128)S(1)}, u32[]{:S(2)}, u32[]{:S(2)}) collective-permute-start(f32[16,38,3]{2,1,0:T(8,128)S(1)} %get-tuple-element.31), channel_id=1, source_target_pairs={{0,1},{1,2},{2,3},{4,5},{5,6},{6,7},{8,9},{9,10},{10,11},{12,13},{... | collective-permute-start | bytes 21896 | tf_op jit(solution)/shard_map/ppermute | solution.py:27
  100.9 1.5 %collective-permute-start.12 = (f32[16,38,3]{2,1,0:T(8,128)S(1)}, f32[16,38,3]{2,1,0:T(8,128)S(1)}, u32[]{:S(2)}, u32[]{:S(2)}) collective-permute-start(f32[16,38,3]{2,1,0:T(8,128)S(1)} %get-tuple-element.32), channel_id=1, source_target_pairs={{1,0},{2,1},{3,2},{5,4},{6,5},{7,6},{9,8},{10,9},{11,10},{13,12},{... | collective-permute-start | bytes 21896 | tf_op jit(solution)/shard_map/ppermute | solution.py:28
  102.7 5.3 %collective-permute-done.11 = f32[16,38,3]{2,1,0:T(8,128)S(1)} collective-permute-done((f32[16,38,3]{2,1,0:T(8,128)S(1)}, f32[16,38,3]{2,1,0:T(8,128)S(1)}, u32[]{:S(2)}, u32[]{:S(2)}) %collective-permute-start.11) | collective-permute-done | bytes 7328 | tf_op jit(solution)/shard_map/ppermute | solution.py:27
  108.0 4.1 %collective-permute-done.12 = f32[16,38,3]{2,1,0:T(8,128)S(1)} collective-permute-done((f32[16,38,3]{2,1,0:T(8,128)S(1)}, f32[16,38,3]{2,1,0:T(8,128)S(1)}, u32[]{:S(2)}, u32[]{:S(2)}) %collective-permute-start.12) | collective-permute-done | bytes 7328 | tf_op jit(solution)/shard_map/ppermute | solution.py:28
  112.6 1.1 fusion.41
  114.1 1.1 fusion.40
  115.3 1.2 %fusion.64 = f32[1,8,32,128]{3,2,1,0:T(8,128)} fusion(f32[1,8,34,130]{3,2,1,0:T(8,128)S(1)} %fusion.40, f32[8,32,128]{2,1,0:T(8,128)S(1)} %select_add_fusion, f32[16,38,3]{2,1,0:T(8,128)S(1)} %collective-permute-done.12, f32[16,3,128]{2,1,0:T(4,128)S(1)} %collective-permute-done.10, f32[8,32,128]{2,1,0:T(8,128)S(1)} %dynamic-slice_bitcast_fusion, ...), kind=kLoop, calls=%fused_computation.122 | loop fusion | flops 1540096 | bytes 2560000 | tf_op jit(solution)/shard_map/jit(_where)/select_n | solution.py:472
  (125 shorter events, 13.4 us)
Async XLA Ops:
  0.6 80.8 %copy-start = (f32[4,8,32,128]{3,2,1,0:T(8,128)S(1)}, f32[4,8,32,128]{3,2,1,0:T(8,128)}, u32[]{:S(2)}) copy-start(f32[4,8,32,128]{3,2,1,0:T(8,128)} %param.13) | copy-start | bytes 1572868
  0.6 1.9 %copy-start.1 = (bf16[3,1,32,64,256]{4,3,2,1,0:T(8,128)(2,1)S(1)}, bf16[3,1,32,64,256]{4,3,2,1,0:T(8,128)(2,1)}, u32[]{:S(2)}) copy-start(bf16[3,1,32,64,256]{4,3,2,1,0:T(8,128)(2,1)} %v_ref.1) | copy-start | bytes 9437188
  2.6 1.6 %copy-start.2 = (f32[1,32,64,256]{3,2,1,0:T(8,128)S(1)}, f32[1,32,64,256]{3,2,1,0:T(8,128)}, u32[]{:S(2)}) copy-start(f32[1,32,64,256]{3,2,1,0:T(8,128)} %param.7) | copy-start | bytes 6291460
  6.9 4.0 %copy-start.6 = (s32[8]{0:T(128)S(1)}, s32[8]{0:T(128)}, u32[]{:S(2)}) copy-start(s32[8]{0:T(128)} %param.11) | copy-start | bytes 100
  6.9 4.2 %copy-start.5 = (s32[4,2]{0,1:T(2,128)S(1)}, s32[4,2]{0,1:T(2,128)}, u32[]{:S(2)}) copy-start(s32[4,2]{0,1:T(2,128)} %param.12) | copy-start | bytes 100
  6.9 7.6 %collective-permute-start = (f32[5,64,256]{2,1,0:T(8,128)S(1)}, f32[5,64,256]{2,1,0:T(8,128)S(1)}, u32[]{:S(2)}, u32[]{:S(2)}) collective-permute-start(f32[5,64,256]{2,1,0:T(8,128)S(1)} %get-tuple-element.10), channel_id=1, source_target_pairs={{0,64},{64,128},{1,65},{65,129},{2,66},{66,130},{3,67},{67,131},{4... | collective-permute-start | bytes 983048 | tf_op jit(solution)/shard_map/ppermute | solution.py:108
  8.9 5.7 %collective-permute-start.1 = (f32[5,64,256]{2,1,0:T(8,128)S(1)}, f32[5,64,256]{2,1,0:T(8,128)S(1)}, u32[]{:S(2)}, u32[]{:S(2)}) collective-permute-start(f32[5,64,256]{2,1,0:T(8,128)S(1)} %get-tuple-element.11), channel_id=1, source_target_pairs={{64,0},{128,64},{65,1},{129,65},{66,2},{130,66},{67,3},{131,67},{6... | collective-permute-start | bytes 983048 | tf_op jit(solution)/shard_map/ppermute | solution.py:109
  14.7 11.1 %collective-permute-start.2 = (f32[36,5,256]{2,0,1:T(8,128)S(1)}, f32[36,5,256]{2,0,1:T(8,128)S(1)}, u32[]{:S(2)}, u32[]{:S(2)}) collective-permute-start(f32[36,5,256]{2,0,1:T(8,128)S(1)} %pad_maximum_fusion.6), channel_id=1, source_target_pairs={{4,0},{8,4},{12,8},{16,12},{20,16},{24,20},{28,24},{32,28},{36,32}... | collective-permute-start | bytes 552968 | tf_op jit(solution)/shard_map/ppermute | solution.py:129
  19.3 11.3 %collective-permute-start.3 = (f32[36,5,256]{2,0,1:T(8,128)S(1)}, f32[36,5,256]{2,0,1:T(8,128)S(1)}, u32[]{:S(2)}, u32[]{:S(2)}) collective-permute-start(f32[36,5,256]{2,0,1:T(8,128)S(1)} %pad_maximum_fusion.7), channel_id=1, source_target_pairs={{0,4},{4,8},{8,12},{12,16},{16,20},{20,24},{24,28},{28,32},{32,36}... | collective-permute-start | bytes 552968 | tf_op jit(solution)/shard_map/ppermute | solution.py:128
  32.0 9.4 %collective-permute-start.4 = (f32[36,68,5]{1,0,2:T(8,128)S(1)}, f32[36,68,5]{1,0,2:T(8,128)S(1)}, u32[]{:S(2)}, u32[]{:S(2)}) collective-permute-start(f32[36,68,5]{1,0,2:T(8,128)S(1)} %pad_maximum_fusion.13), channel_id=1, source_target_pairs={{1,0},{2,1},{3,2},{5,4},{6,5},{7,6},{9,8},{10,9},{11,10},{13,12},{... | collective-permute-start | bytes 146888 | tf_op jit(solution)/shard_map/ppermute | solution.py:150
  34.6 6.8 %collective-permute-start.5 = (f32[36,68,5]{1,0,2:T(8,128)S(1)}, f32[36,68,5]{1,0,2:T(8,128)S(1)}, u32[]{:S(2)}, u32[]{:S(2)}) collective-permute-start(f32[36,68,5]{1,0,2:T(8,128)S(1)} %pad_maximum_fusion.14), channel_id=1, source_target_pairs={{0,1},{1,2},{2,3},{4,5},{5,6},{6,7},{8,9},{9,10},{10,11},{12,13},{... | collective-permute-start | bytes 146888 | tf_op jit(solution)/shard_map/ppermute | solution.py:147
  41.4 0.6 copy-start.4
  71.6 9.9 %collective-permute-start.6 = (f32[8,32,128]{2,1,0:T(8,128)}, f32[8,32,128]{2,1,0:T(8,128)S(1)}, u32[]{:S(2)}, u32[]{:S(2)}) collective-permute-start(f32[8,32,128]{2,1,0:T(8,128)} %get-tuple-element.16), channel_id=1, source_target_pairs={{0,192},{64,0},{128,64},{1,193},{65,1},{129,65},{2,194},{66,2},{13... | collective-permute-start | bytes 393224 | tf_op jit(solution)/shard_map/ppermute | solution.py:367
  73.5 9.7 %collective-permute-start.7 = (f32[8,32,128]{2,1,0:T(8,128)}, f32[8,32,128]{2,1,0:T(8,128)S(1)}, u32[]{:S(2)}, u32[]{:S(2)}) collective-permute-start(f32[8,32,128]{2,1,0:T(8,128)} %get-tuple-element.16), channel_id=1, source_target_pairs={{0,128},{64,192},{128,0},{1,129},{65,193},{129,1},{2,130},{66,194}... | collective-permute-start | bytes 393224 | tf_op jit(solution)/shard_map/ppermute | solution.py:367
  80.0 3.1 %collective-permute-start.8 = (f32[8,32,128]{2,1,0:T(8,128)}, f32[8,32,128]{2,1,0:T(8,128)S(1)}, u32[]{:S(2)}, u32[]{:S(2)}) collective-permute-start(f32[8,32,128]{2,1,0:T(8,128)} %get-tuple-element.16), channel_id=1, source_target_pairs={{0,64},{64,128},{128,192},{1,65},{65,129},{129,193},{2,66},{66,130... | collective-permute-start | bytes 393224 | tf_op jit(solution)/shard_map/ppermute | solution.py:367
  84.1 31.1 %copy-start.3 = (f32[8,32,128]{2,1,0:T(8,128)}, f32[8,32,128]{2,1,0:T(8,128)S(1)}, u32[]{:S(2)}) copy-start(f32[8,32,128]{2,1,0:T(8,128)S(1)} %select_add_fusion) | copy-start | bytes 393220
  84.2 7.5 %collective-permute-start.10 = (f32[16,3,128]{2,1,0:T(4,128)S(1)}, f32[16,3,128]{2,1,0:T(4,128)S(1)}, u32[]{:S(2)}, u32[]{:S(2)}) collective-permute-start(f32[16,3,128]{2,1,0:T(4,128)S(1)} %get-tuple-element.50), channel_id=1, source_target_pairs={{4,0},{8,4},{12,8},{16,12},{20,16},{24,20},{28,24},{32,28},{36,32}... | collective-permute-start | bytes 73736 | tf_op jit(solution)/shard_map/ppermute | solution.py:28
  87.3 9.7 %collective-permute-start.9 = (f32[16,3,128]{2,1,0:T(4,128)S(1)}, f32[16,3,128]{2,1,0:T(4,128)S(1)}, u32[]{:S(2)}, u32[]{:S(2)}) collective-permute-start(f32[16,3,128]{2,1,0:T(4,128)S(1)} %get-tuple-element.49), channel_id=1, source_target_pairs={{0,4},{4,8},{8,12},{12,16},{16,20},{20,24},{24,28},{28,32},{32,36}... | collective-permute-start | bytes 73736 | tf_op jit(solution)/shard_map/ppermute | solution.py:27
  97.1 10.9 %collective-permute-start.11 = (f32[16,38,3]{2,1,0:T(8,128)S(1)}, f32[16,38,3]{2,1,0:T(8,128)S(1)}, u32[]{:S(2)}, u32[]{:S(2)}) collective-permute-start(f32[16,38,3]{2,1,0:T(8,128)S(1)} %get-tuple-element.31), channel_id=1, source_target_pairs={{0,1},{1,2},{2,3},{4,5},{5,6},{6,7},{8,9},{9,10},{10,11},{12,13},{... | collective-permute-start | bytes 21896 | tf_op jit(solution)/shard_map/ppermute | solution.py:27
  100.9 11.2 %collective-permute-start.12 = (f32[16,38,3]{2,1,0:T(8,128)S(1)}, f32[16,38,3]{2,1,0:T(8,128)S(1)}, u32[]{:S(2)}, u32[]{:S(2)}) collective-permute-start(f32[16,38,3]{2,1,0:T(8,128)S(1)} %get-tuple-element.32), channel_id=1, source_target_pairs={{1,0},{2,1},{3,2},{5,4},{6,5},{7,6},{9,8},{10,9},{11,10},{13,12},{... | collective-permute-start | bytes 21896 | tf_op jit(solution)/shard_map/ppermute | solution.py:28

commit v12 on v11

--- a/solution.py
+++ b/solution.py
@@ -358,6 +358,61 @@
     return jnp.concatenate([top, middle, bottom], 1)
 
 
+def sweeps_kernel(cond_ref, pot_ref, rhs_ref, mask_ref, out_ref, P):
+    c = cond_ref[...]
+    center = c[1:-1]
+    faces = []
+    diagonal = jnp.zeros_like(center)
+    for d in range(3):
+        if d == 0:
+            lo, hi = c[:-2], c[2:]
+        else:
+            lo, hi = roll(center, 1, d), roll(center, -1, d)
+        face_below = 0.5 * (center + lo)
+        face_above = 0.5 * (center + hi)
+        faces.append((face_below, face_above))
+        diagonal = diagonal + face_below + face_above
+    keep = mask_ref[...] > 0.0
+    rhs = rhs_ref[...]
+    P[...] = pot_ref[...]
+    for sweep_index in range(SWEEPS):
+        p = P[...]
+        pc = p[1:-1]
+        coupled = jnp.zeros_like(pc)
+        for d in range(3):
+            if d == 0:
+                lo, hi = p[:-2], p[2:]
+            else:
+                lo, hi = roll(pc, 1, d), roll(pc, -1, d)
+            coupled = coupled + faces[d][0] * lo + faces[d][1] * hi
+        applied = diagonal * pc - coupled
+        updated = pc + OMEGA * (rhs - applied) / diagonal
+        P[1:-1] = jnp.where(keep, updated, 0.0)
+    out_ref[...] = P[1:-1]
+
+
+def sweeps_call(cond_wide, potential, source_terms, on_grid):
+    zl, wx, wy = potential.shape[1:]
+    px, py = -wx % 8, -wy % 128
+    f32 = jnp.float32
+    cond = jnp.pad(cond_wide, ((0, 0), (0, px), (0, py)))
+    pot = jnp.pad(potential[0], ((1, 1), (0, px), (0, py)))
+    rhs = jnp.pad(source_terms, ((0, 0), (0, px), (0, py)))
+    mask = jnp.pad(on_grid.astype(f32), ((0, px), (0, py)))
+    vmem = pl.BlockSpec(memory_space=pltpu.VMEM)
+    out = pl.pallas_call(
+        sweeps_kernel,
+        out_shape=jax.ShapeDtypeStruct((zl, wx + px, wy + py), f32),
+        in_specs=[vmem] * 4,
+        out_specs=vmem,
+        scratch_shapes=[pltpu.VMEM((zl + 2, wx + px, wy + py), f32)],
+        cost_estimate=pl.CostEstimate(
+            flops=40 * SWEEPS * zl * wx * wy, transcendentals=0, bytes_accessed=16 * zl * wx * wy
+        ),
+    )(cond, pot, rhs, mask)
+    return out[:, SWEEPS : wx - SWEEPS, SWEEPS : wy - SWEEPS]
+
+
 def grp_sum(partial, slabs):
     groups = lax.axis_size("grp")
     me = lax.axis_index("grp")
@@ -432,44 +487,7 @@
         ((gx_ids >= 0) & (gx_ids < grid_x))[:, None] & ((gy_ids >= 0) & (gy_ids < grid_y))[None, :]
     )
 
-    for sweep_index in range(SWEEPS):
-        m = sweep_index + 1
-        nx, ny = wide_x - 2 * m, wide_y - 2 * m
-        center_c = cond_wide[1:-1, m : m + nx, m : m + ny]
-        faces = []
-        diagonal = jnp.zeros_like(center_c)
-        for d in range(3):
-            if d == 0:
-                lo = cond_wide[0:-2, m : m + nx, m : m + ny]
-                hi = cond_wide[2:, m : m + nx, m : m + ny]
-            elif d == 1:
-                lo = cond_wide[1:-1, m - 1 : m - 1 + nx, m : m + ny]
-                hi = cond_wide[1:-1, m + 1 : m + 1 + nx, m : m + ny]
-            else:
-                lo = cond_wide[1:-1, m : m + nx, m - 1 : m - 1 + ny]
-                hi = cond_wide[1:-1, m : m + nx, m + 1 : m + 1 + ny]
-            face_below = 0.5 * (center_c + lo)
-            face_above = 0.5 * (center_c + hi)
-            faces.append((face_below, face_above))
-            diagonal = diagonal + face_below + face_above
-        pot_z = jnp.pad(potential, ((0, 0), (1, 1), (0, 0), (0, 0)))
-        pot_c = potential[:, :, 1:-1, 1:-1]
-        coupled = jnp.zeros_like(pot_c)
-        for d in range(3):
-            if d == 0:
-                lo = pot_z[:, 0:-2, 1:-1, 1:-1]
-                hi = pot_z[:, 2:, 1:-1, 1:-1]
-            elif d == 1:
-                lo = potential[:, :, 0:-2, 1:-1]
-                hi = potential[:, :, 2:, 1:-1]
-            else:
-                lo = potential[:, :, 1:-1, 0:-2]
-                hi = potential[:, :, 1:-1, 2:]
-            coupled = coupled + faces[d][0] * lo + faces[d][1] * hi
-        applied = diagonal * pot_c - coupled
-        rhs = source_terms[:, :, m : m + nx, m : m + ny]
-        updated = pot_c + OMEGA * (rhs - applied) / diagonal
-        potential = jnp.where(on_grid[m : m + nx, m : m + ny], updated, 0.0)
+    potential = sweeps_call(cond_wide, potential, source_terms[0], on_grid)[None]
 
     return (advanced, conductivity, potential)
 

time: 117 us -> 120 us (1.026)
  local copies, waits for them, and re-layouts: 16.7 us -> 21 us
  Pallas kernels: 26 us -> 29.3 us
  other arithmetic: 12.7 us -> 9.49 us
    select_n x3 -> x0, other arithmetic: 3.48 us -> none  [on_device(): potential = jnp.where(on_grid[m:m + nx, m:m + ny], updated, 0.0)]
    pallas_call x0 -> x1, Pallas kernels: none -> 3.3 us  [sweeps_call(): pl.pallas_call(sweeps_kernel, out_shape=jax.ShapeDtypeStruct((zl, wx + px...]
    pad x0 -> x3, local copies, waits for them, and re-layouts: none -> 2.31 us  [the longest x1 0.79 us: sweeps_call(): cond = jnp.pad(cond_wide, ((0, 0), (0, px), (0, py)))]
    broadcast_in_dim x0 -> x1, local copies, waits for them, and re-layouts: none -> 1.73 us  [on_device(): sweeps_call(cond_wide, potential, source_terms[0], on_grid)[None]]
  transfers between devices with their start and end apart: 13 -> 13, of which waited for: 6 -> 5; matrix products, arithmetic and copies ran while one was open for 10% -> 11% of each run, Pallas kernels for 0% -> 0%
where the time goes in v12:
time: 120 us
  starting transfers between devices  38.5 us (32%)
  Pallas kernels  29.3 us (24%)
  local copies, waits for them, and re-layouts  21 us (18%)
  waiting for transfers between devices  20 us (17%)
  other arithmetic  9.49 us (8%)
  between operations  1.34 us (1%)
    pallas_call x1, Pallas kernels, transport_call(): pl.pallas_call(functools.partial(transport_kernel, grid), out_shape=(jax....  23.2 us
    ppermute x3, starting transfers between devices, grp_sum(): received[shift] = lax.ppermute(partial, 'grp', pairs)  9.87 us
    ppermute x2, waiting for transfers between devices, with_halo(): before = lax.ppermute(last, axis, up)  9.73 us
    ppermute x2, starting transfers between devices, with_halo(): before = lax.ppermute(last, axis, up)  7.81 us
    ppermute x1, starting transfers between devices, transport_halo(): lax.ppermute(jnp.concatenate([xz_c(slice(ny - 2, ny), ycols[0:2]), xz_u(n...  4.55 us
    ppermute x1, starting transfers between devices, transport_halo(): ax = lax.ppermute(send_dn, 'gx', down)  4.48 us
    ppermute x1, waiting for transfers between devices, transport_halo(): bx = lax.ppermute(send_up, 'gx', up)  4.38 us
    ppermute x2, starting transfers between devices, with_halo(): after = lax.ppermute(initial, axis, down)  4.38 us
  transfers between devices with their start and end apart: 13, of which 5 were waited for; matrix products, arithmetic and copies ran while one was open for 11% of the time, Pallas kernels for 0%

profile of v12, /device:TPU:128, one launch (start us, length us, event | category | flops | bytes accessed | tf_op | source)
XLA Modules:
  0.0 119.6 jit_solution(11914672979613120089)
XLA Ops:
  0.7 1.9 %copy-done.1 = bf16[3,1,32,64,256]{4,3,2,1,0:T(8,128)(2,1)S(1)} copy-done((bf16[3,1,32,64,256]{4,3,2,1,0:T(8,128)(2,1)S(1)}, bf16[3,1,32,64,256]{4,3,2,1,0:T(8,128)(2,1)}, u32[]{:S(2)}) %copy-start.1) | copy-done | bytes 3145752
  2.6 1.6 %copy-done.2 = f32[1,32,64,256]{3,2,1,0:T(8,128)S(1)} copy-done((f32[1,32,64,256]{3,2,1,0:T(8,128)S(1)}, f32[1,32,64,256]{3,2,1,0:T(8,128)}, u32[]{:S(2)}) %copy-start.2) | copy-done | bytes 2097176
  4.2 2.8 %shard_map.94 = (f32[5,64,256]{2,1,0:T(8,128)S(1)}, f32[5,64,256]{2,1,0:T(8,128)S(1)}, f32[10,32,256]{2,1,0:T(8,128)S(1)}, f32[8,2048]{1,0:T(8,128)S(1)}, f32[3,8,2048]{2,1,0:T(8,128)S(1)}) custom-call(f32[2048,256]{1,0:T(8,128)S(1)} %bitcast.63, bf16[3,2048,256]{2,1,0:T(8,128)(2,1)S(1)} %bitcast.61), custom_call_target="tpu_custom_call" | custom-call | flops 33554432 | bytes 5242880 | tf_op jit(solution)/shard_map/pallas_call | solution.py:78
  6.9 1.9 %collective-permute-start = (f32[5,64,256]{2,1,0:T(8,128)S(1)}, f32[5,64,256]{2,1,0:T(8,128)S(1)}, u32[]{:S(2)}, u32[]{:S(2)}) collective-permute-start(f32[5,64,256]{2,1,0:T(8,128)S(1)} %get-tuple-element.10), channel_id=1, source_target_pairs={{0,64},{64,128},{1,65},{65,129},{2,66},{66,130},{3,67},{67,131},{4... | collective-permute-start | bytes 983048 | tf_op jit(solution)/shard_map/ppermute | solution.py:108
  8.9 1.3 %collective-permute-start.1 = (f32[5,64,256]{2,1,0:T(8,128)S(1)}, f32[5,64,256]{2,1,0:T(8,128)S(1)}, u32[]{:S(2)}, u32[]{:S(2)}) collective-permute-start(f32[5,64,256]{2,1,0:T(8,128)S(1)} %get-tuple-element.11), channel_id=1, source_target_pairs={{64,0},{128,64},{65,1},{129,65},{66,2},{130,66},{67,3},{131,67},{6... | collective-permute-start | bytes 983048 | tf_op jit(solution)/shard_map/ppermute | solution.py:109
  11.8 1.3 %subtract_multiply_fusion = f32[8,38,134]{2,1,0:T(8,128)S(1)} fusion(s32[]{:T(128)} %bitcast.34, s32[]{:T(128)} %bitcast.33, s32[134]{0:T(256)S(1)} %iota_add_fusion, s32[8,38]{1,0:T(8,128)S(1)} %broadcast_add_fusion), kind=kLoop, calls=%fused_computation.6 | loop fusion | flops 285152 | bytes 164704 | tf_op jit(solution)/shard_map/mul | solution.py:482
  14.7 4.5 %collective-permute-start.2 = (f32[36,5,256]{2,0,1:T(8,128)S(1)}, f32[36,5,256]{2,0,1:T(8,128)S(1)}, u32[]{:S(2)}, u32[]{:S(2)}) collective-permute-start(f32[36,5,256]{2,0,1:T(8,128)S(1)} %pad_maximum_fusion.5), channel_id=1, source_target_pairs={{4,0},{8,4},{12,8},{16,12},{20,16},{24,20},{28,24},{32,28},{36,32}... | collective-permute-start | bytes 552968 | tf_op jit(solution)/shard_map/ppermute | solution.py:129
  19.2 2.9 %collective-permute-start.3 = (f32[36,5,256]{2,0,1:T(8,128)S(1)}, f32[36,5,256]{2,0,1:T(8,128)S(1)}, u32[]{:S(2)}, u32[]{:S(2)}) collective-permute-start(f32[36,5,256]{2,0,1:T(8,128)S(1)} %pad_maximum_fusion.6), channel_id=1, source_target_pairs={{0,4},{4,8},{8,12},{12,16},{16,20},{20,24},{24,28},{28,32},{32,36}... | collective-permute-start | bytes 552968 | tf_op jit(solution)/shard_map/ppermute | solution.py:128
  26.1 4.4 %collective-permute-done.3 = f32[36,5,256]{2,0,1:T(8,128)S(1)} collective-permute-done((f32[36,5,256]{2,0,1:T(8,128)S(1)}, f32[36,5,256]{2,0,1:T(8,128)S(1)}, u32[]{:S(2)}, u32[]{:S(2)}) %collective-permute-start.3) | collective-permute-done | bytes 184352 | tf_op jit(solution)/shard_map/ppermute | solution.py:128
  32.0 1.3 %collective-permute-start.4 = (f32[36,68,5]{1,0,2:T(8,128)S(1)}, f32[36,68,5]{1,0,2:T(8,128)S(1)}, u32[]{:S(2)}, u32[]{:S(2)}) collective-permute-start(f32[36,68,5]{1,0,2:T(8,128)S(1)} %pad_maximum_fusion.8), channel_id=1, source_target_pairs={{1,0},{2,1},{3,2},{5,4},{6,5},{7,6},{9,8},{10,9},{11,10},{13,12},{... | collective-permute-start | bytes 146888 | tf_op jit(solution)/shard_map/ppermute | solution.py:150
  34.5 4.6 %collective-permute-start.5 = (f32[36,68,5]{1,0,2:T(8,128)S(1)}, f32[36,68,5]{1,0,2:T(8,128)S(1)}, u32[]{:S(2)}, u32[]{:S(2)}) collective-permute-start(f32[36,68,5]{1,0,2:T(8,128)S(1)} %pad_maximum_fusion.9), channel_id=1, source_target_pairs={{0,1},{1,2},{2,3},{4,5},{5,6},{6,7},{8,9},{9,10},{10,11},{12,13},{... | collective-permute-start | bytes 146888 | tf_op jit(solution)/shard_map/ppermute | solution.py:147
  39.4 1.1 pad_maximum_fusion.1.xu
  40.5 0.8 pad_maximum_fusion.4.xc
  43.1 0.8 slice.273
  43.9 1.6 %copy.170 = f32[36,68,2]{2,1,0:T(8,128)} copy(f32[36,68,2]{1,0,2:T(8,128)S(1)} %slice.273) | data formatting | bytes 39168 | tf_op jit(solution)/shard_map/slice | solution.py:160
  45.5 2.1 %pad_maximum_fusion = f32[36,68,128]{2,1,0:T(8,128)S(1)} fusion(f32[36,68,2]{2,1,0:T(8,128)} %copy.170, f32[36,68,6]{2,1,0:T(8,128)S(1)} %copy.169, f32[36,68,2]{2,1,0:T(8,128)S(1)} %copy.168, f32[128]{0:T(128)S(1)} %pad.65.clone), kind=kLoop, calls=%fused_computation | loop fusion | flops 940032 | bytes 1351808 | tf_op jit(solution)/shard_map/concatenate | solution.py:160
  47.6 1.2 %pad.44.yt = f32[36,80,128]{2,1,0:T(8,128)} pad(f32[36,68,128]{2,1,0:T(8,128)S(1)} %pad_maximum_fusion, f32[]{:T(128)} %constant.75.clone.1), padding=0_0x6_6x0_0 | pad | bytes 2727940 | tf_op jit(solution)/shard_map/jit(_pad)/pad | solution.py:161
  48.8 23.2 %shard_map.95 = (f32[1,32,64,256]{3,2,1,0:T(8,128)}, f32[8,32,128]{2,1,0:T(8,128)}) custom-call(s32[4]{0:T(128)} %pad_add_fusion.place, f32[8,32]{1,0:T(8,128)} %convert_divide_fusion.weights, f32[32,64,256]{2,1,0:T(8,128)} %bitcast.62, bf16[3,1,32,64,256]{4,3,2,1,0:T(8,128)(2,1)} %v_ref.1, bf16[1,32,64,256]{3,2,1,0:T(8,128)(2,1)} %poro_ref.1, ...), custom_call_target="tpu_custom_call" | custom-call | flops 104857600 | bytes 20971520 | tf_op jit(solution)/shard_map/pallas_call | solution.py:274
  72.1 1.9 %collective-permute-start.6 = (f32[8,32,128]{2,1,0:T(8,128)}, f32[8,32,128]{2,1,0:T(8,128)S(1)}, u32[]{:S(2)}, u32[]{:S(2)}) collective-permute-start(f32[8,32,128]{2,1,0:T(8,128)} %get-tuple-element.16), channel_id=1, source_target_pairs={{0,192},{64,0},{128,64},{1,193},{65,1},{129,65},{2,194},{66,2},{13... | collective-permute-start | bytes 393224 | tf_op jit(solution)/shard_map/ppermute | solution.py:422
  74.0 6.7 %collective-permute-start.7 = (f32[8,32,128]{2,1,0:T(8,128)}, f32[8,32,128]{2,1,0:T(8,128)S(1)}, u32[]{:S(2)}, u32[]{:S(2)}) collective-permute-start(f32[8,32,128]{2,1,0:T(8,128)} %get-tuple-element.16), channel_id=1, source_target_pairs={{0,128},{64,192},{128,0},{1,129},{65,193},{129,1},{2,130},{66,194}... | collective-permute-start | bytes 393224 | tf_op jit(solution)/shard_map/ppermute | solution.py:422
  80.7 1.3 %collective-permute-start.8 = (f32[8,32,128]{2,1,0:T(8,128)}, f32[8,32,128]{2,1,0:T(8,128)S(1)}, u32[]{:S(2)}, u32[]{:S(2)}) collective-permute-start(f32[8,32,128]{2,1,0:T(8,128)} %get-tuple-element.16), channel_id=1, source_target_pairs={{0,64},{64,128},{128,192},{1,65},{65,129},{129,193},{2,66},{66,130... | collective-permute-start | bytes 393224 | tf_op jit(solution)/shard_map/ppermute | solution.py:422
  82.1 1.7 %collective-permute-done.7 = f32[8,32,128]{2,1,0:T(8,128)S(1)} collective-permute-done((f32[8,32,128]{2,1,0:T(8,128)}, f32[8,32,128]{2,1,0:T(8,128)S(1)}, u32[]{:S(2)}, u32[]{:S(2)}) %collective-permute-start.7) | collective-permute-done | bytes 131104 | tf_op jit(solution)/shard_map/ppermute | solution.py:422
  83.8 1.0 select_add_fusion
  84.8 3.1 %collective-permute-start.10 = (f32[16,3,128]{2,1,0:T(4,128)S(1)}, f32[16,3,128]{2,1,0:T(4,128)S(1)}, u32[]{:S(2)}, u32[]{:S(2)}) collective-permute-start(f32[16,3,128]{2,1,0:T(4,128)S(1)} %get-tuple-element.48), channel_id=1, source_target_pairs={{4,0},{8,4},{12,8},{16,12},{20,16},{24,20},{28,24},{32,28},{36,32}... | collective-permute-start | bytes 73736 | tf_op jit(solution)/shard_map/ppermute | solution.py:28
  87.9 4.3 %collective-permute-start.9 = (f32[16,3,128]{2,1,0:T(4,128)S(1)}, f32[16,3,128]{2,1,0:T(4,128)S(1)}, u32[]{:S(2)}, u32[]{:S(2)}) collective-permute-start(f32[16,3,128]{2,1,0:T(4,128)S(1)} %get-tuple-element.47), channel_id=1, source_target_pairs={{0,4},{4,8},{8,12},{12,16},{16,20},{20,24},{24,28},{28,32},{32,36}... | collective-permute-start | bytes 73736 | tf_op jit(solution)/shard_map/ppermute | solution.py:27
  92.3 5.3 %collective-permute-done.9 = f32[16,3,128]{2,1,0:T(4,128)S(1)} collective-permute-done((f32[16,3,128]{2,1,0:T(4,128)S(1)}, f32[16,3,128]{2,1,0:T(4,128)S(1)}, u32[]{:S(2)}, u32[]{:S(2)}) %collective-permute-start.9) | collective-permute-done | bytes 24608 | tf_op jit(solution)/shard_map/ppermute | solution.py:27
  97.8 3.5 %collective-permute-start.11 = (f32[16,38,3]{2,1,0:T(8,128)S(1)}, f32[16,38,3]{2,1,0:T(8,128)S(1)}, u32[]{:S(2)}, u32[]{:S(2)}) collective-permute-start(f32[16,38,3]{2,1,0:T(8,128)S(1)} %get-tuple-element.29), channel_id=1, source_target_pairs={{0,1},{1,2},{2,3},{4,5},{5,6},{6,7},{8,9},{9,10},{10,11},{12,13},{... | collective-permute-start | bytes 21896 | tf_op jit(solution)/shard_map/ppermute | solution.py:27
  101.3 1.3 %collective-permute-start.12 = (f32[16,38,3]{2,1,0:T(8,128)S(1)}, f32[16,38,3]{2,1,0:T(8,128)S(1)}, u32[]{:S(2)}, u32[]{:S(2)}) collective-permute-start(f32[16,38,3]{2,1,0:T(8,128)S(1)} %get-tuple-element.30), channel_id=1, source_target_pairs={{1,0},{2,1},{3,2},{5,4},{6,5},{7,6},{9,8},{10,9},{11,10},{13,12},{... | collective-permute-start | bytes 21896 | tf_op jit(solution)/shard_map/ppermute | solution.py:28
  104.0 4.4 %collective-permute-done.11 = f32[16,38,3]{2,1,0:T(8,128)S(1)} collective-permute-done((f32[16,38,3]{2,1,0:T(8,128)S(1)}, f32[16,38,3]{2,1,0:T(8,128)S(1)}, u32[]{:S(2)}, u32[]{:S(2)}) %collective-permute-start.11) | collective-permute-done | bytes 7328 | tf_op jit(solution)/shard_map/ppermute | solution.py:27
  108.4 4.1 %collective-permute-done.12 = f32[16,38,3]{2,1,0:T(8,128)S(1)} collective-permute-done((f32[16,38,3]{2,1,0:T(8,128)S(1)}, f32[16,38,3]{2,1,0:T(8,128)S(1)}, u32[]{:S(2)}, u32[]{:S(2)}) %collective-permute-start.12) | collective-permute-done | bytes 7328 | tf_op jit(solution)/shard_map/ppermute | solution.py:28
  114.6 3.3 %shard_map.96 = f32[8,40,256]{2,1,0:T(8,128)} custom-call(f32[10,40,256]{2,1,0:T(8,128)} %pad.129.cond_ref, f32[10,40,256]{2,1,0:T(8,128)} %pad.47.pot_ref, f32[8,40,256]{2,1,0:T(8,128)} %pad.48.rhs_ref, f32[40,256]{1,0:T(8,128)} %pad_convert_fusion.mask_ref), custom_call_target="tpu_custom_call" | custom-call | flops 4888320 | bytes 651776 | tf_op jit(solution)/shard_map/pallas_call | solution.py:403
  117.9 1.7 %slice_bitcast_fusion = f32[1,8,32,128]{3,2,1,0:T(8,128)} fusion(f32[8,40,256]{2,1,0:T(8,128)} %shard_map.96), kind=kLoop, calls=%fused_computation.12 | loop fusion | bytes 262144 | tf_op jit(solution)/shard_map/broadcast_in_dim | solution.py:490
  (124 shorter events, 15.5 us)
Async XLA Ops:
  0.6 81.4 %copy-start = (f32[4,8,32,128]{3,2,1,0:T(8,128)S(1)}, f32[4,8,32,128]{3,2,1,0:T(8,128)}, u32[]{:S(2)}) copy-start(f32[4,8,32,128]{3,2,1,0:T(8,128)} %param.13) | copy-start | bytes 1572868
  0.6 1.9 %copy-start.1 = (bf16[3,1,32,64,256]{4,3,2,1,0:T(8,128)(2,1)S(1)}, bf16[3,1,32,64,256]{4,3,2,1,0:T(8,128)(2,1)}, u32[]{:S(2)}) copy-start(bf16[3,1,32,64,256]{4,3,2,1,0:T(8,128)(2,1)} %v_ref.1) | copy-start | bytes 9437188
  2.6 1.6 %copy-start.2 = (f32[1,32,64,256]{3,2,1,0:T(8,128)S(1)}, f32[1,32,64,256]{3,2,1,0:T(8,128)}, u32[]{:S(2)}) copy-start(f32[1,32,64,256]{3,2,1,0:T(8,128)} %param.7) | copy-start | bytes 6291460
  6.9 4.0 %copy-start.6 = (s32[8]{0:T(128)S(1)}, s32[8]{0:T(128)}, u32[]{:S(2)}) copy-start(s32[8]{0:T(128)} %param.11) | copy-start | bytes 100
  6.9 4.2 %copy-start.5 = (s32[4,2]{0,1:T(2,128)S(1)}, s32[4,2]{0,1:T(2,128)}, u32[]{:S(2)}) copy-start(s32[4,2]{0,1:T(2,128)} %param.12) | copy-start | bytes 100
  6.9 7.6 %collective-permute-start = (f32[5,64,256]{2,1,0:T(8,128)S(1)}, f32[5,64,256]{2,1,0:T(8,128)S(1)}, u32[]{:S(2)}, u32[]{:S(2)}) collective-permute-start(f32[5,64,256]{2,1,0:T(8,128)S(1)} %get-tuple-element.10), channel_id=1, source_target_pairs={{0,64},{64,128},{1,65},{65,129},{2,66},{66,130},{3,67},{67,131},{4... | collective-permute-start | bytes 983048 | tf_op jit(solution)/shard_map/ppermute | solution.py:108
  8.9 5.7 %collective-permute-start.1 = (f32[5,64,256]{2,1,0:T(8,128)S(1)}, f32[5,64,256]{2,1,0:T(8,128)S(1)}, u32[]{:S(2)}, u32[]{:S(2)}) collective-permute-start(f32[5,64,256]{2,1,0:T(8,128)S(1)} %get-tuple-element.11), channel_id=1, source_target_pairs={{64,0},{128,64},{65,1},{129,65},{66,2},{130,66},{67,3},{131,67},{6... | collective-permute-start | bytes 983048 | tf_op jit(solution)/shard_map/ppermute | solution.py:109
  14.7 11.2 %collective-permute-start.2 = (f32[36,5,256]{2,0,1:T(8,128)S(1)}, f32[36,5,256]{2,0,1:T(8,128)S(1)}, u32[]{:S(2)}, u32[]{:S(2)}) collective-permute-start(f32[36,5,256]{2,0,1:T(8,128)S(1)} %pad_maximum_fusion.5), channel_id=1, source_target_pairs={{4,0},{8,4},{12,8},{16,12},{20,16},{24,20},{28,24},{32,28},{36,32}... | collective-permute-start | bytes 552968 | tf_op jit(solution)/shard_map/ppermute | solution.py:129
  19.2 11.3 %collective-permute-start.3 = (f32[36,5,256]{2,0,1:T(8,128)S(1)}, f32[36,5,256]{2,0,1:T(8,128)S(1)}, u32[]{:S(2)}, u32[]{:S(2)}) collective-permute-start(f32[36,5,256]{2,0,1:T(8,128)S(1)} %pad_maximum_fusion.6), channel_id=1, source_target_pairs={{0,4},{4,8},{8,12},{12,16},{16,20},{20,24},{24,28},{28,32},{32,36}... | collective-permute-start | bytes 552968 | tf_op jit(solution)/shard_map/ppermute | solution.py:128
  32.0 9.3 %collective-permute-start.4 = (f32[36,68,5]{1,0,2:T(8,128)S(1)}, f32[36,68,5]{1,0,2:T(8,128)S(1)}, u32[]{:S(2)}, u32[]{:S(2)}) collective-permute-start(f32[36,68,5]{1,0,2:T(8,128)S(1)} %pad_maximum_fusion.8), channel_id=1, source_target_pairs={{1,0},{2,1},{3,2},{5,4},{6,5},{7,6},{9,8},{10,9},{11,10},{13,12},{... | collective-permute-start | bytes 146888 | tf_op jit(solution)/shard_map/ppermute | solution.py:150
  34.5 6.8 %collective-permute-start.5 = (f32[36,68,5]{1,0,2:T(8,128)S(1)}, f32[36,68,5]{1,0,2:T(8,128)S(1)}, u32[]{:S(2)}, u32[]{:S(2)}) collective-permute-start(f32[36,68,5]{1,0,2:T(8,128)S(1)} %pad_maximum_fusion.9), channel_id=1, source_target_pairs={{0,1},{1,2},{2,3},{4,5},{5,6},{6,7},{8,9},{9,10},{10,11},{12,13},{... | collective-permute-start | bytes 146888 | tf_op jit(solution)/shard_map/ppermute | solution.py:147
  41.3 0.6 copy-start.4
  72.1 10.0 %collective-permute-start.6 = (f32[8,32,128]{2,1,0:T(8,128)}, f32[8,32,128]{2,1,0:T(8,128)S(1)}, u32[]{:S(2)}, u32[]{:S(2)}) collective-permute-start(f32[8,32,128]{2,1,0:T(8,128)} %get-tuple-element.16), channel_id=1, source_target_pairs={{0,192},{64,0},{128,64},{1,193},{65,1},{129,65},{2,194},{66,2},{13... | collective-permute-start | bytes 393224 | tf_op jit(solution)/shard_map/ppermute | solution.py:422
  74.0 9.8 %collective-permute-start.7 = (f32[8,32,128]{2,1,0:T(8,128)}, f32[8,32,128]{2,1,0:T(8,128)S(1)}, u32[]{:S(2)}, u32[]{:S(2)}) collective-permute-start(f32[8,32,128]{2,1,0:T(8,128)} %get-tuple-element.16), channel_id=1, source_target_pairs={{0,128},{64,192},{128,0},{1,129},{65,193},{129,1},{2,130},{66,194}... | collective-permute-start | bytes 393224 | tf_op jit(solution)/shard_map/ppermute | solution.py:422
  80.7 3.1 %collective-permute-start.8 = (f32[8,32,128]{2,1,0:T(8,128)}, f32[8,32,128]{2,1,0:T(8,128)S(1)}, u32[]{:S(2)}, u32[]{:S(2)}) collective-permute-start(f32[8,32,128]{2,1,0:T(8,128)} %get-tuple-element.16), channel_id=1, source_target_pairs={{0,64},{64,128},{128,192},{1,65},{65,129},{129,193},{2,66},{66,130... | collective-permute-start | bytes 393224 | tf_op jit(solution)/shard_map/ppermute | solution.py:422
  84.8 27.8 %copy-start.3 = (f32[8,32,128]{2,1,0:T(8,128)}, f32[8,32,128]{2,1,0:T(8,128)S(1)}, u32[]{:S(2)}) copy-start(f32[8,32,128]{2,1,0:T(8,128)S(1)} %select_add_fusion) | copy-start | bytes 393220
  84.8 7.5 %collective-permute-start.10 = (f32[16,3,128]{2,1,0:T(4,128)S(1)}, f32[16,3,128]{2,1,0:T(4,128)S(1)}, u32[]{:S(2)}, u32[]{:S(2)}) collective-permute-start(f32[16,3,128]{2,1,0:T(4,128)S(1)} %get-tuple-element.48), channel_id=1, source_target_pairs={{4,0},{8,4},{12,8},{16,12},{20,16},{24,20},{28,24},{32,28},{36,32}... | collective-permute-start | bytes 73736 | tf_op jit(solution)/shard_map/ppermute | solution.py:28
  87.9 9.7 %collective-permute-start.9 = (f32[16,3,128]{2,1,0:T(4,128)S(1)}, f32[16,3,128]{2,1,0:T(4,128)S(1)}, u32[]{:S(2)}, u32[]{:S(2)}) collective-permute-start(f32[16,3,128]{2,1,0:T(4,128)S(1)} %get-tuple-element.47), channel_id=1, source_target_pairs={{0,4},{4,8},{8,12},{12,16},{16,20},{20,24},{24,28},{28,32},{32,36}... | collective-permute-start | bytes 73736 | tf_op jit(solution)/shard_map/ppermute | solution.py:27
  97.8 10.7 %collective-permute-start.11 = (f32[16,38,3]{2,1,0:T(8,128)S(1)}, f32[16,38,3]{2,1,0:T(8,128)S(1)}, u32[]{:S(2)}, u32[]{:S(2)}) collective-permute-start(f32[16,38,3]{2,1,0:T(8,128)S(1)} %get-tuple-element.29), channel_id=1, source_target_pairs={{0,1},{1,2},{2,3},{4,5},{5,6},{6,7},{8,9},{9,10},{10,11},{12,13},{... | collective-permute-start | bytes 21896 | tf_op jit(solution)/shard_map/ppermute | solution.py:27
  101.3 11.2 %collective-permute-start.12 = (f32[16,38,3]{2,1,0:T(8,128)S(1)}, f32[16,38,3]{2,1,0:T(8,128)S(1)}, u32[]{:S(2)}, u32[]{:S(2)}) collective-permute-start(f32[16,38,3]{2,1,0:T(8,128)S(1)} %get-tuple-element.30), channel_id=1, source_target_pairs={{1,0},{2,1},{3,2},{5,4},{6,5},{7,6},{9,8},{10,9},{11,10},{13,12},{... | collective-permute-start | bytes 21896 | tf_op jit(solution)/shard_map/ppermute | solution.py:28

commit v13 on v11

--- a/solution.py
+++ b/solution.py
@@ -158,7 +158,6 @@
     speeds_y = jnp.stack([by[..., 2:5], ay[..., 2:5]], 3).reshape(nz + 4, nx + 4, 6)
     fill = jnp.zeros((nz + 4, nx + 4, 118), f32)
     yt = jnp.concatenate([ay[..., 0:2], speeds_y, fill, by[..., 0:2]], 2)
-    yt = jnp.pad(yt, ((0, 0), (6, 6), (0, 0)))
     return zlo_c, zhi_c, zlo_u, zhi_u, xc, xu, yt
 
 
@@ -197,7 +196,7 @@
     lax.fori_loop(0, nz, put_c, 0)
     F[:, 0:8, 0:ny] = xc[...]
     F[:, wx - 8 : wx, 0:ny] = xc[...]
-    F[:, :, ny:wy] = yt[...]
+    F[:, 6 : 6 + nx + 4, ny:wy] = yt[...]
     for d in range(3):
         U[d, 0, 8 : 8 + nx, 0:ny] = zlo_u[d]
         U[d, nz + 1, 8 : 8 + nx, 0:ny] = zhi_u[d]
@@ -209,7 +208,7 @@
         lax.fori_loop(0, nz, put_u, 0)
         U[d, :, 0:8, 0:ny] = xu[d]
         U[d, :, wx - 8 : wx, 0:ny] = xu[d]
-        U[d, :, :, ny:wy] = roll(yt[1 : nz + 3], -(3 + 2 * d), 2)
+        U[d, :, 6 : 6 + nx + 4, ny:wy] = roll(yt[1 : nz + 3], -(3 + 2 * d), 2)
 
     total_z, total_x, total_y = grid
     gz0 = place[0] * nz - 1

time: 117 us -> 117 us (level)
  local copies, waits for them, and re-layouts: 16.7 us -> 15.5 us
    pad x1 -> x0, local copies, waits for them, and re-layouts: 1.23 us -> none  [transport_halo(): yt = jnp.pad(yt, ((0, 0), (6, 6), (0, 0)))]
where the time goes in v13:
time: 117 us; the launch traced here: 116 us
  starting transfers between devices  38.7 us (33%)
  Pallas kernels  25.8 us (22%)
  waiting for transfers between devices  20.9 us (18%)
  local copies, waits for them, and re-layouts  15.5 us (13%)
  other arithmetic  13.8 us (12%)
  between operations  1.36 us (1%)
    pallas_call x1, Pallas kernels, transport_call(): pl.pallas_call(functools.partial(transport_kernel, grid), out_shape=(jax....  23.1 us
    ppermute x2, waiting for transfers between devices, with_halo(): before = lax.ppermute(last, axis, up)  10.6 us
    ppermute x3, starting transfers between devices, grp_sum(): received[shift] = lax.ppermute(partial, 'grp', pairs)  9.78 us
    ppermute x2, starting transfers between devices, with_halo(): before = lax.ppermute(last, axis, up)  7.97 us
    ppermute x2, starting transfers between devices, with_halo(): after = lax.ppermute(initial, axis, down)  4.55 us
    ppermute x1, starting transfers between devices, transport_halo(): lax.ppermute(jnp.concatenate([xz_c(slice(ny - 2, ny), ycols[0:2]), xz_u(n...  4.55 us
    ppermute x1, starting transfers between devices, transport_halo(): ax = lax.ppermute(send_dn, 'gx', down)  4.48 us
    ppermute x1, waiting for transfers between devices, transport_halo(): bx = lax.ppermute(send_up, 'gx', up)  4.38 us
  transfers between devices with their start and end apart: 13, of which 6 were waited for; matrix products, arithmetic and copies ran while one was open for 10% of the time, Pallas kernels for 0%

profile of v13, /device:TPU:128, one launch (start us, length us, event | category | flops | bytes accessed | tf_op | source)
XLA Modules:
  0.0 116.1 jit_solution(11371824849311780422)
XLA Ops:
  0.7 1.9 %copy-done.1 = bf16[3,1,32,64,256]{4,3,2,1,0:T(8,128)(2,1)S(1)} copy-done((bf16[3,1,32,64,256]{4,3,2,1,0:T(8,128)(2,1)S(1)}, bf16[3,1,32,64,256]{4,3,2,1,0:T(8,128)(2,1)}, u32[]{:S(2)}) %copy-start.1) | copy-done | bytes 3145752
  2.6 1.6 %copy-done.2 = f32[1,32,64,256]{3,2,1,0:T(8,128)S(1)} copy-done((f32[1,32,64,256]{3,2,1,0:T(8,128)S(1)}, f32[1,32,64,256]{3,2,1,0:T(8,128)}, u32[]{:S(2)}) %copy-start.2) | copy-done | bytes 2097176
  4.2 2.8 %shard_map.94 = (f32[5,64,256]{2,1,0:T(8,128)S(1)}, f32[5,64,256]{2,1,0:T(8,128)S(1)}, f32[10,32,256]{2,1,0:T(8,128)S(1)}, f32[8,2048]{1,0:T(8,128)S(1)}, f32[3,8,2048]{2,1,0:T(8,128)S(1)}) custom-call(f32[2048,256]{1,0:T(8,128)S(1)} %bitcast.156, bf16[3,2048,256]{2,1,0:T(8,128)(2,1)S(1)} %bitcast.154), custom_call_target="tpu_custom_call" | custom-call | flops 33554432 | bytes 5242880 | tf_op jit(solution)/shard_map/pallas_call | solution.py:78
  6.9 1.9 %collective-permute-start = (f32[5,64,256]{2,1,0:T(8,128)S(1)}, f32[5,64,256]{2,1,0:T(8,128)S(1)}, u32[]{:S(2)}, u32[]{:S(2)}) collective-permute-start(f32[5,64,256]{2,1,0:T(8,128)S(1)} %get-tuple-element.10), channel_id=1, source_target_pairs={{0,64},{64,128},{1,65},{65,129},{2,66},{66,130},{3,67},{67,131},{4... | collective-permute-start | bytes 983048 | tf_op jit(solution)/shard_map/ppermute | solution.py:108
  8.9 1.3 %collective-permute-start.1 = (f32[5,64,256]{2,1,0:T(8,128)S(1)}, f32[5,64,256]{2,1,0:T(8,128)S(1)}, u32[]{:S(2)}, u32[]{:S(2)}) collective-permute-start(f32[5,64,256]{2,1,0:T(8,128)S(1)} %get-tuple-element.11), channel_id=1, source_target_pairs={{64,0},{128,64},{65,1},{129,65},{66,2},{130,66},{67,3},{131,67},{6... | collective-permute-start | bytes 983048 | tf_op jit(solution)/shard_map/ppermute | solution.py:109
  11.9 1.4 %subtract_multiply_fusion = f32[1,8,38,134]{3,2,1,0:T(8,128)S(1)} fusion(s32[]{:T(128)} %bitcast.35, s32[]{:T(128)} %bitcast.34, s32[134]{0:T(256)S(1)} %iota_add_fusion, s32[8,38]{1,0:T(8,128)S(1)} %broadcast_add_fusion), kind=kLoop, calls=%fused_computation.79 | loop fusion | flops 285152 | bytes 164704 | tf_op jit(solution)/shard_map/mul | solution.py:426
  14.7 4.5 %collective-permute-start.2 = (f32[36,5,256]{2,0,1:T(8,128)S(1)}, f32[36,5,256]{2,0,1:T(8,128)S(1)}, u32[]{:S(2)}, u32[]{:S(2)}) collective-permute-start(f32[36,5,256]{2,0,1:T(8,128)S(1)} %pad_maximum_fusion.6), channel_id=1, source_target_pairs={{4,0},{8,4},{12,8},{16,12},{20,16},{24,20},{28,24},{32,28},{36,32}... | collective-permute-start | bytes 552968 | tf_op jit(solution)/shard_map/ppermute | solution.py:129
  19.3 2.9 %collective-permute-start.3 = (f32[36,5,256]{2,0,1:T(8,128)S(1)}, f32[36,5,256]{2,0,1:T(8,128)S(1)}, u32[]{:S(2)}, u32[]{:S(2)}) collective-permute-start(f32[36,5,256]{2,0,1:T(8,128)S(1)} %pad_maximum_fusion.7), channel_id=1, source_target_pairs={{0,4},{4,8},{8,12},{12,16},{16,20},{20,24},{24,28},{28,32},{32,36}... | collective-permute-start | bytes 552968 | tf_op jit(solution)/shard_map/ppermute | solution.py:128
  26.2 4.4 %collective-permute-done.3 = f32[36,5,256]{2,0,1:T(8,128)S(1)} collective-permute-done((f32[36,5,256]{2,0,1:T(8,128)S(1)}, f32[36,5,256]{2,0,1:T(8,128)S(1)}, u32[]{:S(2)}, u32[]{:S(2)}) %collective-permute-start.3) | collective-permute-done | bytes 184352 | tf_op jit(solution)/shard_map/ppermute | solution.py:128
  32.0 1.3 %collective-permute-start.4 = (f32[36,68,5]{1,0,2:T(8,128)S(1)}, f32[36,68,5]{1,0,2:T(8,128)S(1)}, u32[]{:S(2)}, u32[]{:S(2)}) collective-permute-start(f32[36,68,5]{1,0,2:T(8,128)S(1)} %pad_maximum_fusion.13), channel_id=1, source_target_pairs={{1,0},{2,1},{3,2},{5,4},{6,5},{7,6},{9,8},{10,9},{11,10},{13,12},{... | collective-permute-start | bytes 146888 | tf_op jit(solution)/shard_map/ppermute | solution.py:150
  34.5 4.6 %collective-permute-start.5 = (f32[36,68,5]{1,0,2:T(8,128)S(1)}, f32[36,68,5]{1,0,2:T(8,128)S(1)}, u32[]{:S(2)}, u32[]{:S(2)}) collective-permute-start(f32[36,68,5]{1,0,2:T(8,128)S(1)} %pad_maximum_fusion.14), channel_id=1, source_target_pairs={{0,1},{1,2},{2,3},{4,5},{5,6},{6,7},{8,9},{9,10},{10,11},{12,13},{... | collective-permute-start | bytes 146888 | tf_op jit(solution)/shard_map/ppermute | solution.py:147
  39.4 1.1 pad_maximum_fusion.1.xu
  40.6 0.8 pad_maximum_fusion.5.xc
  42.6 0.8 slice.498
  43.4 1.6 %copy.170 = f32[36,68,2]{2,1,0:T(8,128)} copy(f32[36,68,2]{1,0,2:T(8,128)S(1)} %slice.498) | data formatting | bytes 39168 | tf_op jit(solution)/shard_map/slice | solution.py:160
  45.0 3.2 %pad_maximum_fusion.yt = f32[36,68,128]{2,1,0:T(8,128)} fusion(f32[36,68,2]{2,1,0:T(8,128)} %copy.170, f32[36,68,6]{2,1,0:T(8,128)S(1)} %copy.169, f32[36,68,2]{2,1,0:T(8,128)S(1)} %copy.168, f32[128]{0:T(128)S(1)} %pad.68.clone), kind=kLoop, calls=%fused_computation | loop fusion | flops 940032 | bytes 1351808 | tf_op jit(solution)/shard_map/concatenate | solution.py:160
  48.2 23.1 %shard_map.95 = (f32[1,32,64,256]{3,2,1,0:T(8,128)}, f32[8,32,128]{2,1,0:T(8,128)}) custom-call(s32[4]{0:T(128)} %pad_add_fusion.place, f32[8,32]{1,0:T(8,128)} %convert_divide_fusion.weights, f32[32,64,256]{2,1,0:T(8,128)} %bitcast.155, bf16[3,1,32,64,256]{4,3,2,1,0:T(8,128)(2,1)} %v_ref.1, bf16[1,32,64,256]{3,2,1,0:T(8,128)(2,1)} %poro_ref.1, ...), custom_call_target="tpu_custom_call" | custom-call | flops 104857600 | bytes 20971520 | tf_op jit(solution)/shard_map/pallas_call | solution.py:273
  71.3 1.9 %collective-permute-start.6 = (f32[8,32,128]{2,1,0:T(8,128)}, f32[8,32,128]{2,1,0:T(8,128)S(1)}, u32[]{:S(2)}, u32[]{:S(2)}) collective-permute-start(f32[8,32,128]{2,1,0:T(8,128)} %get-tuple-element.16), channel_id=1, source_target_pairs={{0,192},{64,0},{128,64},{1,193},{65,1},{129,65},{2,194},{66,2},{13... | collective-permute-start | bytes 393224 | tf_op jit(solution)/shard_map/ppermute | solution.py:366
  73.2 6.6 %collective-permute-start.7 = (f32[8,32,128]{2,1,0:T(8,128)}, f32[8,32,128]{2,1,0:T(8,128)S(1)}, u32[]{:S(2)}, u32[]{:S(2)}) collective-permute-start(f32[8,32,128]{2,1,0:T(8,128)} %get-tuple-element.16), channel_id=1, source_target_pairs={{0,128},{64,192},{128,0},{1,129},{65,193},{129,1},{2,130},{66,194}... | collective-permute-start | bytes 393224 | tf_op jit(solution)/shard_map/ppermute | solution.py:366
  79.8 1.3 %collective-permute-start.8 = (f32[8,32,128]{2,1,0:T(8,128)}, f32[8,32,128]{2,1,0:T(8,128)S(1)}, u32[]{:S(2)}, u32[]{:S(2)}) collective-permute-start(f32[8,32,128]{2,1,0:T(8,128)} %get-tuple-element.16), channel_id=1, source_target_pairs={{0,64},{64,128},{128,192},{1,65},{65,129},{129,193},{2,66},{66,130... | collective-permute-start | bytes 393224 | tf_op jit(solution)/shard_map/ppermute | solution.py:366
  81.2 1.7 %collective-permute-done.7 = f32[8,32,128]{2,1,0:T(8,128)S(1)} collective-permute-done((f32[8,32,128]{2,1,0:T(8,128)}, f32[8,32,128]{2,1,0:T(8,128)S(1)}, u32[]{:S(2)}, u32[]{:S(2)}) %collective-permute-start.7) | collective-permute-done | bytes 131104 | tf_op jit(solution)/shard_map/ppermute | solution.py:366
  82.9 1.0 select_add_fusion
  83.9 3.1 %collective-permute-start.10 = (f32[16,3,128]{2,1,0:T(4,128)S(1)}, f32[16,3,128]{2,1,0:T(4,128)S(1)}, u32[]{:S(2)}, u32[]{:S(2)}) collective-permute-start(f32[16,3,128]{2,1,0:T(4,128)S(1)} %get-tuple-element.50), channel_id=1, source_target_pairs={{4,0},{8,4},{12,8},{16,12},{20,16},{24,20},{28,24},{32,28},{36,32}... | collective-permute-start | bytes 73736 | tf_op jit(solution)/shard_map/ppermute | solution.py:28
  87.0 4.3 %collective-permute-start.9 = (f32[16,3,128]{2,1,0:T(4,128)S(1)}, f32[16,3,128]{2,1,0:T(4,128)S(1)}, u32[]{:S(2)}, u32[]{:S(2)}) collective-permute-start(f32[16,3,128]{2,1,0:T(4,128)S(1)} %get-tuple-element.49), channel_id=1, source_target_pairs={{0,4},{4,8},{8,12},{12,16},{16,20},{20,24},{24,28},{28,32},{32,36}... | collective-permute-start | bytes 73736 | tf_op jit(solution)/shard_map/ppermute | solution.py:27
  91.4 5.3 %collective-permute-done.9 = f32[16,3,128]{2,1,0:T(4,128)S(1)} collective-permute-done((f32[16,3,128]{2,1,0:T(4,128)S(1)}, f32[16,3,128]{2,1,0:T(4,128)S(1)}, u32[]{:S(2)}, u32[]{:S(2)}) %collective-permute-start.9) | collective-permute-done | bytes 24608 | tf_op jit(solution)/shard_map/ppermute | solution.py:27
  96.9 3.7 %collective-permute-start.11 = (f32[16,38,3]{2,1,0:T(8,128)S(1)}, f32[16,38,3]{2,1,0:T(8,128)S(1)}, u32[]{:S(2)}, u32[]{:S(2)}) collective-permute-start(f32[16,38,3]{2,1,0:T(8,128)S(1)} %get-tuple-element.31), channel_id=1, source_target_pairs={{0,1},{1,2},{2,3},{4,5},{5,6},{6,7},{8,9},{9,10},{10,11},{12,13},{... | collective-permute-start | bytes 21896 | tf_op jit(solution)/shard_map/ppermute | solution.py:27
  100.6 1.5 %collective-permute-start.12 = (f32[16,38,3]{2,1,0:T(8,128)S(1)}, f32[16,38,3]{2,1,0:T(8,128)S(1)}, u32[]{:S(2)}, u32[]{:S(2)}) collective-permute-start(f32[16,38,3]{2,1,0:T(8,128)S(1)} %get-tuple-element.32), channel_id=1, source_target_pairs={{1,0},{2,1},{3,2},{5,4},{6,5},{7,6},{9,8},{10,9},{11,10},{13,12},{... | collective-permute-start | bytes 21896 | tf_op jit(solution)/shard_map/ppermute | solution.py:28
  102.4 5.3 %collective-permute-done.11 = f32[16,38,3]{2,1,0:T(8,128)S(1)} collective-permute-done((f32[16,38,3]{2,1,0:T(8,128)S(1)}, f32[16,38,3]{2,1,0:T(8,128)S(1)}, u32[]{:S(2)}, u32[]{:S(2)}) %collective-permute-start.11) | collective-permute-done | bytes 7328 | tf_op jit(solution)/shard_map/ppermute | solution.py:27
  107.7 4.1 %collective-permute-done.12 = f32[16,38,3]{2,1,0:T(8,128)S(1)} collective-permute-done((f32[16,38,3]{2,1,0:T(8,128)S(1)}, f32[16,38,3]{2,1,0:T(8,128)S(1)}, u32[]{:S(2)}, u32[]{:S(2)}) %collective-permute-start.12) | collective-permute-done | bytes 7328 | tf_op jit(solution)/shard_map/ppermute | solution.py:28
  112.3 1.1 fusion.41
  113.8 1.1 fusion.40
  114.9 1.2 %fusion.64 = f32[1,8,32,128]{3,2,1,0:T(8,128)} fusion(f32[1,8,34,130]{3,2,1,0:T(8,128)S(1)} %fusion.40, f32[8,32,128]{2,1,0:T(8,128)S(1)} %select_add_fusion, f32[16,38,3]{2,1,0:T(8,128)S(1)} %collective-permute-done.12, f32[16,3,128]{2,1,0:T(4,128)S(1)} %collective-permute-done.10, f32[8,32,128]{2,1,0:T(8,128)S(1)} %dynamic-slice_bitcast_fusion, ...), kind=kLoop, calls=%fused_computation.122 | loop fusion | flops 1540096 | bytes 2560000 | tf_op jit(solution)/shard_map/jit(_where)/select_n | solution.py:471
  (124 shorter events, 12.6 us)
Async XLA Ops:
  0.6 80.5 %copy-start = (f32[4,8,32,128]{3,2,1,0:T(8,128)S(1)}, f32[4,8,32,128]{3,2,1,0:T(8,128)}, u32[]{:S(2)}) copy-start(f32[4,8,32,128]{3,2,1,0:T(8,128)} %param.13) | copy-start | bytes 1572868
  0.6 1.9 %copy-start.1 = (bf16[3,1,32,64,256]{4,3,2,1,0:T(8,128)(2,1)S(1)}, bf16[3,1,32,64,256]{4,3,2,1,0:T(8,128)(2,1)}, u32[]{:S(2)}) copy-start(bf16[3,1,32,64,256]{4,3,2,1,0:T(8,128)(2,1)} %v_ref.1) | copy-start | bytes 9437188
  2.6 1.6 %copy-start.2 = (f32[1,32,64,256]{3,2,1,0:T(8,128)S(1)}, f32[1,32,64,256]{3,2,1,0:T(8,128)}, u32[]{:S(2)}) copy-start(f32[1,32,64,256]{3,2,1,0:T(8,128)} %param.7) | copy-start | bytes 6291460
  6.9 4.0 %copy-start.6 = (s32[8]{0:T(128)S(1)}, s32[8]{0:T(128)}, u32[]{:S(2)}) copy-start(s32[8]{0:T(128)} %param.11) | copy-start | bytes 100
  6.9 4.2 %copy-start.5 = (s32[4,2]{0,1:T(2,128)S(1)}, s32[4,2]{0,1:T(2,128)}, u32[]{:S(2)}) copy-start(s32[4,2]{0,1:T(2,128)} %param.12) | copy-start | bytes 100
  6.9 7.6 %collective-permute-start = (f32[5,64,256]{2,1,0:T(8,128)S(1)}, f32[5,64,256]{2,1,0:T(8,128)S(1)}, u32[]{:S(2)}, u32[]{:S(2)}) collective-permute-start(f32[5,64,256]{2,1,0:T(8,128)S(1)} %get-tuple-element.10), channel_id=1, source_target_pairs={{0,64},{64,128},{1,65},{65,129},{2,66},{66,130},{3,67},{67,131},{4... | collective-permute-start | bytes 983048 | tf_op jit(solution)/shard_map/ppermute | solution.py:108
  8.9 5.7 %collective-permute-start.1 = (f32[5,64,256]{2,1,0:T(8,128)S(1)}, f32[5,64,256]{2,1,0:T(8,128)S(1)}, u32[]{:S(2)}, u32[]{:S(2)}) collective-permute-start(f32[5,64,256]{2,1,0:T(8,128)S(1)} %get-tuple-element.11), channel_id=1, source_target_pairs={{64,0},{128,64},{65,1},{129,65},{66,2},{130,66},{67,3},{131,67},{6... | collective-permute-start | bytes 983048 | tf_op jit(solution)/shard_map/ppermute | solution.py:109
  14.7 11.2 %collective-permute-start.2 = (f32[36,5,256]{2,0,1:T(8,128)S(1)}, f32[36,5,256]{2,0,1:T(8,128)S(1)}, u32[]{:S(2)}, u32[]{:S(2)}) collective-permute-start(f32[36,5,256]{2,0,1:T(8,128)S(1)} %pad_maximum_fusion.6), channel_id=1, source_target_pairs={{4,0},{8,4},{12,8},{16,12},{20,16},{24,20},{28,24},{32,28},{36,32}... | collective-permute-start | bytes 552968 | tf_op jit(solution)/shard_map/ppermute | solution.py:129
  19.3 11.3 %collective-permute-start.3 = (f32[36,5,256]{2,0,1:T(8,128)S(1)}, f32[36,5,256]{2,0,1:T(8,128)S(1)}, u32[]{:S(2)}, u32[]{:S(2)}) collective-permute-start(f32[36,5,256]{2,0,1:T(8,128)S(1)} %pad_maximum_fusion.7), channel_id=1, source_target_pairs={{0,4},{4,8},{8,12},{12,16},{16,20},{20,24},{24,28},{28,32},{32,36}... | collective-permute-start | bytes 552968 | tf_op jit(solution)/shard_map/ppermute | solution.py:128
  32.0 9.4 %collective-permute-start.4 = (f32[36,68,5]{1,0,2:T(8,128)S(1)}, f32[36,68,5]{1,0,2:T(8,128)S(1)}, u32[]{:S(2)}, u32[]{:S(2)}) collective-permute-start(f32[36,68,5]{1,0,2:T(8,128)S(1)} %pad_maximum_fusion.13), channel_id=1, source_target_pairs={{1,0},{2,1},{3,2},{5,4},{6,5},{7,6},{9,8},{10,9},{11,10},{13,12},{... | collective-permute-start | bytes 146888 | tf_op jit(solution)/shard_map/ppermute | solution.py:150
  34.5 6.8 %collective-permute-start.5 = (f32[36,68,5]{1,0,2:T(8,128)S(1)}, f32[36,68,5]{1,0,2:T(8,128)S(1)}, u32[]{:S(2)}, u32[]{:S(2)}) collective-permute-start(f32[36,68,5]{1,0,2:T(8,128)S(1)} %pad_maximum_fusion.14), channel_id=1, source_target_pairs={{0,1},{1,2},{2,3},{4,5},{5,6},{6,7},{8,9},{9,10},{10,11},{12,13},{... | collective-permute-start | bytes 146888 | tf_op jit(solution)/shard_map/ppermute | solution.py:147
  41.4 0.6 copy-start.4
  71.3 9.9 %collective-permute-start.6 = (f32[8,32,128]{2,1,0:T(8,128)}, f32[8,32,128]{2,1,0:T(8,128)S(1)}, u32[]{:S(2)}, u32[]{:S(2)}) collective-permute-start(f32[8,32,128]{2,1,0:T(8,128)} %get-tuple-element.16), channel_id=1, source_target_pairs={{0,192},{64,0},{128,64},{1,193},{65,1},{129,65},{2,194},{66,2},{13... | collective-permute-start | bytes 393224 | tf_op jit(solution)/shard_map/ppermute | solution.py:366
  73.2 9.7 %collective-permute-start.7 = (f32[8,32,128]{2,1,0:T(8,128)}, f32[8,32,128]{2,1,0:T(8,128)S(1)}, u32[]{:S(2)}, u32[]{:S(2)}) collective-permute-start(f32[8,32,128]{2,1,0:T(8,128)} %get-tuple-element.16), channel_id=1, source_target_pairs={{0,128},{64,192},{128,0},{1,129},{65,193},{129,1},{2,130},{66,194}... | collective-permute-start | bytes 393224 | tf_op jit(solution)/shard_map/ppermute | solution.py:366
  79.8 3.1 %collective-permute-start.8 = (f32[8,32,128]{2,1,0:T(8,128)}, f32[8,32,128]{2,1,0:T(8,128)S(1)}, u32[]{:S(2)}, u32[]{:S(2)}) collective-permute-start(f32[8,32,128]{2,1,0:T(8,128)} %get-tuple-element.16), channel_id=1, source_target_pairs={{0,64},{64,128},{128,192},{1,65},{65,129},{129,193},{2,66},{66,130... | collective-permute-start | bytes 393224 | tf_op jit(solution)/shard_map/ppermute | solution.py:366
  83.9 31.0 %copy-start.3 = (f32[8,32,128]{2,1,0:T(8,128)}, f32[8,32,128]{2,1,0:T(8,128)S(1)}, u32[]{:S(2)}) copy-start(f32[8,32,128]{2,1,0:T(8,128)S(1)} %select_add_fusion) | copy-start | bytes 393220
  83.9 7.5 %collective-permute-start.10 = (f32[16,3,128]{2,1,0:T(4,128)S(1)}, f32[16,3,128]{2,1,0:T(4,128)S(1)}, u32[]{:S(2)}, u32[]{:S(2)}) collective-permute-start(f32[16,3,128]{2,1,0:T(4,128)S(1)} %get-tuple-element.50), channel_id=1, source_target_pairs={{4,0},{8,4},{12,8},{16,12},{20,16},{24,20},{28,24},{32,28},{36,32}... | collective-permute-start | bytes 73736 | tf_op jit(solution)/shard_map/ppermute | solution.py:28
  87.0 9.7 %collective-permute-start.9 = (f32[16,3,128]{2,1,0:T(4,128)S(1)}, f32[16,3,128]{2,1,0:T(4,128)S(1)}, u32[]{:S(2)}, u32[]{:S(2)}) collective-permute-start(f32[16,3,128]{2,1,0:T(4,128)S(1)} %get-tuple-element.49), channel_id=1, source_target_pairs={{0,4},{4,8},{8,12},{12,16},{16,20},{20,24},{24,28},{28,32},{32,36}... | collective-permute-start | bytes 73736 | tf_op jit(solution)/shard_map/ppermute | solution.py:27
  96.9 10.8 %collective-permute-start.11 = (f32[16,38,3]{2,1,0:T(8,128)S(1)}, f32[16,38,3]{2,1,0:T(8,128)S(1)}, u32[]{:S(2)}, u32[]{:S(2)}) collective-permute-start(f32[16,38,3]{2,1,0:T(8,128)S(1)} %get-tuple-element.31), channel_id=1, source_target_pairs={{0,1},{1,2},{2,3},{4,5},{5,6},{6,7},{8,9},{9,10},{10,11},{12,13},{... | collective-permute-start | bytes 21896 | tf_op jit(solution)/shard_map/ppermute | solution.py:27
  100.6 11.2 %collective-permute-start.12 = (f32[16,38,3]{2,1,0:T(8,128)S(1)}, f32[16,38,3]{2,1,0:T(8,128)S(1)}, u32[]{:S(2)}, u32[]{:S(2)}) collective-permute-start(f32[16,38,3]{2,1,0:T(8,128)S(1)} %get-tuple-element.32), channel_id=1, source_target_pairs={{1,0},{2,1},{3,2},{5,4},{6,5},{7,6},{9,8},{10,9},{11,10},{13,12},{... | collective-permute-start | bytes 21896 | tf_op jit(solution)/shard_map/ppermute | solution.py:28

commit v14 on v13

--- a/solution.py
+++ b/solution.py
@@ -154,7 +154,7 @@
     xc = jnp.concatenate([ax[:, 0:2], jnp.zeros((nz + 4, 4, ny), f32), bx[:, 0:2]], 1)
     xu_hi = jnp.swapaxes(ax[1:-1, 2:5], 0, 1)[:, :, None]
     xu_lo = jnp.swapaxes(bx[1:-1, 2:5], 0, 1)[:, :, None]
-    xu = jnp.concatenate([xu_hi, jnp.zeros((3, nz + 2, 6, ny), f32), xu_lo], 2)
+    xu = jnp.concatenate([xu_hi, xu_lo], 2)
     speeds_y = jnp.stack([by[..., 2:5], ay[..., 2:5]], 3).reshape(nz + 4, nx + 4, 6)
     fill = jnp.zeros((nz + 4, nx + 4, 118), f32)
     yt = jnp.concatenate([ay[..., 0:2], speeds_y, fill, by[..., 0:2]], 2)
@@ -206,8 +206,8 @@
             return carry
 
         lax.fori_loop(0, nz, put_u, 0)
-        U[d, :, 0:8, 0:ny] = xu[d]
-        U[d, :, wx - 8 : wx, 0:ny] = xu[d]
+        U[d, :, 7:8, 0:ny] = xu[d, :, 1:2]
+        U[d, :, wx - 8 : wx - 7, 0:ny] = xu[d, :, 0:1]
         U[d, :, 6 : 6 + nx + 4, ny:wy] = roll(yt[1 : nz + 3], -(3 + 2 * d), 2)
 
     total_z, total_x, total_y = grid

time: 117 us -> 116 us (level)
  transfers between devices with their start and end apart: 13 -> 13, of which waited for: 6 -> 7; matrix products, arithmetic and copies ran while one was open for 10% -> 10% of each run, Pallas kernels for 0% -> 0%
where the time goes in v14:
time: 116 us
  starting transfers between devices  38.7 us (33%)
  Pallas kernels  25.7 us (22%)
  waiting for transfers between devices  21.1 us (18%)
  local copies, waits for them, and re-layouts  15.4 us (13%)
  other arithmetic  13.6 us (12%)
  between operations  1.33 us (1%)
    pallas_call x1, Pallas kernels, transport_call(): pl.pallas_call(functools.partial(transport_kernel, grid), out_shape=(jax....  22.9 us
    ppermute x2, waiting for transfers between devices, with_halo(): before = lax.ppermute(last, axis, up)  10.6 us
    ppermute x3, starting transfers between devices, grp_sum(): received[shift] = lax.ppermute(partial, 'grp', pairs)  9.68 us
    ppermute x2, starting transfers between devices, with_halo(): before = lax.ppermute(last, axis, up)  8.02 us
    ppermute x2, starting transfers between devices, with_halo(): after = lax.ppermute(initial, axis, down)  4.56 us
    ppermute x1, starting transfers between devices, transport_halo(): lax.ppermute(jnp.concatenate([xz_c(slice(ny - 2, ny), ycols[0:2]), xz_u(n...  4.55 us
    ppermute x1, starting transfers between devices, transport_halo(): ax = lax.ppermute(send_dn, 'gx', down)  4.48 us
    ppermute x1, waiting for transfers between devices, transport_halo(): bx = lax.ppermute(send_up, 'gx', up)  4.38 us
  transfers between devices with their start and end apart: 13, of which 7 were waited for; matrix products, arithmetic and copies ran while one was open for 10% of the time, Pallas kernels for 0%

profile of v14, /device:TPU:128, one launch (start us, length us, event | category | flops | bytes accessed | tf_op | source)
XLA Modules:
  0.0 115.8 jit_solution(14899950315798206915)
XLA Ops:
  0.7 1.9 %copy-done.1 = bf16[3,1,32,64,256]{4,3,2,1,0:T(8,128)(2,1)S(1)} copy-done((bf16[3,1,32,64,256]{4,3,2,1,0:T(8,128)(2,1)S(1)}, bf16[3,1,32,64,256]{4,3,2,1,0:T(8,128)(2,1)}, u32[]{:S(2)}) %copy-start.1) | copy-done | bytes 3145752
  2.6 1.6 %copy-done.2 = f32[1,32,64,256]{3,2,1,0:T(8,128)S(1)} copy-done((f32[1,32,64,256]{3,2,1,0:T(8,128)S(1)}, f32[1,32,64,256]{3,2,1,0:T(8,128)}, u32[]{:S(2)}) %copy-start.2) | copy-done | bytes 2097176
  4.2 2.8 %shard_map.94 = (f32[5,64,256]{2,1,0:T(8,128)S(1)}, f32[5,64,256]{2,1,0:T(8,128)S(1)}, f32[10,32,256]{2,1,0:T(8,128)S(1)}, f32[8,2048]{1,0:T(8,128)S(1)}, f32[3,8,2048]{2,1,0:T(8,128)S(1)}) custom-call(f32[2048,256]{1,0:T(8,128)S(1)} %bitcast.156, bf16[3,2048,256]{2,1,0:T(8,128)(2,1)S(1)} %bitcast.154), custom_call_target="tpu_custom_call" | custom-call | flops 33554432 | bytes 5242880 | tf_op jit(solution)/shard_map/pallas_call | solution.py:78
  6.9 1.9 %collective-permute-start = (f32[5,64,256]{2,1,0:T(8,128)S(1)}, f32[5,64,256]{2,1,0:T(8,128)S(1)}, u32[]{:S(2)}, u32[]{:S(2)}) collective-permute-start(f32[5,64,256]{2,1,0:T(8,128)S(1)} %get-tuple-element.10), channel_id=1, source_target_pairs={{0,64},{64,128},{1,65},{65,129},{2,66},{66,130},{3,67},{67,131},{4... | collective-permute-start | bytes 983048 | tf_op jit(solution)/shard_map/ppermute | solution.py:108
  8.9 1.3 %collective-permute-start.1 = (f32[5,64,256]{2,1,0:T(8,128)S(1)}, f32[5,64,256]{2,1,0:T(8,128)S(1)}, u32[]{:S(2)}, u32[]{:S(2)}) collective-permute-start(f32[5,64,256]{2,1,0:T(8,128)S(1)} %get-tuple-element.11), channel_id=1, source_target_pairs={{64,0},{128,64},{65,1},{129,65},{66,2},{130,66},{67,3},{131,67},{6... | collective-permute-start | bytes 983048 | tf_op jit(solution)/shard_map/ppermute | solution.py:109
  11.8 1.4 %subtract_multiply_fusion = f32[1,8,38,134]{3,2,1,0:T(8,128)S(1)} fusion(s32[]{:T(128)} %bitcast.35, s32[]{:T(128)} %bitcast.34, s32[134]{0:T(256)S(1)} %iota_add_fusion, s32[8,38]{1,0:T(8,128)S(1)} %broadcast_add_fusion), kind=kLoop, calls=%fused_computation.78 | loop fusion | flops 285152 | bytes 164704 | tf_op jit(solution)/shard_map/mul | solution.py:426
  14.7 4.5 %collective-permute-start.2 = (f32[36,5,256]{2,0,1:T(8,128)S(1)}, f32[36,5,256]{2,0,1:T(8,128)S(1)}, u32[]{:S(2)}, u32[]{:S(2)}) collective-permute-start(f32[36,5,256]{2,0,1:T(8,128)S(1)} %pad_maximum_fusion.6), channel_id=1, source_target_pairs={{4,0},{8,4},{12,8},{16,12},{20,16},{24,20},{28,24},{32,28},{36,32}... | collective-permute-start | bytes 552968 | tf_op jit(solution)/shard_map/ppermute | solution.py:129
  19.2 2.9 %collective-permute-start.3 = (f32[36,5,256]{2,0,1:T(8,128)S(1)}, f32[36,5,256]{2,0,1:T(8,128)S(1)}, u32[]{:S(2)}, u32[]{:S(2)}) collective-permute-start(f32[36,5,256]{2,0,1:T(8,128)S(1)} %pad_maximum_fusion.7), channel_id=1, source_target_pairs={{0,4},{4,8},{8,12},{12,16},{16,20},{20,24},{24,28},{28,32},{32,36}... | collective-permute-start | bytes 552968 | tf_op jit(solution)/shard_map/ppermute | solution.py:128
  26.1 4.4 %collective-permute-done.3 = f32[36,5,256]{2,0,1:T(8,128)S(1)} collective-permute-done((f32[36,5,256]{2,0,1:T(8,128)S(1)}, f32[36,5,256]{2,0,1:T(8,128)S(1)}, u32[]{:S(2)}, u32[]{:S(2)}) %collective-permute-start.3) | collective-permute-done | bytes 184352 | tf_op jit(solution)/shard_map/ppermute | solution.py:128
  32.0 1.3 %collective-permute-start.4 = (f32[36,68,5]{1,0,2:T(8,128)S(1)}, f32[36,68,5]{1,0,2:T(8,128)S(1)}, u32[]{:S(2)}, u32[]{:S(2)}) collective-permute-start(f32[36,68,5]{1,0,2:T(8,128)S(1)} %pad_maximum_fusion.13), channel_id=1, source_target_pairs={{1,0},{2,1},{3,2},{5,4},{6,5},{7,6},{9,8},{10,9},{11,10},{13,12},{... | collective-permute-start | bytes 146888 | tf_op jit(solution)/shard_map/ppermute | solution.py:150
  34.5 4.6 %collective-permute-start.5 = (f32[36,68,5]{1,0,2:T(8,128)S(1)}, f32[36,68,5]{1,0,2:T(8,128)S(1)}, u32[]{:S(2)}, u32[]{:S(2)}) collective-permute-start(f32[36,68,5]{1,0,2:T(8,128)S(1)} %pad_maximum_fusion.14), channel_id=1, source_target_pairs={{0,1},{1,2},{2,3},{4,5},{5,6},{6,7},{8,9},{9,10},{10,11},{12,13},{... | collective-permute-start | bytes 146888 | tf_op jit(solution)/shard_map/ppermute | solution.py:147
  39.4 0.8 pad_maximum_fusion.4.xc
  40.2 0.9 pad_maximum_fusion.5.xu
  42.5 0.8 slice.498
  43.3 1.6 %copy.168 = f32[36,68,2]{2,1,0:T(8,128)} copy(f32[36,68,2]{1,0,2:T(8,128)S(1)} %slice.498) | data formatting | bytes 39168 | tf_op jit(solution)/shard_map/slice | solution.py:160
  44.9 3.2 %pad_maximum_fusion.yt = f32[36,68,128]{2,1,0:T(8,128)} fusion(f32[36,68,2]{2,1,0:T(8,128)} %copy.168, f32[36,68,6]{2,1,0:T(8,128)S(1)} %copy.167, f32[36,68,2]{2,1,0:T(8,128)S(1)} %copy.166, f32[128]{0:T(128)S(1)} %pad.68.clone), kind=kLoop, calls=%fused_computation | loop fusion | flops 940032 | bytes 1351808 | tf_op jit(solution)/shard_map/concatenate | solution.py:160
  48.1 22.9 %shard_map.95 = (f32[1,32,64,256]{3,2,1,0:T(8,128)}, f32[8,32,128]{2,1,0:T(8,128)}) custom-call(s32[4]{0:T(128)} %pad_add_fusion.place, f32[8,32]{1,0:T(8,128)} %convert_divide_fusion.weights, f32[32,64,256]{2,1,0:T(8,128)} %bitcast.155, bf16[3,1,32,64,256]{4,3,2,1,0:T(8,128)(2,1)} %v_ref.1, bf16[1,32,64,256]{3,2,1,0:T(8,128)(2,1)} %poro_ref.1, ...), custom_call_target="tpu_custom_call" | custom-call | flops 104857600 | bytes 20971520 | tf_op jit(solution)/shard_map/pallas_call | solution.py:273
  71.0 1.9 %collective-permute-start.6 = (f32[8,32,128]{2,1,0:T(8,128)}, f32[8,32,128]{2,1,0:T(8,128)S(1)}, u32[]{:S(2)}, u32[]{:S(2)}) collective-permute-start(f32[8,32,128]{2,1,0:T(8,128)} %get-tuple-element.16), channel_id=1, source_target_pairs={{0,192},{64,0},{128,64},{1,193},{65,1},{129,65},{2,194},{66,2},{13... | collective-permute-start | bytes 393224 | tf_op jit(solution)/shard_map/ppermute | solution.py:366
  72.9 6.5 %collective-permute-start.7 = (f32[8,32,128]{2,1,0:T(8,128)}, f32[8,32,128]{2,1,0:T(8,128)S(1)}, u32[]{:S(2)}, u32[]{:S(2)}) collective-permute-start(f32[8,32,128]{2,1,0:T(8,128)} %get-tuple-element.16), channel_id=1, source_target_pairs={{0,128},{64,192},{128,0},{1,129},{65,193},{129,1},{2,130},{66,194}... | collective-permute-start | bytes 393224 | tf_op jit(solution)/shard_map/ppermute | solution.py:366
  79.4 1.3 %collective-permute-start.8 = (f32[8,32,128]{2,1,0:T(8,128)}, f32[8,32,128]{2,1,0:T(8,128)S(1)}, u32[]{:S(2)}, u32[]{:S(2)}) collective-permute-start(f32[8,32,128]{2,1,0:T(8,128)} %get-tuple-element.16), channel_id=1, source_target_pairs={{0,64},{64,128},{128,192},{1,65},{65,129},{129,193},{2,66},{66,130... | collective-permute-start | bytes 393224 | tf_op jit(solution)/shard_map/ppermute | solution.py:366
  80.8 1.7 %collective-permute-done.7 = f32[8,32,128]{2,1,0:T(8,128)S(1)} collective-permute-done((f32[8,32,128]{2,1,0:T(8,128)}, f32[8,32,128]{2,1,0:T(8,128)S(1)}, u32[]{:S(2)}, u32[]{:S(2)}) %collective-permute-start.7) | collective-permute-done | bytes 131104 | tf_op jit(solution)/shard_map/ppermute | solution.py:366
  82.6 1.0 select_add_fusion
  83.6 3.1 %collective-permute-start.10 = (f32[16,3,128]{2,1,0:T(4,128)S(1)}, f32[16,3,128]{2,1,0:T(4,128)S(1)}, u32[]{:S(2)}, u32[]{:S(2)}) collective-permute-start(f32[16,3,128]{2,1,0:T(4,128)S(1)} %get-tuple-element.50), channel_id=1, source_target_pairs={{4,0},{8,4},{12,8},{16,12},{20,16},{24,20},{28,24},{32,28},{36,32}... | collective-permute-start | bytes 73736 | tf_op jit(solution)/shard_map/ppermute | solution.py:28
  86.7 4.3 %collective-permute-start.9 = (f32[16,3,128]{2,1,0:T(4,128)S(1)}, f32[16,3,128]{2,1,0:T(4,128)S(1)}, u32[]{:S(2)}, u32[]{:S(2)}) collective-permute-start(f32[16,3,128]{2,1,0:T(4,128)S(1)} %get-tuple-element.49), channel_id=1, source_target_pairs={{0,4},{4,8},{8,12},{12,16},{16,20},{20,24},{24,28},{28,32},{32,36}... | collective-permute-start | bytes 73736 | tf_op jit(solution)/shard_map/ppermute | solution.py:27
  91.0 5.3 %collective-permute-done.9 = f32[16,3,128]{2,1,0:T(4,128)S(1)} collective-permute-done((f32[16,3,128]{2,1,0:T(4,128)S(1)}, f32[16,3,128]{2,1,0:T(4,128)S(1)}, u32[]{:S(2)}, u32[]{:S(2)}) %collective-permute-start.9) | collective-permute-done | bytes 24608 | tf_op jit(solution)/shard_map/ppermute | solution.py:27
  96.5 3.8 %collective-permute-start.11 = (f32[16,38,3]{2,1,0:T(8,128)S(1)}, f32[16,38,3]{2,1,0:T(8,128)S(1)}, u32[]{:S(2)}, u32[]{:S(2)}) collective-permute-start(f32[16,38,3]{2,1,0:T(8,128)S(1)} %get-tuple-element.31), channel_id=1, source_target_pairs={{0,1},{1,2},{2,3},{4,5},{5,6},{6,7},{8,9},{9,10},{10,11},{12,13},{... | collective-permute-start | bytes 21896 | tf_op jit(solution)/shard_map/ppermute | solution.py:27
  100.3 1.5 %collective-permute-start.12 = (f32[16,38,3]{2,1,0:T(8,128)S(1)}, f32[16,38,3]{2,1,0:T(8,128)S(1)}, u32[]{:S(2)}, u32[]{:S(2)}) collective-permute-start(f32[16,38,3]{2,1,0:T(8,128)S(1)} %get-tuple-element.32), channel_id=1, source_target_pairs={{1,0},{2,1},{3,2},{5,4},{6,5},{7,6},{9,8},{10,9},{11,10},{13,12},{... | collective-permute-start | bytes 21896 | tf_op jit(solution)/shard_map/ppermute | solution.py:28
  102.1 5.3 %collective-permute-done.11 = f32[16,38,3]{2,1,0:T(8,128)S(1)} collective-permute-done((f32[16,38,3]{2,1,0:T(8,128)S(1)}, f32[16,38,3]{2,1,0:T(8,128)S(1)}, u32[]{:S(2)}, u32[]{:S(2)}) %collective-permute-start.11) | collective-permute-done | bytes 7328 | tf_op jit(solution)/shard_map/ppermute | solution.py:27
  107.4 4.1 %collective-permute-done.12 = f32[16,38,3]{2,1,0:T(8,128)S(1)} collective-permute-done((f32[16,38,3]{2,1,0:T(8,128)S(1)}, f32[16,38,3]{2,1,0:T(8,128)S(1)}, u32[]{:S(2)}, u32[]{:S(2)}) %collective-permute-start.12) | collective-permute-done | bytes 7328 | tf_op jit(solution)/shard_map/ppermute | solution.py:28
  112.0 1.1 fusion.41
  113.5 1.1 fusion.40
  114.6 1.2 %fusion.64 = f32[1,8,32,128]{3,2,1,0:T(8,128)} fusion(f32[1,8,34,130]{3,2,1,0:T(8,128)S(1)} %fusion.40, f32[8,32,128]{2,1,0:T(8,128)S(1)} %select_add_fusion, f32[16,38,3]{2,1,0:T(8,128)S(1)} %collective-permute-done.12, f32[16,3,128]{2,1,0:T(4,128)S(1)} %collective-permute-done.10, f32[8,32,128]{2,1,0:T(8,128)S(1)} %dynamic-slice_bitcast_fusion, ...), kind=kLoop, calls=%fused_computation.122 | loop fusion | flops 1540096 | bytes 2560000 | tf_op jit(solution)/shard_map/jit(_where)/select_n | solution.py:471
  (122 shorter events, 12.8 us)
Async XLA Ops:
  0.6 80.2 %copy-start = (f32[4,8,32,128]{3,2,1,0:T(8,128)S(1)}, f32[4,8,32,128]{3,2,1,0:T(8,128)}, u32[]{:S(2)}) copy-start(f32[4,8,32,128]{3,2,1,0:T(8,128)} %param.13) | copy-start | bytes 1572868
  0.6 1.9 %copy-start.1 = (bf16[3,1,32,64,256]{4,3,2,1,0:T(8,128)(2,1)S(1)}, bf16[3,1,32,64,256]{4,3,2,1,0:T(8,128)(2,1)}, u32[]{:S(2)}) copy-start(bf16[3,1,32,64,256]{4,3,2,1,0:T(8,128)(2,1)} %v_ref.1) | copy-start | bytes 9437188
  2.6 1.6 %copy-start.2 = (f32[1,32,64,256]{3,2,1,0:T(8,128)S(1)}, f32[1,32,64,256]{3,2,1,0:T(8,128)}, u32[]{:S(2)}) copy-start(f32[1,32,64,256]{3,2,1,0:T(8,128)} %param.7) | copy-start | bytes 6291460
  6.9 3.9 %copy-start.6 = (s32[8]{0:T(128)S(1)}, s32[8]{0:T(128)}, u32[]{:S(2)}) copy-start(s32[8]{0:T(128)} %param.11) | copy-start | bytes 100
  6.9 4.1 %copy-start.5 = (s32[4,2]{0,1:T(2,128)S(1)}, s32[4,2]{0,1:T(2,128)}, u32[]{:S(2)}) copy-start(s32[4,2]{0,1:T(2,128)} %param.12) | copy-start | bytes 100
  6.9 7.6 %collective-permute-start = (f32[5,64,256]{2,1,0:T(8,128)S(1)}, f32[5,64,256]{2,1,0:T(8,128)S(1)}, u32[]{:S(2)}, u32[]{:S(2)}) collective-permute-start(f32[5,64,256]{2,1,0:T(8,128)S(1)} %get-tuple-element.10), channel_id=1, source_target_pairs={{0,64},{64,128},{1,65},{65,129},{2,66},{66,130},{3,67},{67,131},{4... | collective-permute-start | bytes 983048 | tf_op jit(solution)/shard_map/ppermute | solution.py:108
  8.9 5.7 %collective-permute-start.1 = (f32[5,64,256]{2,1,0:T(8,128)S(1)}, f32[5,64,256]{2,1,0:T(8,128)S(1)}, u32[]{:S(2)}, u32[]{:S(2)}) collective-permute-start(f32[5,64,256]{2,1,0:T(8,128)S(1)} %get-tuple-element.11), channel_id=1, source_target_pairs={{64,0},{128,64},{65,1},{129,65},{66,2},{130,66},{67,3},{131,67},{6... | collective-permute-start | bytes 983048 | tf_op jit(solution)/shard_map/ppermute | solution.py:109
  14.7 11.2 %collective-permute-start.2 = (f32[36,5,256]{2,0,1:T(8,128)S(1)}, f32[36,5,256]{2,0,1:T(8,128)S(1)}, u32[]{:S(2)}, u32[]{:S(2)}) collective-permute-start(f32[36,5,256]{2,0,1:T(8,128)S(1)} %pad_maximum_fusion.6), channel_id=1, source_target_pairs={{4,0},{8,4},{12,8},{16,12},{20,16},{24,20},{28,24},{32,28},{36,32}... | collective-permute-start | bytes 552968 | tf_op jit(solution)/shard_map/ppermute | solution.py:129
  19.2 11.3 %collective-permute-start.3 = (f32[36,5,256]{2,0,1:T(8,128)S(1)}, f32[36,5,256]{2,0,1:T(8,128)S(1)}, u32[]{:S(2)}, u32[]{:S(2)}) collective-permute-start(f32[36,5,256]{2,0,1:T(8,128)S(1)} %pad_maximum_fusion.7), channel_id=1, source_target_pairs={{0,4},{4,8},{8,12},{12,16},{16,20},{20,24},{24,28},{28,32},{32,36}... | collective-permute-start | bytes 552968 | tf_op jit(solution)/shard_map/ppermute | solution.py:128
  32.0 9.1 %collective-permute-start.4 = (f32[36,68,5]{1,0,2:T(8,128)S(1)}, f32[36,68,5]{1,0,2:T(8,128)S(1)}, u32[]{:S(2)}, u32[]{:S(2)}) collective-permute-start(f32[36,68,5]{1,0,2:T(8,128)S(1)} %pad_maximum_fusion.13), channel_id=1, source_target_pairs={{1,0},{2,1},{3,2},{5,4},{6,5},{7,6},{9,8},{10,9},{11,10},{13,12},{... | collective-permute-start | bytes 146888 | tf_op jit(solution)/shard_map/ppermute | solution.py:150
  34.5 6.8 %collective-permute-start.5 = (f32[36,68,5]{1,0,2:T(8,128)S(1)}, f32[36,68,5]{1,0,2:T(8,128)S(1)}, u32[]{:S(2)}, u32[]{:S(2)}) collective-permute-start(f32[36,68,5]{1,0,2:T(8,128)S(1)} %pad_maximum_fusion.14), channel_id=1, source_target_pairs={{0,1},{1,2},{2,3},{4,5},{5,6},{6,7},{8,9},{9,10},{10,11},{12,13},{... | collective-permute-start | bytes 146888 | tf_op jit(solution)/shard_map/ppermute | solution.py:147
  41.3 0.6 copy-start.4
  71.0 9.8 %collective-permute-start.6 = (f32[8,32,128]{2,1,0:T(8,128)}, f32[8,32,128]{2,1,0:T(8,128)S(1)}, u32[]{:S(2)}, u32[]{:S(2)}) collective-permute-start(f32[8,32,128]{2,1,0:T(8,128)} %get-tuple-element.16), channel_id=1, source_target_pairs={{0,192},{64,0},{128,64},{1,193},{65,1},{129,65},{2,194},{66,2},{13... | collective-permute-start | bytes 393224 | tf_op jit(solution)/shard_map/ppermute | solution.py:366
  72.9 9.6 %collective-permute-start.7 = (f32[8,32,128]{2,1,0:T(8,128)}, f32[8,32,128]{2,1,0:T(8,128)S(1)}, u32[]{:S(2)}, u32[]{:S(2)}) collective-permute-start(f32[8,32,128]{2,1,0:T(8,128)} %get-tuple-element.16), channel_id=1, source_target_pairs={{0,128},{64,192},{128,0},{1,129},{65,193},{129,1},{2,130},{66,194}... | collective-permute-start | bytes 393224 | tf_op jit(solution)/shard_map/ppermute | solution.py:366
  79.4 3.1 %collective-permute-start.8 = (f32[8,32,128]{2,1,0:T(8,128)}, f32[8,32,128]{2,1,0:T(8,128)S(1)}, u32[]{:S(2)}, u32[]{:S(2)}) collective-permute-start(f32[8,32,128]{2,1,0:T(8,128)} %get-tuple-element.16), channel_id=1, source_target_pairs={{0,64},{64,128},{128,192},{1,65},{65,129},{129,193},{2,66},{66,130... | collective-permute-start | bytes 393224 | tf_op jit(solution)/shard_map/ppermute | solution.py:366
  83.5 31.1 %copy-start.3 = (f32[8,32,128]{2,1,0:T(8,128)}, f32[8,32,128]{2,1,0:T(8,128)S(1)}, u32[]{:S(2)}) copy-start(f32[8,32,128]{2,1,0:T(8,128)S(1)} %select_add_fusion) | copy-start | bytes 393220
  83.6 7.5 %collective-permute-start.10 = (f32[16,3,128]{2,1,0:T(4,128)S(1)}, f32[16,3,128]{2,1,0:T(4,128)S(1)}, u32[]{:S(2)}, u32[]{:S(2)}) collective-permute-start(f32[16,3,128]{2,1,0:T(4,128)S(1)} %get-tuple-element.50), channel_id=1, source_target_pairs={{4,0},{8,4},{12,8},{16,12},{20,16},{24,20},{28,24},{32,28},{36,32}... | collective-permute-start | bytes 73736 | tf_op jit(solution)/shard_map/ppermute | solution.py:28
  86.7 9.7 %collective-permute-start.9 = (f32[16,3,128]{2,1,0:T(4,128)S(1)}, f32[16,3,128]{2,1,0:T(4,128)S(1)}, u32[]{:S(2)}, u32[]{:S(2)}) collective-permute-start(f32[16,3,128]{2,1,0:T(4,128)S(1)} %get-tuple-element.49), channel_id=1, source_target_pairs={{0,4},{4,8},{8,12},{12,16},{16,20},{20,24},{24,28},{28,32},{32,36}... | collective-permute-start | bytes 73736 | tf_op jit(solution)/shard_map/ppermute | solution.py:27
  96.5 10.9 %collective-permute-start.11 = (f32[16,38,3]{2,1,0:T(8,128)S(1)}, f32[16,38,3]{2,1,0:T(8,128)S(1)}, u32[]{:S(2)}, u32[]{:S(2)}) collective-permute-start(f32[16,38,3]{2,1,0:T(8,128)S(1)} %get-tuple-element.31), channel_id=1, source_target_pairs={{0,1},{1,2},{2,3},{4,5},{5,6},{6,7},{8,9},{9,10},{10,11},{12,13},{... | collective-permute-start | bytes 21896 | tf_op jit(solution)/shard_map/ppermute | solution.py:27
  100.3 11.2 %collective-permute-start.12 = (f32[16,38,3]{2,1,0:T(8,128)S(1)}, f32[16,38,3]{2,1,0:T(8,128)S(1)}, u32[]{:S(2)}, u32[]{:S(2)}) collective-permute-start(f32[16,38,3]{2,1,0:T(8,128)S(1)} %get-tuple-element.32), channel_id=1, source_target_pairs={{1,0},{2,1},{3,2},{5,4},{6,5},{7,6},{9,8},{10,9},{11,10},{13,12},{... | collective-permute-start | bytes 21896 | tf_op jit(solution)/shard_map/ppermute | solution.py:28

commit v15 on v14

--- a/solution.py
+++ b/solution.py
@@ -151,7 +151,7 @@
         jnp.concatenate([xz_c(slice(0, 2), ycols[2:4]), xz_u(0, ucols[:, 1])], 2), "gy", down
     )
 
-    xc = jnp.concatenate([ax[:, 0:2], jnp.zeros((nz + 4, 4, ny), f32), bx[:, 0:2]], 1)
+    xc = jnp.concatenate([ax[:, 0:2], bx[:, 0:2]], 1)
     xu_hi = jnp.swapaxes(ax[1:-1, 2:5], 0, 1)[:, :, None]
     xu_lo = jnp.swapaxes(bx[1:-1, 2:5], 0, 1)[:, :, None]
     xu = jnp.concatenate([xu_hi, xu_lo], 2)
@@ -194,8 +194,8 @@
         return carry
 
     lax.fori_loop(0, nz, put_c, 0)
-    F[:, 0:8, 0:ny] = xc[...]
-    F[:, wx - 8 : wx, 0:ny] = xc[...]
+    F[:, 6:8, 0:ny] = xc[:, 2:4]
+    F[:, wx - 8 : wx - 6, 0:ny] = xc[:, 0:2]
     F[:, 6 : 6 + nx + 4, ny:wy] = yt[...]
     for d in range(3):
         U[d, 0, 8 : 8 + nx, 0:ny] = zlo_u[d]

time: 116 us -> 121 us (1.043)
  the two profiles are of different devices: /device:TPU:128 before, /device:TPU:152 now
where the time goes in v15:
time: 121 us; the launch traced here: 120 us
  starting transfers between devices  38.3 us (32%)
  Pallas kernels  25.7 us (21%)
  waiting for transfers between devices  25.6 us (21%)
  local copies, waits for them, and re-layouts  16.1 us (13%)
  other arithmetic  13.4 us (11%)
  between operations  1.37 us (1%)
    pallas_call x1, Pallas kernels, transport_call(): pl.pallas_call(functools.partial(transport_kernel, grid), out_shape=(jax....  22.9 us
    ppermute x2, waiting for transfers between devices, with_halo(): before = lax.ppermute(last, axis, up)  11.6 us
    ppermute x2, starting transfers between devices, with_halo(): after = lax.ppermute(initial, axis, down)  9.59 us
    ppermute x3, starting transfers between devices, grp_sum(): received[shift] = lax.ppermute(partial, 'grp', pairs)  6.62 us
    ppermute x2, waiting for transfers between devices, with_halo(): after = lax.ppermute(initial, axis, down)  5.41 us
    ppermute x1, starting transfers between devices, transport_halo(): bx = lax.ppermute(send_up, 'gx', up)  4.93 us
    ppermute x1, starting transfers between devices, transport_halo(): lax.ppermute(jnp.concatenate([xz_c(slice(0, 2), ycols[2:4]), xz_u(0, ucol...  4.54 us
    ppermute x1, starting transfers between devices, transport_halo(): ax = lax.ppermute(send_dn, 'gx', down)  4.52 us
  transfers between devices with their start and end apart: 13, of which 7 were waited for; matrix products, arithmetic and copies ran while one was open for 10% of the time, Pallas kernels for 0%

profile of v15, /device:TPU:152, one launch (start us, length us, event | category | flops | bytes accessed | tf_op | source)
XLA Modules:
  0.0 120.4 jit_solution(14108346966363178473)
XLA Ops:
  0.7 1.9 %copy-done.1 = bf16[3,1,32,64,256]{4,3,2,1,0:T(8,128)(2,1)S(1)} copy-done((bf16[3,1,32,64,256]{4,3,2,1,0:T(8,128)(2,1)S(1)}, bf16[3,1,32,64,256]{4,3,2,1,0:T(8,128)(2,1)}, u32[]{:S(2)}) %copy-start.1) | copy-done | bytes 3145752
  2.6 1.6 %copy-done.2 = f32[1,32,64,256]{3,2,1,0:T(8,128)S(1)} copy-done((f32[1,32,64,256]{3,2,1,0:T(8,128)S(1)}, f32[1,32,64,256]{3,2,1,0:T(8,128)}, u32[]{:S(2)}) %copy-start.2) | copy-done | bytes 2097176
  4.2 2.8 %shard_map.94 = (f32[5,64,256]{2,1,0:T(8,128)S(1)}, f32[5,64,256]{2,1,0:T(8,128)S(1)}, f32[10,32,256]{2,1,0:T(8,128)S(1)}, f32[8,2048]{1,0:T(8,128)S(1)}, f32[3,8,2048]{2,1,0:T(8,128)S(1)}) custom-call(f32[2048,256]{1,0:T(8,128)S(1)} %bitcast.158, bf16[3,2048,256]{2,1,0:T(8,128)(2,1)S(1)} %bitcast.156), custom_call_target="tpu_custom_call" | custom-call | flops 33554432 | bytes 5242880 | tf_op jit(solution)/shard_map/pallas_call | solution.py:78
  6.9 1.9 %collective-permute-start = (f32[5,64,256]{2,1,0:T(8,128)S(1)}, f32[5,64,256]{2,1,0:T(8,128)S(1)}, u32[]{:S(2)}, u32[]{:S(2)}) collective-permute-start(f32[5,64,256]{2,1,0:T(8,128)S(1)} %get-tuple-element.10), channel_id=1, source_target_pairs={{0,64},{64,128},{1,65},{65,129},{2,66},{66,130},{3,67},{67,131},{4... | collective-permute-start | bytes 983048 | tf_op jit(solution)/shard_map/ppermute | solution.py:108
  8.9 1.3 %collective-permute-start.1 = (f32[5,64,256]{2,1,0:T(8,128)S(1)}, f32[5,64,256]{2,1,0:T(8,128)S(1)}, u32[]{:S(2)}, u32[]{:S(2)}) collective-permute-start(f32[5,64,256]{2,1,0:T(8,128)S(1)} %get-tuple-element.11), channel_id=1, source_target_pairs={{64,0},{128,64},{65,1},{129,65},{66,2},{130,66},{67,3},{131,67},{6... | collective-permute-start | bytes 983048 | tf_op jit(solution)/shard_map/ppermute | solution.py:109
  11.8 1.4 %subtract_multiply_fusion = f32[1,8,38,134]{3,2,1,0:T(8,128)S(1)} fusion(s32[]{:T(128)} %bitcast.36, s32[]{:T(128)} %bitcast.35, s32[134]{0:T(256)S(1)} %iota_add_fusion, s32[8,38]{1,0:T(8,128)S(1)} %broadcast_add_fusion), kind=kLoop, calls=%fused_computation.78 | loop fusion | flops 285152 | bytes 164704 | tf_op jit(solution)/shard_map/mul | solution.py:426
  14.6 4.9 %collective-permute-start.3 = (f32[36,5,256]{2,0,1:T(8,128)S(1)}, f32[36,5,256]{2,0,1:T(8,128)S(1)}, u32[]{:S(2)}, u32[]{:S(2)}) collective-permute-start(f32[36,5,256]{2,0,1:T(8,128)S(1)} %pad_maximum_fusion.6), channel_id=1, source_target_pairs={{0,4},{4,8},{8,12},{12,16},{16,20},{20,24},{24,28},{28,32},{32,36}... | collective-permute-start | bytes 552968 | tf_op jit(solution)/shard_map/ppermute | solution.py:128
  19.6 4.5 %collective-permute-start.2 = (f32[36,5,256]{2,0,1:T(8,128)S(1)}, f32[36,5,256]{2,0,1:T(8,128)S(1)}, u32[]{:S(2)}, u32[]{:S(2)}) collective-permute-start(f32[36,5,256]{2,0,1:T(8,128)S(1)} %pad_maximum_fusion.5), channel_id=1, source_target_pairs={{4,0},{8,4},{12,8},{16,12},{20,16},{24,20},{28,24},{32,28},{36,32}... | collective-permute-start | bytes 552968 | tf_op jit(solution)/shard_map/ppermute | solution.py:129
  27.9 4.0 %collective-permute-done.2 = f32[36,5,256]{2,0,1:T(8,128)S(1)} collective-permute-done((f32[36,5,256]{2,0,1:T(8,128)S(1)}, f32[36,5,256]{2,0,1:T(8,128)S(1)}, u32[]{:S(2)}, u32[]{:S(2)}) %collective-permute-start.2) | collective-permute-done | bytes 184352 | tf_op jit(solution)/shard_map/ppermute | solution.py:129
  33.8 1.3 %collective-permute-start.5 = (f32[36,68,5]{1,0,2:T(8,128)S(1)}, f32[36,68,5]{1,0,2:T(8,128)S(1)}, u32[]{:S(2)}, u32[]{:S(2)}) collective-permute-start(f32[36,68,5]{1,0,2:T(8,128)S(1)} %pad_maximum_fusion.14), channel_id=1, source_target_pairs={{0,1},{1,2},{2,3},{4,5},{5,6},{6,7},{8,9},{9,10},{10,11},{12,13},{... | collective-permute-start | bytes 146888 | tf_op jit(solution)/shard_map/ppermute | solution.py:147
  36.3 0.9 pad_maximum_fusion.4.xu
  38.0 4.5 %collective-permute-start.4 = (f32[36,68,5]{1,0,2:T(8,128)S(1)}, f32[36,68,5]{1,0,2:T(8,128)S(1)}, u32[]{:S(2)}, u32[]{:S(2)}) collective-permute-start(f32[36,68,5]{1,0,2:T(8,128)S(1)} %pad_maximum_fusion.13), channel_id=1, source_target_pairs={{1,0},{2,1},{3,2},{5,4},{6,5},{7,6},{9,8},{10,9},{11,10},{13,12},{... | collective-permute-start | bytes 146888 | tf_op jit(solution)/shard_map/ppermute | solution.py:150
  43.2 2.4 %collective-permute-done.4 = f32[36,68,5]{1,0,2:T(8,128)S(1)} collective-permute-done((f32[36,68,5]{1,0,2:T(8,128)S(1)}, f32[36,68,5]{1,0,2:T(8,128)S(1)}, u32[]{:S(2)}, u32[]{:S(2)}) %collective-permute-start.4) | collective-permute-done | bytes 48992 | tf_op jit(solution)/shard_map/ppermute | solution.py:150
  46.3 1.5 %copy.166 = f32[36,68,6]{2,1,0:T(8,128)S(1)} copy(f32[36,68,6]{1,0,2:T(8,128)} %bitcast.159) | data formatting | bytes 117504 | tf_op jit(solution)/shard_map/reshape | solution.py:158
  47.8 1.6 %copy.165 = f32[36,68,2]{2,1,0:T(8,128)} copy(f32[36,68,2]{1,0,2:T(8,128)S(1)} %slice-done) | data formatting | bytes 39168 | tf_op jit(solution)/shard_map/slice | solution.py:160
  49.4 3.2 %pad_maximum_fusion.yt = f32[36,68,128]{2,1,0:T(8,128)} fusion(f32[36,68,2]{2,1,0:T(8,128)S(1)} %copy.167, f32[36,68,6]{2,1,0:T(8,128)S(1)} %copy.166, f32[36,68,2]{2,1,0:T(8,128)} %copy.165, f32[128]{0:T(128)S(1)} %pad.68.clone), kind=kLoop, calls=%fused_computation | loop fusion | flops 940032 | bytes 1351808 | tf_op jit(solution)/shard_map/concatenate | solution.py:160
  52.5 22.9 %shard_map.95 = (f32[1,32,64,256]{3,2,1,0:T(8,128)}, f32[8,32,128]{2,1,0:T(8,128)}) custom-call(s32[4]{0:T(128)} %pad_add_fusion.place, f32[8,32]{1,0:T(8,128)} %convert_divide_fusion.weights, f32[32,64,256]{2,1,0:T(8,128)} %bitcast.157, bf16[3,1,32,64,256]{4,3,2,1,0:T(8,128)(2,1)} %v_ref.1, bf16[1,32,64,256]{3,2,1,0:T(8,128)(2,1)} %poro_ref.1, ...), custom_call_target="tpu_custom_call" | custom-call | flops 104857600 | bytes 20971520 | tf_op jit(solution)/shard_map/pallas_call | solution.py:273
  75.4 1.9 %collective-permute-start.6 = (f32[8,32,128]{2,1,0:T(8,128)}, f32[8,32,128]{2,1,0:T(8,128)S(1)}, u32[]{:S(2)}, u32[]{:S(2)}) collective-permute-start(f32[8,32,128]{2,1,0:T(8,128)} %get-tuple-element.16), channel_id=1, source_target_pairs={{0,192},{64,0},{128,64},{1,193},{65,1},{129,65},{2,194},{66,2},{13... | collective-permute-start | bytes 393224 | tf_op jit(solution)/shard_map/ppermute | solution.py:366
  77.3 3.4 %collective-permute-start.7 = (f32[8,32,128]{2,1,0:T(8,128)}, f32[8,32,128]{2,1,0:T(8,128)S(1)}, u32[]{:S(2)}, u32[]{:S(2)}) collective-permute-start(f32[8,32,128]{2,1,0:T(8,128)} %get-tuple-element.16), channel_id=1, source_target_pairs={{0,128},{64,192},{128,0},{1,129},{65,193},{129,1},{2,130},{66,194}... | collective-permute-start | bytes 393224 | tf_op jit(solution)/shard_map/ppermute | solution.py:366
  80.8 1.3 %collective-permute-start.8 = (f32[8,32,128]{2,1,0:T(8,128)}, f32[8,32,128]{2,1,0:T(8,128)S(1)}, u32[]{:S(2)}, u32[]{:S(2)}) collective-permute-start(f32[8,32,128]{2,1,0:T(8,128)} %get-tuple-element.16), channel_id=1, source_target_pairs={{0,64},{64,128},{128,192},{1,65},{65,129},{129,193},{2,66},{66,130... | collective-permute-start | bytes 393224 | tf_op jit(solution)/shard_map/ppermute | solution.py:366
  82.2 2.2 %collective-permute-done.7 = f32[8,32,128]{2,1,0:T(8,128)S(1)} collective-permute-done((f32[8,32,128]{2,1,0:T(8,128)}, f32[8,32,128]{2,1,0:T(8,128)S(1)}, u32[]{:S(2)}, u32[]{:S(2)}) %collective-permute-start.7) | collective-permute-done | bytes 131104 | tf_op jit(solution)/shard_map/ppermute | solution.py:366
  84.4 1.0 select_add_fusion
  85.4 5.3 %collective-permute-start.10 = (f32[16,3,128]{2,1,0:T(4,128)S(1)}, f32[16,3,128]{2,1,0:T(4,128)S(1)}, u32[]{:S(2)}, u32[]{:S(2)}) collective-permute-start(f32[16,3,128]{2,1,0:T(4,128)S(1)} %get-tuple-element.50), channel_id=1, source_target_pairs={{4,0},{8,4},{12,8},{16,12},{20,16},{24,20},{28,24},{32,28},{36,32}... | collective-permute-start | bytes 73736 | tf_op jit(solution)/shard_map/ppermute | solution.py:28
  90.7 2.1 %collective-permute-start.9 = (f32[16,3,128]{2,1,0:T(4,128)S(1)}, f32[16,3,128]{2,1,0:T(4,128)S(1)}, u32[]{:S(2)}, u32[]{:S(2)}) collective-permute-start(f32[16,3,128]{2,1,0:T(4,128)S(1)} %get-tuple-element.49), channel_id=1, source_target_pairs={{0,4},{4,8},{8,12},{12,16},{16,20},{20,24},{24,28},{28,32},{32,36}... | collective-permute-start | bytes 73736 | tf_op jit(solution)/shard_map/ppermute | solution.py:27
  92.9 7.4 %collective-permute-done.9 = f32[16,3,128]{2,1,0:T(4,128)S(1)} collective-permute-done((f32[16,3,128]{2,1,0:T(4,128)S(1)}, f32[16,3,128]{2,1,0:T(4,128)S(1)}, u32[]{:S(2)}, u32[]{:S(2)}) %collective-permute-start.9) | collective-permute-done | bytes 24608 | tf_op jit(solution)/shard_map/ppermute | solution.py:27
  100.6 4.3 %collective-permute-start.12 = (f32[16,38,3]{2,1,0:T(8,128)S(1)}, f32[16,38,3]{2,1,0:T(8,128)S(1)}, u32[]{:S(2)}, u32[]{:S(2)}) collective-permute-start(f32[16,38,3]{2,1,0:T(8,128)S(1)} %get-tuple-element.32), channel_id=1, source_target_pairs={{1,0},{2,1},{3,2},{5,4},{6,5},{7,6},{9,8},{10,9},{11,10},{13,12},{... | collective-permute-start | bytes 21896 | tf_op jit(solution)/shard_map/ppermute | solution.py:28
  104.9 1.5 %collective-permute-start.11 = (f32[16,38,3]{2,1,0:T(8,128)S(1)}, f32[16,38,3]{2,1,0:T(8,128)S(1)}, u32[]{:S(2)}, u32[]{:S(2)}) collective-permute-start(f32[16,38,3]{2,1,0:T(8,128)S(1)} %get-tuple-element.31), channel_id=1, source_target_pairs={{0,1},{1,2},{2,3},{4,5},{5,6},{6,7},{8,9},{9,10},{10,11},{12,13},{... | collective-permute-start | bytes 21896 | tf_op jit(solution)/shard_map/ppermute | solution.py:27
  106.7 5.3 %collective-permute-done.12 = f32[16,38,3]{2,1,0:T(8,128)S(1)} collective-permute-done((f32[16,38,3]{2,1,0:T(8,128)S(1)}, f32[16,38,3]{2,1,0:T(8,128)S(1)}, u32[]{:S(2)}, u32[]{:S(2)}) %collective-permute-start.12) | collective-permute-done | bytes 7328 | tf_op jit(solution)/shard_map/ppermute | solution.py:28
  112.0 4.1 %collective-permute-done.11 = f32[16,38,3]{2,1,0:T(8,128)S(1)} collective-permute-done((f32[16,38,3]{2,1,0:T(8,128)S(1)}, f32[16,38,3]{2,1,0:T(8,128)S(1)}, u32[]{:S(2)}, u32[]{:S(2)}) %collective-permute-start.11) | collective-permute-done | bytes 7328 | tf_op jit(solution)/shard_map/ppermute | solution.py:27
  116.6 1.1 fusion.41
  118.1 1.1 fusion.40
  119.2 1.2 fusion.64
  (120 shorter events, 13.2 us)
Async XLA Ops:
  0.6 81.5 %copy-start = (f32[4,8,32,128]{3,2,1,0:T(8,128)S(1)}, f32[4,8,32,128]{3,2,1,0:T(8,128)}, u32[]{:S(2)}) copy-start(f32[4,8,32,128]{3,2,1,0:T(8,128)} %param.13) | copy-start | bytes 1572868
  0.6 1.9 %copy-start.1 = (bf16[3,1,32,64,256]{4,3,2,1,0:T(8,128)(2,1)S(1)}, bf16[3,1,32,64,256]{4,3,2,1,0:T(8,128)(2,1)}, u32[]{:S(2)}) copy-start(bf16[3,1,32,64,256]{4,3,2,1,0:T(8,128)(2,1)} %v_ref.1) | copy-start | bytes 9437188
  2.6 1.6 %copy-start.2 = (f32[1,32,64,256]{3,2,1,0:T(8,128)S(1)}, f32[1,32,64,256]{3,2,1,0:T(8,128)}, u32[]{:S(2)}) copy-start(f32[1,32,64,256]{3,2,1,0:T(8,128)} %param.7) | copy-start | bytes 6291460
  4.2 6.0 %copy-start.6 = (s32[8]{0:T(128)S(1)}, s32[8]{0:T(128)}, u32[]{:S(2)}) copy-start(s32[8]{0:T(128)} %param.11) | copy-start | bytes 100
  6.9 4.0 %copy-start.5 = (s32[4,2]{0,1:T(2,128)S(1)}, s32[4,2]{0,1:T(2,128)}, u32[]{:S(2)}) copy-start(s32[4,2]{0,1:T(2,128)} %param.12) | copy-start | bytes 100
  6.9 7.5 %collective-permute-start = (f32[5,64,256]{2,1,0:T(8,128)S(1)}, f32[5,64,256]{2,1,0:T(8,128)S(1)}, u32[]{:S(2)}, u32[]{:S(2)}) collective-permute-start(f32[5,64,256]{2,1,0:T(8,128)S(1)} %get-tuple-element.10), channel_id=1, source_target_pairs={{0,64},{64,128},{1,65},{65,129},{2,66},{66,130},{3,67},{67,131},{4... | collective-permute-start | bytes 983048 | tf_op jit(solution)/shard_map/ppermute | solution.py:108
  8.9 5.5 %collective-permute-start.1 = (f32[5,64,256]{2,1,0:T(8,128)S(1)}, f32[5,64,256]{2,1,0:T(8,128)S(1)}, u32[]{:S(2)}, u32[]{:S(2)}) collective-permute-start(f32[5,64,256]{2,1,0:T(8,128)S(1)} %get-tuple-element.11), channel_id=1, source_target_pairs={{64,0},{128,64},{65,1},{129,65},{66,2},{130,66},{67,3},{131,67},{6... | collective-permute-start | bytes 983048 | tf_op jit(solution)/shard_map/ppermute | solution.py:109
  14.6 13.3 %collective-permute-start.3 = (f32[36,5,256]{2,0,1:T(8,128)S(1)}, f32[36,5,256]{2,0,1:T(8,128)S(1)}, u32[]{:S(2)}, u32[]{:S(2)}) collective-permute-start(f32[36,5,256]{2,0,1:T(8,128)S(1)} %pad_maximum_fusion.6), channel_id=1, source_target_pairs={{0,4},{4,8},{8,12},{12,16},{16,20},{20,24},{24,28},{28,32},{32,36}... | collective-permute-start | bytes 552968 | tf_op jit(solution)/shard_map/ppermute | solution.py:128
  19.6 12.3 %collective-permute-start.2 = (f32[36,5,256]{2,0,1:T(8,128)S(1)}, f32[36,5,256]{2,0,1:T(8,128)S(1)}, u32[]{:S(2)}, u32[]{:S(2)}) collective-permute-start(f32[36,5,256]{2,0,1:T(8,128)S(1)} %pad_maximum_fusion.5), channel_id=1, source_target_pairs={{4,0},{8,4},{12,8},{16,12},{20,16},{24,20},{28,24},{32,28},{36,32}... | collective-permute-start | bytes 552968 | tf_op jit(solution)/shard_map/ppermute | solution.py:129
  33.8 8.7 %collective-permute-start.5 = (f32[36,68,5]{1,0,2:T(8,128)S(1)}, f32[36,68,5]{1,0,2:T(8,128)S(1)}, u32[]{:S(2)}, u32[]{:S(2)}) collective-permute-start(f32[36,68,5]{1,0,2:T(8,128)S(1)} %pad_maximum_fusion.14), channel_id=1, source_target_pairs={{0,1},{1,2},{2,3},{4,5},{5,6},{6,7},{8,9},{9,10},{10,11},{12,13},{... | collective-permute-start | bytes 146888 | tf_op jit(solution)/shard_map/ppermute | solution.py:147
  38.0 7.6 %collective-permute-start.4 = (f32[36,68,5]{1,0,2:T(8,128)S(1)}, f32[36,68,5]{1,0,2:T(8,128)S(1)}, u32[]{:S(2)}, u32[]{:S(2)}) collective-permute-start(f32[36,68,5]{1,0,2:T(8,128)S(1)} %pad_maximum_fusion.13), channel_id=1, source_target_pairs={{1,0},{2,1},{3,2},{5,4},{6,5},{7,6},{9,8},{10,9},{11,10},{13,12},{... | collective-permute-start | bytes 146888 | tf_op jit(solution)/shard_map/ppermute | solution.py:150
  45.6 0.7 copy-start.4
  46.3 1.5 %slice-start = ((f32[36,68,5]{1,0,2:T(8,128)}), f32[36,68,2]{1,0,2:T(8,128)S(1)}, s32[]{:S(2)}) async-start(f32[36,68,5]{1,0,2:T(8,128)} %copy-done.4), calls=%async_computation | async-start | bytes 81920 | tf_op jit(solution)/shard_map/slice | solution.py:160
  75.4 6.8 %collective-permute-start.6 = (f32[8,32,128]{2,1,0:T(8,128)}, f32[8,32,128]{2,1,0:T(8,128)S(1)}, u32[]{:S(2)}, u32[]{:S(2)}) collective-permute-start(f32[8,32,128]{2,1,0:T(8,128)} %get-tuple-element.16), channel_id=1, source_target_pairs={{0,192},{64,0},{128,64},{1,193},{65,1},{129,65},{2,194},{66,2},{13... | collective-permute-start | bytes 393224 | tf_op jit(solution)/shard_map/ppermute | solution.py:366
  77.3 7.1 %collective-permute-start.7 = (f32[8,32,128]{2,1,0:T(8,128)}, f32[8,32,128]{2,1,0:T(8,128)S(1)}, u32[]{:S(2)}, u32[]{:S(2)}) collective-permute-start(f32[8,32,128]{2,1,0:T(8,128)} %get-tuple-element.16), channel_id=1, source_target_pairs={{0,128},{64,192},{128,0},{1,129},{65,193},{129,1},{2,130},{66,194}... | collective-permute-start | bytes 393224 | tf_op jit(solution)/shard_map/ppermute | solution.py:366
  80.8 3.6 %collective-permute-start.8 = (f32[8,32,128]{2,1,0:T(8,128)}, f32[8,32,128]{2,1,0:T(8,128)S(1)}, u32[]{:S(2)}, u32[]{:S(2)}) collective-permute-start(f32[8,32,128]{2,1,0:T(8,128)} %get-tuple-element.16), channel_id=1, source_target_pairs={{0,64},{64,128},{128,192},{1,65},{65,129},{129,193},{2,66},{66,130... | collective-permute-start | bytes 393224 | tf_op jit(solution)/shard_map/ppermute | solution.py:366
  85.4 33.8 %copy-start.3 = (f32[8,32,128]{2,1,0:T(8,128)}, f32[8,32,128]{2,1,0:T(8,128)S(1)}, u32[]{:S(2)}) copy-start(f32[8,32,128]{2,1,0:T(8,128)S(1)} %select_add_fusion) | copy-start | bytes 393220
  85.4 7.5 %collective-permute-start.10 = (f32[16,3,128]{2,1,0:T(4,128)S(1)}, f32[16,3,128]{2,1,0:T(4,128)S(1)}, u32[]{:S(2)}, u32[]{:S(2)}) collective-permute-start(f32[16,3,128]{2,1,0:T(4,128)S(1)} %get-tuple-element.50), channel_id=1, source_target_pairs={{4,0},{8,4},{12,8},{16,12},{20,16},{24,20},{28,24},{32,28},{36,32}... | collective-permute-start | bytes 73736 | tf_op jit(solution)/shard_map/ppermute | solution.py:28
  90.7 9.7 %collective-permute-start.9 = (f32[16,3,128]{2,1,0:T(4,128)S(1)}, f32[16,3,128]{2,1,0:T(4,128)S(1)}, u32[]{:S(2)}, u32[]{:S(2)}) collective-permute-start(f32[16,3,128]{2,1,0:T(4,128)S(1)} %get-tuple-element.49), channel_id=1, source_target_pairs={{0,4},{4,8},{8,12},{12,16},{16,20},{20,24},{24,28},{28,32},{32,36}... | collective-permute-start | bytes 73736 | tf_op jit(solution)/shard_map/ppermute | solution.py:27
  100.6 11.5 %collective-permute-start.12 = (f32[16,38,3]{2,1,0:T(8,128)S(1)}, f32[16,38,3]{2,1,0:T(8,128)S(1)}, u32[]{:S(2)}, u32[]{:S(2)}) collective-permute-start(f32[16,38,3]{2,1,0:T(8,128)S(1)} %get-tuple-element.32), channel_id=1, source_target_pairs={{1,0},{2,1},{3,2},{5,4},{6,5},{7,6},{9,8},{10,9},{11,10},{13,12},{... | collective-permute-start | bytes 21896 | tf_op jit(solution)/shard_map/ppermute | solution.py:28
  104.9 11.2 %collective-permute-start.11 = (f32[16,38,3]{2,1,0:T(8,128)S(1)}, f32[16,38,3]{2,1,0:T(8,128)S(1)}, u32[]{:S(2)}, u32[]{:S(2)}) collective-permute-start(f32[16,38,3]{2,1,0:T(8,128)S(1)} %get-tuple-element.31), channel_id=1, source_target_pairs={{0,1},{1,2},{2,3},{4,5},{5,6},{6,7},{8,9},{9,10},{10,11},{12,13},{... | collective-permute-start | bytes 21896 | tf_op jit(solution)/shard_map/ppermute | solution.py:27
